TPU v7x, 256 devices: a whole 4x4x8 slice. The times are simulated.
256 devices in a mesh: grp: 4 (over y_lo, core), shard: 64 (over z, x, y_hi).
Axes of the slice: x: 4, y: 4 (y_hi: 2, y_lo: 2; y = y_hi * 2 + y_lo), z: 8, core: 2. Of those that a mesh axis runs over, the one named last changes fastest.
Arguments:
- layer_inner: float32 [4, 1600, 1600], P('grp', 'shard'), may hold values from -6 to 6
- layer_weights: float32 [1600, 1600], P('shard'), may hold values from -6 to 6
- layer_moment: float32 [1600, 1600], P('shard'), may hold values from -6 to 6
- embed_inner: float32 [4, 25600, 1600], P('grp', 'shard'), may hold values from -6 to 6
- embed_weights: float32 [25600, 1600], P(('shard', 'grp')), may hold values from -6 to 6
- embed_moment: float32 [25600, 1600], P(('shard', 'grp')), may hold values from -6 to 6
- basis: float32 [1600, 64], replicated, may hold values from -0.15625 to 0.15625
Outputs:
- layer_new: float32 [1600, 1600], P('shard')
- layer_moment_new: float32 [1600, 1600], P('shard')
- layer_copy: bfloat16 [1600, 1600], replicated
- embed_new: float32 [25600, 1600], P(('shard', 'grp'))
- embed_moment_new: float32 [25600, 1600], P(('shard', 'grp'))
All inputs are finite; a program needn't handle non-finite values.
Results may differ from a plain program's by a relative error of at most 0.0015.
Values may be sent and summed in bfloat16 or wider, within the bound.
No kernel may reach another device: no remote copies, remote signals or barrier semaphores. Data moves between devices by JAX's collectives and lax.ppermute only.
A program may use at most 128 MiB of HBM per device.

v0:
```python
import jax
import jax.numpy as jnp
from jax import lax
from jax.sharding import PartitionSpec as P

outer_rate = 0.7
momentum_coef = 0.9


def nesterov(weights, moment, average):
    moment_new = momentum_coef * moment + average
    return (weights - outer_rate * (average + momentum_coef * moment_new), moment_new)


def per_device(
    layer_inner, layer_weights, layer_moment, embed_inner, embed_weights, embed_moment, basis
):
    groups = lax.axis_size("grp")
    inner_proj = jnp.dot(embed_inner[0], basis, precision=lax.Precision.HIGHEST)
    mean_proj = (
        lax.psum_scatter(
            inner_proj.astype(jnp.bfloat16), "grp", scatter_dimension=0, tiled=True
        ).astype(jnp.float32)
        / groups
    )
    factors = jnp.dot(embed_weights, basis, precision=lax.Precision.HIGHEST) - mean_proj
    embed_step = jnp.dot(factors, basis.T, precision=lax.Precision.HIGHEST)
    embed_new, embed_moment_new = nesterov(embed_weights, embed_moment, embed_step)
    own_diff = layer_weights - layer_inner[0]
    average = lax.psum(own_diff, "grp") / groups
    layer_new, layer_moment_new = nesterov(layer_weights, layer_moment, average)
    layer_copy = lax.all_gather(layer_new.astype(jnp.bfloat16), "shard", axis=0, tiled=True)
    return (layer_new, layer_moment_new, layer_copy, embed_new, embed_moment_new)


def solution(mesh):
    in_specs = (
        P("grp", "shard", None),
        P("shard", None),
        P("shard", None),
        P("grp", "shard", None),
        P(("shard", "grp"), None),
        P(("shard", "grp"), None),
        P(),
    )
    out_specs = (
        P("shard", None),
        P("shard", None),
        P(),
        P(("shard", "grp"), None),
        P(("shard", "grp"), None),
    )
    return jax.shard_map(
        per_device, mesh=mesh, in_specs=in_specs, out_specs=out_specs, check_vma=False
    )
```

profile of v0, /device:TPU:1, one launch (start us, length us, event | category | flops | bytes accessed | tf_op | source)
XLA Modules:
  0.0 212.7 jit_solution(13905958962458578667)
XLA Ops:
  7.2 0.0 copy-start
  7.2 0.0 copy-start.1
  7.2 0.0 all-reduce.4.cloned.1.call-start
  7.2 1.9 bitcast_subtract_fusion
  9.1 0.0 all-reduce.4.cloned.1.call-update
  9.1 0.0 all-gather.3.cloned.1.call-start
  9.2 47.6 %all-reduce.4.cloned.1.call-done = f32[25,1600]{1,0:T(8,128)} async-done(((f32[25,1600]{1,0:T(8,128)}), f32[25,1600]{1,0:T(8,128)}) %all-reduce.4.cloned.1.call-update) | async-done | bytes 160016 | tf_op jit(solution)/shard_map/psum | solution.py:30
  56.8 2.0 convert_bitcast_fusion
  58.8 0.0 copy-start.2
  58.8 0.0 all-gather.3.cloned.1.call-update
  58.8 0.0 copy-done
  58.8 3.6 %fusion.3 = bf16[400,64]{0,1:T(8,128)(2,1)S(1)} fusion(f32[1600,64]{0,1:T(8,128)} %param.13, f32[1,400,1600]{2,1,0:T(8,128)S(1)} %copy-done), kind=kOutput, calls=%fused_computation.2 | convolution fusion | flops 491545600 | bytes 3020800 | tf_op jit(solution)/shard_map/dot_general | solution.py:19
  62.4 0.1 copy.12
  62.5 6.4 %fusion = bf16[112,64]{1,0:T(8,128)(2,1)S(1)} fusion(bf16[400,64]{1,0:T(8,128)(2,1)S(1)} %copy.12), kind=kCustom, calls=%all-reduce-scatter | all-reduce-scatter fusion | flops 28673 | bytes 66560
  69.0 4.1 %collective-permute-start = (bf16[36,64]{1,0:T(8,128)(2,1)S(1)}, bf16[36,64]{1,0:T(8,128)(2,1)S(1)}, u32[]{:S(2)}, u32[]{:S(2)}) collective-permute-start(bf16[36,64]{1,0:T(8,128)(2,1)S(1)} %slice), channel_id=1, source_target_pairs={{0,64},{64,128},{128,192},{1,65},{65,129},{129,193},{2,66},{66,130... | collective-permute-start | bytes 13832
  73.1 0.0 copy-done.1
  73.1 2.0 fusion.12
  75.1 0.0 copy-done.2
  75.1 0.6 dynamic-slice.4
  76.3 0.0 collective-permute-done
  76.3 0.3 concatenate
  76.6 0.1 copy.13
  76.7 3.2 %multiply_subtract_fusion = (f32[100,1600]{1,0:T(8,128)}, f32[100,1600]{1,0:T(8,128)}) fusion(f32[100,1600]{1,0:T(8,128)} %param.11, f32[100,1600]{1,0:T(8,128)} %param.12, f32[1600,64]{0,1:T(8,128)S(1)} %copy-done.1, f32[100,64]{0,1:T(8,128)S(1)} %fusion.12, bf16[100,64]{0,1:T(8,128)(2,1)S(1)} %copy.13), kind=kOutput, calls=%fused_computation.3 | convolution fusion | flops 123859200 | bytes 3008000 | tf_op jit(solution)/shard_map/dot_general | solution.py:27
  80.0 117.3 %all-gather.3.cloned.1.call-done = bf16[64,25,1600]{2,1,0:T(8,128)(2,1)} async-done(((bf16[1,25,1600]{2,1,0:T(8,128)(2,1)}), bf16[64,25,1600]{2,1,0:T(8,128)(2,1)}) %all-gather.3.cloned.1.call-update) | async-done | bytes 5120016 | tf_op jit(solution)/shard_map/all_gather | solution.py:32
  197.3 8.6 %reshape.11 = bf16[1600,1600]{1,0:T(8,128)(2,1)} reshape(bf16[64,25,1600]{2,1,0:T(8,128)(2,1)} %all-gather.3.cloned.1.call-done) | data formatting | bytes 10240000
  (2 shorter events, 0.0 us)
Async XLA Ops:
  7.2 51.6 %copy-start = (f32[1,400,1600]{2,1,0:T(8,128)S(1)}, f32[1,400,1600]{2,1,0:T(8,128)}, u32[]{:S(2)}) copy-start(f32[1,400,1600]{2,1,0:T(8,128)} %param.10) | copy-start | bytes 7680004
  7.2 65.9 %copy-start.1 = (f32[1600,64]{0,1:T(8,128)S(1)}, f32[1600,64]{0,1:T(8,128)}, u32[]{:S(2)}) copy-start(f32[1600,64]{0,1:T(8,128)} %param.13) | copy-start | bytes 1228804
  7.2 49.6 %all-reduce.4.cloned.1.call-start = ((), (), s32[]{:S(2)}) async-start(), calls=%async_computation | async-start | bytes 425984 | tf_op jit(solution)/shard_map/psum | solution.py:30
  9.1 188.1 %all-gather.3.cloned.1.call-start = ((), (), s32[]{:S(2)}) async-start(), calls=%async_computation.1 | async-start | bytes 6922240 | tf_op jit(solution)/shard_map/all_gather | solution.py:32
  58.8 16.3 %copy-start.2 = (u32[256]{0:T(256)S(1)}, u32[256]{0:T(256)}, u32[]{:S(2)}) copy-start(u32[256]{0:T(256)} %constant.19) | copy-start | bytes 3076
  69.0 7.4 %collective-permute-start = (bf16[36,64]{1,0:T(8,128)(2,1)S(1)}, bf16[36,64]{1,0:T(8,128)(2,1)S(1)}, u32[]{:S(2)}, u32[]{:S(2)}) collective-permute-start(bf16[36,64]{1,0:T(8,128)(2,1)S(1)} %slice), channel_id=1, source_target_pairs={{0,64},{64,128},{128,192},{1,65},{65,129},{129,193},{2,66},{66,130... | collective-permute-start | bytes 13832
Sparse Core Ops, SparseCore 0:
  11.2 45.5 all-reduce.3
  61.0 136.2 all-gather.2
where the time goes:
time: 216 us; the launch traced here: 213 us
  waiting for transfers between devices  165 us (76%)
  between operations  14.8 us (7%)
  local copies, waits for them, and re-layouts  9.74 us (5%)
  matrix products  8.84 us (4%)
  blocking collectives  6.38 us (3%)
  starting transfers between devices  4.19 us (2%)
  other arithmetic  3.85 us (2%)
    all_gather x1, waiting for transfers between devices, per_device(): lax.all_gather(layer_new.astype(jnp.bfloat16), 'shard', axis=0, tiled=True)  117 us
    psum x1, waiting for transfers between devices, per_device(): average = lax.psum(own_diff, 'grp') / groups  47.6 us
    unnamed x11, local copies, waits for them, and re-layouts  9.52 us
    unnamed x1, blocking collectives  6.38 us
  transfers between devices with their start and end apart: 3, of which 2 were waited for; matrix products, arithmetic and copies ran while one was open for 8% of the time, Pallas kernels for 0%

commit v1 on v0

v1 whole, which is shorter than its diff:
```python
import jax
import jax.numpy as jnp
from jax import lax
from jax.sharding import PartitionSpec as P

outer_rate = 0.7
momentum_coef = 0.9

NZ, NX, NYH = 8, 4, 2
NG = 4


def nesterov(weights, moment, average):
    moment_new = momentum_coef * moment + average
    return (weights - outer_rate * (average + momentum_coef * moment_new), moment_new)


def both(fn):
    pairs = []
    for g in range(NG):
        for s in range(NZ * NX * NYH):
            tg, ts = fn(g, s)
            pairs.append((g * NZ * NX * NYH + s, tg * NZ * NX * NYH + ts))
    return pairs


def zxy(s):
    return s // (NX * NYH), (s // NYH) % NX, s % NYH


def sidx(z, x, y):
    return (z % NZ) * NX * NYH + (x % NX) * NYH + (y % NYH)


def butterfly_sum(v):
    v = v + lax.ppermute(v, "grp", [(i, i ^ 1) for i in range(NG)])
    return v + lax.ppermute(v, "grp", [(i, i ^ 2) for i in range(NG)])


def gather_copy(blk):
    rows, d = blk.shape
    gi = lax.axis_index("grp")
    si = lax.axis_index("shard")
    z = si // (NX * NYH)
    x = (si // NYH) % NX
    yh = si % NYH
    core = gi % 2

    other = lax.ppermute(
        blk, ("grp", "shard"), both(lambda g, s: (g ^ 2, s ^ 1))
    )
    b50 = jnp.where(yh == 0, jnp.concatenate([blk, other]), jnp.concatenate([other, blk]))

    rel = [b50]
    for k in range(1, NX):
        rel.append(
            lax.ppermute(
                b50,
                "shard",
                [(sidx(zxy(s)[0], zxy(s)[1] + k, zxy(s)[2]), s) for s in range(NZ * NX * NYH)],
            )
        )
    stacked = jnp.stack(rel)
    xi = (jnp.arange(NX) - x) % NX
    b200 = jnp.take(stacked, xi, axis=0).reshape(NX * 2 * rows, d)

    def zring(g, s):
        zz, xx, yy = zxy(s)
        return g, sidx(zz - 1, xx, yy) if g % 2 == 0 else sidx(zz + 1, xx, yy)

    zpairs = both(zring)
    cur = b200
    mine = []
    for _ in range(NZ // 2 - 1):
        cur = lax.ppermute(cur, ("grp", "shard"), zpairs)
        mine.append(cur)
    half = b200.shape[0] // 2
    send_half = jnp.where(core == 0, cur[:half], cur[half:])
    mine_half = lax.ppermute(send_half, ("grp", "shard"), zpairs)
    pack = jnp.concatenate(mine + [mine_half])
    theirs = lax.ppermute(pack, "grp", [(i, i ^ 1) for i in range(NG)])

    pieces = jnp.concatenate([b200, pack, theirs]).reshape(2 * NZ, half, d)
    nb = NZ // 2 - 1
    sign = jnp.where(core == 0, 1, -1)
    pos = [2 * z, 2 * z + 1]
    for k in range(1, nb + 1):
        zz = (z + sign * k) % NZ
        pos += [2 * zz, 2 * zz + 1]
    z4 = (z + NZ // 2) % NZ
    pos.append(2 * z4 + core)
    for k in range(1, nb + 1):
        zz = (z - sign * k) % NZ
        pos += [2 * zz, 2 * zz + 1]
    pos.append(2 * z4 + 1 - core)
    pos = jnp.stack(pos)
    src = jnp.zeros((2 * NZ,), jnp.int32).at[pos].set(jnp.arange(2 * NZ, dtype=jnp.int32))
    return jnp.take(pieces, src, axis=0).reshape(2 * NZ * half, d)


def per_device(
    layer_inner, layer_weights, layer_moment, embed_inner, embed_weights, embed_moment, basis
):
    gi = lax.axis_index("grp")
    inner_proj = jnp.dot(embed_inner[0], basis, precision=lax.Precision.HIGHEST)
    q = inner_proj.shape[0] // NG
    parts = inner_proj.reshape(NG, q, -1)
    keep1 = jnp.stack([gi, gi ^ 2])
    send1 = jnp.stack([gi ^ 1, gi ^ 3])
    a = jnp.take(parts, keep1, axis=0) + lax.ppermute(
        jnp.take(parts, send1, axis=0), "grp", [(i, i ^ 1) for i in range(NG)]
    )
    mean_proj = (a[0] + lax.ppermute(a[1], "grp", [(i, i ^ 2) for i in range(NG)])) / NG
    factors = jnp.dot(embed_weights, basis, precision=lax.Precision.HIGHEST) - mean_proj
    embed_step = jnp.dot(factors, basis.T, precision=lax.Precision.HIGHEST)
    embed_new, embed_moment_new = nesterov(embed_weights, embed_moment, embed_step)

    own_diff = layer_weights - layer_inner[0]
    average = butterfly_sum(own_diff) / NG
    layer_new, layer_moment_new = nesterov(layer_weights, layer_moment, average)
    layer_copy = gather_copy(layer_new.astype(jnp.bfloat16))
    return (layer_new, layer_moment_new, layer_copy, embed_new, embed_moment_new)


def solution(mesh):
    assert mesh.shape["shard"] == NZ * NX * NYH and mesh.shape["grp"] == NG
    in_specs = (
        P("grp", "shard", None),
        P("shard", None),
        P("shard", None),
        P("grp", "shard", None),
        P(("shard", "grp"), None),
        P(("shard", "grp"), None),
        P(),
    )
    out_specs = (
        P("shard", None),
        P("shard", None),
        P(),
        P(("shard", "grp"), None),
        P(("shard", "grp"), None),
    )
    return jax.shard_map(
        per_device, mesh=mesh, in_specs=in_specs, out_specs=out_specs, check_vma=False
    )
```

time: 216 us -> 153 us (0.71)
  waiting for transfers between devices: 165 us -> 52.9 us
  local copies, waits for them, and re-layouts: 9.74 us -> 57.1 us
  between operations: 14.8 us -> 0.87 us
  starting transfers between devices: 4.19 us -> 17.5 us
  other arithmetic: 3.85 us -> 15 us
  blocking collectives: 6.38 us -> 0 us
    all_gather x1 -> x0, waiting for transfers between devices: 117 us -> none  [per_device(): lax.all_gather(layer_new.astype(jnp.bfloat16), 'shard', axis=0, tiled=True)]
    ppermute x0 -> x13, waiting for transfers between devices: none -> 52.9 us  [the longest x3 32.4 us: gather_copy(): cur = lax.ppermute(cur, ('grp', 'shard'), zpairs)]
    psum x1 -> x0, waiting for transfers between devices: 47.6 us -> none  [per_device(): average = lax.psum(own_diff, 'grp') / groups]
    concatenate x0 -> x1, local copies, waits for them, and re-layouts: none -> 26.8 us  [gather_copy(): pieces = jnp.concatenate([b200, pack, theirs]).reshape(2 * NZ, half, d)]
    gather x0 -> x6, local copies, waits for them, and re-layouts: none -> 18.2 us  [the longest x2 14.3 us: gather_copy(): return jnp.take(pieces, src, axis=0).reshape(2 * NZ * half, d)]
    ppermute x0 -> x13, starting transfers between devices: none -> 17.5 us  [the longest x1 9.76 us: gather_copy(): theirs = lax.ppermute(pack, 'grp', [(i, i ^ 1) for i in range(NG)])]
    unnamed x11 -> x20, local copies, waits for them, and re-layouts: 9.52 us -> 1.55 us
    reshape x0 -> x1, local copies, waits for them, and re-layouts: none -> 7.6 us  [gather_copy(): pieces = jnp.concatenate([b200, pack, theirs]).reshape(2 * NZ, half, d)]
  transfers between devices with their start and end apart: 3 -> 13, of which waited for: 2 -> 11; matrix products, arithmetic and copies ran while one was open for 8% -> 11% of each run, Pallas kernels for 0% -> 0%
where the time goes in v1:
time: 153 us; the launch traced here: 152 us
  local copies, waits for them, and re-layouts  57.1 us (37%)
  waiting for transfers between devices  52.9 us (35%)
  starting transfers between devices  17.5 us (11%)
  other arithmetic  15 us (10%)
  matrix products  8.52 us (6%)
    ppermute x3, waiting for transfers between devices, gather_copy(): cur = lax.ppermute(cur, ('grp', 'shard'), zpairs)  32.4 us
    concatenate x1, local copies, waits for them, and re-layouts, gather_copy(): pieces = jnp.concatenate([b200, pack, theirs]).reshape(2 * NZ, half, d)  26.8 us
    gather x2, local copies, waits for them, and re-layouts, gather_copy(): return jnp.take(pieces, src, axis=0).reshape(2 * NZ * half, d)  14.3 us
    ppermute x1, starting transfers between devices, gather_copy(): theirs = lax.ppermute(pack, 'grp', [(i, i ^ 1) for i in range(NG)])  9.76 us
    reshape x1, local copies, waits for them, and re-layouts, gather_copy(): pieces = jnp.concatenate([b200, pack, theirs]).reshape(2 * NZ, half, d)  7.6 us
    ppermute x3, waiting for transfers between devices, gather_copy(): lax.ppermute(b50, 'shard', [(sidx(zxy(s)[0], zxy(s)[1] + k, zxy(s)[2]), s...  6.74 us
    ppermute x1, waiting for transfers between devices, butterfly_sum(): return v + lax.ppermute(v, 'grp', [(i, i ^ 2) for i in range(NG)])  6.22 us
    select_n x2, other arithmetic, gather_copy(): return jnp.take(pieces, src, axis=0).reshape(2 * NZ * half, d)  5.56 us
  transfers between devices with their start and end apart: 13, of which 11 were waited for; matrix products, arithmetic and copies ran while one was open for 11% of the time, Pallas kernels for 0%

profile of v1, /device:TPU:1, one launch (start us, length us, event | category | flops | bytes accessed | tf_op | source)
XLA Modules:
  0.0 151.8 jit_solution(13081120496954011652)
XLA Ops:
  0.6 0.0 copy-start
  0.6 1.1 bitcast_subtract_fusion
  1.7 3.3 %collective-permute-start = (f32[25,1600]{1,0:T(8,128)S(1)}, f32[25,1600]{1,0:T(8,128)S(1)}, u32[]{:S(2)}, u32[]{:S(2)}) collective-permute-start(f32[25,1600]{1,0:T(8,128)S(1)} %bitcast_subtract_fusion), channel_id=1, source_target_pairs={{0,64},{64,0},{128,192},{192,128},{1,65},{65,1},{129,193},{193,129... | collective-permute-start | bytes 480008 | tf_op jit(solution)/shard_map/ppermute | solution.py:36
  5.0 1.1 collective-permute-done
  6.2 0.1 collective-permute-start.1
  6.3 0.1 broadcast_in_dim.43
  6.4 0.1 broadcast_in_dim.44
  6.5 6.2 %collective-permute-done.1 = f32[25,1600]{1,0:T(8,128)S(1)} collective-permute-done((f32[25,1600]{1,0:T(8,128)S(1)}, f32[25,1600]{1,0:T(8,128)S(1)}, u32[]{:S(2)}, u32[]{:S(2)}) %collective-permute-start.1) | collective-permute-done | bytes 160032 | tf_op jit(solution)/shard_map/ppermute | solution.py:37
  12.7 1.9 %fusion.15 = (bf16[25,1600]{1,0:T(8,128)(2,1)S(1)}, f32[25,1600]{1,0:T(8,128)}, f32[25,1600]{1,0:T(8,128)}) fusion(f32[25,1600]{1,0:T(8,128)} %param.10, f32[25,1600]{1,0:T(8,128)S(1)} %add.145, f32[25,1600]{1,0:T(8,128)S(1)} %collective-permute-done.1, f32[25,1600]{1,0:T(8,128)} %param.11), kind=kLoop, calls=%fused_computation.56 | loop fusion | flops 360000 | bytes 1040000 | tf_op jit(solution)/shard_map/convert_element_type | solution.py:121
  14.5 1.0 collective-permute-start.2
  15.6 3.7 %collective-permute-done.2 = bf16[25,1600]{1,0:T(8,128)(2,1)S(1)} collective-permute-done((bf16[25,1600]{1,0:T(8,128)(2,1)S(1)}, bf16[25,1600]{1,0:T(8,128)(2,1)S(1)}, u32[]{:S(2)}, u32[]{:S(2)}) %collective-permute-start.2) | collective-permute-done | bytes 80032 | tf_op jit(solution)/shard_map/ppermute | solution.py:49
  19.3 0.1 maximum_select_fusion.1
  19.4 0.1 collective-permute-start.5
  19.5 2.0 %collective-permute-start.4 = (bf16[50,1600]{1,0:T(8,128)(2,1)S(1)}, bf16[50,1600]{1,0:T(8,128)(2,1)S(1)}, u32[]{:S(2)}, u32[]{:S(2)}) collective-permute-start(bf16[50,1600]{1,0:T(8,128)(2,1)S(1)} %maximum_select_fusion.1), channel_id=1, source_target_pairs={{4,0},{5,1},{6,2},{7,3},{0,4},{1,5},{2,6},{3,7},{12,8},{13,9},{14,... | collective-permute-start | bytes 480008 | tf_op jit(solution)/shard_map/ppermute | solution.py:57
  21.5 1.2 collective-permute-start.3
  22.6 0.1 maximum_select_fusion
  22.7 4.7 %collective-permute-done.5 = bf16[50,1600]{1,0:T(8,128)(2,1)S(1)} collective-permute-done((bf16[50,1600]{1,0:T(8,128)(2,1)S(1)}, bf16[50,1600]{1,0:T(8,128)(2,1)S(1)}, u32[]{:S(2)}, u32[]{:S(2)}) %collective-permute-start.5) | collective-permute-done | bytes 160032 | tf_op jit(solution)/shard_map/ppermute | solution.py:57
  27.4 0.2 collective-permute-done.4
  27.6 1.8 %collective-permute-done.3 = bf16[50,1600]{1,0:T(8,128)(2,1)S(1)} collective-permute-done((bf16[50,1600]{1,0:T(8,128)(2,1)S(1)}, bf16[50,1600]{1,0:T(8,128)(2,1)S(1)}, u32[]{:S(2)}, u32[]{:S(2)}) %collective-permute-start.3) | collective-permute-done | bytes 160032 | tf_op jit(solution)/shard_map/ppermute | solution.py:57
  29.4 0.1 pad_maximum_fusion.1
  29.6 0.7 gather_fusion
  30.3 0.3 gather.16
  30.6 0.1 broadcast_select_fusion.1
  30.7 0.0 copy-start.8
  30.7 0.1 collective-permute-start.6
  30.8 11.8 %collective-permute-done.6 = bf16[200,1600]{1,0:T(8,128)(2,1)S(1)} collective-permute-done((bf16[200,1600]{1,0:T(8,128)(2,1)S(1)}, bf16[200,1600]{1,0:T(8,128)(2,1)S(1)}, u32[]{:S(2)}, u32[]{:S(2)}) %collective-permute-start.6) | collective-permute-done | bytes 640032 | tf_op jit(solution)/shard_map/ppermute | solution.py:75
  42.7 0.0 collective-permute-start.7
  42.7 0.8 copy-done.4
  43.5 9.9 %collective-permute-done.7 = bf16[200,1600]{1,0:T(8,128)(2,1)S(1)} collective-permute-done((bf16[200,1600]{1,0:T(8,128)(2,1)S(1)}, bf16[200,1600]{1,0:T(8,128)(2,1)S(1)}, u32[]{:S(2)}, u32[]{:S(2)}) %collective-permute-start.7) | collective-permute-done | bytes 640032 | tf_op jit(solution)/shard_map/ppermute | solution.py:75
  53.4 0.0 copy-done.8
  53.4 0.0 collective-permute-start.8
  53.4 0.1 compare_and_fusion
  53.5 10.7 %collective-permute-done.8 = bf16[200,1600]{1,0:T(8,128)(2,1)S(1)} collective-permute-done((bf16[200,1600]{1,0:T(8,128)(2,1)S(1)}, bf16[200,1600]{1,0:T(8,128)(2,1)S(1)}, u32[]{:S(2)}, u32[]{:S(2)}) %collective-permute-start.8) | collective-permute-done | bytes 640032 | tf_op jit(solution)/shard_map/ppermute | solution.py:75
  64.2 0.9 slice_select_fusion
  65.1 0.0 collective-permute-start.9
  65.1 0.0 copy-done.1
  65.2 1.9 %dot_general.12 = f32[4,100,1600]{2,1,0:T(8,128)S(1)} reshape(f32[1,400,1600]{2,1,0:T(8,128)} %param.12) | data formatting | bytes 5120000 | tf_op jit(solution)/shard_map/dot_general | solution.py:105
  67.1 3.9 %fusion = f32[4,100,64]{1,2,0:T(8,128)} fusion(f32[4,100,1600]{2,1,0:T(8,128)S(1)} %dot_general.12, f32[1600,64]{0,1:T(8,128)S(1)} %copy-done), kind=kOutput, calls=%fused_computation.11 | convolution fusion | flops 491520000 | bytes 3072000 | tf_op jit(solution)/shard_map/dot_general | solution.py:105
  71.0 1.5 %gather_fusion.3 = f32[2,100,64]{1,2,0:T(8,128)S(1)} fusion(f32[4,100,64]{1,2,0:T(8,128)} %fusion, s32[1024]{0:T(1024)S(1)} %pad_clamp_fusion), kind=kCustom, calls=%fused_computation.1.clone | custom fusion | bytes 102408 | tf_op jit(solution)/shard_map/jit(_take)/gather | solution.py:111
  72.6 0.1 collective-permute-done.9
  72.7 3.2 %pad_maximum_fusion = bf16[700,1600]{1,0:T(8,128)(2,1)} fusion(bf16[100,1600]{1,0:T(8,128)(2,1)S(1)} %collective-permute-done.9, bf16[200,1600]{1,0:T(8,128)(2,1)} %copy-done.1, bf16[200,1600]{1,0:T(8,128)(2,1)} %copy-done.6, bf16[200,1600]{1,0:T(8,128)(2,1)} %copy-done.4), kind=kLoop, calls=%fused_computation.6 | loop fusion | flops 8960000 | bytes 4480000 | tf_op jit(solution)/shard_map/concatenate | solution.py:80
  75.9 9.8 %collective-permute-start.10 = (bf16[700,1600]{1,0:T(8,128)(2,1)}, bf16[700,1600]{1,0:T(8,128)(2,1)}, u32[]{:S(2)}, u32[]{:S(2)}) collective-permute-start(bf16[700,1600]{1,0:T(8,128)(2,1)} %pad_maximum_fusion), channel_id=1, source_target_pairs={{0,64},{64,0},{128,192},{192,128},{1,65},{65,1},{129,193},{193,129... | collective-permute-start | bytes 6720008 | tf_op jit(solution)/shard_map/ppermute | solution.py:81
  85.6 0.7 broadcast_select_fusion.2
  86.3 0.0 collective-permute-start.11
  86.3 0.1 stack.98
  86.5 0.6 scatter_custom_fusion
  87.1 0.1 compare_and_fusion.1
  87.2 1.5 fusion.16
  88.7 1.5 gather_fusion.2
  90.1 0.0 collective-permute-done.11
  90.2 0.9 select_add_fusion
  91.1 0.6 copy-done.9
  91.7 0.0 collective-permute-start.12
  91.8 0.1 broadcast_in_dim.40
  91.9 0.1 broadcast_in_dim.41
  92.0 2.6 %collective-permute-done.12 = f32[100,64]{0,1:T(8,128)S(1)} collective-permute-done((f32[100,64]{0,1:T(8,128)S(1)}, f32[100,64]{0,1:T(8,128)S(1)}, u32[]{:S(2)}, u32[]{:S(2)}) %collective-permute-start.12) | collective-permute-done | bytes 25632 | tf_op jit(solution)/shard_map/ppermute | solution.py:113
  94.5 3.1 %multiply_subtract_fusion = (f32[100,1600]{1,0:T(8,128)}, f32[100,1600]{1,0:T(8,128)}) fusion(f32[100,1600]{1,0:T(8,128)S(1)} %copy-done.3, f32[100,1600]{1,0:T(8,128)} %param.14, f32[1600,64]{0,1:T(8,128)S(1)} %copy-done, f32[100,64]{0,1:T(8,128)} %fusion.16, f32[100,64]{0,1:T(8,128)S(1)} %collective-permute-done.12, f32[2,100,64]{1,2,0:T(8,128)} %copy-done.9), kind=kOutput, calls=%fused_computation.8 | convolution fusion | flops 123859200 | bytes 3112960 | tf_op jit(solution)/shard_map/dot_general | solution.py:115
  97.6 0.0 collective-permute-done.10
  97.6 0.0 copy-done.2
  97.6 26.8 %concatenate.61 = bf16[1600,1600]{1,0:T(8,128)(2,1)} concatenate(bf16[200,1600]{1,0:T(8,128)(2,1)} %copy-done.8, bf16[200,1600]{1,0:T(8,128)(2,1)S(1)} %copy-done.5, bf16[200,1600]{1,0:T(8,128)(2,1)S(1)} %copy-done.7, bf16[200,1600]{1,0:T(8,128)(2,1)S(1)} %copy-done.2, bf16[100,1600]{1,0:T(8,128)(2,1)S(1)} %collective-permute-done.9, bf16[700,1600]{1,0:T(8,128)(2,1)} %collective-permute-done.10), dimensions={0} | concatenate | bytes 10240000 | tf_op jit(solution)/shard_map/concatenate | solution.py:83
  124.4 7.6 %reshape.758 = bf16[16,100,1600]{2,1,0:T(8,128)(2,1)} reshape(bf16[1600,1600]{1,0:T(8,128)(2,1)} %concatenate.61) | data formatting | bytes 10240000 | tf_op jit(solution)/shard_map/reshape | solution.py:83
  132.0 6.3 %gather_fusion.1 = bf16[16,100,1600]{2,1,0:T(8,128)(2,1)} fusion(bf16[16,100,1600]{2,1,0:T(8,128)(2,1)} %reshape.758, s32[1024]{0:T(1024)S(1)} %pad_clamp_fusion.2), kind=kCustom, calls=%fused_computation.3 | custom fusion | bytes 10240064 | tf_op jit(solution)/shard_map/jit(_take)/gather | solution.py:98
  138.3 8.0 %gather.18 = bf16[1600,1600]{1,0:T(8,128)(2,1)} reshape(bf16[16,100,1600]{2,1,0:T(8,128)(2,1)} %gather_fusion.1) | data formatting | bytes 10240000 | tf_op jit(solution)/shard_map/jit(_take)/gather | solution.py:98
  146.3 5.6 %broadcast_select_fusion = bf16[1600,1600]{1,0:T(8,128)(2,1)} fusion(bf16[1600,1600]{1,0:T(8,128)(2,1)} %gather.18, pred[1600]{0:T(1024)(128)(4,1)S(1)} %broadcast_in_dim.41), kind=kLoop, calls=%fused_computation.5 | loop fusion | flops 2560000 | bytes 10241600 | tf_op jit(solution)/shard_map/jit(_take)/select_n | solution.py:98
  (25 shorter events, 0.1 us)
Async XLA Ops:
  0.6 66.4 %copy-start = (f32[1600,64]{0,1:T(8,128)S(1)}, f32[1600,64]{0,1:T(8,128)}, u32[]{:S(2)}) copy-start(f32[1600,64]{0,1:T(8,128)} %param.15) | copy-start | bytes 1228804
  1.7 4.4 %collective-permute-start = (f32[25,1600]{1,0:T(8,128)S(1)}, f32[25,1600]{1,0:T(8,128)S(1)}, u32[]{:S(2)}, u32[]{:S(2)}) collective-permute-start(f32[25,1600]{1,0:T(8,128)S(1)} %bitcast_subtract_fusion), channel_id=1, source_target_pairs={{0,64},{64,0},{128,192},{192,128},{1,65},{65,1},{129,193},{193,129... | collective-permute-start | bytes 480008 | tf_op jit(solution)/shard_map/ppermute | solution.py:36
  6.2 6.5 %collective-permute-start.1 = (f32[25,1600]{1,0:T(8,128)S(1)}, f32[25,1600]{1,0:T(8,128)S(1)}, u32[]{:S(2)}, u32[]{:S(2)}) collective-permute-start(f32[25,1600]{1,0:T(8,128)S(1)} %add.145), channel_id=1, source_target_pairs={{0,128},{64,192},{128,0},{192,64},{1,129},{65,193},{129,1},{193,65... | collective-permute-start | bytes 480008 | tf_op jit(solution)/shard_map/ppermute | solution.py:37
  14.5 4.8 %collective-permute-start.2 = (bf16[25,1600]{1,0:T(8,128)(2,1)S(1)}, bf16[25,1600]{1,0:T(8,128)(2,1)S(1)}, u32[]{:S(2)}, u32[]{:S(2)}) collective-permute-start(bf16[25,1600]{1,0:T(8,128)(2,1)S(1)} %get-tuple-element.12), channel_id=1, source_target_pairs={{0,129},{1,128},{2,131},{3,130},{4,133},{5,132},{6,135},{7,134},{8... | collective-permute-start | bytes 240008 | tf_op jit(solution)/shard_map/ppermute | solution.py:49
  19.4 8.0 %collective-permute-start.5 = (bf16[50,1600]{1,0:T(8,128)(2,1)S(1)}, bf16[50,1600]{1,0:T(8,128)(2,1)S(1)}, u32[]{:S(2)}, u32[]{:S(2)}) collective-permute-start(bf16[50,1600]{1,0:T(8,128)(2,1)S(1)} %maximum_select_fusion.1), channel_id=1, source_target_pairs={{6,0},{7,1},{0,2},{1,3},{2,4},{3,5},{4,6},{5,7},{14,8},{15,9},{8,1... | collective-permute-start | bytes 480008 | tf_op jit(solution)/shard_map/ppermute | solution.py:57
  19.5 8.2 %collective-permute-start.4 = (bf16[50,1600]{1,0:T(8,128)(2,1)S(1)}, bf16[50,1600]{1,0:T(8,128)(2,1)S(1)}, u32[]{:S(2)}, u32[]{:S(2)}) collective-permute-start(bf16[50,1600]{1,0:T(8,128)(2,1)S(1)} %maximum_select_fusion.1), channel_id=1, source_target_pairs={{4,0},{5,1},{6,2},{7,3},{0,4},{1,5},{2,6},{3,7},{12,8},{13,9},{14,... | collective-permute-start | bytes 480008 | tf_op jit(solution)/shard_map/ppermute | solution.py:57
  21.5 8.0 %collective-permute-start.3 = (bf16[50,1600]{1,0:T(8,128)(2,1)S(1)}, bf16[50,1600]{1,0:T(8,128)(2,1)S(1)}, u32[]{:S(2)}, u32[]{:S(2)}) collective-permute-start(bf16[50,1600]{1,0:T(8,128)(2,1)S(1)} %maximum_select_fusion.1), channel_id=1, source_target_pairs={{2,0},{3,1},{4,2},{5,3},{6,4},{7,5},{0,6},{1,7},{10,8},{11,9},{12,... | collective-permute-start | bytes 480008 | tf_op jit(solution)/shard_map/ppermute | solution.py:57
  30.7 22.7 %copy-start.8 = (bf16[200,1600]{1,0:T(8,128)(2,1)}, bf16[200,1600]{1,0:T(8,128)(2,1)S(1)}, u32[]{:S(2)}) copy-start(bf16[200,1600]{1,0:T(8,128)(2,1)S(1)} %broadcast_select_fusion.1) | copy-start | bytes 1920004
  30.7 11.9 %collective-permute-start.6 = (bf16[200,1600]{1,0:T(8,128)(2,1)S(1)}, bf16[200,1600]{1,0:T(8,128)(2,1)S(1)}, u32[]{:S(2)}, u32[]{:S(2)}) collective-permute-start(bf16[200,1600]{1,0:T(8,128)(2,1)S(1)} %broadcast_select_fusion.1), channel_id=1, source_target_pairs={{0,56},{1,57},{2,58},{3,59},{4,60},{5,61},{6,62},{7,63},{8,0},{9,1... | collective-permute-start | bytes 1920008 | tf_op jit(solution)/shard_map/ppermute | solution.py:75
  42.7 0.9 copy-start.4
  42.7 10.8 %collective-permute-start.7 = (bf16[200,1600]{1,0:T(8,128)(2,1)S(1)}, bf16[200,1600]{1,0:T(8,128)(2,1)S(1)}, u32[]{:S(2)}, u32[]{:S(2)}) collective-permute-start(bf16[200,1600]{1,0:T(8,128)(2,1)S(1)} %collective-permute-done.6), channel_id=1, source_target_pairs={{0,56},{1,57},{2,58},{3,59},{4,60},{5,61},{6,62},{7,63},{8,0},{9,1... | collective-permute-start | bytes 1920008 | tf_op jit(solution)/shard_map/ppermute | solution.py:75
  53.4 11.7 %copy-start.6 = (bf16[200,1600]{1,0:T(8,128)(2,1)}, bf16[200,1600]{1,0:T(8,128)(2,1)S(1)}, u32[]{:S(2)}) copy-start(bf16[200,1600]{1,0:T(8,128)(2,1)S(1)} %collective-permute-done.7) | copy-start | bytes 1920004
  53.4 10.8 %collective-permute-start.8 = (bf16[200,1600]{1,0:T(8,128)(2,1)S(1)}, bf16[200,1600]{1,0:T(8,128)(2,1)S(1)}, u32[]{:S(2)}, u32[]{:S(2)}) collective-permute-start(bf16[200,1600]{1,0:T(8,128)(2,1)S(1)} %collective-permute-done.7), channel_id=1, source_target_pairs={{0,56},{1,57},{2,58},{3,59},{4,60},{5,61},{6,62},{7,63},{8,0},{9,1... | collective-permute-start | bytes 1920008 | tf_op jit(solution)/shard_map/ppermute | solution.py:75
  64.2 1.0 copy-start.1
  65.1 7.5 %collective-permute-start.9 = (bf16[100,1600]{1,0:T(8,128)(2,1)}, bf16[100,1600]{1,0:T(8,128)(2,1)S(1)}, u32[]{:S(2)}, u32[]{:S(2)}) collective-permute-start(bf16[100,1600]{1,0:T(8,128)(2,1)} %slice_select_fusion), channel_id=1, source_target_pairs={{0,56},{1,57},{2,58},{3,59},{4,60},{5,61},{6,62},{7,63},{8,0},{9,1... | collective-permute-start | bytes 960008 | tf_op jit(solution)/shard_map/ppermute | solution.py:79
  71.0 16.2 %copy-start.3 = (f32[100,1600]{1,0:T(8,128)S(1)}, f32[100,1600]{1,0:T(8,128)}, u32[]{:S(2)}) copy-start(f32[100,1600]{1,0:T(8,128)} %param.13) | copy-start | bytes 1920004
  72.5 25.1 %copy-start.2 = (bf16[200,1600]{1,0:T(8,128)(2,1)S(1)}, bf16[200,1600]{1,0:T(8,128)(2,1)}, u32[]{:S(2)}) copy-start(bf16[200,1600]{1,0:T(8,128)(2,1)} %copy-done.1) | copy-start | bytes 1920004
  72.6 25.1 %copy-start.5 = (bf16[200,1600]{1,0:T(8,128)(2,1)S(1)}, bf16[200,1600]{1,0:T(8,128)(2,1)}, u32[]{:S(2)}) copy-start(bf16[200,1600]{1,0:T(8,128)(2,1)} %copy-done.4) | copy-start | bytes 1920004
  72.6 25.1 %copy-start.7 = (bf16[200,1600]{1,0:T(8,128)(2,1)S(1)}, bf16[200,1600]{1,0:T(8,128)(2,1)}, u32[]{:S(2)}) copy-start(bf16[200,1600]{1,0:T(8,128)(2,1)} %copy-done.6) | copy-start | bytes 1920004
  75.9 21.8 %collective-permute-start.10 = (bf16[700,1600]{1,0:T(8,128)(2,1)}, bf16[700,1600]{1,0:T(8,128)(2,1)}, u32[]{:S(2)}, u32[]{:S(2)}) collective-permute-start(bf16[700,1600]{1,0:T(8,128)(2,1)} %pad_maximum_fusion), channel_id=1, source_target_pairs={{0,64},{64,0},{128,192},{192,128},{1,65},{65,1},{129,193},{193,129... | collective-permute-start | bytes 6720008 | tf_op jit(solution)/shard_map/ppermute | solution.py:81
  86.3 3.9 %collective-permute-start.11 = (f32[2,100,64]{1,2,0:T(8,128)}, f32[2,100,64]{1,2,0:T(8,128)}, u32[]{:S(2)}, u32[]{:S(2)}) collective-permute-start(f32[2,100,64]{1,2,0:T(8,128)} %broadcast_select_fusion.2), channel_id=1, source_target_pairs={{0,64},{64,0},{128,192},{192,128},{1,65},{65,1},{129,193},{193,129... | collective-permute-start | bytes 153608 | tf_op jit(solution)/shard_map/ppermute | solution.py:110
  91.1 0.6 copy-start.9
  91.7 2.8 %collective-permute-start.12 = (f32[100,64]{0,1:T(8,128)S(1)}, f32[100,64]{0,1:T(8,128)S(1)}, u32[]{:S(2)}, u32[]{:S(2)}) collective-permute-start(f32[100,64]{0,1:T(8,128)S(1)} %slice_bitcast_fusion), channel_id=1, source_target_pairs={{0,128},{64,192},{128,0},{192,64},{1,129},{65,193},{129,1},{193,65... | collective-permute-start | bytes 76808 | tf_op jit(solution)/shard_map/ppermute | solution.py:113

commit v2 on v1

--- a/solution.py
+++ b/solution.py
@@ -45,57 +45,44 @@
     x = (si // NYH) % NX
     yh = si % NYH
     core = gi % 2
+    swap = [(i, i ^ 1) for i in range(NG)]
 
-    other = lax.ppermute(
-        blk, ("grp", "shard"), both(lambda g, s: (g ^ 2, s ^ 1))
-    )
-    b50 = jnp.where(yh == 0, jnp.concatenate([blk, other]), jnp.concatenate([other, blk]))
+    other = lax.ppermute(blk, ("grp", "shard"), both(lambda g, s: (g ^ 2, s ^ 1)))
+    b50 = jnp.zeros((NYH * rows, d), blk.dtype)
+    b50 = lax.dynamic_update_slice(b50, blk, (yh * rows, 0))
+    b50 = lax.dynamic_update_slice(b50, other, ((1 - yh) * rows, 0))
 
-    rel = [b50]
+    zb = NX * NYH * rows
+    b200 = lax.dynamic_update_slice(jnp.zeros((zb, d), blk.dtype), b50, (x * NYH * rows, 0))
     for k in range(1, NX):
-        rel.append(
-            lax.ppermute(
-                b50,
-                "shard",
-                [(sidx(zxy(s)[0], zxy(s)[1] + k, zxy(s)[2]), s) for s in range(NZ * NX * NYH)],
-            )
+        got = lax.ppermute(
+            b50,
+            "shard",
+            [(sidx(zxy(s)[0], zxy(s)[1] + k, zxy(s)[2]), s) for s in range(NZ * NX * NYH)],
         )
-    stacked = jnp.stack(rel)
-    xi = (jnp.arange(NX) - x) % NX
-    b200 = jnp.take(stacked, xi, axis=0).reshape(NX * 2 * rows, d)
+        b200 = lax.dynamic_update_slice(b200, got, (((x + k) % NX) * NYH * rows, 0))
 
     def zring(g, s):
         zz, xx, yy = zxy(s)
         return g, sidx(zz - 1, xx, yy) if g % 2 == 0 else sidx(zz + 1, xx, yy)
 
     zpairs = both(zring)
+    sign = 1 - 2 * core
+    out = lax.dynamic_update_slice(jnp.zeros((NZ * zb, d), blk.dtype), b200, (z * zb, 0))
     cur = b200
-    mine = []
-    for _ in range(NZ // 2 - 1):
+    for k in range(1, NZ // 2):
         cur = lax.ppermute(cur, ("grp", "shard"), zpairs)
-        mine.append(cur)
-    half = b200.shape[0] // 2
-    send_half = jnp.where(core == 0, cur[:half], cur[half:])
-    mine_half = lax.ppermute(send_half, ("grp", "shard"), zpairs)
-    pack = jnp.concatenate(mine + [mine_half])
-    theirs = lax.ppermute(pack, "grp", [(i, i ^ 1) for i in range(NG)])
-
-    pieces = jnp.concatenate([b200, pack, theirs]).reshape(2 * NZ, half, d)
-    nb = NZ // 2 - 1
-    sign = jnp.where(core == 0, 1, -1)
-    pos = [2 * z, 2 * z + 1]
-    for k in range(1, nb + 1):
-        zz = (z + sign * k) % NZ
-        pos += [2 * zz, 2 * zz + 1]
+        mate = lax.ppermute(cur, "grp", swap)
+        out = lax.dynamic_update_slice(out, cur, (((z + sign * k) % NZ) * zb, 0))
+        out = lax.dynamic_update_slice(out, mate, (((z - sign * k) % NZ) * zb, 0))
+    half = zb // 2
+    send_half = lax.dynamic_slice_in_dim(cur, core * half, half, 0)
+    got = lax.ppermute(send_half, ("grp", "shard"), zpairs)
+    mate = lax.ppermute(got, "grp", swap)
     z4 = (z + NZ // 2) % NZ
-    pos.append(2 * z4 + core)
-    for k in range(1, nb + 1):
-        zz = (z - sign * k) % NZ
-        pos += [2 * zz, 2 * zz + 1]
-    pos.append(2 * z4 + 1 - core)
-    pos = jnp.stack(pos)
-    src = jnp.zeros((2 * NZ,), jnp.int32).at[pos].set(jnp.arange(2 * NZ, dtype=jnp.int32))
-    return jnp.take(pieces, src, axis=0).reshape(2 * NZ * half, d)
+    out = lax.dynamic_update_slice(out, got, (z4 * zb + core * half, 0))
+    out = lax.dynamic_update_slice(out, mate, (z4 * zb + (1 - core) * half, 0))
+    return out
 
 
 def per_device(

time: 153 us -> 92.3 us (0.60)
  waiting for transfers between devices: 52.9 us -> 19.5 us
  local copies, waits for them, and re-layouts: 57.1 us -> 25.9 us
  starting transfers between devices: 17.5 us -> 34.8 us
  other arithmetic: 15 us -> 3.4 us
    concatenate x1 -> x0, local copies, waits for them, and re-layouts: 26.8 us -> none  [gather_copy(): pieces = jnp.concatenate([b200, pack, theirs]).reshape(2 * NZ, half, d)]
    ppermute x3, waiting for transfers between devices: 32.4 us -> 7.37 us  [gather_copy(): cur = lax.ppermute(cur, ('grp', 'shard'), zpairs)]
    dynamic_update_slice x0 -> x15, local copies, waits for them, and re-layouts: none -> 20 us  [the longest x3 3.75 us: gather_copy(): out = lax.dynamic_update_slice(out, cur, ((z + sign * k) % NZ * zb, 0))]
    gather x4 -> x0, local copies, waits for them, and re-layouts: 15.2 us -> none  [the longest x2 14.3 us: gather_copy(): return jnp.take(pieces, src, axis=0).reshape(2 * NZ * half, d)]
    ppermute x2 -> x5, starting transfers between devices: 9.77 us -> 19.8 us  [the longest x3 16.9 us: gather_copy(): mate = lax.ppermute(cur, 'grp', swap)]
    reshape x1 -> x0, local copies, waits for them, and re-layouts: 7.6 us -> none  [gather_copy(): pieces = jnp.concatenate([b200, pack, theirs]).reshape(2 * NZ, half, d)]
    select_n x8 -> x0, other arithmetic: 6.82 us -> none  [the longest x2 5.56 us: gather_copy(): return jnp.take(pieces, src, axis=0).reshape(2 * NZ * half, d)]
    ppermute x1, starting transfers between devices: 0.01 us -> 5.15 us  [per_device(): lax.ppermute(jnp.take(parts, send1, axis=0), 'grp', [(i, i ^ 1) for i in...]
  transfers between devices with their start and end apart: 13 -> 16, of which waited for: 11 -> 9; matrix products, arithmetic and copies ran while one was open for 11% -> 31% of each run, Pallas kernels for 0% -> 0%
where the time goes in v2:
time: 92.3 us; the launch traced here: 91.9 us
  starting transfers between devices  34.8 us (38%)
  local copies, waits for them, and re-layouts  25.9 us (28%)
  waiting for transfers between devices  19.5 us (21%)
  matrix products  7.19 us (8%)
  other arithmetic  3.4 us (4%)
  between operations  1.06 us (1%)
    ppermute x3, starting transfers between devices, gather_copy(): mate = lax.ppermute(cur, 'grp', swap)  16.9 us
    ppermute x3, waiting for transfers between devices, gather_copy(): cur = lax.ppermute(cur, ('grp', 'shard'), zpairs)  7.37 us
    ppermute x3, waiting for transfers between devices, gather_copy(): lax.ppermute(b50, 'shard', [(sidx(zxy(s)[0], zxy(s)[1] + k, zxy(s)[2]), s...  6 us
    ppermute x1, starting transfers between devices, per_device(): lax.ppermute(jnp.take(parts, send1, axis=0), 'grp', [(i, i ^ 1) for i in...  5.15 us
    ppermute x1, waiting for transfers between devices, butterfly_sum(): return v + lax.ppermute(v, 'grp', [(i, i ^ 2) for i in range(NG)])  4.64 us
    dynamic_update_slice x3, local copies, waits for them, and re-layouts, gather_copy(): out = lax.dynamic_update_slice(out, cur, ((z + sign * k) % NZ * zb, 0))  3.75 us
    ppermute x3, starting transfers between devices, gather_copy(): lax.ppermute(b50, 'shard', [(sidx(zxy(s)[0], zxy(s)[1] + k, zxy(s)[2]), s...  3.68 us
    dynamic_update_slice x3, local copies, waits for them, and re-layouts, gather_copy(): b200 = lax.dynamic_update_slice(b200, got, ((x + k) % NX * NYH * rows, 0))  3.52 us
  transfers between devices with their start and end apart: 16, of which 9 were waited for; matrix products, arithmetic and copies ran while one was open for 31% of the time, Pallas kernels for 0%

profile of v2, /device:TPU:1, one launch (start us, length us, event | category | flops | bytes accessed | tf_op | source)
XLA Modules:
  0.0 91.9 jit_solution(2475973093602172401)
XLA Ops:
  0.6 0.0 copy-start
  0.6 1.1 %bitcast_subtract_fusion = f32[25,1600]{1,0:T(8,128)S(1)} fusion(f32[25,1600]{1,0:T(8,128)} %param.10, f32[1,25,1600]{2,0,1:T(1,128)} %param.9), kind=kLoop, calls=%fused_computation.6 | loop fusion | flops 40000 | bytes 480000 | tf_op jit(solution)/shard_map/sub | solution.py:105
  1.7 3.3 %collective-permute-start = (f32[25,1600]{1,0:T(8,128)S(1)}, f32[25,1600]{1,0:T(8,128)S(1)}, u32[]{:S(2)}, u32[]{:S(2)}) collective-permute-start(f32[25,1600]{1,0:T(8,128)S(1)} %bitcast_subtract_fusion), channel_id=1, source_target_pairs={{0,64},{64,0},{128,192},{192,128},{1,65},{65,1},{129,193},{193,129... | collective-permute-start | bytes 480008 | tf_op jit(solution)/shard_map/ppermute | solution.py:36
  5.0 1.1 %collective-permute-done = f32[25,1600]{1,0:T(8,128)S(1)} collective-permute-done((f32[25,1600]{1,0:T(8,128)S(1)}, f32[25,1600]{1,0:T(8,128)S(1)}, u32[]{:S(2)}, u32[]{:S(2)}) %collective-permute-start) | collective-permute-done | bytes 160032 | tf_op jit(solution)/shard_map/ppermute | solution.py:36
  6.2 0.1 collective-permute-start.1
  6.3 1.9 %dot_general.12 = f32[4,100,1600]{2,1,0:T(8,128)S(1)} reshape(f32[1,400,1600]{2,1,0:T(8,128)} %param.12) | data formatting | bytes 5120000 | tf_op jit(solution)/shard_map/dot_general | solution.py:92
  8.1 4.6 %collective-permute-done.1 = f32[25,1600]{1,0:T(8,128)} collective-permute-done((f32[25,1600]{1,0:T(8,128)S(1)}, f32[25,1600]{1,0:T(8,128)}, u32[]{:S(2)}, u32[]{:S(2)}) %collective-permute-start.1) | collective-permute-done | bytes 160032 | tf_op jit(solution)/shard_map/ppermute | solution.py:37
  12.8 2.0 %fusion.9 = (bf16[25,1600]{1,0:T(8,128)(2,1)S(1)}, f32[25,1600]{1,0:T(8,128)}, f32[25,1600]{1,0:T(8,128)}) fusion(f32[25,1600]{1,0:T(8,128)} %param.10, f32[25,1600]{1,0:T(8,128)S(1)} %add.144, f32[25,1600]{1,0:T(8,128)} %collective-permute-done.1, f32[25,1600]{1,0:T(8,128)} %param.11), kind=kLoop, calls=%fused_computation.34 | loop fusion | flops 360000 | bytes 1040000 | tf_op jit(solution)/shard_map/convert_element_type | solution.py:108
  14.7 1.0 %collective-permute-start.2 = (bf16[25,1600]{1,0:T(8,128)(2,1)S(1)}, bf16[25,1600]{1,0:T(8,128)(2,1)}, u32[]{:S(2)}, u32[]{:S(2)}) collective-permute-start(bf16[25,1600]{1,0:T(8,128)(2,1)S(1)} %get-tuple-element.12), channel_id=1, source_target_pairs={{0,129},{1,128},{2,131},{3,130},{4,133},{5,132},{6,135},{7,134},{8... | collective-permute-start | bytes 240008 | tf_op jit(solution)/shard_map/ppermute | solution.py:50
  15.8 3.3 %fusion = f32[4,100,64]{1,2,0:T(8,128)S(1)} fusion(f32[4,100,1600]{2,1,0:T(8,128)S(1)} %dot_general.12, f32[1600,64]{0,1:T(8,128)S(1)} %copy-done), kind=kOutput, calls=%fused_computation.4 | convolution fusion | flops 491520000 | bytes 3072000 | tf_op jit(solution)/shard_map/dot_general | solution.py:92
  19.1 0.0 copy-start.2
  19.1 0.9 %dynamic_update_slice.45 = bf16[50,1600]{1,0:T(8,128)(2,1)S(1)} dynamic-update-slice(bf16[50,1600]{1,0:T(8,128)(2,1)S(1)} %broadcast_in_dim.20, bf16[25,1600]{1,0:T(8,128)(2,1)S(1)} %get-tuple-element.12, s32[]{:T(128)S(6)} %select_n.118, s32[]{:T(128)} %constant.128.clone.1) | dynamic-update-slice | bytes 160004 | tf_op jit(solution)/shard_map/dynamic_update_slice | solution.py:52
  20.1 0.0 collective-permute-done.2
  20.1 1.5 %dynamic_update_slice.46 = bf16[50,1600]{1,0:T(8,128)(2,1)S(1)} dynamic-update-slice(bf16[50,1600]{1,0:T(8,128)(2,1)S(1)} %dynamic_update_slice.45, bf16[25,1600]{1,0:T(8,128)(2,1)} %collective-permute-done.2, s32[]{:T(128)S(6)} %select_n.119, s32[]{:T(128)} %constant.128.clone.1) | dynamic-update-slice | bytes 160004 | tf_op jit(solution)/shard_map/dynamic_update_slice | solution.py:53
  21.5 2.6 %collective-permute-start.3 = (bf16[50,1600]{1,0:T(8,128)(2,1)S(1)}, bf16[50,1600]{1,0:T(8,128)(2,1)S(1)}, u32[]{:S(2)}, u32[]{:S(2)}) collective-permute-start(bf16[50,1600]{1,0:T(8,128)(2,1)S(1)} %dynamic_update_slice.46), channel_id=1, source_target_pairs={{2,0},{3,1},{4,2},{5,3},{6,4},{7,5},{0,6},{1,7},{10,8},{11,9},{12,... | collective-permute-start | bytes 480008 | tf_op jit(solution)/shard_map/ppermute | solution.py:58
  24.1 0.5 collective-permute-start.4
  24.6 0.6 collective-permute-start.5
  25.2 0.1 compare_and_fusion
  25.3 0.6 gather_fusion.1
  26.0 1.3 %dynamic_update_slice.47 = bf16[200,1600]{1,0:T(8,128)(2,1)S(1)} dynamic-update-slice(bf16[200,1600]{1,0:T(8,128)(2,1)S(1)} %broadcast_in_dim.19, bf16[50,1600]{1,0:T(8,128)(2,1)S(1)} %dynamic_update_slice.46, s32[]{:T(128)S(6)} %select_n.122, s32[]{:T(128)} %constant.128.clone.1) | dynamic-update-slice | bytes 320004 | tf_op jit(solution)/shard_map/dynamic_update_slice | solution.py:56
  27.3 1.5 %collective-permute-done.3 = bf16[50,1600]{1,0:T(8,128)(2,1)S(1)} collective-permute-done((bf16[50,1600]{1,0:T(8,128)(2,1)S(1)}, bf16[50,1600]{1,0:T(8,128)(2,1)S(1)}, u32[]{:S(2)}, u32[]{:S(2)}) %collective-permute-start.3) | collective-permute-done | bytes 160032 | tf_op jit(solution)/shard_map/ppermute | solution.py:58
  28.8 1.2 %dynamic_update_slice.48 = bf16[200,1600]{1,0:T(8,128)(2,1)S(1)} dynamic-update-slice(bf16[200,1600]{1,0:T(8,128)(2,1)S(1)} %dynamic_update_slice.47, bf16[50,1600]{1,0:T(8,128)(2,1)S(1)} %collective-permute-done.3, s32[]{:T(128)S(6)} %select_n.124, s32[]{:T(128)} %constant.128.clone.1) | dynamic-update-slice | bytes 320004 | tf_op jit(solution)/shard_map/dynamic_update_slice | solution.py:63
  30.0 0.1 collective-permute-done.4
  30.1 1.3 %dynamic_update_slice.49 = bf16[200,1600]{1,0:T(8,128)(2,1)S(1)} dynamic-update-slice(bf16[200,1600]{1,0:T(8,128)(2,1)S(1)} %dynamic_update_slice.48, bf16[50,1600]{1,0:T(8,128)(2,1)S(1)} %collective-permute-done.4, s32[]{:T(128)S(6)} %select_n.126, s32[]{:T(128)} %constant.128.clone.1) | dynamic-update-slice | bytes 320004 | tf_op jit(solution)/shard_map/dynamic_update_slice | solution.py:63
  31.4 4.4 %collective-permute-done.5 = bf16[50,1600]{1,0:T(8,128)(2,1)S(1)} collective-permute-done((bf16[50,1600]{1,0:T(8,128)(2,1)S(1)}, bf16[50,1600]{1,0:T(8,128)(2,1)S(1)}, u32[]{:S(2)}, u32[]{:S(2)}) %collective-permute-start.5) | collective-permute-done | bytes 160032 | tf_op jit(solution)/shard_map/ppermute | solution.py:58
  35.8 1.0 %dynamic_update_slice.50 = bf16[200,1600]{1,0:T(8,128)(2,1)S(1)} dynamic-update-slice(bf16[200,1600]{1,0:T(8,128)(2,1)S(1)} %dynamic_update_slice.49, bf16[50,1600]{1,0:T(8,128)(2,1)S(1)} %collective-permute-done.5, s32[]{:T(128)S(6)} %select_n.128, s32[]{:T(128)} %constant.128.clone.1) | dynamic-update-slice | bytes 320004 | tf_op jit(solution)/shard_map/dynamic_update_slice | solution.py:63
  36.8 1.7 %collective-permute-start.6 = (bf16[200,1600]{1,0:T(8,128)(2,1)S(1)}, bf16[200,1600]{1,0:T(8,128)(2,1)}, u32[]{:S(2)}, u32[]{:S(2)}) collective-permute-start(bf16[200,1600]{1,0:T(8,128)(2,1)S(1)} %dynamic_update_slice.50), channel_id=1, source_target_pairs={{0,56},{1,57},{2,58},{3,59},{4,60},{5,61},{6,62},{7,63},{8,0},{9,1... | collective-permute-start | bytes 1920008 | tf_op jit(solution)/shard_map/ppermute | solution.py:74
  38.5 0.1 broadcast_select_fusion
  38.6 5.1 %collective-permute-start.14 = (f32[2,100,64]{1,2,0:T(8,128)S(1)}, f32[2,100,64]{1,2,0:T(8,128)S(1)}, u32[]{:S(2)}, u32[]{:S(2)}) collective-permute-start(f32[2,100,64]{1,2,0:T(8,128)S(1)} %broadcast_select_fusion), channel_id=1, source_target_pairs={{0,64},{64,0},{128,192},{192,128},{1,65},{65,1},{129,193},{193,129... | collective-permute-start | bytes 153608 | tf_op jit(solution)/shard_map/ppermute | solution.py:97
  43.8 0.1 compare_and_fusion.1
  43.8 0.6 gather_fusion
  44.4 0.3 collective-permute-done.14
  44.7 0.1 select_add_fusion
  44.7 5.9 %collective-permute-done.6 = bf16[200,1600]{1,0:T(8,128)(2,1)} collective-permute-done((bf16[200,1600]{1,0:T(8,128)(2,1)S(1)}, bf16[200,1600]{1,0:T(8,128)(2,1)}, u32[]{:S(2)}, u32[]{:S(2)}) %collective-permute-start.6) | collective-permute-done | bytes 640032 | tf_op jit(solution)/shard_map/ppermute | solution.py:74
  50.7 0.0 collective-permute-start.8
  50.7 0.0 collective-permute-start.15
  50.7 2.0 %fusion.10 = f32[100,64]{0,1:T(8,128)S(1)} fusion(f32[100,1600]{1,0:T(8,128)} %param.13, f32[1600,64]{0,1:T(8,128)S(1)} %copy-done), kind=kOutput, calls=%fused_computation.35 | convolution fusion | flops 122880000 | bytes 1075200 | tf_op jit(solution)/shard_map/dot_general | solution.py:101
  52.8 5.4 %collective-permute-start.7 = (bf16[200,1600]{1,0:T(8,128)(2,1)}, bf16[200,1600]{1,0:T(8,128)(2,1)S(1)}, u32[]{:S(2)}, u32[]{:S(2)}) collective-permute-start(bf16[200,1600]{1,0:T(8,128)(2,1)} %collective-permute-done.6), channel_id=1, source_target_pairs={{0,64},{64,0},{128,192},{192,128},{1,65},{65,1},{129,193},{193,129... | collective-permute-start | bytes 1920008 | tf_op jit(solution)/shard_map/ppermute | solution.py:75
  58.2 0.0 collective-permute-done.15
  58.2 0.0 copy-done.1
  58.2 2.0 %multiply_subtract_fusion = (f32[100,1600]{1,0:T(8,128)}, f32[100,1600]{1,0:T(8,128)}) fusion(f32[100,1600]{1,0:T(8,128)S(1)} %copy-done.1, f32[100,1600]{1,0:T(8,128)S(1)} %copy-done.2, f32[1600,64]{0,1:T(8,128)S(1)} %copy-done, f32[100,64]{0,1:T(8,128)S(1)} %fusion.10, f32[100,64]{0,1:T(8,128)S(1)} %collective-permute-done.15, ...), kind=kOutput, calls=%fused_computation.2 | convolution fusion | flops 123859200 | bytes 3188736 | tf_op jit(solution)/shard_map/dot_general | solution.py:102
  60.2 1.4 %collective-permute-done.8 = bf16[200,1600]{1,0:T(8,128)(2,1)S(1)} collective-permute-done((bf16[200,1600]{1,0:T(8,128)(2,1)}, bf16[200,1600]{1,0:T(8,128)(2,1)S(1)}, u32[]{:S(2)}, u32[]{:S(2)}) %collective-permute-start.8) | collective-permute-done | bytes 640032 | tf_op jit(solution)/shard_map/ppermute | solution.py:74
  61.6 0.0 collective-permute-start.10
  61.6 2.8 %broadcast_in_dim.18 = bf16[1600,1600]{1,0:T(8,128)(2,1)} broadcast(bf16[]{:T(256)} %constant.126.clone.1), dimensions={} | broadcast | bytes 5120002 | tf_op jit(solution)/shard_map/broadcast_in_dim | solution.py:71
  64.4 0.9 constant_dynamic-update-slice_fusion.6
  65.3 2.0 %constant_dynamic-update-slice_fusion.5 = bf16[1600,1600]{1,0:T(8,128)(2,1)} fusion(bf16[1600,1600]{1,0:T(8,128)(2,1)} %constant_dynamic-update-slice_fusion.6, bf16[200,1600]{1,0:T(8,128)(2,1)} %collective-permute-done.6, s32[]{:T(128)S(6)} %select_n.133), kind=kLoop, calls=%fused_computation.29 | loop fusion | bytes 1331204 | tf_op jit(solution)/shard_map/dynamic_update_slice | solution.py:76
  67.3 6.1 %collective-permute-start.9 = (bf16[200,1600]{1,0:T(8,128)(2,1)S(1)}, bf16[200,1600]{1,0:T(8,128)(2,1)S(1)}, u32[]{:S(2)}, u32[]{:S(2)}) collective-permute-start(bf16[200,1600]{1,0:T(8,128)(2,1)S(1)} %collective-permute-done.8), channel_id=1, source_target_pairs={{0,64},{64,0},{128,192},{192,128},{1,65},{65,1},{129,193},{193,129... | collective-permute-start | bytes 1920008 | tf_op jit(solution)/shard_map/ppermute | solution.py:75
  73.4 0.0 collective-permute-done.7
  73.4 0.9 constant_dynamic-update-slice_fusion.4
  74.3 0.0 collective-permute-done.10
  74.3 0.1 constant_dynamic-slice_fusion
  74.4 0.1 collective-permute-start.12
  74.5 5.4 %collective-permute-start.11 = (bf16[200,1600]{1,0:T(8,128)(2,1)S(1)}, bf16[200,1600]{1,0:T(8,128)(2,1)S(1)}, u32[]{:S(2)}, u32[]{:S(2)}) collective-permute-start(bf16[200,1600]{1,0:T(8,128)(2,1)S(1)} %collective-permute-done.10), channel_id=1, source_target_pairs={{0,64},{64,0},{128,192},{192,128},{1,65},{65,1},{129,193},{193,129... | collective-permute-start | bytes 1920008 | tf_op jit(solution)/shard_map/ppermute | solution.py:75
  79.9 0.9 constant_dynamic-update-slice_fusion.3
  80.8 0.0 collective-permute-done.9
  80.8 0.9 constant_dynamic-update-slice_fusion.2
  81.6 0.2 collective-permute-done.12
  81.8 2.8 %collective-permute-start.13 = (bf16[100,1600]{1,0:T(8,128)(2,1)S(1)}, bf16[100,1600]{1,0:T(8,128)(2,1)S(1)}, u32[]{:S(2)}, u32[]{:S(2)}) collective-permute-start(bf16[100,1600]{1,0:T(8,128)(2,1)S(1)} %collective-permute-done.12), channel_id=1, source_target_pairs={{0,64},{64,0},{128,192},{192,128},{1,65},{65,1},{129,193},{193,129... | collective-permute-start | bytes 960008 | tf_op jit(solution)/shard_map/ppermute | solution.py:81
  84.7 0.9 constant_dynamic-update-slice_fusion.1
  85.5 0.0 collective-permute-done.11
  85.5 0.9 constant_dynamic-update-slice_fusion
  86.4 2.7 %dynamic_update_slice.58 = bf16[1600,1600]{1,0:T(8,128)(2,1)} dynamic-update-slice(bf16[1600,1600]{1,0:T(8,128)(2,1)} %constant_dynamic-update-slice_fusion, bf16[100,1600]{1,0:T(8,128)(2,1)S(1)} %collective-permute-done.12, s32[]{:T(128)S(6)} %select_n.146, s32[]{:T(128)} %constant.128.clone.1) | dynamic-update-slice | bytes 640004 | tf_op jit(solution)/shard_map/dynamic_update_slice | solution.py:83
  89.2 0.0 collective-permute-done.13
  89.2 2.7 %dynamic_update_slice.59 = bf16[1600,1600]{1,0:T(8,128)(2,1)} dynamic-update-slice(bf16[1600,1600]{1,0:T(8,128)(2,1)} %dynamic_update_slice.58, bf16[100,1600]{1,0:T(8,128)(2,1)S(1)} %collective-permute-done.13, s32[]{:T(128)S(6)} %select_n.147, s32[]{:T(128)} %constant.128.clone.1) | dynamic-update-slice | bytes 640004 | tf_op jit(solution)/shard_map/dynamic_update_slice | solution.py:84
  (9 shorter events, 0.1 us)
Async XLA Ops:
  0.6 15.1 %copy-start = (f32[1600,64]{0,1:T(8,128)S(1)}, f32[1600,64]{0,1:T(8,128)}, u32[]{:S(2)}) copy-start(f32[1600,64]{0,1:T(8,128)} %param.15) | copy-start | bytes 1228804
  1.7 4.4 %collective-permute-start = (f32[25,1600]{1,0:T(8,128)S(1)}, f32[25,1600]{1,0:T(8,128)S(1)}, u32[]{:S(2)}, u32[]{:S(2)}) collective-permute-start(f32[25,1600]{1,0:T(8,128)S(1)} %bitcast_subtract_fusion), channel_id=1, source_target_pairs={{0,64},{64,0},{128,192},{192,128},{1,65},{65,1},{129,193},{193,129... | collective-permute-start | bytes 480008 | tf_op jit(solution)/shard_map/ppermute | solution.py:36
  6.2 6.6 %collective-permute-start.1 = (f32[25,1600]{1,0:T(8,128)S(1)}, f32[25,1600]{1,0:T(8,128)}, u32[]{:S(2)}, u32[]{:S(2)}) collective-permute-start(f32[25,1600]{1,0:T(8,128)S(1)} %add.144), channel_id=1, source_target_pairs={{0,128},{64,192},{128,0},{192,64},{1,129},{65,193},{129,1},{193,65... | collective-permute-start | bytes 480008 | tf_op jit(solution)/shard_map/ppermute | solution.py:37
  14.7 5.3 %collective-permute-start.2 = (bf16[25,1600]{1,0:T(8,128)(2,1)S(1)}, bf16[25,1600]{1,0:T(8,128)(2,1)}, u32[]{:S(2)}, u32[]{:S(2)}) collective-permute-start(bf16[25,1600]{1,0:T(8,128)(2,1)S(1)} %get-tuple-element.12), channel_id=1, source_target_pairs={{0,129},{1,128},{2,131},{3,130},{4,133},{5,132},{6,135},{7,134},{8... | collective-permute-start | bytes 240008 | tf_op jit(solution)/shard_map/ppermute | solution.py:50
  19.1 39.2 %copy-start.1 = (f32[100,1600]{1,0:T(8,128)S(1)}, f32[100,1600]{1,0:T(8,128)}, u32[]{:S(2)}) copy-start(f32[100,1600]{1,0:T(8,128)} %param.13) | copy-start | bytes 1920004
  19.1 39.2 %copy-start.2 = (f32[100,1600]{1,0:T(8,128)S(1)}, f32[100,1600]{1,0:T(8,128)}, u32[]{:S(2)}) copy-start(f32[100,1600]{1,0:T(8,128)} %param.14) | copy-start | bytes 1920004
  21.5 7.3 %collective-permute-start.3 = (bf16[50,1600]{1,0:T(8,128)(2,1)S(1)}, bf16[50,1600]{1,0:T(8,128)(2,1)S(1)}, u32[]{:S(2)}, u32[]{:S(2)}) collective-permute-start(bf16[50,1600]{1,0:T(8,128)(2,1)S(1)} %dynamic_update_slice.46), channel_id=1, source_target_pairs={{2,0},{3,1},{4,2},{5,3},{6,4},{7,5},{0,6},{1,7},{10,8},{11,9},{12,... | collective-permute-start | bytes 480008 | tf_op jit(solution)/shard_map/ppermute | solution.py:58
  24.1 6.0 %collective-permute-start.4 = (bf16[50,1600]{1,0:T(8,128)(2,1)S(1)}, bf16[50,1600]{1,0:T(8,128)(2,1)S(1)}, u32[]{:S(2)}, u32[]{:S(2)}) collective-permute-start(bf16[50,1600]{1,0:T(8,128)(2,1)S(1)} %dynamic_update_slice.46), channel_id=1, source_target_pairs={{4,0},{5,1},{6,2},{7,3},{0,4},{1,5},{2,6},{3,7},{12,8},{13,9},{14,... | collective-permute-start | bytes 480008 | tf_op jit(solution)/shard_map/ppermute | solution.py:58
  24.6 11.2 %collective-permute-start.5 = (bf16[50,1600]{1,0:T(8,128)(2,1)S(1)}, bf16[50,1600]{1,0:T(8,128)(2,1)S(1)}, u32[]{:S(2)}, u32[]{:S(2)}) collective-permute-start(bf16[50,1600]{1,0:T(8,128)(2,1)S(1)} %dynamic_update_slice.46), channel_id=1, source_target_pairs={{6,0},{7,1},{0,2},{1,3},{2,4},{3,5},{4,6},{5,7},{14,8},{15,9},{8,1... | collective-permute-start | bytes 480008 | tf_op jit(solution)/shard_map/ppermute | solution.py:58
  36.8 13.8 %collective-permute-start.6 = (bf16[200,1600]{1,0:T(8,128)(2,1)S(1)}, bf16[200,1600]{1,0:T(8,128)(2,1)}, u32[]{:S(2)}, u32[]{:S(2)}) collective-permute-start(bf16[200,1600]{1,0:T(8,128)(2,1)S(1)} %dynamic_update_slice.50), channel_id=1, source_target_pairs={{0,56},{1,57},{2,58},{3,59},{4,60},{5,61},{6,62},{7,63},{8,0},{9,1... | collective-permute-start | bytes 1920008 | tf_op jit(solution)/shard_map/ppermute | solution.py:74
  38.6 6.0 %collective-permute-start.14 = (f32[2,100,64]{1,2,0:T(8,128)S(1)}, f32[2,100,64]{1,2,0:T(8,128)S(1)}, u32[]{:S(2)}, u32[]{:S(2)}) collective-permute-start(f32[2,100,64]{1,2,0:T(8,128)S(1)} %broadcast_select_fusion), channel_id=1, source_target_pairs={{0,64},{64,0},{128,192},{192,128},{1,65},{65,1},{129,193},{193,129... | collective-permute-start | bytes 153608 | tf_op jit(solution)/shard_map/ppermute | solution.py:97
  50.7 11.0 %collective-permute-start.8 = (bf16[200,1600]{1,0:T(8,128)(2,1)}, bf16[200,1600]{1,0:T(8,128)(2,1)S(1)}, u32[]{:S(2)}, u32[]{:S(2)}) collective-permute-start(bf16[200,1600]{1,0:T(8,128)(2,1)} %collective-permute-done.6), channel_id=1, source_target_pairs={{0,56},{1,57},{2,58},{3,59},{4,60},{5,61},{6,62},{7,63},{8,0},{9,1... | collective-permute-start | bytes 1920008 | tf_op jit(solution)/shard_map/ppermute | solution.py:74
  50.7 7.6 %collective-permute-start.15 = (f32[100,64]{0,1:T(8,128)S(1)}, f32[100,64]{0,1:T(8,128)S(1)}, u32[]{:S(2)}, u32[]{:S(2)}) collective-permute-start(f32[100,64]{0,1:T(8,128)S(1)} %slice_bitcast_fusion), channel_id=1, source_target_pairs={{0,128},{64,192},{128,0},{192,64},{1,129},{65,193},{129,1},{193,65... | collective-permute-start | bytes 76808 | tf_op jit(solution)/shard_map/ppermute | solution.py:100
  52.8 20.6 %collective-permute-start.7 = (bf16[200,1600]{1,0:T(8,128)(2,1)}, bf16[200,1600]{1,0:T(8,128)(2,1)S(1)}, u32[]{:S(2)}, u32[]{:S(2)}) collective-permute-start(bf16[200,1600]{1,0:T(8,128)(2,1)} %collective-permute-done.6), channel_id=1, source_target_pairs={{0,64},{64,0},{128,192},{192,128},{1,65},{65,1},{129,193},{193,129... | collective-permute-start | bytes 1920008 | tf_op jit(solution)/shard_map/ppermute | solution.py:75
  61.6 12.7 %collective-permute-start.10 = (bf16[200,1600]{1,0:T(8,128)(2,1)S(1)}, bf16[200,1600]{1,0:T(8,128)(2,1)S(1)}, u32[]{:S(2)}, u32[]{:S(2)}) collective-permute-start(bf16[200,1600]{1,0:T(8,128)(2,1)S(1)} %collective-permute-done.8), channel_id=1, source_target_pairs={{0,56},{1,57},{2,58},{3,59},{4,60},{5,61},{6,62},{7,63},{8,0},{9,1... | collective-permute-start | bytes 1920008 | tf_op jit(solution)/shard_map/ppermute | solution.py:74
  67.3 13.5 %collective-permute-start.9 = (bf16[200,1600]{1,0:T(8,128)(2,1)S(1)}, bf16[200,1600]{1,0:T(8,128)(2,1)S(1)}, u32[]{:S(2)}, u32[]{:S(2)}) collective-permute-start(bf16[200,1600]{1,0:T(8,128)(2,1)S(1)} %collective-permute-done.8), channel_id=1, source_target_pairs={{0,64},{64,0},{128,192},{192,128},{1,65},{65,1},{129,193},{193,129... | collective-permute-start | bytes 1920008 | tf_op jit(solution)/shard_map/ppermute | solution.py:75
  74.4 7.4 %collective-permute-start.12 = (bf16[100,1600]{1,0:T(8,128)(2,1)S(1)}, bf16[100,1600]{1,0:T(8,128)(2,1)S(1)}, u32[]{:S(2)}, u32[]{:S(2)}) collective-permute-start(bf16[100,1600]{1,0:T(8,128)(2,1)S(1)} %constant_dynamic-slice_fusion), channel_id=1, source_target_pairs={{0,56},{1,57},{2,58},{3,59},{4,60},{5,61},{6,62},{7,63},{8,0},{9,1... | collective-permute-start | bytes 960008 | tf_op jit(solution)/shard_map/ppermute | solution.py:80
  74.5 11.1 %collective-permute-start.11 = (bf16[200,1600]{1,0:T(8,128)(2,1)S(1)}, bf16[200,1600]{1,0:T(8,128)(2,1)S(1)}, u32[]{:S(2)}, u32[]{:S(2)}) collective-permute-start(bf16[200,1600]{1,0:T(8,128)(2,1)S(1)} %collective-permute-done.10), channel_id=1, source_target_pairs={{0,64},{64,0},{128,192},{192,128},{1,65},{65,1},{129,193},{193,129... | collective-permute-start | bytes 1920008 | tf_op jit(solution)/shard_map/ppermute | solution.py:75
  81.8 7.4 %collective-permute-start.13 = (bf16[100,1600]{1,0:T(8,128)(2,1)S(1)}, bf16[100,1600]{1,0:T(8,128)(2,1)S(1)}, u32[]{:S(2)}, u32[]{:S(2)}) collective-permute-start(bf16[100,1600]{1,0:T(8,128)(2,1)S(1)} %collective-permute-done.12), channel_id=1, source_target_pairs={{0,64},{64,0},{128,192},{192,128},{1,65},{65,1},{129,193},{193,129... | collective-permute-start | bytes 960008 | tf_op jit(solution)/shard_map/ppermute | solution.py:81

commit v3 on v2

--- a/solution.py
+++ b/solution.py
@@ -42,46 +42,62 @@
     gi = lax.axis_index("grp")
     si = lax.axis_index("shard")
     z = si // (NX * NYH)
-    x = (si // NYH) % NX
-    yh = si % NYH
+    xy = si % (NX * NYH)
     core = gi % 2
+    ns = NZ * NX * NYH
     swap = [(i, i ^ 1) for i in range(NG)]
 
-    other = lax.ppermute(blk, ("grp", "shard"), both(lambda g, s: (g ^ 2, s ^ 1)))
-    b50 = jnp.zeros((NYH * rows, d), blk.dtype)
-    b50 = lax.dynamic_update_slice(b50, blk, (yh * rows, 0))
-    b50 = lax.dynamic_update_slice(b50, other, ((1 - yh) * rows, 0))
+    rel = [blk]
+    for k in range(1, NX * NYH):
+        def src_of(g, s, k=k):
+            zz, xx, yy = zxy(s)
+            dx, dy = k // NYH, k % NYH
+            return (g ^ 2 if dy else g), sidx(zz, xx + dx, yy + dy)
 
+        pairs = []
+        for g in range(NG):
+            for s in range(ns):
+                sg, ss = src_of(g, s)
+                pairs.append((sg * ns + ss, g * ns + s))
+        rel.append(lax.ppermute(blk, ("grp", "shard"), pairs))
+    stacked = jnp.stack(rel)
+    x = xy // NYH
+    yh = xy % NYH
+    k_of = []
+    for a in range(NX * NYH):
+        ax, ay = a // NYH, a % NYH
+        k_of.append(((ax - x) % NX) * NYH + (ay - yh) % NYH)
     zb = NX * NYH * rows
-    b200 = lax.dynamic_update_slice(jnp.zeros((zb, d), blk.dtype), b50, (x * NYH * rows, 0))
-    for k in range(1, NX):
-        got = lax.ppermute(
-            b50,
-            "shard",
-            [(sidx(zxy(s)[0], zxy(s)[1] + k, zxy(s)[2]), s) for s in range(NZ * NX * NYH)],
-        )
-        b200 = lax.dynamic_update_slice(b200, got, (((x + k) % NX) * NYH * rows, 0))
+    b200 = jnp.take(stacked, jnp.stack(k_of), axis=0).reshape(zb, d)
 
     def zring(g, s):
         zz, xx, yy = zxy(s)
         return g, sidx(zz - 1, xx, yy) if g % 2 == 0 else sidx(zz + 1, xx, yy)
 
     zpairs = both(zring)
+    cut = (d // 2) // 128 * 128
     sign = 1 - 2 * core
     out = lax.dynamic_update_slice(jnp.zeros((NZ * zb, d), blk.dtype), b200, (z * zb, 0))
-    cur = b200
+    cur = [b200[:, :cut], b200[:, cut:]]
     for k in range(1, NZ // 2):
-        cur = lax.ppermute(cur, ("grp", "shard"), zpairs)
-        mate = lax.ppermute(cur, "grp", swap)
-        out = lax.dynamic_update_slice(out, cur, (((z + sign * k) % NZ) * zb, 0))
-        out = lax.dynamic_update_slice(out, mate, (((z - sign * k) % NZ) * zb, 0))
-    half = zb // 2
-    send_half = lax.dynamic_slice_in_dim(cur, core * half, half, 0)
-    got = lax.ppermute(send_half, ("grp", "shard"), zpairs)
-    mate = lax.ppermute(got, "grp", swap)
-    z4 = (z + NZ // 2) % NZ
-    out = lax.dynamic_update_slice(out, got, (z4 * zb + core * half, 0))
-    out = lax.dynamic_update_slice(out, mate, (z4 * zb + (1 - core) * half, 0))
+        cur = [lax.ppermute(c, ("grp", "shard"), zpairs) for c in cur]
+        mate = [lax.ppermute(c, "grp", swap) for c in cur]
+        mine_at = ((z + sign * k) % NZ) * zb
+        mate_at = ((z - sign * k) % NZ) * zb
+        for c, m, col in zip(cur, mate, (0, cut)):
+            out = lax.dynamic_update_slice(out, c, (mine_at, col))
+            out = lax.dynamic_update_slice(out, m, (mate_at, col))
+    z4 = ((z + NZ // 2) % NZ) * zb
+    first = [p for p in zpairs if (p[1] // ns) % 2 == 0]
+    second = [p for p in zpairs if (p[1] // ns) % 2 == 1]
+    got_a = lax.ppermute(cur[0], ("grp", "shard"), first)
+    got_b = lax.ppermute(cur[1], ("grp", "shard"), second)
+    sw_a = lax.ppermute(got_a, "grp", [(i, i ^ 1) for i in range(NG) if i % 2 == 0])
+    sw_b = lax.ppermute(got_b, "grp", [(i, i ^ 1) for i in range(NG) if i % 2 == 1])
+    got_a = jnp.where(core == 0, got_a, sw_a)
+    got_b = jnp.where(core == 0, sw_b, got_b)
+    out = lax.dynamic_update_slice(out, got_a, (z4, 0))
+    out = lax.dynamic_update_slice(out, got_b, (z4, cut))
     return out
 
 

time: 92.3 us -> 93.7 us (1.015)
  local copies, waits for them, and re-layouts: 25.9 us -> 16.3 us
  waiting for transfers between devices: 19.5 us -> 29 us
  other arithmetic: 3.4 us -> 6.91 us
  matrix products: 7.19 us -> 6.11 us
    dynamic_update_slice x15 -> x12, local copies, waits for them, and re-layouts: 20 us -> 9.03 us  [the longest x6 4.53 us: gather_copy(): out = lax.dynamic_update_slice(out, m, (mate_at, col))]
    ppermute x12 -> x23, waiting for transfers between devices: 13.6 us -> 23.3 us  [the longest x6 12.3 us: gather_copy(): cur = [lax.ppermute(c, ('grp', 'shard'), zpairs) for c in cur]]
    ppermute x1, starting transfers between devices: 5.15 us -> 0.06 us  [per_device(): lax.ppermute(jnp.take(parts, send1, axis=0), 'grp', [(i, i ^ 1) for i in...]
    ppermute x12 -> x23, starting transfers between devices: 26.3 us -> 30.5 us  [the longest x6 11.5 us: gather_copy(): mate = [lax.ppermute(c, 'grp', swap) for c in cur]]
    dynamic_update_slice x0 -> x3, other arithmetic: none -> 2.66 us  [the longest x1 1.02 us: gather_copy(): lax.dynamic_update_slice(jnp.zeros((NZ * zb, d), blk.dtype), b200, (z * z...]
    convert_element_type x1 -> x0, other arithmetic: 1.95 us -> none  [per_device(): layer_copy = gather_copy(layer_new.astype(jnp.bfloat16))]
    unnamed x0 -> x1, other arithmetic: none -> 1.85 us
    dot_general x1, matrix products: 1.96 us -> 0.87 us  [per_device(): jnp.dot(embed_weights, basis, precision=lax.Precision.HIGHEST) - mean_proj]
  transfers between devices with their start and end apart: 16 -> 27, of which waited for: 9 -> 10; matrix products, arithmetic and copies ran while one was open for 31% -> 24% of each run, Pallas kernels for 0% -> 0%
where the time goes in v3:
time: 93.7 us; the launch traced here: 93.5 us
  starting transfers between devices  33.9 us (36%)
  waiting for transfers between devices  29 us (31%)
  local copies, waits for them, and re-layouts  16.3 us (17%)
  other arithmetic  6.91 us (7%)
  matrix products  6.11 us (7%)
  between operations  1.2 us (1%)
    ppermute x6, waiting for transfers between devices, gather_copy(): cur = [lax.ppermute(c, ('grp', 'shard'), zpairs) for c in cur]  12.3 us
    ppermute x6, starting transfers between devices, gather_copy(): mate = [lax.ppermute(c, 'grp', swap) for c in cur]  11.5 us
    ppermute x7, starting transfers between devices, gather_copy(): rel.append(lax.ppermute(blk, ('grp', 'shard'), pairs))  10.5 us
    ppermute x7, waiting for transfers between devices, gather_copy(): rel.append(lax.ppermute(blk, ('grp', 'shard'), pairs))  7.91 us
    ppermute x1, waiting for transfers between devices, butterfly_sum(): return v + lax.ppermute(v, 'grp', [(i, i ^ 2) for i in range(NG)])  5.66 us
    dynamic_update_slice x6, local copies, waits for them, and re-layouts, gather_copy(): out = lax.dynamic_update_slice(out, m, (mate_at, col))  4.53 us
    dynamic_update_slice x6, local copies, waits for them, and re-layouts, gather_copy(): out = lax.dynamic_update_slice(out, c, (mine_at, col))  4.5 us
    ppermute x1, starting transfers between devices, butterfly_sum(): v = v + lax.ppermute(v, 'grp', [(i, i ^ 1) for i in range(NG)])  3.29 us
  transfers between devices with their start and end apart: 27, of which 10 were waited for; matrix products, arithmetic and copies ran while one was open for 24% of the time, Pallas kernels for 0%

profile of v3, /device:TPU:1, one launch (start us, length us, event | category | flops | bytes accessed | tf_op | source)
XLA Modules:
  0.0 93.5 jit_solution(6516609833767067682)
XLA Ops:
  0.6 1.1 %bitcast_subtract_fusion = f32[25,1600]{1,0:T(8,128)S(1)} fusion(f32[25,1600]{1,0:T(8,128)} %param.10, f32[1,25,1600]{2,0,1:T(1,128)} %param.9), kind=kLoop, calls=%fused_computation.10 | loop fusion | flops 40000 | bytes 480000 | tf_op jit(solution)/shard_map/sub | solution.py:121
  1.7 3.3 %collective-permute-start = (f32[25,1600]{1,0:T(8,128)S(1)}, f32[25,1600]{1,0:T(8,128)}, u32[]{:S(2)}, u32[]{:S(2)}) collective-permute-start(f32[25,1600]{1,0:T(8,128)S(1)} %bitcast_subtract_fusion), channel_id=1, source_target_pairs={{0,64},{64,0},{128,192},{192,128},{1,65},{65,1},{129,193},{193,129... | collective-permute-start | bytes 480008 | tf_op jit(solution)/shard_map/ppermute | solution.py:36
  5.0 1.9 %dot_general.12 = f32[4,100,1600]{2,1,0:T(8,128)S(1)} reshape(f32[1,400,1600]{2,1,0:T(8,128)} %param.12) | data formatting | bytes 5120000 | tf_op jit(solution)/shard_map/dot_general | solution.py:108
  6.9 0.1 compare_and_fusion
  7.0 3.3 %fusion = f32[4,100,64]{1,2,0:T(8,128)S(1)} fusion(f32[4,100,1600]{2,1,0:T(8,128)S(1)} %dot_general.12, f32[1600,64]{0,1:T(8,128)S(1)} %copy-done), kind=kOutput, calls=%fused_computation.6 | convolution fusion | flops 491520000 | bytes 3072000 | tf_op jit(solution)/shard_map/dot_general | solution.py:108
  10.3 0.6 gather_fusion.2
  10.9 0.1 broadcast_select_fusion.1
  11.1 0.1 stack.116
  11.2 0.1 stack.98
  11.3 0.1 compare_and_fusion.1
  11.4 1.0 %add.170 = f32[25,1600]{1,0:T(8,128)S(1)} add(f32[25,1600]{1,0:T(8,128)S(1)} %bitcast_subtract_fusion, f32[25,1600]{1,0:T(8,128)} %collective-permute-done) | non-fusion elementwise | flops 40000 | bytes 480000 | tf_op jit(solution)/shard_map/add | solution.py:36
  12.4 0.1 collective-permute-start.1
  12.6 0.1 broadcast_in_dim.28
  12.7 0.6 gather_fusion.1
  13.3 5.7 %collective-permute-done.1 = f32[25,1600]{1,0:T(8,128)S(1)} collective-permute-done((f32[25,1600]{1,0:T(8,128)S(1)}, f32[25,1600]{1,0:T(8,128)S(1)}, u32[]{:S(2)}, u32[]{:S(2)}) %collective-permute-start.1) | collective-permute-done | bytes 160032 | tf_op jit(solution)/shard_map/ppermute | solution.py:37
  18.9 1.9 %bitcast_dynamic-update-slice_fusion.7 = (bf16[8,25,1600]{2,1,0:T(8,128)(2,1)S(1)}, bf16[25,1600]{1,0:T(8,128)(2,1)S(1)}, f32[25,1600]{1,0:T(8,128)}, f32[25,1600]{1,0:T(8,128)}) fusion(f32[25,1600]{1,0:T(8,128)} %param.10, f32[25,1600]{1,0:T(8,128)S(1)} %add.170, f32[25,1600]{1,0:T(8,128)S(1)} %collective-permute-done.1, f32[25,1600]{1,0:T(8,128)} %param.11), kind=kLoop, calls=%fused_computation.21 | loop fusion | flops 359999 | bytes 1172992
  20.8 1.0 %collective-permute-start.2 = (bf16[25,1600]{1,0:T(8,128)(2,1)S(1)}, bf16[25,1600]{1,0:T(8,128)(2,1)S(1)}, u32[]{:S(2)}, u32[]{:S(2)}) collective-permute-start(bf16[25,1600]{1,0:T(8,128)(2,1)S(1)} %get-tuple-element.15), channel_id=1, source_target_pairs={{129,0},{128,1},{131,2},{130,3},{133,4},{132,5},{135,6},{134,7},{1... | collective-permute-start | bytes 240008 | tf_op jit(solution)/shard_map/ppermute | solution.py:62
  21.9 2.5 %collective-permute-start.3 = (bf16[25,1600]{1,0:T(8,128)(2,1)S(1)}, bf16[25,1600]{1,0:T(8,128)(2,1)S(1)}, u32[]{:S(2)}, u32[]{:S(2)}) collective-permute-start(bf16[25,1600]{1,0:T(8,128)(2,1)S(1)} %get-tuple-element.15), channel_id=1, source_target_pairs={{2,0},{3,1},{4,2},{5,3},{6,4},{7,5},{0,6},{1,7},{10,8},{11,9},{12,... | collective-permute-start | bytes 240008 | tf_op jit(solution)/shard_map/ppermute | solution.py:62
  24.4 0.3 collective-permute-start.4
  24.7 1.9 %collective-permute-start.5 = (bf16[25,1600]{1,0:T(8,128)(2,1)S(1)}, bf16[25,1600]{1,0:T(8,128)(2,1)S(1)}, u32[]{:S(2)}, u32[]{:S(2)}) collective-permute-start(bf16[25,1600]{1,0:T(8,128)(2,1)S(1)} %get-tuple-element.15), channel_id=1, source_target_pairs={{4,0},{5,1},{6,2},{7,3},{0,4},{1,5},{2,6},{3,7},{12,8},{13,9},{14,... | collective-permute-start | bytes 240008 | tf_op jit(solution)/shard_map/ppermute | solution.py:62
  26.5 3.5 %collective-permute-start.6 = (bf16[25,1600]{1,0:T(8,128)(2,1)S(1)}, bf16[25,1600]{1,0:T(8,128)(2,1)S(1)}, u32[]{:S(2)}, u32[]{:S(2)}) collective-permute-start(bf16[25,1600]{1,0:T(8,128)(2,1)S(1)} %get-tuple-element.15), channel_id=1, source_target_pairs={{133,0},{132,1},{135,2},{134,3},{129,4},{128,5},{131,6},{130,7},{1... | collective-permute-start | bytes 240008 | tf_op jit(solution)/shard_map/ppermute | solution.py:62
  30.0 0.9 collective-permute-start.7
  31.0 0.4 collective-permute-start.8
  31.5 2.5 %collective-permute-done.6 = bf16[25,1600]{1,0:T(8,128)(2,1)S(1)} collective-permute-done((bf16[25,1600]{1,0:T(8,128)(2,1)S(1)}, bf16[25,1600]{1,0:T(8,128)(2,1)S(1)}, u32[]{:S(2)}, u32[]{:S(2)}) %collective-permute-start.6) | collective-permute-done | bytes 80032 | tf_op jit(solution)/shard_map/ppermute | solution.py:62
  34.0 1.6 %collective-permute-done.7 = bf16[25,1600]{1,0:T(8,128)(2,1)S(1)} collective-permute-done((bf16[25,1600]{1,0:T(8,128)(2,1)S(1)}, bf16[25,1600]{1,0:T(8,128)(2,1)S(1)}, u32[]{:S(2)}, u32[]{:S(2)}) %collective-permute-start.7) | collective-permute-done | bytes 80032 | tf_op jit(solution)/shard_map/ppermute | solution.py:62
  35.6 3.8 %collective-permute-done.8 = bf16[25,1600]{1,0:T(8,128)(2,1)S(1)} collective-permute-done((bf16[25,1600]{1,0:T(8,128)(2,1)S(1)}, bf16[25,1600]{1,0:T(8,128)(2,1)S(1)}, u32[]{:S(2)}, u32[]{:S(2)}) %collective-permute-start.8) | collective-permute-done | bytes 80032 | tf_op jit(solution)/shard_map/ppermute | solution.py:62
  39.4 0.7 gather_fusion
  40.1 0.3 gather.10
  40.5 2.8 %broadcast_in_dim.26 = bf16[1600,1600]{1,0:T(8,128)(2,1)} broadcast(bf16[]{:T(256)} %constant.162.clone.1), dimensions={} | broadcast | bytes 5120002 | tf_op jit(solution)/shard_map/broadcast_in_dim | solution.py:80
  43.2 1.0 %constant_dynamic-update-slice_fusion.12 = (bf16[1600,1600]{1,0:T(8,128)(2,1)}, bf16[200,1600]{1,0:T(8,128)(2,1)S(1)}) fusion(bf16[1600,1600]{1,0:T(8,128)(2,1)} %broadcast_in_dim.26, s32[]{:T(128)S(6)} %select_n.182, bf16[200,1600]{1,0:T(8,128)(2,1)S(1)} %gather.10, pred[200]{0:T(512)(128)(4,1)S(1)} %broadcast_in_dim.28), kind=kLoop, calls=%fused_computation.50 | loop fusion | flops 320000 | bytes 1945804 | tf_op jit(solution)/shard_map/dynamic_update_slice | solution.py:80
  44.3 1.4 %collective-permute-start.9 = (bf16[200,768]{1,0:T(8,128)(2,1)S(1)}, bf16[200,768]{1,0:T(8,128)(2,1)S(1)}, u32[]{:S(2)}, u32[]{:S(2)}) collective-permute-start(bf16[200,768]{1,0:T(8,128)(2,1)S(1)} %slice.22), channel_id=1, source_target_pairs={{0,56},{1,57},{2,58},{3,59},{4,60},{5,61},{6,62},{7,63},{8,0},{9,1... | collective-permute-start | bytes 921608 | tf_op jit(solution)/shard_map/ppermute | solution.py:83
  45.7 1.9 %collective-permute-start.11 = (bf16[200,832]{1,0:T(8,128)(2,1)S(1)}, bf16[200,832]{1,0:T(8,128)(2,1)S(1)}, u32[]{:S(2)}, u32[]{:S(2)}) collective-permute-start(bf16[200,832]{1,0:T(8,128)(2,1)S(1)} %slice.23), channel_id=1, source_target_pairs={{0,56},{1,57},{2,58},{3,59},{4,60},{5,61},{6,62},{7,63},{8,0},{9,1... | collective-permute-start | bytes 998408 | tf_op jit(solution)/shard_map/ppermute | solution.py:83
  47.6 0.9 fusion.10
  48.6 5.2 %collective-permute-done.9 = bf16[200,768]{1,0:T(8,128)(2,1)S(1)} collective-permute-done((bf16[200,768]{1,0:T(8,128)(2,1)S(1)}, bf16[200,768]{1,0:T(8,128)(2,1)S(1)}, u32[]{:S(2)}, u32[]{:S(2)}) %collective-permute-start.9) | collective-permute-done | bytes 307232 | tf_op jit(solution)/shard_map/ppermute | solution.py:83
  53.8 3.3 %collective-permute-start.10 = (bf16[200,768]{1,0:T(8,128)(2,1)S(1)}, bf16[200,768]{1,0:T(8,128)(2,1)S(1)}, u32[]{:S(2)}, u32[]{:S(2)}) collective-permute-start(bf16[200,768]{1,0:T(8,128)(2,1)S(1)} %collective-permute-done.9), channel_id=1, source_target_pairs={{0,64},{64,0},{128,192},{192,128},{1,65},{65,1},{129,193},{193,129... | collective-permute-start | bytes 921608 | tf_op jit(solution)/shard_map/ppermute | solution.py:84
  57.1 2.0 %multiply_subtract_fusion = (f32[100,1600]{1,0:T(8,128)}, f32[100,1600]{1,0:T(8,128)}) fusion(f32[100,1600]{1,0:T(8,128)S(1)} %copy-done.1, f32[100,1600]{1,0:T(8,128)S(1)} %copy-done.2, f32[1600,64]{0,1:T(8,128)S(1)} %copy-done, f32[100,64]{0,1:T(8,128)S(1)} %fusion.10, f32[100,64]{0,1:T(8,128)S(1)} %collective-permute-done.26, ...), kind=kOutput, calls=%fused_computation.3 | convolution fusion | flops 123859200 | bytes 3188736 | tf_op jit(solution)/shard_map/dot_general | solution.py:118
  59.1 3.7 %collective-permute-start.12 = (bf16[200,832]{1,0:T(8,128)(2,1)S(1)}, bf16[200,832]{1,0:T(8,128)(2,1)S(1)}, u32[]{:S(2)}, u32[]{:S(2)}) collective-permute-start(bf16[200,832]{1,0:T(8,128)(2,1)S(1)} %collective-permute-done.11), channel_id=1, source_target_pairs={{0,64},{64,0},{128,192},{192,128},{1,65},{65,1},{129,193},{193,129... | collective-permute-start | bytes 998408 | tf_op jit(solution)/shard_map/ppermute | solution.py:84
  62.8 0.7 constant_dynamic-update-slice_fusion.11
  63.5 1.3 %collective-permute-done.13 = bf16[200,768]{1,0:T(8,128)(2,1)S(1)} collective-permute-done((bf16[200,768]{1,0:T(8,128)(2,1)S(1)}, bf16[200,768]{1,0:T(8,128)(2,1)S(1)}, u32[]{:S(2)}, u32[]{:S(2)}) %collective-permute-start.13) | collective-permute-done | bytes 307232 | tf_op jit(solution)/shard_map/ppermute | solution.py:83
  64.8 0.6 collective-permute-start.14
  65.4 0.7 constant_dynamic-update-slice_fusion.10
  66.1 0.8 constant_dynamic-update-slice_fusion.5
  66.9 3.3 %collective-permute-done.15 = bf16[200,832]{1,0:T(8,128)(2,1)S(1)} collective-permute-done((bf16[200,832]{1,0:T(8,128)(2,1)S(1)}, bf16[200,832]{1,0:T(8,128)(2,1)S(1)}, u32[]{:S(2)}, u32[]{:S(2)}) %collective-permute-start.15) | collective-permute-done | bytes 332832 | tf_op jit(solution)/shard_map/ppermute | solution.py:83
  70.2 0.1 collective-permute-start.16
  70.4 0.8 constant_dynamic-update-slice_fusion.4
  71.2 0.7 constant_dynamic-update-slice_fusion.9
  71.9 1.6 %collective-permute-done.17 = bf16[200,768]{1,0:T(8,128)(2,1)S(1)} collective-permute-done((bf16[200,768]{1,0:T(8,128)(2,1)S(1)}, bf16[200,768]{1,0:T(8,128)(2,1)S(1)}, u32[]{:S(2)}, u32[]{:S(2)}) %collective-permute-start.17) | collective-permute-done | bytes 307232 | tf_op jit(solution)/shard_map/ppermute | solution.py:83
  73.5 1.2 %collective-permute-start.18 = (bf16[200,768]{1,0:T(8,128)(2,1)S(1)}, bf16[200,768]{1,0:T(8,128)(2,1)S(1)}, u32[]{:S(2)}, u32[]{:S(2)}) collective-permute-start(bf16[200,768]{1,0:T(8,128)(2,1)S(1)} %collective-permute-done.17), channel_id=1, source_target_pairs={{0,64},{64,0},{128,192},{192,128},{1,65},{65,1},{129,193},{193,129... | collective-permute-start | bytes 921608 | tf_op jit(solution)/shard_map/ppermute | solution.py:84
  74.8 0.7 collective-permute-start.21
  75.5 0.7 constant_dynamic-update-slice_fusion.8
  76.2 0.8 constant_dynamic-update-slice_fusion.3
  77.0 0.9 collective-permute-done.19
  77.9 2.5 %collective-permute-start.20 = (bf16[200,832]{1,0:T(8,128)(2,1)S(1)}, bf16[200,832]{1,0:T(8,128)(2,1)S(1)}, u32[]{:S(2)}, u32[]{:S(2)}) collective-permute-start(bf16[200,832]{1,0:T(8,128)(2,1)S(1)} %collective-permute-done.19), channel_id=1, source_target_pairs={{0,64},{64,0},{128,192},{192,128},{1,65},{65,1},{129,193},{193,129... | collective-permute-start | bytes 998408 | tf_op jit(solution)/shard_map/ppermute | solution.py:84
  80.4 1.9 %collective-permute-start.23 = (bf16[200,832]{1,0:T(8,128)(2,1)S(1)}, bf16[200,832]{1,0:T(8,128)(2,1)S(1)}, u32[]{:S(2)}, u32[]{:S(2)}) collective-permute-start(bf16[200,832]{1,0:T(8,128)(2,1)S(1)} %collective-permute-done.19), channel_id=1, source_target_pairs={{64,72},{65,73},{66,74},{67,75},{68,76},{69,77},{70,78},{71,79},{7... | collective-permute-start | bytes 998408 | tf_op jit(solution)/shard_map/ppermute | solution.py:94
  82.3 0.8 constant_dynamic-update-slice_fusion.2
  83.1 0.7 constant_dynamic-update-slice_fusion.7
  83.8 1.3 %collective-permute-start.22 = (bf16[200,768]{1,0:T(8,128)(2,1)S(1)}, bf16[200,768]{1,0:T(8,128)(2,1)S(1)}, u32[]{:S(2)}, u32[]{:S(2)}) collective-permute-start(bf16[200,768]{1,0:T(8,128)(2,1)S(1)} %collective-permute-done.21), channel_id=1, source_target_pairs={{0,64},{128,192},{1,65},{129,193},{2,66},{130,194},{3,67},{131,195... | collective-permute-start | bytes 921608 | tf_op jit(solution)/shard_map/ppermute | solution.py:95
  85.1 0.7 constant_dynamic-update-slice_fusion.6
  85.9 0.8 constant_dynamic-update-slice_fusion.1
  86.6 3.1 %collective-permute-done.23 = bf16[200,832]{1,0:T(8,128)(2,1)S(1)} collective-permute-done((bf16[200,832]{1,0:T(8,128)(2,1)S(1)}, bf16[200,832]{1,0:T(8,128)(2,1)S(1)}, u32[]{:S(2)}, u32[]{:S(2)}) %collective-permute-start.23) | collective-permute-done | bytes 332832 | tf_op jit(solution)/shard_map/ppermute | solution.py:94
  89.7 1.3 %collective-permute-start.24 = (bf16[200,832]{1,0:T(8,128)(2,1)S(1)}, bf16[200,832]{1,0:T(8,128)(2,1)S(1)}, u32[]{:S(2)}, u32[]{:S(2)}) collective-permute-start(bf16[200,832]{1,0:T(8,128)(2,1)S(1)} %collective-permute-done.23), channel_id=1, source_target_pairs={{64,0},{192,128},{65,1},{193,129},{66,2},{194,130},{67,3},{195,131... | collective-permute-start | bytes 998408 | tf_op jit(solution)/shard_map/ppermute | solution.py:96
  91.0 0.8 constant_dynamic-update-slice_fusion
  91.8 0.8 select_dynamic-update-slice_fusion.1
  92.6 0.8 select_dynamic-update-slice_fusion
  (46 shorter events, 0.5 us)
Async XLA Ops:
  0.6 6.4 %copy-start = (f32[1600,64]{0,1:T(8,128)S(1)}, f32[1600,64]{0,1:T(8,128)}, u32[]{:S(2)}) copy-start(f32[1600,64]{0,1:T(8,128)} %param.15) | copy-start | bytes 1228804
  1.7 9.7 %collective-permute-start = (f32[25,1600]{1,0:T(8,128)S(1)}, f32[25,1600]{1,0:T(8,128)}, u32[]{:S(2)}, u32[]{:S(2)}) collective-permute-start(f32[25,1600]{1,0:T(8,128)S(1)} %bitcast_subtract_fusion), channel_id=1, source_target_pairs={{0,64},{64,0},{128,192},{192,128},{1,65},{65,1},{129,193},{193,129... | collective-permute-start | bytes 480008 | tf_op jit(solution)/shard_map/ppermute | solution.py:36
  10.9 10.9 %collective-permute-start.25 = (f32[2,100,64]{1,2,0:T(8,128)S(1)}, f32[2,100,64]{1,2,0:T(8,128)S(1)}, u32[]{:S(2)}, u32[]{:S(2)}) collective-permute-start(f32[2,100,64]{1,2,0:T(8,128)S(1)} %broadcast_select_fusion.1), channel_id=1, source_target_pairs={{0,64},{64,0},{128,192},{192,128},{1,65},{65,1},{129,193},{193,129... | collective-permute-start | bytes 153608 | tf_op jit(solution)/shard_map/ppermute | solution.py:113
  12.4 6.5 %collective-permute-start.1 = (f32[25,1600]{1,0:T(8,128)S(1)}, f32[25,1600]{1,0:T(8,128)S(1)}, u32[]{:S(2)}, u32[]{:S(2)}) collective-permute-start(f32[25,1600]{1,0:T(8,128)S(1)} %add.170), channel_id=1, source_target_pairs={{0,128},{64,192},{128,0},{192,64},{1,129},{65,193},{129,1},{193,65... | collective-permute-start | bytes 480008 | tf_op jit(solution)/shard_map/ppermute | solution.py:37
  20.8 9.2 %collective-permute-start.2 = (bf16[25,1600]{1,0:T(8,128)(2,1)S(1)}, bf16[25,1600]{1,0:T(8,128)(2,1)S(1)}, u32[]{:S(2)}, u32[]{:S(2)}) collective-permute-start(bf16[25,1600]{1,0:T(8,128)(2,1)S(1)} %get-tuple-element.15), channel_id=1, source_target_pairs={{129,0},{128,1},{131,2},{130,3},{133,4},{132,5},{135,6},{134,7},{1... | collective-permute-start | bytes 240008 | tf_op jit(solution)/shard_map/ppermute | solution.py:62
  21.9 9.1 %collective-permute-start.3 = (bf16[25,1600]{1,0:T(8,128)(2,1)S(1)}, bf16[25,1600]{1,0:T(8,128)(2,1)S(1)}, u32[]{:S(2)}, u32[]{:S(2)}) collective-permute-start(bf16[25,1600]{1,0:T(8,128)(2,1)S(1)} %get-tuple-element.15), channel_id=1, source_target_pairs={{2,0},{3,1},{4,2},{5,3},{6,4},{7,5},{0,6},{1,7},{10,8},{11,9},{12,... | collective-permute-start | bytes 240008 | tf_op jit(solution)/shard_map/ppermute | solution.py:62
  24.4 7.0 %collective-permute-start.4 = (bf16[25,1600]{1,0:T(8,128)(2,1)S(1)}, bf16[25,1600]{1,0:T(8,128)(2,1)S(1)}, u32[]{:S(2)}, u32[]{:S(2)}) collective-permute-start(bf16[25,1600]{1,0:T(8,128)(2,1)S(1)} %get-tuple-element.15), channel_id=1, source_target_pairs={{131,0},{130,1},{133,2},{132,3},{135,4},{134,5},{129,6},{128,7},{1... | collective-permute-start | bytes 240008 | tf_op jit(solution)/shard_map/ppermute | solution.py:62
  24.7 6.8 %collective-permute-start.5 = (bf16[25,1600]{1,0:T(8,128)(2,1)S(1)}, bf16[25,1600]{1,0:T(8,128)(2,1)S(1)}, u32[]{:S(2)}, u32[]{:S(2)}) collective-permute-start(bf16[25,1600]{1,0:T(8,128)(2,1)S(1)} %get-tuple-element.15), channel_id=1, source_target_pairs={{4,0},{5,1},{6,2},{7,3},{0,4},{1,5},{2,6},{3,7},{12,8},{13,9},{14,... | collective-permute-start | bytes 240008 | tf_op jit(solution)/shard_map/ppermute | solution.py:62
  26.5 7.4 %collective-permute-start.6 = (bf16[25,1600]{1,0:T(8,128)(2,1)S(1)}, bf16[25,1600]{1,0:T(8,128)(2,1)S(1)}, u32[]{:S(2)}, u32[]{:S(2)}) collective-permute-start(bf16[25,1600]{1,0:T(8,128)(2,1)S(1)} %get-tuple-element.15), channel_id=1, source_target_pairs={{133,0},{132,1},{135,2},{134,3},{129,4},{128,5},{131,6},{130,7},{1... | collective-permute-start | bytes 240008 | tf_op jit(solution)/shard_map/ppermute | solution.py:62
  30.0 5.6 %collective-permute-start.7 = (bf16[25,1600]{1,0:T(8,128)(2,1)S(1)}, bf16[25,1600]{1,0:T(8,128)(2,1)S(1)}, u32[]{:S(2)}, u32[]{:S(2)}) collective-permute-start(bf16[25,1600]{1,0:T(8,128)(2,1)S(1)} %get-tuple-element.15), channel_id=1, source_target_pairs={{6,0},{7,1},{0,2},{1,3},{2,4},{3,5},{4,6},{5,7},{14,8},{15,9},{8,1... | collective-permute-start | bytes 240008 | tf_op jit(solution)/shard_map/ppermute | solution.py:62
  31.0 8.4 %collective-permute-start.8 = (bf16[25,1600]{1,0:T(8,128)(2,1)S(1)}, bf16[25,1600]{1,0:T(8,128)(2,1)S(1)}, u32[]{:S(2)}, u32[]{:S(2)}) collective-permute-start(bf16[25,1600]{1,0:T(8,128)(2,1)S(1)} %get-tuple-element.15), channel_id=1, source_target_pairs={{135,0},{134,1},{129,2},{128,3},{131,4},{130,5},{133,6},{132,7},{1... | collective-permute-start | bytes 240008 | tf_op jit(solution)/shard_map/ppermute | solution.py:62
  40.1 7.5 %copy-start.1 = (f32[100,1600]{1,0:T(8,128)S(1)}, f32[100,1600]{1,0:T(8,128)}, u32[]{:S(2)}) copy-start(f32[100,1600]{1,0:T(8,128)} %param.13) | copy-start | bytes 1920004
  40.4 16.7 %copy-start.2 = (f32[100,1600]{1,0:T(8,128)S(1)}, f32[100,1600]{1,0:T(8,128)}, u32[]{:S(2)}) copy-start(f32[100,1600]{1,0:T(8,128)} %param.14) | copy-start | bytes 1920004
  44.3 9.6 %collective-permute-start.9 = (bf16[200,768]{1,0:T(8,128)(2,1)S(1)}, bf16[200,768]{1,0:T(8,128)(2,1)S(1)}, u32[]{:S(2)}, u32[]{:S(2)}) collective-permute-start(bf16[200,768]{1,0:T(8,128)(2,1)S(1)} %slice.22), channel_id=1, source_target_pairs={{0,56},{1,57},{2,58},{3,59},{4,60},{5,61},{6,62},{7,63},{8,0},{9,1... | collective-permute-start | bytes 921608 | tf_op jit(solution)/shard_map/ppermute | solution.py:83
  45.6 11.5 %collective-permute-start.26 = (f32[100,64]{0,1:T(8,128)S(1)}, f32[100,64]{0,1:T(8,128)S(1)}, u32[]{:S(2)}, u32[]{:S(2)}) collective-permute-start(f32[100,64]{0,1:T(8,128)S(1)} %slice_bitcast_fusion), channel_id=1, source_target_pairs={{0,128},{64,192},{128,0},{192,64},{1,129},{65,193},{129,1},{193,65... | collective-permute-start | bytes 76808 | tf_op jit(solution)/shard_map/ppermute | solution.py:116
  45.7 13.4 %collective-permute-start.11 = (bf16[200,832]{1,0:T(8,128)(2,1)S(1)}, bf16[200,832]{1,0:T(8,128)(2,1)S(1)}, u32[]{:S(2)}, u32[]{:S(2)}) collective-permute-start(bf16[200,832]{1,0:T(8,128)(2,1)S(1)} %slice.23), channel_id=1, source_target_pairs={{0,56},{1,57},{2,58},{3,59},{4,60},{5,61},{6,62},{7,63},{8,0},{9,1... | collective-permute-start | bytes 998408 | tf_op jit(solution)/shard_map/ppermute | solution.py:83
  53.8 11.6 %collective-permute-start.10 = (bf16[200,768]{1,0:T(8,128)(2,1)S(1)}, bf16[200,768]{1,0:T(8,128)(2,1)S(1)}, u32[]{:S(2)}, u32[]{:S(2)}) collective-permute-start(bf16[200,768]{1,0:T(8,128)(2,1)S(1)} %collective-permute-done.9), channel_id=1, source_target_pairs={{0,64},{64,0},{128,192},{192,128},{1,65},{65,1},{129,193},{193,129... | collective-permute-start | bytes 921608 | tf_op jit(solution)/shard_map/ppermute | solution.py:84
  57.1 7.7 %collective-permute-start.13 = (bf16[200,768]{1,0:T(8,128)(2,1)S(1)}, bf16[200,768]{1,0:T(8,128)(2,1)S(1)}, u32[]{:S(2)}, u32[]{:S(2)}) collective-permute-start(bf16[200,768]{1,0:T(8,128)(2,1)S(1)} %collective-permute-done.9), channel_id=1, source_target_pairs={{0,56},{1,57},{2,58},{3,59},{4,60},{5,61},{6,62},{7,63},{8,0},{9,1... | collective-permute-start | bytes 921608 | tf_op jit(solution)/shard_map/ppermute | solution.py:83
  59.1 11.3 %collective-permute-start.12 = (bf16[200,832]{1,0:T(8,128)(2,1)S(1)}, bf16[200,832]{1,0:T(8,128)(2,1)S(1)}, u32[]{:S(2)}, u32[]{:S(2)}) collective-permute-start(bf16[200,832]{1,0:T(8,128)(2,1)S(1)} %collective-permute-done.11), channel_id=1, source_target_pairs={{0,64},{64,0},{128,192},{192,128},{1,65},{65,1},{129,193},{193,129... | collective-permute-start | bytes 998408 | tf_op jit(solution)/shard_map/ppermute | solution.py:84
  62.8 7.5 %collective-permute-start.15 = (bf16[200,832]{1,0:T(8,128)(2,1)S(1)}, bf16[200,832]{1,0:T(8,128)(2,1)S(1)}, u32[]{:S(2)}, u32[]{:S(2)}) collective-permute-start(bf16[200,832]{1,0:T(8,128)(2,1)S(1)} %collective-permute-done.11), channel_id=1, source_target_pairs={{0,56},{1,57},{2,58},{3,59},{4,60},{5,61},{6,62},{7,63},{8,0},{9,1... | collective-permute-start | bytes 998408 | tf_op jit(solution)/shard_map/ppermute | solution.py:83
  64.8 10.7 %collective-permute-start.14 = (bf16[200,768]{1,0:T(8,128)(2,1)S(1)}, bf16[200,768]{1,0:T(8,128)(2,1)S(1)}, u32[]{:S(2)}, u32[]{:S(2)}) collective-permute-start(bf16[200,768]{1,0:T(8,128)(2,1)S(1)} %collective-permute-done.13), channel_id=1, source_target_pairs={{0,64},{64,0},{128,192},{192,128},{1,65},{65,1},{129,193},{193,129... | collective-permute-start | bytes 921608 | tf_op jit(solution)/shard_map/ppermute | solution.py:84
  65.4 8.1 %collective-permute-start.17 = (bf16[200,768]{1,0:T(8,128)(2,1)S(1)}, bf16[200,768]{1,0:T(8,128)(2,1)S(1)}, u32[]{:S(2)}, u32[]{:S(2)}) collective-permute-start(bf16[200,768]{1,0:T(8,128)(2,1)S(1)} %collective-permute-done.13), channel_id=1, source_target_pairs={{0,56},{1,57},{2,58},{3,59},{4,60},{5,61},{6,62},{7,63},{8,0},{9,1... | collective-permute-start | bytes 921608 | tf_op jit(solution)/shard_map/ppermute | solution.py:83
  70.2 12.1 %collective-permute-start.16 = (bf16[200,832]{1,0:T(8,128)(2,1)S(1)}, bf16[200,832]{1,0:T(8,128)(2,1)S(1)}, u32[]{:S(2)}, u32[]{:S(2)}) collective-permute-start(bf16[200,832]{1,0:T(8,128)(2,1)S(1)} %collective-permute-done.15), channel_id=1, source_target_pairs={{0,64},{64,0},{128,192},{192,128},{1,65},{65,1},{129,193},{193,129... | collective-permute-start | bytes 998408 | tf_op jit(solution)/shard_map/ppermute | solution.py:84
  70.4 7.5 %collective-permute-start.19 = (bf16[200,832]{1,0:T(8,128)(2,1)S(1)}, bf16[200,832]{1,0:T(8,128)(2,1)S(1)}, u32[]{:S(2)}, u32[]{:S(2)}) collective-permute-start(bf16[200,832]{1,0:T(8,128)(2,1)S(1)} %collective-permute-done.15), channel_id=1, source_target_pairs={{0,56},{1,57},{2,58},{3,59},{4,60},{5,61},{6,62},{7,63},{8,0},{9,1... | collective-permute-start | bytes 998408 | tf_op jit(solution)/shard_map/ppermute | solution.py:83
  73.5 11.6 %collective-permute-start.18 = (bf16[200,768]{1,0:T(8,128)(2,1)S(1)}, bf16[200,768]{1,0:T(8,128)(2,1)S(1)}, u32[]{:S(2)}, u32[]{:S(2)}) collective-permute-start(bf16[200,768]{1,0:T(8,128)(2,1)S(1)} %collective-permute-done.17), channel_id=1, source_target_pairs={{0,64},{64,0},{128,192},{192,128},{1,65},{65,1},{129,193},{193,129... | collective-permute-start | bytes 921608 | tf_op jit(solution)/shard_map/ppermute | solution.py:84
  74.8 9.0 %collective-permute-start.21 = (bf16[200,768]{1,0:T(8,128)(2,1)S(1)}, bf16[200,768]{1,0:T(8,128)(2,1)S(1)}, u32[]{:S(2)}, u32[]{:S(2)}) collective-permute-start(bf16[200,768]{1,0:T(8,128)(2,1)S(1)} %collective-permute-done.17), channel_id=1, source_target_pairs={{0,56},{1,57},{2,58},{3,59},{4,60},{5,61},{6,62},{7,63},{8,0},{9,1... | collective-permute-start | bytes 921608 | tf_op jit(solution)/shard_map/ppermute | solution.py:93
  77.9 13.2 %collective-permute-start.20 = (bf16[200,832]{1,0:T(8,128)(2,1)S(1)}, bf16[200,832]{1,0:T(8,128)(2,1)S(1)}, u32[]{:S(2)}, u32[]{:S(2)}) collective-permute-start(bf16[200,832]{1,0:T(8,128)(2,1)S(1)} %collective-permute-done.19), channel_id=1, source_target_pairs={{0,64},{64,0},{128,192},{192,128},{1,65},{65,1},{129,193},{193,129... | collective-permute-start | bytes 998408 | tf_op jit(solution)/shard_map/ppermute | solution.py:84
  80.4 9.3 %collective-permute-start.23 = (bf16[200,832]{1,0:T(8,128)(2,1)S(1)}, bf16[200,832]{1,0:T(8,128)(2,1)S(1)}, u32[]{:S(2)}, u32[]{:S(2)}) collective-permute-start(bf16[200,832]{1,0:T(8,128)(2,1)S(1)} %collective-permute-done.19), channel_id=1, source_target_pairs={{64,72},{65,73},{66,74},{67,75},{68,76},{69,77},{70,78},{71,79},{7... | collective-permute-start | bytes 998408 | tf_op jit(solution)/shard_map/ppermute | solution.py:94
  83.8 8.0 %collective-permute-start.22 = (bf16[200,768]{1,0:T(8,128)(2,1)S(1)}, bf16[200,768]{1,0:T(8,128)(2,1)S(1)}, u32[]{:S(2)}, u32[]{:S(2)}) collective-permute-start(bf16[200,768]{1,0:T(8,128)(2,1)S(1)} %collective-permute-done.21), channel_id=1, source_target_pairs={{0,64},{128,192},{1,65},{129,193},{2,66},{130,194},{3,67},{131,195... | collective-permute-start | bytes 921608 | tf_op jit(solution)/shard_map/ppermute | solution.py:95
  89.7 2.9 %collective-permute-start.24 = (bf16[200,832]{1,0:T(8,128)(2,1)S(1)}, bf16[200,832]{1,0:T(8,128)(2,1)S(1)}, u32[]{:S(2)}, u32[]{:S(2)}) collective-permute-start(bf16[200,832]{1,0:T(8,128)(2,1)S(1)} %collective-permute-done.23), channel_id=1, source_target_pairs={{64,0},{192,128},{65,1},{193,129},{66,2},{194,130},{67,3},{195,131... | collective-permute-start | bytes 998408 | tf_op jit(solution)/shard_map/ppermute | solution.py:96

commit v4 on v2

--- a/solution.py
+++ b/solution.py
@@ -48,19 +48,20 @@
     swap = [(i, i ^ 1) for i in range(NG)]
 
     other = lax.ppermute(blk, ("grp", "shard"), both(lambda g, s: (g ^ 2, s ^ 1)))
-    b50 = jnp.zeros((NYH * rows, d), blk.dtype)
-    b50 = lax.dynamic_update_slice(b50, blk, (yh * rows, 0))
-    b50 = lax.dynamic_update_slice(b50, other, ((1 - yh) * rows, 0))
+    b50 = jnp.where(yh == 0, jnp.concatenate([blk, other]), jnp.concatenate([other, blk]))
 
     zb = NX * NYH * rows
-    b200 = lax.dynamic_update_slice(jnp.zeros((zb, d), blk.dtype), b50, (x * NYH * rows, 0))
+    rel = [b50]
     for k in range(1, NX):
-        got = lax.ppermute(
-            b50,
-            "shard",
-            [(sidx(zxy(s)[0], zxy(s)[1] + k, zxy(s)[2]), s) for s in range(NZ * NX * NYH)],
+        rel.append(
+            lax.ppermute(
+                b50,
+                "shard",
+                [(sidx(zxy(s)[0], zxy(s)[1] + k, zxy(s)[2]), s) for s in range(NZ * NX * NYH)],
+            )
         )
-        b200 = lax.dynamic_update_slice(b200, got, (((x + k) % NX) * NYH * rows, 0))
+    xi = (jnp.arange(NX) - x) % NX
+    b200 = jnp.take(jnp.stack(rel), xi, axis=0).reshape(zb, d)
 
     def zring(g, s):
         zz, xx, yy = zxy(s)
@@ -75,13 +76,14 @@
         mate = lax.ppermute(cur, "grp", swap)
         out = lax.dynamic_update_slice(out, cur, (((z + sign * k) % NZ) * zb, 0))
         out = lax.dynamic_update_slice(out, mate, (((z - sign * k) % NZ) * zb, 0))
-    half = zb // 2
-    send_half = lax.dynamic_slice_in_dim(cur, core * half, half, 0)
+    cut = (d // 2) // 128 * 128
+    width = d - cut
+    send_half = lax.dynamic_slice_in_dim(cur, core * cut, width, 1)
     got = lax.ppermute(send_half, ("grp", "shard"), zpairs)
     mate = lax.ppermute(got, "grp", swap)
-    z4 = (z + NZ // 2) % NZ
-    out = lax.dynamic_update_slice(out, got, (z4 * zb + core * half, 0))
-    out = lax.dynamic_update_slice(out, mate, (z4 * zb + (1 - core) * half, 0))
+    z4 = ((z + NZ // 2) % NZ) * zb
+    out = lax.dynamic_update_slice(out, got, (z4, core * cut))
+    out = lax.dynamic_update_slice(out, mate, (z4, (1 - core) * cut))
     return out
 
 

time: 92.3 us -> 99.8 us (1.081)
  starting transfers between devices: 34.8 us -> 40.1 us
  waiting for transfers between devices: 19.5 us -> 23.1 us
  local copies, waits for them, and re-layouts: 25.9 us -> 23.2 us
  other arithmetic: 3.4 us -> 5.8 us
  matrix products: 7.19 us -> 6.09 us
    ppermute x3, starting transfers between devices: 16.9 us -> 21.9 us  [gather_copy(): mate = lax.ppermute(cur, 'grp', swap)]
    dynamic_update_slice x9 -> x2, local copies, waits for them, and re-layouts: 13.6 us -> 8.59 us  [the longest x1 4.5 us: gather_copy(): out = lax.dynamic_update_slice(out, mate, (z4, (1 - core) * cut))]
    ppermute x1, waiting for transfers between devices: 0.01 us -> 3.73 us  [gather_copy(): lax.ppermute(blk, ('grp', 'shard'), both(lambda g, s: (g ^ 2, s ^ 1)))]
    ppermute x1, starting transfers between devices: 5.15 us -> 7.22 us  [per_device(): lax.ppermute(jnp.take(parts, send1, axis=0), 'grp', [(i, i ^ 1) for i in...]
    ppermute x1, waiting for transfers between devices: 4.64 us -> 6.52 us  [butterfly_sum(): return v + lax.ppermute(v, 'grp', [(i, i ^ 2) for i in range(NG)])]
    ppermute x3, starting transfers between devices: 1.72 us -> 0.01 us  [gather_copy(): cur = lax.ppermute(cur, ('grp', 'shard'), zpairs)]
    ppermute x3, waiting for transfers between devices: 7.37 us -> 5.75 us  [gather_copy(): cur = lax.ppermute(cur, ('grp', 'shard'), zpairs)]
    dynamic_update_slice x0 -> x1, other arithmetic: none -> 1.24 us  [gather_copy(): lax.dynamic_update_slice(jnp.zeros((NZ * zb, d), blk.dtype), b200, (z * z...]
  transfers between devices with their start and end apart: 16 -> 16, of which waited for: 9 -> 7; matrix products, arithmetic and copies ran while one was open for 31% -> 22% of each run, Pallas kernels for 0% -> 0%
where the time goes in v4:
time: 99.8 us; the launch traced here: 99.2 us
  starting transfers between devices  40.1 us (40%)
  local copies, waits for them, and re-layouts  23.2 us (23%)
  waiting for transfers between devices  23.1 us (23%)
  matrix products  6.09 us (6%)
  other arithmetic  5.8 us (6%)
  between operations  1.02 us (1%)
    ppermute x3, starting transfers between devices, gather_copy(): mate = lax.ppermute(cur, 'grp', swap)  21.9 us
    ppermute x1, starting transfers between devices, per_device(): lax.ppermute(jnp.take(parts, send1, axis=0), 'grp', [(i, i ^ 1) for i in...  7.22 us
    ppermute x3, waiting for transfers between devices, gather_copy(): lax.ppermute(b50, 'shard', [(sidx(zxy(s)[0], zxy(s)[1] + k, zxy(s)[2]), s...  7.06 us
    ppermute x1, waiting for transfers between devices, butterfly_sum(): return v + lax.ppermute(v, 'grp', [(i, i ^ 2) for i in range(NG)])  6.52 us
    ppermute x3, waiting for transfers between devices, gather_copy(): cur = lax.ppermute(cur, ('grp', 'shard'), zpairs)  5.75 us
    dynamic_update_slice x1, local copies, waits for them, and re-layouts, gather_copy(): out = lax.dynamic_update_slice(out, mate, (z4, (1 - core) * cut))  4.5 us
    dynamic_update_slice x1, local copies, waits for them, and re-layouts, gather_copy(): out = lax.dynamic_update_slice(out, got, (z4, core * cut))  4.08 us
    dynamic_update_slice x3, local copies, waits for them, and re-layouts, gather_copy(): out = lax.dynamic_update_slice(out, mate, ((z - sign * k) % NZ * zb, 0))  3.76 us
  transfers between devices with their start and end apart: 16, of which 7 were waited for; matrix products, arithmetic and copies ran while one was open for 22% of the time, Pallas kernels for 0%

profile of v4, /device:TPU:1, one launch (start us, length us, event | category | flops | bytes accessed | tf_op | source)
XLA Modules:
  0.0 99.2 jit_solution(11819865578293177944)
XLA Ops:
  0.6 0.0 copy-start
  0.6 1.1 %bitcast_subtract_fusion = f32[25,1600]{1,0:T(8,128)S(1)} fusion(f32[25,1600]{1,0:T(8,128)} %param.10, f32[1,25,1600]{2,0,1:T(1,128)} %param.9), kind=kLoop, calls=%fused_computation.9 | loop fusion | flops 40000 | bytes 480000 | tf_op jit(solution)/shard_map/sub | solution.py:107
  1.7 3.3 %collective-permute-start = (f32[25,1600]{1,0:T(8,128)S(1)}, f32[25,1600]{1,0:T(8,128)}, u32[]{:S(2)}, u32[]{:S(2)}) collective-permute-start(f32[25,1600]{1,0:T(8,128)S(1)} %bitcast_subtract_fusion), channel_id=1, source_target_pairs={{0,64},{64,0},{128,192},{192,128},{1,65},{65,1},{129,193},{193,129... | collective-permute-start | bytes 480008 | tf_op jit(solution)/shard_map/ppermute | solution.py:36
  5.0 1.9 %dot_general.12 = f32[4,100,1600]{2,1,0:T(8,128)S(1)} reshape(f32[1,400,1600]{2,1,0:T(8,128)} %param.12) | data formatting | bytes 5120000 | tf_op jit(solution)/shard_map/dot_general | solution.py:94
  6.9 3.3 %fusion = f32[4,100,64]{1,2,0:T(8,128)S(1)} fusion(f32[4,100,1600]{2,1,0:T(8,128)S(1)} %dot_general.12, f32[1600,64]{0,1:T(8,128)S(1)} %copy-done), kind=kOutput, calls=%fused_computation.7 | convolution fusion | flops 491520000 | bytes 3072000 | tf_op jit(solution)/shard_map/dot_general | solution.py:94
  10.2 0.0 collective-permute-done
  10.2 1.0 add.136
  11.2 0.1 collective-permute-start.1
  11.3 0.1 broadcast_in_dim.27
  11.4 0.1 broadcast_in_dim.28
  11.5 6.5 %collective-permute-done.1 = f32[25,1600]{1,0:T(8,128)S(1)} collective-permute-done((f32[25,1600]{1,0:T(8,128)S(1)}, f32[25,1600]{1,0:T(8,128)S(1)}, u32[]{:S(2)}, u32[]{:S(2)}) %collective-permute-start.1) | collective-permute-done | bytes 160032 | tf_op jit(solution)/shard_map/ppermute | solution.py:37
  18.0 1.9 %fusion.12 = (bf16[25,1600]{1,0:T(8,128)(2,1)S(1)}, f32[25,1600]{1,0:T(8,128)}, f32[25,1600]{1,0:T(8,128)}) fusion(f32[25,1600]{1,0:T(8,128)} %param.10, f32[25,1600]{1,0:T(8,128)S(1)} %add.136, f32[25,1600]{1,0:T(8,128)S(1)} %collective-permute-done.1, f32[25,1600]{1,0:T(8,128)} %param.11), kind=kLoop, calls=%fused_computation.52 | loop fusion | flops 360000 | bytes 1040000 | tf_op jit(solution)/shard_map/convert_element_type | solution.py:110
  19.9 1.0 %collective-permute-start.2 = (bf16[25,1600]{1,0:T(8,128)(2,1)S(1)}, bf16[25,1600]{1,0:T(8,128)(2,1)S(1)}, u32[]{:S(2)}, u32[]{:S(2)}) collective-permute-start(bf16[25,1600]{1,0:T(8,128)(2,1)S(1)} %get-tuple-element.14), channel_id=1, source_target_pairs={{0,129},{1,128},{2,131},{3,130},{4,133},{5,132},{6,135},{7,134},{8... | collective-permute-start | bytes 240008 | tf_op jit(solution)/shard_map/ppermute | solution.py:50
  20.9 3.7 %collective-permute-done.2 = bf16[25,1600]{1,0:T(8,128)(2,1)S(1)} collective-permute-done((bf16[25,1600]{1,0:T(8,128)(2,1)S(1)}, bf16[25,1600]{1,0:T(8,128)(2,1)S(1)}, u32[]{:S(2)}, u32[]{:S(2)}) %collective-permute-start.2) | collective-permute-done | bytes 80032 | tf_op jit(solution)/shard_map/ppermute | solution.py:50
  24.6 0.1 maximum_select_fusion.1
  24.7 0.1 collective-permute-start.5
  24.8 2.0 %collective-permute-start.4 = (bf16[50,1600]{1,0:T(8,128)(2,1)S(1)}, bf16[50,1600]{1,0:T(8,128)(2,1)S(1)}, u32[]{:S(2)}, u32[]{:S(2)}) collective-permute-start(bf16[50,1600]{1,0:T(8,128)(2,1)S(1)} %maximum_select_fusion.1), channel_id=1, source_target_pairs={{4,0},{5,1},{6,2},{7,3},{0,4},{1,5},{2,6},{3,7},{12,8},{13,9},{14,... | collective-permute-start | bytes 480008 | tf_op jit(solution)/shard_map/ppermute | solution.py:57
  26.8 1.2 %collective-permute-start.3 = (bf16[50,1600]{1,0:T(8,128)(2,1)S(1)}, bf16[50,1600]{1,0:T(8,128)(2,1)S(1)}, u32[]{:S(2)}, u32[]{:S(2)}) collective-permute-start(bf16[50,1600]{1,0:T(8,128)(2,1)S(1)} %maximum_select_fusion.1), channel_id=1, source_target_pairs={{2,0},{3,1},{4,2},{5,3},{6,4},{7,5},{0,6},{1,7},{10,8},{11,9},{12,... | collective-permute-start | bytes 480008 | tf_op jit(solution)/shard_map/ppermute | solution.py:57
  28.0 0.1 maximum_select_fusion
  28.1 4.4 %collective-permute-done.5 = bf16[50,1600]{1,0:T(8,128)(2,1)S(1)} collective-permute-done((bf16[50,1600]{1,0:T(8,128)(2,1)S(1)}, bf16[50,1600]{1,0:T(8,128)(2,1)S(1)}, u32[]{:S(2)}, u32[]{:S(2)}) %collective-permute-start.5) | collective-permute-done | bytes 160032 | tf_op jit(solution)/shard_map/ppermute | solution.py:57
  32.4 0.9 collective-permute-done.4
  33.3 1.8 %collective-permute-done.3 = bf16[50,1600]{1,0:T(8,128)(2,1)S(1)} collective-permute-done((bf16[50,1600]{1,0:T(8,128)(2,1)S(1)}, bf16[50,1600]{1,0:T(8,128)(2,1)S(1)}, u32[]{:S(2)}, u32[]{:S(2)}) %collective-permute-start.3) | collective-permute-done | bytes 160032 | tf_op jit(solution)/shard_map/ppermute | solution.py:57
  35.1 0.1 pad_maximum_fusion
  35.3 0.0 copy-start.1
  35.3 0.7 gather_fusion
  35.9 0.3 gather.10
  36.3 0.0 copy-start.2
  36.3 2.8 %broadcast_in_dim.26 = bf16[1600,1600]{1,0:T(8,128)(2,1)} broadcast(bf16[]{:T(256)} %constant.128.clone.1), dimensions={} | broadcast | bytes 5120002 | tf_op jit(solution)/shard_map/broadcast_in_dim | solution.py:72
  39.0 1.2 %constant_dynamic-update-slice_fusion.6 = (bf16[1600,1600]{1,0:T(8,128)(2,1)}, bf16[200,1600]{1,0:T(8,128)(2,1)}) fusion(bf16[1600,1600]{1,0:T(8,128)(2,1)} %broadcast_in_dim.26, s32[]{:T(128)S(6)} %select_n.159, bf16[200,1600]{1,0:T(8,128)(2,1)S(1)} %gather.10, pred[200]{0:T(512)(128)(4,1)S(1)} %broadcast_in_dim.28), kind=kLoop, calls=%fused_computation.42 | loop fusion | flops 320000 | bytes 1971404 | tf_op jit(solution)/shard_map/dynamic_update_slice | solution.py:72
  40.3 0.0 collective-permute-start.6
  40.3 0.1 compare_and_fusion
  40.4 0.6 gather_fusion.2
  40.9 0.1 broadcast_select_fusion.1
  41.0 7.2 %collective-permute-start.14 = (f32[2,100,64]{1,2,0:T(8,128)S(1)}, f32[2,100,64]{1,2,0:T(8,128)S(1)}, u32[]{:S(2)}, u32[]{:S(2)}) collective-permute-start(f32[2,100,64]{1,2,0:T(8,128)S(1)} %broadcast_select_fusion.1), channel_id=1, source_target_pairs={{0,64},{64,0},{128,192},{192,128},{1,65},{65,1},{129,193},{193,129... | collective-permute-start | bytes 153608 | tf_op jit(solution)/shard_map/ppermute | solution.py:99
  48.2 0.1 compare_and_fusion.1
  48.3 0.6 gather_fusion.1
  48.9 3.6 %collective-permute-done.6 = bf16[200,1600]{1,0:T(8,128)(2,1)} collective-permute-done((bf16[200,1600]{1,0:T(8,128)(2,1)}, bf16[200,1600]{1,0:T(8,128)(2,1)}, u32[]{:S(2)}, u32[]{:S(2)}) %collective-permute-start.6) | collective-permute-done | bytes 640032 | tf_op jit(solution)/shard_map/ppermute | solution.py:75
  52.4 0.0 collective-permute-start.8
  52.4 0.0 collective-permute-done.14
  52.4 0.1 select_add_fusion
  52.5 0.1 collective-permute-start.15
  52.6 7.5 %collective-permute-start.7 = (bf16[200,1600]{1,0:T(8,128)(2,1)}, bf16[200,1600]{1,0:T(8,128)(2,1)}, u32[]{:S(2)}, u32[]{:S(2)}) collective-permute-start(bf16[200,1600]{1,0:T(8,128)(2,1)} %collective-permute-done.6), channel_id=1, source_target_pairs={{0,64},{64,0},{128,192},{192,128},{1,65},{65,1},{129,193},{193,129... | collective-permute-start | bytes 1920008 | tf_op jit(solution)/shard_map/ppermute | solution.py:76
  60.2 0.9 fusion.13
  61.2 2.2 %collective-permute-done.8 = bf16[200,1600]{1,0:T(8,128)(2,1)S(1)} collective-permute-done((bf16[200,1600]{1,0:T(8,128)(2,1)}, bf16[200,1600]{1,0:T(8,128)(2,1)S(1)}, u32[]{:S(2)}, u32[]{:S(2)}) %collective-permute-start.8) | collective-permute-done | bytes 640032 | tf_op jit(solution)/shard_map/ppermute | solution.py:75
  63.4 0.0 collective-permute-start.10
  63.4 0.0 collective-permute-done.15
  63.4 1.9 %multiply_subtract_fusion = (f32[100,1600]{1,0:T(8,128)}, f32[100,1600]{1,0:T(8,128)}) fusion(f32[100,1600]{1,0:T(8,128)S(1)} %copy-done.1, f32[100,1600]{1,0:T(8,128)S(1)} %copy-done.2, f32[1600,64]{0,1:T(8,128)S(1)} %copy-done, f32[100,64]{0,1:T(8,128)S(1)} %fusion.13, f32[100,64]{0,1:T(8,128)S(1)} %collective-permute-done.15, ...), kind=kOutput, calls=%fused_computation.4 | convolution fusion | flops 123859200 | bytes 3188736 | tf_op jit(solution)/shard_map/dot_general | solution.py:104
  65.4 8.4 %collective-permute-start.9 = (bf16[200,1600]{1,0:T(8,128)(2,1)S(1)}, bf16[200,1600]{1,0:T(8,128)(2,1)S(1)}, u32[]{:S(2)}, u32[]{:S(2)}) collective-permute-start(bf16[200,1600]{1,0:T(8,128)(2,1)S(1)} %collective-permute-done.8), channel_id=1, source_target_pairs={{0,64},{64,0},{128,192},{192,128},{1,65},{65,1},{129,193},{193,129... | collective-permute-start | bytes 1920008 | tf_op jit(solution)/shard_map/ppermute | solution.py:76
  73.7 2.0 %constant_dynamic-update-slice_fusion.5 = bf16[1600,1600]{1,0:T(8,128)(2,1)} fusion(bf16[1600,1600]{1,0:T(8,128)(2,1)} %get-tuple-element.12, bf16[200,1600]{1,0:T(8,128)(2,1)} %collective-permute-done.6, s32[]{:T(128)S(6)} %select_n.162), kind=kLoop, calls=%fused_computation.41 | loop fusion | bytes 1331204 | tf_op jit(solution)/shard_map/dynamic_update_slice | solution.py:77
  75.7 0.0 collective-permute-done.7
  75.7 2.0 %constant_dynamic-update-slice_fusion.4 = bf16[1600,1600]{1,0:T(8,128)(2,1)} fusion(bf16[1600,1600]{1,0:T(8,128)(2,1)} %constant_dynamic-update-slice_fusion.5, bf16[200,1600]{1,0:T(8,128)(2,1)} %collective-permute-done.7, s32[]{:T(128)S(6)} %select_n.164), kind=kLoop, calls=%fused_computation.40 | loop fusion | bytes 1331204 | tf_op jit(solution)/shard_map/dynamic_update_slice | solution.py:78
  77.7 0.2 constant_dynamic-slice_fusion
  77.9 0.1 collective-permute-start.12
  78.0 6.0 %collective-permute-start.11 = (bf16[200,1600]{1,0:T(8,128)(2,1)S(1)}, bf16[200,1600]{1,0:T(8,128)(2,1)S(1)}, u32[]{:S(2)}, u32[]{:S(2)}) collective-permute-start(bf16[200,1600]{1,0:T(8,128)(2,1)S(1)} %collective-permute-done.10), channel_id=1, source_target_pairs={{0,64},{64,0},{128,192},{192,128},{1,65},{65,1},{129,193},{193,129... | collective-permute-start | bytes 1920008 | tf_op jit(solution)/shard_map/ppermute | solution.py:76
  84.0 0.9 constant_dynamic-update-slice_fusion.3
  84.8 0.9 constant_dynamic-update-slice_fusion.2
  85.7 0.0 collective-permute-done.12
  85.7 3.1 %collective-permute-start.13 = (bf16[200,832]{1,0:T(8,128)(2,1)}, bf16[200,832]{1,0:T(8,128)(2,1)S(1)}, u32[]{:S(2)}, u32[]{:S(2)}) collective-permute-start(bf16[200,832]{1,0:T(8,128)(2,1)} %collective-permute-done.12), channel_id=1, source_target_pairs={{0,64},{64,0},{128,192},{192,128},{1,65},{65,1},{129,193},{193,129... | collective-permute-start | bytes 998408 | tf_op jit(solution)/shard_map/ppermute | solution.py:83
  88.9 0.9 constant_dynamic-update-slice_fusion.1
  89.8 0.0 collective-permute-done.11
  89.8 0.9 constant_dynamic-update-slice_fusion
  90.7 4.1 %dynamic_update_slice.34 = bf16[1600,1600]{1,0:T(8,128)(2,1)} dynamic-update-slice(bf16[1600,1600]{1,0:T(8,128)(2,1)} %constant_dynamic-update-slice_fusion, bf16[200,832]{1,0:T(8,128)(2,1)} %collective-permute-done.12, s32[]{:T(128)S(6)} %select_n.175, s32[]{:T(128)S(6)} %select_n.173) | dynamic-update-slice | bytes 665604 | tf_op jit(solution)/shard_map/dynamic_update_slice | solution.py:85
  94.7 0.0 collective-permute-done.13
  94.7 4.5 %dynamic_update_slice.35 = bf16[1600,1600]{1,0:T(8,128)(2,1)} dynamic-update-slice(bf16[1600,1600]{1,0:T(8,128)(2,1)} %dynamic_update_slice.34, bf16[200,832]{1,0:T(8,128)(2,1)S(1)} %collective-permute-done.13, s32[]{:T(128)S(6)} %select_n.175, s32[]{:T(128)S(6)} %select_n.176) | dynamic-update-slice | bytes 665604 | tf_op jit(solution)/shard_map/dynamic_update_slice | solution.py:86
  (11 shorter events, 0.1 us)
Async XLA Ops:
  0.6 6.3 %copy-start = (f32[1600,64]{0,1:T(8,128)S(1)}, f32[1600,64]{0,1:T(8,128)}, u32[]{:S(2)}) copy-start(f32[1600,64]{0,1:T(8,128)} %param.15) | copy-start | bytes 1228804
  1.7 8.5 %collective-permute-start = (f32[25,1600]{1,0:T(8,128)S(1)}, f32[25,1600]{1,0:T(8,128)}, u32[]{:S(2)}, u32[]{:S(2)}) collective-permute-start(f32[25,1600]{1,0:T(8,128)S(1)} %bitcast_subtract_fusion), channel_id=1, source_target_pairs={{0,64},{64,0},{128,192},{192,128},{1,65},{65,1},{129,193},{193,129... | collective-permute-start | bytes 480008 | tf_op jit(solution)/shard_map/ppermute | solution.py:36
  11.2 6.8 %collective-permute-start.1 = (f32[25,1600]{1,0:T(8,128)S(1)}, f32[25,1600]{1,0:T(8,128)S(1)}, u32[]{:S(2)}, u32[]{:S(2)}) collective-permute-start(f32[25,1600]{1,0:T(8,128)S(1)} %add.136), channel_id=1, source_target_pairs={{0,128},{64,192},{128,0},{192,64},{1,129},{65,193},{129,1},{193,65... | collective-permute-start | bytes 480008 | tf_op jit(solution)/shard_map/ppermute | solution.py:37
  19.9 4.8 %collective-permute-start.2 = (bf16[25,1600]{1,0:T(8,128)(2,1)S(1)}, bf16[25,1600]{1,0:T(8,128)(2,1)S(1)}, u32[]{:S(2)}, u32[]{:S(2)}) collective-permute-start(bf16[25,1600]{1,0:T(8,128)(2,1)S(1)} %get-tuple-element.14), channel_id=1, source_target_pairs={{0,129},{1,128},{2,131},{3,130},{4,133},{5,132},{6,135},{7,134},{8... | collective-permute-start | bytes 240008 | tf_op jit(solution)/shard_map/ppermute | solution.py:50
  24.7 7.7 %collective-permute-start.5 = (bf16[50,1600]{1,0:T(8,128)(2,1)S(1)}, bf16[50,1600]{1,0:T(8,128)(2,1)S(1)}, u32[]{:S(2)}, u32[]{:S(2)}) collective-permute-start(bf16[50,1600]{1,0:T(8,128)(2,1)S(1)} %maximum_select_fusion.1), channel_id=1, source_target_pairs={{6,0},{7,1},{0,2},{1,3},{2,4},{3,5},{4,6},{5,7},{14,8},{15,9},{8,1... | collective-permute-start | bytes 480008 | tf_op jit(solution)/shard_map/ppermute | solution.py:57
  24.8 8.5 %collective-permute-start.4 = (bf16[50,1600]{1,0:T(8,128)(2,1)S(1)}, bf16[50,1600]{1,0:T(8,128)(2,1)S(1)}, u32[]{:S(2)}, u32[]{:S(2)}) collective-permute-start(bf16[50,1600]{1,0:T(8,128)(2,1)S(1)} %maximum_select_fusion.1), channel_id=1, source_target_pairs={{4,0},{5,1},{6,2},{7,3},{0,4},{1,5},{2,6},{3,7},{12,8},{13,9},{14,... | collective-permute-start | bytes 480008 | tf_op jit(solution)/shard_map/ppermute | solution.py:57
  26.8 8.3 %collective-permute-start.3 = (bf16[50,1600]{1,0:T(8,128)(2,1)S(1)}, bf16[50,1600]{1,0:T(8,128)(2,1)S(1)}, u32[]{:S(2)}, u32[]{:S(2)}) collective-permute-start(bf16[50,1600]{1,0:T(8,128)(2,1)S(1)} %maximum_select_fusion.1), channel_id=1, source_target_pairs={{2,0},{3,1},{4,2},{5,3},{6,4},{7,5},{0,6},{1,7},{10,8},{11,9},{12,... | collective-permute-start | bytes 480008 | tf_op jit(solution)/shard_map/ppermute | solution.py:57
  35.3 24.9 %copy-start.1 = (f32[100,1600]{1,0:T(8,128)S(1)}, f32[100,1600]{1,0:T(8,128)}, u32[]{:S(2)}) copy-start(f32[100,1600]{1,0:T(8,128)} %param.13) | copy-start | bytes 1920004
  36.3 27.1 %copy-start.2 = (f32[100,1600]{1,0:T(8,128)S(1)}, f32[100,1600]{1,0:T(8,128)}, u32[]{:S(2)}) copy-start(f32[100,1600]{1,0:T(8,128)} %param.14) | copy-start | bytes 1920004
  40.3 12.2 %collective-permute-start.6 = (bf16[200,1600]{1,0:T(8,128)(2,1)}, bf16[200,1600]{1,0:T(8,128)(2,1)}, u32[]{:S(2)}, u32[]{:S(2)}) collective-permute-start(bf16[200,1600]{1,0:T(8,128)(2,1)} %get-tuple-element.13), channel_id=1, source_target_pairs={{0,56},{1,57},{2,58},{3,59},{4,60},{5,61},{6,62},{7,63},{8,0},{9,1... | collective-permute-start | bytes 1920008 | tf_op jit(solution)/shard_map/ppermute | solution.py:75
  41.0 11.4 %collective-permute-start.14 = (f32[2,100,64]{1,2,0:T(8,128)S(1)}, f32[2,100,64]{1,2,0:T(8,128)S(1)}, u32[]{:S(2)}, u32[]{:S(2)}) collective-permute-start(f32[2,100,64]{1,2,0:T(8,128)S(1)} %broadcast_select_fusion.1), channel_id=1, source_target_pairs={{0,64},{64,0},{128,192},{192,128},{1,65},{65,1},{129,193},{193,129... | collective-permute-start | bytes 153608 | tf_op jit(solution)/shard_map/ppermute | solution.py:99
  52.4 11.0 %collective-permute-start.8 = (bf16[200,1600]{1,0:T(8,128)(2,1)}, bf16[200,1600]{1,0:T(8,128)(2,1)S(1)}, u32[]{:S(2)}, u32[]{:S(2)}) collective-permute-start(bf16[200,1600]{1,0:T(8,128)(2,1)} %collective-permute-done.6), channel_id=1, source_target_pairs={{0,56},{1,57},{2,58},{3,59},{4,60},{5,61},{6,62},{7,63},{8,0},{9,1... | collective-permute-start | bytes 1920008 | tf_op jit(solution)/shard_map/ppermute | solution.py:75
  52.5 10.9 %collective-permute-start.15 = (f32[100,64]{0,1:T(8,128)S(1)}, f32[100,64]{0,1:T(8,128)S(1)}, u32[]{:S(2)}, u32[]{:S(2)}) collective-permute-start(f32[100,64]{0,1:T(8,128)S(1)} %slice_bitcast_fusion), channel_id=1, source_target_pairs={{0,128},{64,192},{128,0},{192,64},{1,129},{65,193},{129,1},{193,65... | collective-permute-start | bytes 76808 | tf_op jit(solution)/shard_map/ppermute | solution.py:102
  52.6 23.1 %collective-permute-start.7 = (bf16[200,1600]{1,0:T(8,128)(2,1)}, bf16[200,1600]{1,0:T(8,128)(2,1)}, u32[]{:S(2)}, u32[]{:S(2)}) collective-permute-start(bf16[200,1600]{1,0:T(8,128)(2,1)} %collective-permute-done.6), channel_id=1, source_target_pairs={{0,64},{64,0},{128,192},{192,128},{1,65},{65,1},{129,193},{193,129... | collective-permute-start | bytes 1920008 | tf_op jit(solution)/shard_map/ppermute | solution.py:76
  63.4 14.3 %collective-permute-start.10 = (bf16[200,1600]{1,0:T(8,128)(2,1)S(1)}, bf16[200,1600]{1,0:T(8,128)(2,1)S(1)}, u32[]{:S(2)}, u32[]{:S(2)}) collective-permute-start(bf16[200,1600]{1,0:T(8,128)(2,1)S(1)} %collective-permute-done.8), channel_id=1, source_target_pairs={{0,56},{1,57},{2,58},{3,59},{4,60},{5,61},{6,62},{7,63},{8,0},{9,1... | collective-permute-start | bytes 1920008 | tf_op jit(solution)/shard_map/ppermute | solution.py:75
  65.4 19.5 %collective-permute-start.9 = (bf16[200,1600]{1,0:T(8,128)(2,1)S(1)}, bf16[200,1600]{1,0:T(8,128)(2,1)S(1)}, u32[]{:S(2)}, u32[]{:S(2)}) collective-permute-start(bf16[200,1600]{1,0:T(8,128)(2,1)S(1)} %collective-permute-done.8), channel_id=1, source_target_pairs={{0,64},{64,0},{128,192},{192,128},{1,65},{65,1},{129,193},{193,129... | collective-permute-start | bytes 1920008 | tf_op jit(solution)/shard_map/ppermute | solution.py:76
  77.9 7.9 %collective-permute-start.12 = (bf16[200,832]{1,0:T(8,128)(2,1)S(1)}, bf16[200,832]{1,0:T(8,128)(2,1)}, u32[]{:S(2)}, u32[]{:S(2)}) collective-permute-start(bf16[200,832]{1,0:T(8,128)(2,1)S(1)} %constant_dynamic-slice_fusion), channel_id=1, source_target_pairs={{0,56},{1,57},{2,58},{3,59},{4,60},{5,61},{6,62},{7,63},{8,0},{9,1... | collective-permute-start | bytes 998408 | tf_op jit(solution)/shard_map/ppermute | solution.py:82
  78.0 11.8 %collective-permute-start.11 = (bf16[200,1600]{1,0:T(8,128)(2,1)S(1)}, bf16[200,1600]{1,0:T(8,128)(2,1)S(1)}, u32[]{:S(2)}, u32[]{:S(2)}) collective-permute-start(bf16[200,1600]{1,0:T(8,128)(2,1)S(1)} %collective-permute-done.10), channel_id=1, source_target_pairs={{0,64},{64,0},{128,192},{192,128},{1,65},{65,1},{129,193},{193,129... | collective-permute-start | bytes 1920008 | tf_op jit(solution)/shard_map/ppermute | solution.py:76
  85.7 9.0 %collective-permute-start.13 = (bf16[200,832]{1,0:T(8,128)(2,1)}, bf16[200,832]{1,0:T(8,128)(2,1)S(1)}, u32[]{:S(2)}, u32[]{:S(2)}) collective-permute-start(bf16[200,832]{1,0:T(8,128)(2,1)} %collective-permute-done.12), channel_id=1, source_target_pairs={{0,64},{64,0},{128,192},{192,128},{1,65},{65,1},{129,193},{193,129... | collective-permute-start | bytes 998408 | tf_op jit(solution)/shard_map/ppermute | solution.py:83

commit v5 on v2

--- a/solution.py
+++ b/solution.py
@@ -46,6 +46,7 @@
     yh = si % NYH
     core = gi % 2
     swap = [(i, i ^ 1) for i in range(NG)]
+    ns = NZ * NX * NYH
 
     other = lax.ppermute(blk, ("grp", "shard"), both(lambda g, s: (g ^ 2, s ^ 1)))
     b50 = jnp.zeros((NYH * rows, d), blk.dtype)
@@ -67,21 +68,29 @@
         return g, sidx(zz - 1, xx, yy) if g % 2 == 0 else sidx(zz + 1, xx, yy)
 
     zpairs = both(zring)
+    cut = (d // 2) // 128 * 128
     sign = 1 - 2 * core
     out = lax.dynamic_update_slice(jnp.zeros((NZ * zb, d), blk.dtype), b200, (z * zb, 0))
-    cur = b200
+    cur = [b200[:, :cut], b200[:, cut:]]
     for k in range(1, NZ // 2):
-        cur = lax.ppermute(cur, ("grp", "shard"), zpairs)
-        mate = lax.ppermute(cur, "grp", swap)
-        out = lax.dynamic_update_slice(out, cur, (((z + sign * k) % NZ) * zb, 0))
-        out = lax.dynamic_update_slice(out, mate, (((z - sign * k) % NZ) * zb, 0))
-    half = zb // 2
-    send_half = lax.dynamic_slice_in_dim(cur, core * half, half, 0)
-    got = lax.ppermute(send_half, ("grp", "shard"), zpairs)
-    mate = lax.ppermute(got, "grp", swap)
-    z4 = (z + NZ // 2) % NZ
-    out = lax.dynamic_update_slice(out, got, (z4 * zb + core * half, 0))
-    out = lax.dynamic_update_slice(out, mate, (z4 * zb + (1 - core) * half, 0))
+        cur = [lax.ppermute(c, ("grp", "shard"), zpairs) for c in cur]
+        mate = [lax.ppermute(c, "grp", swap) for c in cur]
+        mine_at = ((z + sign * k) % NZ) * zb
+        mate_at = ((z - sign * k) % NZ) * zb
+        for c, m, col in zip(cur, mate, (0, cut)):
+            out = lax.dynamic_update_slice(out, c, (mine_at, col))
+            out = lax.dynamic_update_slice(out, m, (mate_at, col))
+    z4 = ((z + NZ // 2) % NZ) * zb
+    first = [p for p in zpairs if (p[1] // ns) % 2 == 0]
+    second = [p for p in zpairs if (p[1] // ns) % 2 == 1]
+    got_a = lax.ppermute(cur[0], ("grp", "shard"), first)
+    got_b = lax.ppermute(cur[1], ("grp", "shard"), second)
+    sw_a = lax.ppermute(got_a, "grp", [(i, i ^ 1) for i in range(NG) if i % 2 == 0])
+    sw_b = lax.ppermute(got_b, "grp", [(i, i ^ 1) for i in range(NG) if i % 2 == 1])
+    got_a = jnp.where(core == 0, got_a, sw_a)
+    got_b = jnp.where(core == 0, sw_b, got_b)
+    out = lax.dynamic_update_slice(out, got_a, (z4, 0))
+    out = lax.dynamic_update_slice(out, got_b, (z4, cut))
     return out
 
 

time: 92.3 us -> 87.9 us (0.952)
  waiting for transfers between devices: 19.5 us -> 39.1 us
  local copies, waits for them, and re-layouts: 25.9 us -> 12.9 us
  starting transfers between devices: 34.8 us -> 22.6 us
  other arithmetic: 3.4 us -> 4.43 us
    ppermute x8 -> x16, waiting for transfers between devices: 7.55 us -> 26.7 us  [the longest x6 19.7 us: gather_copy(): cur = [lax.ppermute(c, ('grp', 'shard'), zpairs) for c in cur]]
    dynamic_update_slice x8 -> x12, local copies, waits for them, and re-layouts: 11.9 us -> 0.43 us  [the longest x6 0.22 us: gather_copy(): out = lax.dynamic_update_slice(out, c, (mine_at, col))]
    ppermute x8 -> x16, starting transfers between devices: 21.6 us -> 16.1 us  [the longest x6 7.59 us: gather_copy(): mate = [lax.ppermute(c, 'grp', swap) for c in cur]]
    ppermute x1, starting transfers between devices: 5.15 us -> 0.06 us  [per_device(): lax.ppermute(jnp.take(parts, send1, axis=0), 'grp', [(i, i ^ 1) for i in...]
    ppermute x1, waiting for transfers between devices: 0.01 us -> 2.77 us  [gather_copy(): lax.ppermute(blk, ('grp', 'shard'), both(lambda g, s: (g ^ 2, s ^ 1)))]
    ppermute x3, waiting for transfers between devices: 6 us -> 3.41 us  [gather_copy(): lax.ppermute(b50, 'shard', [(sidx(zxy(s)[0], zxy(s)[1] + k, zxy(s)[2]), s...]
    broadcast_in_dim x1, local copies, waits for them, and re-layouts: 2.76 us -> 0.37 us  [gather_copy(): jnp.zeros((NZ * zb, d), blk.dtype)]
    unnamed x6 -> x8, local copies, waits for them, and re-layouts: 0.02 us -> 2.4 us
  transfers between devices with their start and end apart: 16 -> 24, of which waited for: 9 -> 11; matrix products, arithmetic and copies ran while one was open for 31% -> 22% of each run, Pallas kernels for 0% -> 0%
where the time goes in v5:
time: 87.9 us; the launch traced here: 87.6 us
  waiting for transfers between devices  39.1 us (44%)
  starting transfers between devices  22.6 us (26%)
  local copies, waits for them, and re-layouts  12.9 us (15%)
  matrix products  7.2 us (8%)
  other arithmetic  4.43 us (5%)
  between operations  1.33 us (2%)
    ppermute x6, waiting for transfers between devices, gather_copy(): cur = [lax.ppermute(c, ('grp', 'shard'), zpairs) for c in cur]  19.7 us
    ppermute x6, starting transfers between devices, gather_copy(): mate = [lax.ppermute(c, 'grp', swap) for c in cur]  7.59 us
    ppermute x1, waiting for transfers between devices, butterfly_sum(): return v + lax.ppermute(v, 'grp', [(i, i ^ 2) for i in range(NG)])  6.22 us
    ppermute x1, waiting for transfers between devices, gather_copy(): got_b = lax.ppermute(cur[1], ('grp', 'shard'), second)  5.92 us
    dynamic_update_slice x3, local copies, waits for them, and re-layouts, gather_copy(): b200 = lax.dynamic_update_slice(b200, got, ((x + k) % NX * NYH * rows, 0))  3.64 us
    ppermute x3, waiting for transfers between devices, gather_copy(): lax.ppermute(b50, 'shard', [(sidx(zxy(s)[0], zxy(s)[1] + k, zxy(s)[2]), s...  3.41 us
    ppermute x6, starting transfers between devices, gather_copy(): cur = [lax.ppermute(c, ('grp', 'shard'), zpairs) for c in cur]  3.37 us
    ppermute x1, starting transfers between devices, butterfly_sum(): v = v + lax.ppermute(v, 'grp', [(i, i ^ 1) for i in range(NG)])  3.29 us
  transfers between devices with their start and end apart: 24, of which 11 were waited for; matrix products, arithmetic and copies ran while one was open for 22% of the time, Pallas kernels for 0%

profile of v5, /device:TPU:1, one launch (start us, length us, event | category | flops | bytes accessed | tf_op | source)
XLA Modules:
  0.0 87.6 jit_solution(766601584173698288)
XLA Ops:
  0.6 0.0 copy-start
  0.6 1.1 %bitcast_subtract_fusion = f32[25,1600]{1,0:T(8,128)S(1)} fusion(f32[25,1600]{1,0:T(8,128)} %param.10, f32[1,25,1600]{2,0,1:T(1,128)} %param.9), kind=kLoop, calls=%fused_computation.8 | loop fusion | flops 40000 | bytes 480000 | tf_op jit(solution)/shard_map/sub | solution.py:114
  1.7 3.3 %collective-permute-start = (f32[25,1600]{1,0:T(8,128)S(1)}, f32[25,1600]{1,0:T(8,128)}, u32[]{:S(2)}, u32[]{:S(2)}) collective-permute-start(f32[25,1600]{1,0:T(8,128)S(1)} %bitcast_subtract_fusion), channel_id=1, source_target_pairs={{0,64},{64,0},{128,192},{192,128},{1,65},{65,1},{129,193},{193,129... | collective-permute-start | bytes 480008 | tf_op jit(solution)/shard_map/ppermute | solution.py:36
  5.0 1.9 %dot_general.12 = f32[4,100,1600]{2,1,0:T(8,128)S(1)} reshape(f32[1,400,1600]{2,1,0:T(8,128)} %param.12) | data formatting | bytes 5120000 | tf_op jit(solution)/shard_map/dot_general | solution.py:101
  6.9 0.1 compare_and_fusion
  7.0 3.3 %fusion = f32[4,100,64]{1,2,0:T(8,128)S(1)} fusion(f32[4,100,1600]{2,1,0:T(8,128)S(1)} %dot_general.12, f32[1600,64]{0,1:T(8,128)S(1)} %copy-done), kind=kOutput, calls=%fused_computation.4 | convolution fusion | flops 491520000 | bytes 3072000 | tf_op jit(solution)/shard_map/dot_general | solution.py:101
  10.3 0.0 copy-start.3
  10.3 0.6 gather_fusion.1
  10.9 0.1 broadcast_select_fusion
  11.0 0.1 collective-permute-start.22
  11.0 0.1 compare_and_fusion.1
  11.1 0.6 gather_fusion
  11.7 0.0 collective-permute-done
  11.7 1.0 %add.139 = f32[25,1600]{1,0:T(8,128)S(1)} add(f32[25,1600]{1,0:T(8,128)S(1)} %bitcast_subtract_fusion, f32[25,1600]{1,0:T(8,128)} %collective-permute-done) | non-fusion elementwise | flops 40000 | bytes 480000 | tf_op jit(solution)/shard_map/add | solution.py:36
  12.7 0.1 collective-permute-start.1
  12.8 0.0 collective-permute-done.22
  12.8 0.1 select_add_fusion
  12.9 6.2 %collective-permute-done.1 = f32[25,1600]{1,0:T(8,128)S(1)} collective-permute-done((f32[25,1600]{1,0:T(8,128)S(1)}, f32[25,1600]{1,0:T(8,128)S(1)}, u32[]{:S(2)}, u32[]{:S(2)}) %collective-permute-start.1) | collective-permute-done | bytes 160032 | tf_op jit(solution)/shard_map/ppermute | solution.py:37
  19.1 1.9 %fusion.9 = (bf16[25,1600]{1,0:T(8,128)(2,1)S(1)}, f32[25,1600]{1,0:T(8,128)}, f32[25,1600]{1,0:T(8,128)}) fusion(f32[25,1600]{1,0:T(8,128)} %param.10, f32[25,1600]{1,0:T(8,128)S(1)} %add.139, f32[25,1600]{1,0:T(8,128)S(1)} %collective-permute-done.1, f32[25,1600]{1,0:T(8,128)} %param.11), kind=kLoop, calls=%fused_computation.41 | loop fusion | flops 360000 | bytes 1040000 | tf_op jit(solution)/shard_map/convert_element_type | solution.py:117
  20.9 1.0 %collective-permute-start.2 = (bf16[25,1600]{1,0:T(8,128)(2,1)S(1)}, bf16[25,1600]{1,0:T(8,128)(2,1)S(1)}, u32[]{:S(2)}, u32[]{:S(2)}) collective-permute-start(bf16[25,1600]{1,0:T(8,128)(2,1)S(1)} %get-tuple-element.12), channel_id=1, source_target_pairs={{0,129},{1,128},{2,131},{3,130},{4,133},{5,132},{6,135},{7,134},{8... | collective-permute-start | bytes 240008 | tf_op jit(solution)/shard_map/ppermute | solution.py:51
  22.0 0.0 collective-permute-start.23
  22.0 0.9 %dynamic_update_slice.63 = bf16[50,1600]{1,0:T(8,128)(2,1)S(1)} dynamic-update-slice(bf16[50,1600]{1,0:T(8,128)(2,1)S(1)} %broadcast_in_dim.20, bf16[25,1600]{1,0:T(8,128)(2,1)S(1)} %get-tuple-element.12, s32[]{:T(128)S(6)} %select_n.135, s32[]{:T(128)} %constant.128.clone.1) | dynamic-update-slice | bytes 160004 | tf_op jit(solution)/shard_map/dynamic_update_slice | solution.py:53
  22.9 2.8 %collective-permute-done.2 = bf16[25,1600]{1,0:T(8,128)(2,1)S(1)} collective-permute-done((bf16[25,1600]{1,0:T(8,128)(2,1)S(1)}, bf16[25,1600]{1,0:T(8,128)(2,1)S(1)}, u32[]{:S(2)}, u32[]{:S(2)}) %collective-permute-start.2) | collective-permute-done | bytes 80032 | tf_op jit(solution)/shard_map/ppermute | solution.py:51
  25.7 0.6 dynamic_update_slice.64
  26.3 0.9 %collective-permute-start.3 = (bf16[50,1600]{1,0:T(8,128)(2,1)S(1)}, bf16[50,1600]{1,0:T(8,128)(2,1)S(1)}, u32[]{:S(2)}, u32[]{:S(2)}) collective-permute-start(bf16[50,1600]{1,0:T(8,128)(2,1)S(1)} %dynamic_update_slice.64), channel_id=1, source_target_pairs={{2,0},{3,1},{4,2},{5,3},{6,4},{7,5},{0,6},{1,7},{10,8},{11,9},{12,... | collective-permute-start | bytes 480008 | tf_op jit(solution)/shard_map/ppermute | solution.py:59
  27.2 0.5 collective-permute-start.4
  27.7 0.6 collective-permute-start.5
  28.3 2.0 %fusion.10 = f32[100,64]{0,1:T(8,128)S(1)} fusion(f32[100,1600]{1,0:T(8,128)} %param.13, f32[1600,64]{0,1:T(8,128)S(1)} %copy-done), kind=kOutput, calls=%fused_computation.42 | convolution fusion | flops 122880000 | bytes 1075200 | tf_op jit(solution)/shard_map/dot_general | solution.py:110
  30.6 1.3 %dynamic_update_slice.65 = bf16[200,1600]{1,0:T(8,128)(2,1)S(1)} dynamic-update-slice(bf16[200,1600]{1,0:T(8,128)(2,1)S(1)} %broadcast_in_dim.19, bf16[50,1600]{1,0:T(8,128)(2,1)S(1)} %dynamic_update_slice.64, s32[]{:T(128)S(6)} %select_n.139, s32[]{:T(128)} %constant.128.clone.1) | dynamic-update-slice | bytes 320004 | tf_op jit(solution)/shard_map/dynamic_update_slice | solution.py:57
  32.0 1.3 %dynamic_update_slice.66 = bf16[200,1600]{1,0:T(8,128)(2,1)S(1)} dynamic-update-slice(bf16[200,1600]{1,0:T(8,128)(2,1)S(1)} %dynamic_update_slice.65, bf16[50,1600]{1,0:T(8,128)(2,1)S(1)} %collective-permute-done.3, s32[]{:T(128)S(6)} %select_n.141, s32[]{:T(128)} %constant.128.clone.1) | dynamic-update-slice | bytes 320004 | tf_op jit(solution)/shard_map/dynamic_update_slice | solution.py:64
  33.3 0.0 collective-permute-done.4
  33.3 1.3 %dynamic_update_slice.67 = bf16[200,1600]{1,0:T(8,128)(2,1)S(1)} dynamic-update-slice(bf16[200,1600]{1,0:T(8,128)(2,1)S(1)} %dynamic_update_slice.66, bf16[50,1600]{1,0:T(8,128)(2,1)S(1)} %collective-permute-done.4, s32[]{:T(128)S(6)} %select_n.143, s32[]{:T(128)} %constant.128.clone.1) | dynamic-update-slice | bytes 320004 | tf_op jit(solution)/shard_map/dynamic_update_slice | solution.py:64
  34.6 3.4 %collective-permute-done.5 = bf16[50,1600]{1,0:T(8,128)(2,1)S(1)} collective-permute-done((bf16[50,1600]{1,0:T(8,128)(2,1)S(1)}, bf16[50,1600]{1,0:T(8,128)(2,1)S(1)}, u32[]{:S(2)}, u32[]{:S(2)}) %collective-permute-start.5) | collective-permute-done | bytes 160032 | tf_op jit(solution)/shard_map/ppermute | solution.py:59
  38.0 1.0 %dynamic_update_slice.68 = bf16[200,1600]{1,0:T(8,128)(2,1)S(1)} dynamic-update-slice(bf16[200,1600]{1,0:T(8,128)(2,1)S(1)} %dynamic_update_slice.67, bf16[50,1600]{1,0:T(8,128)(2,1)S(1)} %collective-permute-done.5, s32[]{:T(128)S(6)} %select_n.145, s32[]{:T(128)} %constant.128.clone.1) | dynamic-update-slice | bytes 320004 | tf_op jit(solution)/shard_map/dynamic_update_slice | solution.py:64
  39.1 1.7 %collective-permute-start.6 = (bf16[200,768]{1,0:T(8,128)(2,1)S(1)}, bf16[200,768]{1,0:T(8,128)(2,1)S(1)}, u32[]{:S(2)}, u32[]{:S(2)}) collective-permute-start(bf16[200,768]{1,0:T(8,128)(2,1)S(1)} %slice.20), channel_id=1, source_target_pairs={{0,56},{1,57},{2,58},{3,59},{4,60},{5,61},{6,62},{7,63},{8,0},{9,1... | collective-permute-start | bytes 921608 | tf_op jit(solution)/shard_map/ppermute | solution.py:76
  40.8 1.6 %collective-permute-start.8 = (bf16[200,832]{1,0:T(8,128)(2,1)S(1)}, bf16[200,832]{1,0:T(8,128)(2,1)S(1)}, u32[]{:S(2)}, u32[]{:S(2)}) collective-permute-start(bf16[200,832]{1,0:T(8,128)(2,1)S(1)} %slice.21), channel_id=1, source_target_pairs={{0,56},{1,57},{2,58},{3,59},{4,60},{5,61},{6,62},{7,63},{8,0},{9,1... | collective-permute-start | bytes 998408 | tf_op jit(solution)/shard_map/ppermute | solution.py:76
  42.5 0.0 collective-permute-done.23
  42.5 2.0 %multiply_subtract_fusion = (f32[100,1600]{1,0:T(8,128)}, f32[100,1600]{1,0:T(8,128)}) fusion(f32[100,1600]{1,0:T(8,128)S(1)} %copy-done.2, f32[100,1600]{1,0:T(8,128)S(1)} %copy-done.3, f32[1600,64]{0,1:T(8,128)S(1)} %copy-done, f32[100,64]{0,1:T(8,128)S(1)} %fusion.10, f32[100,64]{0,1:T(8,128)S(1)} %collective-permute-done.23, ...), kind=kOutput, calls=%fused_computation.2 | convolution fusion | flops 123859200 | bytes 3188736 | tf_op jit(solution)/shard_map/dot_general | solution.py:111
  44.4 4.6 %collective-permute-done.6 = bf16[200,768]{1,0:T(8,128)(2,1)S(1)} collective-permute-done((bf16[200,768]{1,0:T(8,128)(2,1)S(1)}, bf16[200,768]{1,0:T(8,128)(2,1)S(1)}, u32[]{:S(2)}, u32[]{:S(2)}) %collective-permute-start.6) | collective-permute-done | bytes 307232 | tf_op jit(solution)/shard_map/ppermute | solution.py:76
  49.0 2.2 %collective-permute-start.7 = (bf16[200,768]{1,0:T(8,128)(2,1)S(1)}, bf16[200,768]{1,0:T(8,128)(2,1)S(1)}, u32[]{:S(2)}, u32[]{:S(2)}) collective-permute-start(bf16[200,768]{1,0:T(8,128)(2,1)S(1)} %collective-permute-done.6), channel_id=1, source_target_pairs={{0,64},{64,0},{128,192},{192,128},{1,65},{65,1},{129,193},{193,129... | collective-permute-start | bytes 921608 | tf_op jit(solution)/shard_map/ppermute | solution.py:77
  51.2 0.4 broadcast_in_dim.18
  51.6 0.1 constant_dynamic-update-slice_fusion.12
  51.7 1.1 %collective-permute-done.8 = bf16[200,832]{1,0:T(8,128)(2,1)S(1)} collective-permute-done((bf16[200,832]{1,0:T(8,128)(2,1)S(1)}, bf16[200,832]{1,0:T(8,128)(2,1)S(1)}, u32[]{:S(2)}, u32[]{:S(2)}) %collective-permute-start.8) | collective-permute-done | bytes 332832 | tf_op jit(solution)/shard_map/ppermute | solution.py:76
  52.8 2.6 %collective-permute-start.9 = (bf16[200,832]{1,0:T(8,128)(2,1)S(1)}, bf16[200,832]{1,0:T(8,128)(2,1)S(1)}, u32[]{:S(2)}, u32[]{:S(2)}) collective-permute-start(bf16[200,832]{1,0:T(8,128)(2,1)S(1)} %collective-permute-done.8), channel_id=1, source_target_pairs={{0,64},{64,0},{128,192},{192,128},{1,65},{65,1},{129,193},{193,129... | collective-permute-start | bytes 998408 | tf_op jit(solution)/shard_map/ppermute | solution.py:77
  55.5 0.0 collective-permute-start.12
  55.5 3.4 %collective-permute-done.10 = bf16[200,768]{1,0:T(8,128)(2,1)S(1)} collective-permute-done((bf16[200,768]{1,0:T(8,128)(2,1)S(1)}, bf16[200,768]{1,0:T(8,128)(2,1)S(1)}, u32[]{:S(2)}, u32[]{:S(2)}) %collective-permute-start.10) | collective-permute-done | bytes 307232 | tf_op jit(solution)/shard_map/ppermute | solution.py:76
  58.9 0.4 collective-permute-start.11
  59.4 3.9 %collective-permute-done.12 = bf16[200,832]{1,0:T(8,128)(2,1)S(1)} collective-permute-done((bf16[200,832]{1,0:T(8,128)(2,1)S(1)}, bf16[200,832]{1,0:T(8,128)(2,1)S(1)}, u32[]{:S(2)}, u32[]{:S(2)}) %collective-permute-start.12) | collective-permute-done | bytes 332832 | tf_op jit(solution)/shard_map/ppermute | solution.py:76
  63.3 0.4 collective-permute-start.13
  63.8 3.2 %collective-permute-done.14 = bf16[200,768]{1,0:T(8,128)(2,1)S(1)} collective-permute-done((bf16[200,768]{1,0:T(8,128)(2,1)S(1)}, bf16[200,768]{1,0:T(8,128)(2,1)S(1)}, u32[]{:S(2)}, u32[]{:S(2)}) %collective-permute-start.14) | collective-permute-done | bytes 307232 | tf_op jit(solution)/shard_map/ppermute | solution.py:76
  67.0 0.6 collective-permute-start.15
  67.6 0.7 collective-permute-start.18
  68.3 3.6 %collective-permute-done.16 = bf16[200,832]{1,0:T(8,128)(2,1)S(1)} collective-permute-done((bf16[200,832]{1,0:T(8,128)(2,1)S(1)}, bf16[200,832]{1,0:T(8,128)(2,1)S(1)}, u32[]{:S(2)}, u32[]{:S(2)}) %collective-permute-start.16) | collective-permute-done | bytes 332832 | tf_op jit(solution)/shard_map/ppermute | solution.py:76
  71.9 1.3 %collective-permute-start.17 = (bf16[200,832]{1,0:T(8,128)(2,1)S(1)}, bf16[200,832]{1,0:T(8,128)(2,1)S(1)}, u32[]{:S(2)}, u32[]{:S(2)}) collective-permute-start(bf16[200,832]{1,0:T(8,128)(2,1)S(1)} %collective-permute-done.16), channel_id=1, source_target_pairs={{0,64},{64,0},{128,192},{192,128},{1,65},{65,1},{129,193},{193,129... | collective-permute-start | bytes 998408 | tf_op jit(solution)/shard_map/ppermute | solution.py:77
  73.2 1.9 %collective-permute-start.20 = (bf16[200,832]{1,0:T(8,128)(2,1)S(1)}, bf16[200,832]{1,0:T(8,128)(2,1)S(1)}, u32[]{:S(2)}, u32[]{:S(2)}) collective-permute-start(bf16[200,832]{1,0:T(8,128)(2,1)S(1)} %collective-permute-done.16), channel_id=1, source_target_pairs={{64,72},{65,73},{66,74},{67,75},{68,76},{69,77},{70,78},{71,79},{7... | collective-permute-start | bytes 998408 | tf_op jit(solution)/shard_map/ppermute | solution.py:87
  75.2 0.0 collective-permute-done.18
  75.2 1.3 %collective-permute-start.19 = (bf16[200,768]{1,0:T(8,128)(2,1)S(1)}, bf16[200,768]{1,0:T(8,128)(2,1)S(1)}, u32[]{:S(2)}, u32[]{:S(2)}) collective-permute-start(bf16[200,768]{1,0:T(8,128)(2,1)S(1)} %collective-permute-done.18), channel_id=1, source_target_pairs={{0,64},{128,192},{1,65},{129,193},{2,66},{130,194},{3,67},{131,195... | collective-permute-start | bytes 921608 | tf_op jit(solution)/shard_map/ppermute | solution.py:88
  76.6 5.9 %collective-permute-done.20 = bf16[200,832]{1,0:T(8,128)(2,1)S(1)} collective-permute-done((bf16[200,832]{1,0:T(8,128)(2,1)S(1)}, bf16[200,832]{1,0:T(8,128)(2,1)S(1)}, u32[]{:S(2)}, u32[]{:S(2)}) %collective-permute-start.20) | collective-permute-done | bytes 332832 | tf_op jit(solution)/shard_map/ppermute | solution.py:87
  82.5 1.3 %collective-permute-start.21 = (bf16[200,832]{1,0:T(8,128)(2,1)S(1)}, bf16[200,832]{1,0:T(8,128)(2,1)S(1)}, u32[]{:S(2)}, u32[]{:S(2)}) collective-permute-start(bf16[200,832]{1,0:T(8,128)(2,1)S(1)} %collective-permute-done.20), channel_id=1, source_target_pairs={{64,0},{192,128},{65,1},{193,129},{66,2},{194,130},{67,3},{195,131... | collective-permute-start | bytes 998408 | tf_op jit(solution)/shard_map/ppermute | solution.py:89
  83.9 0.1 select_dynamic-update-slice_fusion.1
  84.0 1.1 %collective-permute-done.21 = bf16[200,832]{1,0:T(8,128)(2,1)S(1)} collective-permute-done((bf16[200,832]{1,0:T(8,128)(2,1)S(1)}, bf16[200,832]{1,0:T(8,128)(2,1)S(1)}, u32[]{:S(2)}, u32[]{:S(2)}) %collective-permute-start.21) | collective-permute-done | bytes 332832 | tf_op jit(solution)/shard_map/ppermute | solution.py:89
  85.1 0.1 select_dynamic-update-slice_fusion
  85.2 0.0 copy-start.1
  85.2 2.4 %copy-done.1 = bf16[1600,1600]{1,0:T(8,128)(2,1)} copy-done((bf16[1600,1600]{1,0:T(8,128)(2,1)}, bf16[1600,1600]{1,0:T(8,128)(2,1)S(1)}, u32[]{:S(2)}) %copy-start.1) | copy-done | bytes 5120024
  (34 shorter events, 0.6 us)
Async XLA Ops:
  0.6 6.4 %copy-start = (f32[1600,64]{0,1:T(8,128)S(1)}, f32[1600,64]{0,1:T(8,128)}, u32[]{:S(2)}) copy-start(f32[1600,64]{0,1:T(8,128)} %param.15) | copy-start | bytes 1228804
  1.7 10.0 %collective-permute-start = (f32[25,1600]{1,0:T(8,128)S(1)}, f32[25,1600]{1,0:T(8,128)}, u32[]{:S(2)}, u32[]{:S(2)}) collective-permute-start(f32[25,1600]{1,0:T(8,128)S(1)} %bitcast_subtract_fusion), channel_id=1, source_target_pairs={{0,64},{64,0},{128,192},{192,128},{1,65},{65,1},{129,193},{193,129... | collective-permute-start | bytes 480008 | tf_op jit(solution)/shard_map/ppermute | solution.py:36
  10.3 32.2 %copy-start.2 = (f32[100,1600]{1,0:T(8,128)S(1)}, f32[100,1600]{1,0:T(8,128)}, u32[]{:S(2)}) copy-start(f32[100,1600]{1,0:T(8,128)} %param.13) | copy-start | bytes 1920004
  10.3 32.2 %copy-start.3 = (f32[100,1600]{1,0:T(8,128)S(1)}, f32[100,1600]{1,0:T(8,128)}, u32[]{:S(2)}) copy-start(f32[100,1600]{1,0:T(8,128)} %param.14) | copy-start | bytes 1920004
  11.0 1.8 %collective-permute-start.22 = (f32[2,100,64]{1,2,0:T(8,128)S(1)}, f32[2,100,64]{1,2,0:T(8,128)S(1)}, u32[]{:S(2)}, u32[]{:S(2)}) collective-permute-start(f32[2,100,64]{1,2,0:T(8,128)S(1)} %broadcast_select_fusion), channel_id=1, source_target_pairs={{0,64},{64,0},{128,192},{192,128},{1,65},{65,1},{129,193},{193,129... | collective-permute-start | bytes 153608 | tf_op jit(solution)/shard_map/ppermute | solution.py:106
  12.7 6.4 %collective-permute-start.1 = (f32[25,1600]{1,0:T(8,128)S(1)}, f32[25,1600]{1,0:T(8,128)S(1)}, u32[]{:S(2)}, u32[]{:S(2)}) collective-permute-start(f32[25,1600]{1,0:T(8,128)S(1)} %add.139), channel_id=1, source_target_pairs={{0,128},{64,192},{128,0},{192,64},{1,129},{65,193},{129,1},{193,65... | collective-permute-start | bytes 480008 | tf_op jit(solution)/shard_map/ppermute | solution.py:37
  20.9 4.8 %collective-permute-start.2 = (bf16[25,1600]{1,0:T(8,128)(2,1)S(1)}, bf16[25,1600]{1,0:T(8,128)(2,1)S(1)}, u32[]{:S(2)}, u32[]{:S(2)}) collective-permute-start(bf16[25,1600]{1,0:T(8,128)(2,1)S(1)} %get-tuple-element.12), channel_id=1, source_target_pairs={{0,129},{1,128},{2,131},{3,130},{4,133},{5,132},{6,135},{7,134},{8... | collective-permute-start | bytes 240008 | tf_op jit(solution)/shard_map/ppermute | solution.py:51
  22.0 20.5 %collective-permute-start.23 = (f32[100,64]{0,1:T(8,128)S(1)}, f32[100,64]{0,1:T(8,128)S(1)}, u32[]{:S(2)}, u32[]{:S(2)}) collective-permute-start(f32[100,64]{0,1:T(8,128)S(1)} %slice_bitcast_fusion), channel_id=1, source_target_pairs={{0,128},{64,192},{128,0},{192,64},{1,129},{65,193},{129,1},{193,65... | collective-permute-start | bytes 76808 | tf_op jit(solution)/shard_map/ppermute | solution.py:109
  26.3 5.6 %collective-permute-start.3 = (bf16[50,1600]{1,0:T(8,128)(2,1)S(1)}, bf16[50,1600]{1,0:T(8,128)(2,1)S(1)}, u32[]{:S(2)}, u32[]{:S(2)}) collective-permute-start(bf16[50,1600]{1,0:T(8,128)(2,1)S(1)} %dynamic_update_slice.64), channel_id=1, source_target_pairs={{2,0},{3,1},{4,2},{5,3},{6,4},{7,5},{0,6},{1,7},{10,8},{11,9},{12,... | collective-permute-start | bytes 480008 | tf_op jit(solution)/shard_map/ppermute | solution.py:59
  27.2 6.0 %collective-permute-start.4 = (bf16[50,1600]{1,0:T(8,128)(2,1)S(1)}, bf16[50,1600]{1,0:T(8,128)(2,1)S(1)}, u32[]{:S(2)}, u32[]{:S(2)}) collective-permute-start(bf16[50,1600]{1,0:T(8,128)(2,1)S(1)} %dynamic_update_slice.64), channel_id=1, source_target_pairs={{4,0},{5,1},{6,2},{7,3},{0,4},{1,5},{2,6},{3,7},{12,8},{13,9},{14,... | collective-permute-start | bytes 480008 | tf_op jit(solution)/shard_map/ppermute | solution.py:59
  27.7 10.2 %collective-permute-start.5 = (bf16[50,1600]{1,0:T(8,128)(2,1)S(1)}, bf16[50,1600]{1,0:T(8,128)(2,1)S(1)}, u32[]{:S(2)}, u32[]{:S(2)}) collective-permute-start(bf16[50,1600]{1,0:T(8,128)(2,1)S(1)} %dynamic_update_slice.64), channel_id=1, source_target_pairs={{6,0},{7,1},{0,2},{1,3},{2,4},{3,5},{4,6},{5,7},{14,8},{15,9},{8,1... | collective-permute-start | bytes 480008 | tf_op jit(solution)/shard_map/ppermute | solution.py:59
  39.1 9.9 %collective-permute-start.6 = (bf16[200,768]{1,0:T(8,128)(2,1)S(1)}, bf16[200,768]{1,0:T(8,128)(2,1)S(1)}, u32[]{:S(2)}, u32[]{:S(2)}) collective-permute-start(bf16[200,768]{1,0:T(8,128)(2,1)S(1)} %slice.20), channel_id=1, source_target_pairs={{0,56},{1,57},{2,58},{3,59},{4,60},{5,61},{6,62},{7,63},{8,0},{9,1... | collective-permute-start | bytes 921608 | tf_op jit(solution)/shard_map/ppermute | solution.py:76
  40.8 12.0 %collective-permute-start.8 = (bf16[200,832]{1,0:T(8,128)(2,1)S(1)}, bf16[200,832]{1,0:T(8,128)(2,1)S(1)}, u32[]{:S(2)}, u32[]{:S(2)}) collective-permute-start(bf16[200,832]{1,0:T(8,128)(2,1)S(1)} %slice.21), channel_id=1, source_target_pairs={{0,56},{1,57},{2,58},{3,59},{4,60},{5,61},{6,62},{7,63},{8,0},{9,1... | collective-permute-start | bytes 998408 | tf_op jit(solution)/shard_map/ppermute | solution.py:76
  49.0 10.3 %collective-permute-start.7 = (bf16[200,768]{1,0:T(8,128)(2,1)S(1)}, bf16[200,768]{1,0:T(8,128)(2,1)S(1)}, u32[]{:S(2)}, u32[]{:S(2)}) collective-permute-start(bf16[200,768]{1,0:T(8,128)(2,1)S(1)} %collective-permute-done.6), channel_id=1, source_target_pairs={{0,64},{64,0},{128,192},{192,128},{1,65},{65,1},{129,193},{193,129... | collective-permute-start | bytes 921608 | tf_op jit(solution)/shard_map/ppermute | solution.py:77
  51.2 7.7 %collective-permute-start.10 = (bf16[200,768]{1,0:T(8,128)(2,1)S(1)}, bf16[200,768]{1,0:T(8,128)(2,1)S(1)}, u32[]{:S(2)}, u32[]{:S(2)}) collective-permute-start(bf16[200,768]{1,0:T(8,128)(2,1)S(1)} %collective-permute-done.6), channel_id=1, source_target_pairs={{0,56},{1,57},{2,58},{3,59},{4,60},{5,61},{6,62},{7,63},{8,0},{9,1... | collective-permute-start | bytes 921608 | tf_op jit(solution)/shard_map/ppermute | solution.py:76
  52.8 10.9 %collective-permute-start.9 = (bf16[200,832]{1,0:T(8,128)(2,1)S(1)}, bf16[200,832]{1,0:T(8,128)(2,1)S(1)}, u32[]{:S(2)}, u32[]{:S(2)}) collective-permute-start(bf16[200,832]{1,0:T(8,128)(2,1)S(1)} %collective-permute-done.8), channel_id=1, source_target_pairs={{0,64},{64,0},{128,192},{192,128},{1,65},{65,1},{129,193},{193,129... | collective-permute-start | bytes 998408 | tf_op jit(solution)/shard_map/ppermute | solution.py:77
  55.5 7.8 %collective-permute-start.12 = (bf16[200,832]{1,0:T(8,128)(2,1)S(1)}, bf16[200,832]{1,0:T(8,128)(2,1)S(1)}, u32[]{:S(2)}, u32[]{:S(2)}) collective-permute-start(bf16[200,832]{1,0:T(8,128)(2,1)S(1)} %collective-permute-done.8), channel_id=1, source_target_pairs={{0,56},{1,57},{2,58},{3,59},{4,60},{5,61},{6,62},{7,63},{8,0},{9,1... | collective-permute-start | bytes 998408 | tf_op jit(solution)/shard_map/ppermute | solution.py:76
  58.9 9.4 %collective-permute-start.11 = (bf16[200,768]{1,0:T(8,128)(2,1)S(1)}, bf16[200,768]{1,0:T(8,128)(2,1)S(1)}, u32[]{:S(2)}, u32[]{:S(2)}) collective-permute-start(bf16[200,768]{1,0:T(8,128)(2,1)S(1)} %collective-permute-done.10), channel_id=1, source_target_pairs={{0,64},{64,0},{128,192},{192,128},{1,65},{65,1},{129,193},{193,129... | collective-permute-start | bytes 921608 | tf_op jit(solution)/shard_map/ppermute | solution.py:77
  59.3 7.7 %collective-permute-start.14 = (bf16[200,768]{1,0:T(8,128)(2,1)S(1)}, bf16[200,768]{1,0:T(8,128)(2,1)S(1)}, u32[]{:S(2)}, u32[]{:S(2)}) collective-permute-start(bf16[200,768]{1,0:T(8,128)(2,1)S(1)} %collective-permute-done.10), channel_id=1, source_target_pairs={{0,56},{1,57},{2,58},{3,59},{4,60},{5,61},{6,62},{7,63},{8,0},{9,1... | collective-permute-start | bytes 921608 | tf_op jit(solution)/shard_map/ppermute | solution.py:76
  63.3 11.8 %collective-permute-start.13 = (bf16[200,832]{1,0:T(8,128)(2,1)S(1)}, bf16[200,832]{1,0:T(8,128)(2,1)S(1)}, u32[]{:S(2)}, u32[]{:S(2)}) collective-permute-start(bf16[200,832]{1,0:T(8,128)(2,1)S(1)} %collective-permute-done.12), channel_id=1, source_target_pairs={{0,64},{64,0},{128,192},{192,128},{1,65},{65,1},{129,193},{193,129... | collective-permute-start | bytes 998408 | tf_op jit(solution)/shard_map/ppermute | solution.py:77
  63.7 8.2 %collective-permute-start.16 = (bf16[200,832]{1,0:T(8,128)(2,1)S(1)}, bf16[200,832]{1,0:T(8,128)(2,1)S(1)}, u32[]{:S(2)}, u32[]{:S(2)}) collective-permute-start(bf16[200,832]{1,0:T(8,128)(2,1)S(1)} %collective-permute-done.12), channel_id=1, source_target_pairs={{0,56},{1,57},{2,58},{3,59},{4,60},{5,61},{6,62},{7,63},{8,0},{9,1... | collective-permute-start | bytes 998408 | tf_op jit(solution)/shard_map/ppermute | solution.py:76
  67.0 9.5 %collective-permute-start.15 = (bf16[200,768]{1,0:T(8,128)(2,1)S(1)}, bf16[200,768]{1,0:T(8,128)(2,1)S(1)}, u32[]{:S(2)}, u32[]{:S(2)}) collective-permute-start(bf16[200,768]{1,0:T(8,128)(2,1)S(1)} %collective-permute-done.14), channel_id=1, source_target_pairs={{0,64},{64,0},{128,192},{192,128},{1,65},{65,1},{129,193},{193,129... | collective-permute-start | bytes 921608 | tf_op jit(solution)/shard_map/ppermute | solution.py:77
  67.6 7.6 %collective-permute-start.18 = (bf16[200,768]{1,0:T(8,128)(2,1)S(1)}, bf16[200,768]{1,0:T(8,128)(2,1)S(1)}, u32[]{:S(2)}, u32[]{:S(2)}) collective-permute-start(bf16[200,768]{1,0:T(8,128)(2,1)S(1)} %collective-permute-done.14), channel_id=1, source_target_pairs={{0,56},{1,57},{2,58},{3,59},{4,60},{5,61},{6,62},{7,63},{8,0},{9,1... | collective-permute-start | bytes 921608 | tf_op jit(solution)/shard_map/ppermute | solution.py:86
  71.9 11.9 %collective-permute-start.17 = (bf16[200,832]{1,0:T(8,128)(2,1)S(1)}, bf16[200,832]{1,0:T(8,128)(2,1)S(1)}, u32[]{:S(2)}, u32[]{:S(2)}) collective-permute-start(bf16[200,832]{1,0:T(8,128)(2,1)S(1)} %collective-permute-done.16), channel_id=1, source_target_pairs={{0,64},{64,0},{128,192},{192,128},{1,65},{65,1},{129,193},{193,129... | collective-permute-start | bytes 998408 | tf_op jit(solution)/shard_map/ppermute | solution.py:77
  73.2 9.3 %collective-permute-start.20 = (bf16[200,832]{1,0:T(8,128)(2,1)S(1)}, bf16[200,832]{1,0:T(8,128)(2,1)S(1)}, u32[]{:S(2)}, u32[]{:S(2)}) collective-permute-start(bf16[200,832]{1,0:T(8,128)(2,1)S(1)} %collective-permute-done.16), channel_id=1, source_target_pairs={{64,72},{65,73},{66,74},{67,75},{68,76},{69,77},{70,78},{71,79},{7... | collective-permute-start | bytes 998408 | tf_op jit(solution)/shard_map/ppermute | solution.py:87
  75.2 8.7 %collective-permute-start.19 = (bf16[200,768]{1,0:T(8,128)(2,1)S(1)}, bf16[200,768]{1,0:T(8,128)(2,1)S(1)}, u32[]{:S(2)}, u32[]{:S(2)}) collective-permute-start(bf16[200,768]{1,0:T(8,128)(2,1)S(1)} %collective-permute-done.18), channel_id=1, source_target_pairs={{0,64},{128,192},{1,65},{129,193},{2,66},{130,194},{3,67},{131,195... | collective-permute-start | bytes 921608 | tf_op jit(solution)/shard_map/ppermute | solution.py:88
  82.5 2.6 %collective-permute-start.21 = (bf16[200,832]{1,0:T(8,128)(2,1)S(1)}, bf16[200,832]{1,0:T(8,128)(2,1)S(1)}, u32[]{:S(2)}, u32[]{:S(2)}) collective-permute-start(bf16[200,832]{1,0:T(8,128)(2,1)S(1)} %collective-permute-done.20), channel_id=1, source_target_pairs={{64,0},{192,128},{65,1},{193,129},{66,2},{194,130},{67,3},{195,131... | collective-permute-start | bytes 998408 | tf_op jit(solution)/shard_map/ppermute | solution.py:89
  85.2 2.4 %copy-start.1 = (bf16[1600,1600]{1,0:T(8,128)(2,1)}, bf16[1600,1600]{1,0:T(8,128)(2,1)S(1)}, u32[]{:S(2)}) copy-start(bf16[1600,1600]{1,0:T(8,128)(2,1)S(1)} %select_dynamic-update-slice_fusion) | copy-start | bytes 15360004

commit v6 on v5

--- a/solution.py
+++ b/solution.py
@@ -2,6 +2,7 @@
 import jax.numpy as jnp
 from jax import lax
 from jax.sharding import PartitionSpec as P
+
 
 outer_rate = 0.7
 momentum_coef = 0.9
@@ -34,7 +35,8 @@
 
 def butterfly_sum(v):
     v = v + lax.ppermute(v, "grp", [(i, i ^ 1) for i in range(NG)])
-    return v + lax.ppermute(v, "grp", [(i, i ^ 2) for i in range(NG)])
+    far = lax.ppermute(v, "grp", [(i, i ^ 2) for i in range(NG)])
+    return v + far
 
 
 def gather_copy(blk):
@@ -94,11 +96,10 @@
     return out
 
 
-def per_device(
-    layer_inner, layer_weights, layer_moment, embed_inner, embed_weights, embed_moment, basis
-):
+def body(layer_inner, layer_weights, layer_moment, embed_inner, embed_weights, embed_moment, basis):
     gi = lax.axis_index("grp")
     inner_proj = jnp.dot(embed_inner[0], basis, precision=lax.Precision.HIGHEST)
+    own_proj = jnp.dot(embed_weights, basis, precision=lax.Precision.HIGHEST)
     q = inner_proj.shape[0] // NG
     parts = inner_proj.reshape(NG, q, -1)
     keep1 = jnp.stack([gi, gi ^ 2])
@@ -107,7 +108,7 @@
         jnp.take(parts, send1, axis=0), "grp", [(i, i ^ 1) for i in range(NG)]
     )
     mean_proj = (a[0] + lax.ppermute(a[1], "grp", [(i, i ^ 2) for i in range(NG)])) / NG
-    factors = jnp.dot(embed_weights, basis, precision=lax.Precision.HIGHEST) - mean_proj
+    factors = own_proj - mean_proj
     embed_step = jnp.dot(factors, basis.T, precision=lax.Precision.HIGHEST)
     embed_new, embed_moment_new = nesterov(embed_weights, embed_moment, embed_step)
 
@@ -136,6 +137,4 @@
         P(("shard", "grp"), None),
         P(("shard", "grp"), None),
     )
-    return jax.shard_map(
-        per_device, mesh=mesh, in_specs=in_specs, out_specs=out_specs, check_vma=False
-    )
+    return jax.shard_map(body, mesh=mesh, in_specs=in_specs, out_specs=out_specs, check_vma=False)

time: 87.9 us -> 87.9 us (level)
  no operation moved by 1% of the time
where the time goes in v6:
time: 87.9 us; the launch traced here: 87.6 us
  waiting for transfers between devices  39.1 us (44%)
  starting transfers between devices  22.6 us (26%)
  local copies, waits for them, and re-layouts  12.9 us (15%)
  matrix products  7.2 us (8%)
  other arithmetic  4.43 us (5%)
  between operations  1.33 us (2%)
    ppermute x6, waiting for transfers between devices, gather_copy(): cur = [lax.ppermute(c, ('grp', 'shard'), zpairs) for c in cur]  19.7 us
    ppermute x6, starting transfers between devices, gather_copy(): mate = [lax.ppermute(c, 'grp', swap) for c in cur]  7.59 us
    ppermute x1, waiting for transfers between devices, butterfly_sum(): far = lax.ppermute(v, 'grp', [(i, i ^ 2) for i in range(NG)])  6.22 us
    ppermute x1, waiting for transfers between devices, gather_copy(): got_b = lax.ppermute(cur[1], ('grp', 'shard'), second)  5.92 us
    dynamic_update_slice x3, local copies, waits for them, and re-layouts, gather_copy(): b200 = lax.dynamic_update_slice(b200, got, ((x + k) % NX * NYH * rows, 0))  3.64 us
    ppermute x3, waiting for transfers between devices, gather_copy(): lax.ppermute(b50, 'shard', [(sidx(zxy(s)[0], zxy(s)[1] + k, zxy(s)[2]), s...  3.41 us
    ppermute x6, starting transfers between devices, gather_copy(): cur = [lax.ppermute(c, ('grp', 'shard'), zpairs) for c in cur]  3.37 us
    ppermute x1, starting transfers between devices, butterfly_sum(): v = v + lax.ppermute(v, 'grp', [(i, i ^ 1) for i in range(NG)])  3.29 us
  transfers between devices with their start and end apart: 24, of which 11 were waited for; matrix products, arithmetic and copies ran while one was open for 22% of the time, Pallas kernels for 0%

profile of v6, /device:TPU:1, one launch (start us, length us, event | category | flops | bytes accessed | tf_op | source)
XLA Modules:
  0.0 87.6 jit_solution(766601584173698288)
XLA Ops:
  0.6 0.0 copy-start
  0.6 1.1 %bitcast_subtract_fusion = f32[25,1600]{1,0:T(8,128)S(1)} fusion(f32[25,1600]{1,0:T(8,128)} %param.10, f32[1,25,1600]{2,0,1:T(1,128)} %param.9), kind=kLoop, calls=%fused_computation.8 | loop fusion | flops 40000 | bytes 480000 | tf_op jit(solution)/shard_map/sub | solution.py:115
  1.7 3.3 %collective-permute-start = (f32[25,1600]{1,0:T(8,128)S(1)}, f32[25,1600]{1,0:T(8,128)}, u32[]{:S(2)}, u32[]{:S(2)}) collective-permute-start(f32[25,1600]{1,0:T(8,128)S(1)} %bitcast_subtract_fusion), channel_id=1, source_target_pairs={{0,64},{64,0},{128,192},{192,128},{1,65},{65,1},{129,193},{193,129... | collective-permute-start | bytes 480008 | tf_op jit(solution)/shard_map/ppermute | solution.py:37
  5.0 1.9 %dot_general.12 = f32[4,100,1600]{2,1,0:T(8,128)S(1)} reshape(f32[1,400,1600]{2,1,0:T(8,128)} %param.12) | data formatting | bytes 5120000 | tf_op jit(solution)/shard_map/dot_general | solution.py:101
  6.9 0.1 compare_and_fusion
  7.0 3.3 %fusion = f32[4,100,64]{1,2,0:T(8,128)S(1)} fusion(f32[4,100,1600]{2,1,0:T(8,128)S(1)} %dot_general.12, f32[1600,64]{0,1:T(8,128)S(1)} %copy-done), kind=kOutput, calls=%fused_computation.4 | convolution fusion | flops 491520000 | bytes 3072000 | tf_op jit(solution)/shard_map/dot_general | solution.py:101
  10.3 0.0 copy-start.3
  10.3 0.6 gather_fusion.1
  10.9 0.1 broadcast_select_fusion
  11.0 0.1 collective-permute-start.22
  11.0 0.1 compare_and_fusion.1
  11.1 0.6 gather_fusion
  11.7 0.0 collective-permute-done
  11.7 1.0 %add.139 = f32[25,1600]{1,0:T(8,128)S(1)} add(f32[25,1600]{1,0:T(8,128)S(1)} %bitcast_subtract_fusion, f32[25,1600]{1,0:T(8,128)} %collective-permute-done) | non-fusion elementwise | flops 40000 | bytes 480000 | tf_op jit(solution)/shard_map/add | solution.py:37
  12.7 0.1 collective-permute-start.1
  12.8 0.0 collective-permute-done.22
  12.8 0.1 select_add_fusion
  12.9 6.2 %collective-permute-done.1 = f32[25,1600]{1,0:T(8,128)S(1)} collective-permute-done((f32[25,1600]{1,0:T(8,128)S(1)}, f32[25,1600]{1,0:T(8,128)S(1)}, u32[]{:S(2)}, u32[]{:S(2)}) %collective-permute-start.1) | collective-permute-done | bytes 160032 | tf_op jit(solution)/shard_map/ppermute | solution.py:38
  19.1 1.9 %fusion.9 = (bf16[25,1600]{1,0:T(8,128)(2,1)S(1)}, f32[25,1600]{1,0:T(8,128)}, f32[25,1600]{1,0:T(8,128)}) fusion(f32[25,1600]{1,0:T(8,128)} %param.10, f32[25,1600]{1,0:T(8,128)S(1)} %add.139, f32[25,1600]{1,0:T(8,128)S(1)} %collective-permute-done.1, f32[25,1600]{1,0:T(8,128)} %param.11), kind=kLoop, calls=%fused_computation.41 | loop fusion | flops 360000 | bytes 1040000 | tf_op jit(solution)/shard_map/convert_element_type | solution.py:118
  20.9 1.0 %collective-permute-start.2 = (bf16[25,1600]{1,0:T(8,128)(2,1)S(1)}, bf16[25,1600]{1,0:T(8,128)(2,1)S(1)}, u32[]{:S(2)}, u32[]{:S(2)}) collective-permute-start(bf16[25,1600]{1,0:T(8,128)(2,1)S(1)} %get-tuple-element.12), channel_id=1, source_target_pairs={{0,129},{1,128},{2,131},{3,130},{4,133},{5,132},{6,135},{7,134},{8... | collective-permute-start | bytes 240008 | tf_op jit(solution)/shard_map/ppermute | solution.py:53
  22.0 0.9 %dynamic_update_slice.63 = bf16[50,1600]{1,0:T(8,128)(2,1)S(1)} dynamic-update-slice(bf16[50,1600]{1,0:T(8,128)(2,1)S(1)} %broadcast_in_dim.20, bf16[25,1600]{1,0:T(8,128)(2,1)S(1)} %get-tuple-element.12, s32[]{:T(128)S(6)} %select_n.135, s32[]{:T(128)} %constant.128.clone.1) | dynamic-update-slice | bytes 160004 | tf_op jit(solution)/shard_map/dynamic_update_slice | solution.py:55
  22.9 2.8 %collective-permute-done.2 = bf16[25,1600]{1,0:T(8,128)(2,1)S(1)} collective-permute-done((bf16[25,1600]{1,0:T(8,128)(2,1)S(1)}, bf16[25,1600]{1,0:T(8,128)(2,1)S(1)}, u32[]{:S(2)}, u32[]{:S(2)}) %collective-permute-start.2) | collective-permute-done | bytes 80032 | tf_op jit(solution)/shard_map/ppermute | solution.py:53
  25.7 0.6 dynamic_update_slice.64
  26.3 0.9 %collective-permute-start.3 = (bf16[50,1600]{1,0:T(8,128)(2,1)S(1)}, bf16[50,1600]{1,0:T(8,128)(2,1)S(1)}, u32[]{:S(2)}, u32[]{:S(2)}) collective-permute-start(bf16[50,1600]{1,0:T(8,128)(2,1)S(1)} %dynamic_update_slice.64), channel_id=1, source_target_pairs={{2,0},{3,1},{4,2},{5,3},{6,4},{7,5},{0,6},{1,7},{10,8},{11,9},{12,... | collective-permute-start | bytes 480008 | tf_op jit(solution)/shard_map/ppermute | solution.py:61
  27.2 0.5 collective-permute-start.4
  27.7 0.6 collective-permute-start.5
  28.3 2.0 %fusion.10 = f32[100,64]{0,1:T(8,128)S(1)} fusion(f32[100,1600]{1,0:T(8,128)} %param.13, f32[1600,64]{0,1:T(8,128)S(1)} %copy-done), kind=kOutput, calls=%fused_computation.42 | convolution fusion | flops 122880000 | bytes 1075200 | tf_op jit(solution)/shard_map/dot_general | solution.py:102
  30.6 1.3 %dynamic_update_slice.65 = bf16[200,1600]{1,0:T(8,128)(2,1)S(1)} dynamic-update-slice(bf16[200,1600]{1,0:T(8,128)(2,1)S(1)} %broadcast_in_dim.19, bf16[50,1600]{1,0:T(8,128)(2,1)S(1)} %dynamic_update_slice.64, s32[]{:T(128)S(6)} %select_n.139, s32[]{:T(128)} %constant.128.clone.1) | dynamic-update-slice | bytes 320004 | tf_op jit(solution)/shard_map/dynamic_update_slice | solution.py:59
  31.9 0.0 collective-permute-done.3
  32.0 1.3 %dynamic_update_slice.66 = bf16[200,1600]{1,0:T(8,128)(2,1)S(1)} dynamic-update-slice(bf16[200,1600]{1,0:T(8,128)(2,1)S(1)} %dynamic_update_slice.65, bf16[50,1600]{1,0:T(8,128)(2,1)S(1)} %collective-permute-done.3, s32[]{:T(128)S(6)} %select_n.141, s32[]{:T(128)} %constant.128.clone.1) | dynamic-update-slice | bytes 320004 | tf_op jit(solution)/shard_map/dynamic_update_slice | solution.py:66
  33.3 1.3 %dynamic_update_slice.67 = bf16[200,1600]{1,0:T(8,128)(2,1)S(1)} dynamic-update-slice(bf16[200,1600]{1,0:T(8,128)(2,1)S(1)} %dynamic_update_slice.66, bf16[50,1600]{1,0:T(8,128)(2,1)S(1)} %collective-permute-done.4, s32[]{:T(128)S(6)} %select_n.143, s32[]{:T(128)} %constant.128.clone.1) | dynamic-update-slice | bytes 320004 | tf_op jit(solution)/shard_map/dynamic_update_slice | solution.py:66
  34.6 3.4 %collective-permute-done.5 = bf16[50,1600]{1,0:T(8,128)(2,1)S(1)} collective-permute-done((bf16[50,1600]{1,0:T(8,128)(2,1)S(1)}, bf16[50,1600]{1,0:T(8,128)(2,1)S(1)}, u32[]{:S(2)}, u32[]{:S(2)}) %collective-permute-start.5) | collective-permute-done | bytes 160032 | tf_op jit(solution)/shard_map/ppermute | solution.py:61
  38.0 1.0 %dynamic_update_slice.68 = bf16[200,1600]{1,0:T(8,128)(2,1)S(1)} dynamic-update-slice(bf16[200,1600]{1,0:T(8,128)(2,1)S(1)} %dynamic_update_slice.67, bf16[50,1600]{1,0:T(8,128)(2,1)S(1)} %collective-permute-done.5, s32[]{:T(128)S(6)} %select_n.145, s32[]{:T(128)} %constant.128.clone.1) | dynamic-update-slice | bytes 320004 | tf_op jit(solution)/shard_map/dynamic_update_slice | solution.py:66
  39.1 1.7 %collective-permute-start.6 = (bf16[200,768]{1,0:T(8,128)(2,1)S(1)}, bf16[200,768]{1,0:T(8,128)(2,1)S(1)}, u32[]{:S(2)}, u32[]{:S(2)}) collective-permute-start(bf16[200,768]{1,0:T(8,128)(2,1)S(1)} %slice.20), channel_id=1, source_target_pairs={{0,56},{1,57},{2,58},{3,59},{4,60},{5,61},{6,62},{7,63},{8,0},{9,1... | collective-permute-start | bytes 921608 | tf_op jit(solution)/shard_map/ppermute | solution.py:78
  40.8 1.6 %collective-permute-start.8 = (bf16[200,832]{1,0:T(8,128)(2,1)S(1)}, bf16[200,832]{1,0:T(8,128)(2,1)S(1)}, u32[]{:S(2)}, u32[]{:S(2)}) collective-permute-start(bf16[200,832]{1,0:T(8,128)(2,1)S(1)} %slice.21), channel_id=1, source_target_pairs={{0,56},{1,57},{2,58},{3,59},{4,60},{5,61},{6,62},{7,63},{8,0},{9,1... | collective-permute-start | bytes 998408 | tf_op jit(solution)/shard_map/ppermute | solution.py:78
  42.5 2.0 %multiply_subtract_fusion = (f32[100,1600]{1,0:T(8,128)}, f32[100,1600]{1,0:T(8,128)}) fusion(f32[100,1600]{1,0:T(8,128)S(1)} %copy-done.2, f32[100,1600]{1,0:T(8,128)S(1)} %copy-done.3, f32[1600,64]{0,1:T(8,128)S(1)} %copy-done, f32[100,64]{0,1:T(8,128)S(1)} %fusion.10, f32[100,64]{0,1:T(8,128)S(1)} %collective-permute-done.23, ...), kind=kOutput, calls=%fused_computation.2 | convolution fusion | flops 123859200 | bytes 3188736 | tf_op jit(solution)/shard_map/dot_general | solution.py:112
  44.4 4.6 %collective-permute-done.6 = bf16[200,768]{1,0:T(8,128)(2,1)S(1)} collective-permute-done((bf16[200,768]{1,0:T(8,128)(2,1)S(1)}, bf16[200,768]{1,0:T(8,128)(2,1)S(1)}, u32[]{:S(2)}, u32[]{:S(2)}) %collective-permute-start.6) | collective-permute-done | bytes 307232 | tf_op jit(solution)/shard_map/ppermute | solution.py:78
  49.0 2.2 %collective-permute-start.7 = (bf16[200,768]{1,0:T(8,128)(2,1)S(1)}, bf16[200,768]{1,0:T(8,128)(2,1)S(1)}, u32[]{:S(2)}, u32[]{:S(2)}) collective-permute-start(bf16[200,768]{1,0:T(8,128)(2,1)S(1)} %collective-permute-done.6), channel_id=1, source_target_pairs={{0,64},{64,0},{128,192},{192,128},{1,65},{65,1},{129,193},{193,129... | collective-permute-start | bytes 921608 | tf_op jit(solution)/shard_map/ppermute | solution.py:79
  51.2 0.0 collective-permute-start.10
  51.2 0.4 broadcast_in_dim.18
  51.6 0.1 constant_dynamic-update-slice_fusion.12
  51.7 1.1 %collective-permute-done.8 = bf16[200,832]{1,0:T(8,128)(2,1)S(1)} collective-permute-done((bf16[200,832]{1,0:T(8,128)(2,1)S(1)}, bf16[200,832]{1,0:T(8,128)(2,1)S(1)}, u32[]{:S(2)}, u32[]{:S(2)}) %collective-permute-start.8) | collective-permute-done | bytes 332832 | tf_op jit(solution)/shard_map/ppermute | solution.py:78
  52.8 2.6 %collective-permute-start.9 = (bf16[200,832]{1,0:T(8,128)(2,1)S(1)}, bf16[200,832]{1,0:T(8,128)(2,1)S(1)}, u32[]{:S(2)}, u32[]{:S(2)}) collective-permute-start(bf16[200,832]{1,0:T(8,128)(2,1)S(1)} %collective-permute-done.8), channel_id=1, source_target_pairs={{0,64},{64,0},{128,192},{192,128},{1,65},{65,1},{129,193},{193,129... | collective-permute-start | bytes 998408 | tf_op jit(solution)/shard_map/ppermute | solution.py:79
  55.5 0.0 collective-permute-start.12
  55.5 3.4 %collective-permute-done.10 = bf16[200,768]{1,0:T(8,128)(2,1)S(1)} collective-permute-done((bf16[200,768]{1,0:T(8,128)(2,1)S(1)}, bf16[200,768]{1,0:T(8,128)(2,1)S(1)}, u32[]{:S(2)}, u32[]{:S(2)}) %collective-permute-start.10) | collective-permute-done | bytes 307232 | tf_op jit(solution)/shard_map/ppermute | solution.py:78
  58.9 0.4 collective-permute-start.11
  59.3 0.0 collective-permute-start.14
  59.3 0.0 collective-permute-done.7
  59.4 3.9 %collective-permute-done.12 = bf16[200,832]{1,0:T(8,128)(2,1)S(1)} collective-permute-done((bf16[200,832]{1,0:T(8,128)(2,1)S(1)}, bf16[200,832]{1,0:T(8,128)(2,1)S(1)}, u32[]{:S(2)}, u32[]{:S(2)}) %collective-permute-start.12) | collective-permute-done | bytes 332832 | tf_op jit(solution)/shard_map/ppermute | solution.py:78
  63.3 0.4 collective-permute-start.13
  63.8 3.2 %collective-permute-done.14 = bf16[200,768]{1,0:T(8,128)(2,1)S(1)} collective-permute-done((bf16[200,768]{1,0:T(8,128)(2,1)S(1)}, bf16[200,768]{1,0:T(8,128)(2,1)S(1)}, u32[]{:S(2)}, u32[]{:S(2)}) %collective-permute-start.14) | collective-permute-done | bytes 307232 | tf_op jit(solution)/shard_map/ppermute | solution.py:78
  67.0 0.6 collective-permute-start.15
  67.6 0.7 collective-permute-start.18
  68.3 3.6 %collective-permute-done.16 = bf16[200,832]{1,0:T(8,128)(2,1)S(1)} collective-permute-done((bf16[200,832]{1,0:T(8,128)(2,1)S(1)}, bf16[200,832]{1,0:T(8,128)(2,1)S(1)}, u32[]{:S(2)}, u32[]{:S(2)}) %collective-permute-start.16) | collective-permute-done | bytes 332832 | tf_op jit(solution)/shard_map/ppermute | solution.py:78
  71.9 1.3 %collective-permute-start.17 = (bf16[200,832]{1,0:T(8,128)(2,1)S(1)}, bf16[200,832]{1,0:T(8,128)(2,1)S(1)}, u32[]{:S(2)}, u32[]{:S(2)}) collective-permute-start(bf16[200,832]{1,0:T(8,128)(2,1)S(1)} %collective-permute-done.16), channel_id=1, source_target_pairs={{0,64},{64,0},{128,192},{192,128},{1,65},{65,1},{129,193},{193,129... | collective-permute-start | bytes 998408 | tf_op jit(solution)/shard_map/ppermute | solution.py:79
  73.2 1.9 %collective-permute-start.20 = (bf16[200,832]{1,0:T(8,128)(2,1)S(1)}, bf16[200,832]{1,0:T(8,128)(2,1)S(1)}, u32[]{:S(2)}, u32[]{:S(2)}) collective-permute-start(bf16[200,832]{1,0:T(8,128)(2,1)S(1)} %collective-permute-done.16), channel_id=1, source_target_pairs={{64,72},{65,73},{66,74},{67,75},{68,76},{69,77},{70,78},{71,79},{7... | collective-permute-start | bytes 998408 | tf_op jit(solution)/shard_map/ppermute | solution.py:89
  75.2 1.3 %collective-permute-start.19 = (bf16[200,768]{1,0:T(8,128)(2,1)S(1)}, bf16[200,768]{1,0:T(8,128)(2,1)S(1)}, u32[]{:S(2)}, u32[]{:S(2)}) collective-permute-start(bf16[200,768]{1,0:T(8,128)(2,1)S(1)} %collective-permute-done.18), channel_id=1, source_target_pairs={{0,64},{128,192},{1,65},{129,193},{2,66},{130,194},{3,67},{131,195... | collective-permute-start | bytes 921608 | tf_op jit(solution)/shard_map/ppermute | solution.py:90
  76.6 5.9 %collective-permute-done.20 = bf16[200,832]{1,0:T(8,128)(2,1)S(1)} collective-permute-done((bf16[200,832]{1,0:T(8,128)(2,1)S(1)}, bf16[200,832]{1,0:T(8,128)(2,1)S(1)}, u32[]{:S(2)}, u32[]{:S(2)}) %collective-permute-start.20) | collective-permute-done | bytes 332832 | tf_op jit(solution)/shard_map/ppermute | solution.py:89
  82.5 1.3 %collective-permute-start.21 = (bf16[200,832]{1,0:T(8,128)(2,1)S(1)}, bf16[200,832]{1,0:T(8,128)(2,1)S(1)}, u32[]{:S(2)}, u32[]{:S(2)}) collective-permute-start(bf16[200,832]{1,0:T(8,128)(2,1)S(1)} %collective-permute-done.20), channel_id=1, source_target_pairs={{64,0},{192,128},{65,1},{193,129},{66,2},{194,130},{67,3},{195,131... | collective-permute-start | bytes 998408 | tf_op jit(solution)/shard_map/ppermute | solution.py:91
  83.9 0.1 select_dynamic-update-slice_fusion.1
  84.0 1.1 %collective-permute-done.21 = bf16[200,832]{1,0:T(8,128)(2,1)S(1)} collective-permute-done((bf16[200,832]{1,0:T(8,128)(2,1)S(1)}, bf16[200,832]{1,0:T(8,128)(2,1)S(1)}, u32[]{:S(2)}, u32[]{:S(2)}) %collective-permute-start.21) | collective-permute-done | bytes 332832 | tf_op jit(solution)/shard_map/ppermute | solution.py:91
  85.1 0.1 select_dynamic-update-slice_fusion
  85.2 0.0 copy-start.1
  85.2 2.4 %copy-done.1 = bf16[1600,1600]{1,0:T(8,128)(2,1)} copy-done((bf16[1600,1600]{1,0:T(8,128)(2,1)}, bf16[1600,1600]{1,0:T(8,128)(2,1)S(1)}, u32[]{:S(2)}) %copy-start.1) | copy-done | bytes 5120024
  (34 shorter events, 0.6 us)
Async XLA Ops:
  0.6 6.4 %copy-start = (f32[1600,64]{0,1:T(8,128)S(1)}, f32[1600,64]{0,1:T(8,128)}, u32[]{:S(2)}) copy-start(f32[1600,64]{0,1:T(8,128)} %param.15) | copy-start | bytes 1228804
  1.7 10.0 %collective-permute-start = (f32[25,1600]{1,0:T(8,128)S(1)}, f32[25,1600]{1,0:T(8,128)}, u32[]{:S(2)}, u32[]{:S(2)}) collective-permute-start(f32[25,1600]{1,0:T(8,128)S(1)} %bitcast_subtract_fusion), channel_id=1, source_target_pairs={{0,64},{64,0},{128,192},{192,128},{1,65},{65,1},{129,193},{193,129... | collective-permute-start | bytes 480008 | tf_op jit(solution)/shard_map/ppermute | solution.py:37
  10.3 32.2 %copy-start.2 = (f32[100,1600]{1,0:T(8,128)S(1)}, f32[100,1600]{1,0:T(8,128)}, u32[]{:S(2)}) copy-start(f32[100,1600]{1,0:T(8,128)} %param.13) | copy-start | bytes 1920004
  10.3 32.2 %copy-start.3 = (f32[100,1600]{1,0:T(8,128)S(1)}, f32[100,1600]{1,0:T(8,128)}, u32[]{:S(2)}) copy-start(f32[100,1600]{1,0:T(8,128)} %param.14) | copy-start | bytes 1920004
  11.0 1.8 %collective-permute-start.22 = (f32[2,100,64]{1,2,0:T(8,128)S(1)}, f32[2,100,64]{1,2,0:T(8,128)S(1)}, u32[]{:S(2)}, u32[]{:S(2)}) collective-permute-start(f32[2,100,64]{1,2,0:T(8,128)S(1)} %broadcast_select_fusion), channel_id=1, source_target_pairs={{0,64},{64,0},{128,192},{192,128},{1,65},{65,1},{129,193},{193,129... | collective-permute-start | bytes 153608 | tf_op jit(solution)/shard_map/ppermute | solution.py:107
  12.7 6.4 %collective-permute-start.1 = (f32[25,1600]{1,0:T(8,128)S(1)}, f32[25,1600]{1,0:T(8,128)S(1)}, u32[]{:S(2)}, u32[]{:S(2)}) collective-permute-start(f32[25,1600]{1,0:T(8,128)S(1)} %add.139), channel_id=1, source_target_pairs={{0,128},{64,192},{128,0},{192,64},{1,129},{65,193},{129,1},{193,65... | collective-permute-start | bytes 480008 | tf_op jit(solution)/shard_map/ppermute | solution.py:38
  20.9 4.8 %collective-permute-start.2 = (bf16[25,1600]{1,0:T(8,128)(2,1)S(1)}, bf16[25,1600]{1,0:T(8,128)(2,1)S(1)}, u32[]{:S(2)}, u32[]{:S(2)}) collective-permute-start(bf16[25,1600]{1,0:T(8,128)(2,1)S(1)} %get-tuple-element.12), channel_id=1, source_target_pairs={{0,129},{1,128},{2,131},{3,130},{4,133},{5,132},{6,135},{7,134},{8... | collective-permute-start | bytes 240008 | tf_op jit(solution)/shard_map/ppermute | solution.py:53
  22.0 20.5 %collective-permute-start.23 = (f32[100,64]{0,1:T(8,128)S(1)}, f32[100,64]{0,1:T(8,128)S(1)}, u32[]{:S(2)}, u32[]{:S(2)}) collective-permute-start(f32[100,64]{0,1:T(8,128)S(1)} %slice_bitcast_fusion), channel_id=1, source_target_pairs={{0,128},{64,192},{128,0},{192,64},{1,129},{65,193},{129,1},{193,65... | collective-permute-start | bytes 76808 | tf_op jit(solution)/shard_map/ppermute | solution.py:110
  26.3 5.6 %collective-permute-start.3 = (bf16[50,1600]{1,0:T(8,128)(2,1)S(1)}, bf16[50,1600]{1,0:T(8,128)(2,1)S(1)}, u32[]{:S(2)}, u32[]{:S(2)}) collective-permute-start(bf16[50,1600]{1,0:T(8,128)(2,1)S(1)} %dynamic_update_slice.64), channel_id=1, source_target_pairs={{2,0},{3,1},{4,2},{5,3},{6,4},{7,5},{0,6},{1,7},{10,8},{11,9},{12,... | collective-permute-start | bytes 480008 | tf_op jit(solution)/shard_map/ppermute | solution.py:61
  27.2 6.0 %collective-permute-start.4 = (bf16[50,1600]{1,0:T(8,128)(2,1)S(1)}, bf16[50,1600]{1,0:T(8,128)(2,1)S(1)}, u32[]{:S(2)}, u32[]{:S(2)}) collective-permute-start(bf16[50,1600]{1,0:T(8,128)(2,1)S(1)} %dynamic_update_slice.64), channel_id=1, source_target_pairs={{4,0},{5,1},{6,2},{7,3},{0,4},{1,5},{2,6},{3,7},{12,8},{13,9},{14,... | collective-permute-start | bytes 480008 | tf_op jit(solution)/shard_map/ppermute | solution.py:61
  27.7 10.2 %collective-permute-start.5 = (bf16[50,1600]{1,0:T(8,128)(2,1)S(1)}, bf16[50,1600]{1,0:T(8,128)(2,1)S(1)}, u32[]{:S(2)}, u32[]{:S(2)}) collective-permute-start(bf16[50,1600]{1,0:T(8,128)(2,1)S(1)} %dynamic_update_slice.64), channel_id=1, source_target_pairs={{6,0},{7,1},{0,2},{1,3},{2,4},{3,5},{4,6},{5,7},{14,8},{15,9},{8,1... | collective-permute-start | bytes 480008 | tf_op jit(solution)/shard_map/ppermute | solution.py:61
  39.1 9.9 %collective-permute-start.6 = (bf16[200,768]{1,0:T(8,128)(2,1)S(1)}, bf16[200,768]{1,0:T(8,128)(2,1)S(1)}, u32[]{:S(2)}, u32[]{:S(2)}) collective-permute-start(bf16[200,768]{1,0:T(8,128)(2,1)S(1)} %slice.20), channel_id=1, source_target_pairs={{0,56},{1,57},{2,58},{3,59},{4,60},{5,61},{6,62},{7,63},{8,0},{9,1... | collective-permute-start | bytes 921608 | tf_op jit(solution)/shard_map/ppermute | solution.py:78
  40.8 12.0 %collective-permute-start.8 = (bf16[200,832]{1,0:T(8,128)(2,1)S(1)}, bf16[200,832]{1,0:T(8,128)(2,1)S(1)}, u32[]{:S(2)}, u32[]{:S(2)}) collective-permute-start(bf16[200,832]{1,0:T(8,128)(2,1)S(1)} %slice.21), channel_id=1, source_target_pairs={{0,56},{1,57},{2,58},{3,59},{4,60},{5,61},{6,62},{7,63},{8,0},{9,1... | collective-permute-start | bytes 998408 | tf_op jit(solution)/shard_map/ppermute | solution.py:78
  49.0 10.3 %collective-permute-start.7 = (bf16[200,768]{1,0:T(8,128)(2,1)S(1)}, bf16[200,768]{1,0:T(8,128)(2,1)S(1)}, u32[]{:S(2)}, u32[]{:S(2)}) collective-permute-start(bf16[200,768]{1,0:T(8,128)(2,1)S(1)} %collective-permute-done.6), channel_id=1, source_target_pairs={{0,64},{64,0},{128,192},{192,128},{1,65},{65,1},{129,193},{193,129... | collective-permute-start | bytes 921608 | tf_op jit(solution)/shard_map/ppermute | solution.py:79
  51.2 7.7 %collective-permute-start.10 = (bf16[200,768]{1,0:T(8,128)(2,1)S(1)}, bf16[200,768]{1,0:T(8,128)(2,1)S(1)}, u32[]{:S(2)}, u32[]{:S(2)}) collective-permute-start(bf16[200,768]{1,0:T(8,128)(2,1)S(1)} %collective-permute-done.6), channel_id=1, source_target_pairs={{0,56},{1,57},{2,58},{3,59},{4,60},{5,61},{6,62},{7,63},{8,0},{9,1... | collective-permute-start | bytes 921608 | tf_op jit(solution)/shard_map/ppermute | solution.py:78
  52.8 10.9 %collective-permute-start.9 = (bf16[200,832]{1,0:T(8,128)(2,1)S(1)}, bf16[200,832]{1,0:T(8,128)(2,1)S(1)}, u32[]{:S(2)}, u32[]{:S(2)}) collective-permute-start(bf16[200,832]{1,0:T(8,128)(2,1)S(1)} %collective-permute-done.8), channel_id=1, source_target_pairs={{0,64},{64,0},{128,192},{192,128},{1,65},{65,1},{129,193},{193,129... | collective-permute-start | bytes 998408 | tf_op jit(solution)/shard_map/ppermute | solution.py:79
  55.5 7.8 %collective-permute-start.12 = (bf16[200,832]{1,0:T(8,128)(2,1)S(1)}, bf16[200,832]{1,0:T(8,128)(2,1)S(1)}, u32[]{:S(2)}, u32[]{:S(2)}) collective-permute-start(bf16[200,832]{1,0:T(8,128)(2,1)S(1)} %collective-permute-done.8), channel_id=1, source_target_pairs={{0,56},{1,57},{2,58},{3,59},{4,60},{5,61},{6,62},{7,63},{8,0},{9,1... | collective-permute-start | bytes 998408 | tf_op jit(solution)/shard_map/ppermute | solution.py:78
  58.9 9.4 %collective-permute-start.11 = (bf16[200,768]{1,0:T(8,128)(2,1)S(1)}, bf16[200,768]{1,0:T(8,128)(2,1)S(1)}, u32[]{:S(2)}, u32[]{:S(2)}) collective-permute-start(bf16[200,768]{1,0:T(8,128)(2,1)S(1)} %collective-permute-done.10), channel_id=1, source_target_pairs={{0,64},{64,0},{128,192},{192,128},{1,65},{65,1},{129,193},{193,129... | collective-permute-start | bytes 921608 | tf_op jit(solution)/shard_map/ppermute | solution.py:79
  59.3 7.7 %collective-permute-start.14 = (bf16[200,768]{1,0:T(8,128)(2,1)S(1)}, bf16[200,768]{1,0:T(8,128)(2,1)S(1)}, u32[]{:S(2)}, u32[]{:S(2)}) collective-permute-start(bf16[200,768]{1,0:T(8,128)(2,1)S(1)} %collective-permute-done.10), channel_id=1, source_target_pairs={{0,56},{1,57},{2,58},{3,59},{4,60},{5,61},{6,62},{7,63},{8,0},{9,1... | collective-permute-start | bytes 921608 | tf_op jit(solution)/shard_map/ppermute | solution.py:78
  63.3 11.8 %collective-permute-start.13 = (bf16[200,832]{1,0:T(8,128)(2,1)S(1)}, bf16[200,832]{1,0:T(8,128)(2,1)S(1)}, u32[]{:S(2)}, u32[]{:S(2)}) collective-permute-start(bf16[200,832]{1,0:T(8,128)(2,1)S(1)} %collective-permute-done.12), channel_id=1, source_target_pairs={{0,64},{64,0},{128,192},{192,128},{1,65},{65,1},{129,193},{193,129... | collective-permute-start | bytes 998408 | tf_op jit(solution)/shard_map/ppermute | solution.py:79
  63.7 8.2 %collective-permute-start.16 = (bf16[200,832]{1,0:T(8,128)(2,1)S(1)}, bf16[200,832]{1,0:T(8,128)(2,1)S(1)}, u32[]{:S(2)}, u32[]{:S(2)}) collective-permute-start(bf16[200,832]{1,0:T(8,128)(2,1)S(1)} %collective-permute-done.12), channel_id=1, source_target_pairs={{0,56},{1,57},{2,58},{3,59},{4,60},{5,61},{6,62},{7,63},{8,0},{9,1... | collective-permute-start | bytes 998408 | tf_op jit(solution)/shard_map/ppermute | solution.py:78
  67.0 9.5 %collective-permute-start.15 = (bf16[200,768]{1,0:T(8,128)(2,1)S(1)}, bf16[200,768]{1,0:T(8,128)(2,1)S(1)}, u32[]{:S(2)}, u32[]{:S(2)}) collective-permute-start(bf16[200,768]{1,0:T(8,128)(2,1)S(1)} %collective-permute-done.14), channel_id=1, source_target_pairs={{0,64},{64,0},{128,192},{192,128},{1,65},{65,1},{129,193},{193,129... | collective-permute-start | bytes 921608 | tf_op jit(solution)/shard_map/ppermute | solution.py:79
  67.6 7.6 %collective-permute-start.18 = (bf16[200,768]{1,0:T(8,128)(2,1)S(1)}, bf16[200,768]{1,0:T(8,128)(2,1)S(1)}, u32[]{:S(2)}, u32[]{:S(2)}) collective-permute-start(bf16[200,768]{1,0:T(8,128)(2,1)S(1)} %collective-permute-done.14), channel_id=1, source_target_pairs={{0,56},{1,57},{2,58},{3,59},{4,60},{5,61},{6,62},{7,63},{8,0},{9,1... | collective-permute-start | bytes 921608 | tf_op jit(solution)/shard_map/ppermute | solution.py:88
  71.9 11.9 %collective-permute-start.17 = (bf16[200,832]{1,0:T(8,128)(2,1)S(1)}, bf16[200,832]{1,0:T(8,128)(2,1)S(1)}, u32[]{:S(2)}, u32[]{:S(2)}) collective-permute-start(bf16[200,832]{1,0:T(8,128)(2,1)S(1)} %collective-permute-done.16), channel_id=1, source_target_pairs={{0,64},{64,0},{128,192},{192,128},{1,65},{65,1},{129,193},{193,129... | collective-permute-start | bytes 998408 | tf_op jit(solution)/shard_map/ppermute | solution.py:79
  73.2 9.3 %collective-permute-start.20 = (bf16[200,832]{1,0:T(8,128)(2,1)S(1)}, bf16[200,832]{1,0:T(8,128)(2,1)S(1)}, u32[]{:S(2)}, u32[]{:S(2)}) collective-permute-start(bf16[200,832]{1,0:T(8,128)(2,1)S(1)} %collective-permute-done.16), channel_id=1, source_target_pairs={{64,72},{65,73},{66,74},{67,75},{68,76},{69,77},{70,78},{71,79},{7... | collective-permute-start | bytes 998408 | tf_op jit(solution)/shard_map/ppermute | solution.py:89
  75.2 8.7 %collective-permute-start.19 = (bf16[200,768]{1,0:T(8,128)(2,1)S(1)}, bf16[200,768]{1,0:T(8,128)(2,1)S(1)}, u32[]{:S(2)}, u32[]{:S(2)}) collective-permute-start(bf16[200,768]{1,0:T(8,128)(2,1)S(1)} %collective-permute-done.18), channel_id=1, source_target_pairs={{0,64},{128,192},{1,65},{129,193},{2,66},{130,194},{3,67},{131,195... | collective-permute-start | bytes 921608 | tf_op jit(solution)/shard_map/ppermute | solution.py:90
  82.5 2.6 %collective-permute-start.21 = (bf16[200,832]{1,0:T(8,128)(2,1)S(1)}, bf16[200,832]{1,0:T(8,128)(2,1)S(1)}, u32[]{:S(2)}, u32[]{:S(2)}) collective-permute-start(bf16[200,832]{1,0:T(8,128)(2,1)S(1)} %collective-permute-done.20), channel_id=1, source_target_pairs={{64,0},{192,128},{65,1},{193,129},{66,2},{194,130},{67,3},{195,131... | collective-permute-start | bytes 998408 | tf_op jit(solution)/shard_map/ppermute | solution.py:91
  85.2 2.4 %copy-start.1 = (bf16[1600,1600]{1,0:T(8,128)(2,1)}, bf16[1600,1600]{1,0:T(8,128)(2,1)S(1)}, u32[]{:S(2)}) copy-start(bf16[1600,1600]{1,0:T(8,128)(2,1)S(1)} %select_dynamic-update-slice_fusion) | copy-start | bytes 15360004

commit v7 on v6

--- a/solution.py
+++ b/solution.py
@@ -9,6 +9,7 @@
 
 NZ, NX, NYH = 8, 4, 2
 NG = 4
+NST = 4
 
 
 def nesterov(weights, moment, average):
@@ -51,48 +52,53 @@
     ns = NZ * NX * NYH
 
     other = lax.ppermute(blk, ("grp", "shard"), both(lambda g, s: (g ^ 2, s ^ 1)))
-    b50 = jnp.zeros((NYH * rows, d), blk.dtype)
-    b50 = lax.dynamic_update_slice(b50, blk, (yh * rows, 0))
-    b50 = lax.dynamic_update_slice(b50, other, ((1 - yh) * rows, 0))
+    b50 = jnp.where(yh == 0, jnp.concatenate([blk, other]), jnp.concatenate([other, blk]))
 
     zb = NX * NYH * rows
-    b200 = lax.dynamic_update_slice(jnp.zeros((zb, d), blk.dtype), b50, (x * NYH * rows, 0))
+    rel = [b50]
     for k in range(1, NX):
-        got = lax.ppermute(
-            b50,
-            "shard",
-            [(sidx(zxy(s)[0], zxy(s)[1] + k, zxy(s)[2]), s) for s in range(NZ * NX * NYH)],
+        rel.append(
+            lax.ppermute(
+                b50,
+                "shard",
+                [(sidx(zxy(s)[0], zxy(s)[1] + k, zxy(s)[2]), s) for s in range(NZ * NX * NYH)],
+            )
         )
-        b200 = lax.dynamic_update_slice(b200, got, (((x + k) % NX) * NYH * rows, 0))
+    xi = (jnp.arange(NX) - x) % NX
+    b200 = jnp.take(jnp.stack(rel), xi, axis=0).reshape(zb, d)
 
     def zring(g, s):
         zz, xx, yy = zxy(s)
         return g, sidx(zz - 1, xx, yy) if g % 2 == 0 else sidx(zz + 1, xx, yy)
 
     zpairs = both(zring)
-    cut = (d // 2) // 128 * 128
+    step_cols = (d // NST) // 128 * 128
+    bounds = [i * step_cols for i in range(NST)] + [d]
+    spans = list(zip(bounds[:-1], bounds[1:]))
     sign = 1 - 2 * core
     out = lax.dynamic_update_slice(jnp.zeros((NZ * zb, d), blk.dtype), b200, (z * zb, 0))
-    cur = [b200[:, :cut], b200[:, cut:]]
+    cur = [b200[:, lo:hi] for lo, hi in spans]
     for k in range(1, NZ // 2):
         cur = [lax.ppermute(c, ("grp", "shard"), zpairs) for c in cur]
         mate = [lax.ppermute(c, "grp", swap) for c in cur]
         mine_at = ((z + sign * k) % NZ) * zb
         mate_at = ((z - sign * k) % NZ) * zb
-        for c, m, col in zip(cur, mate, (0, cut)):
-            out = lax.dynamic_update_slice(out, c, (mine_at, col))
-            out = lax.dynamic_update_slice(out, m, (mate_at, col))
+        for c, m, (lo, _) in zip(cur, mate, spans):
+            out = lax.dynamic_update_slice(out, c, (mine_at, lo))
+            out = lax.dynamic_update_slice(out, m, (mate_at, lo))
     z4 = ((z + NZ // 2) % NZ) * zb
     first = [p for p in zpairs if (p[1] // ns) % 2 == 0]
     second = [p for p in zpairs if (p[1] // ns) % 2 == 1]
-    got_a = lax.ppermute(cur[0], ("grp", "shard"), first)
-    got_b = lax.ppermute(cur[1], ("grp", "shard"), second)
-    sw_a = lax.ppermute(got_a, "grp", [(i, i ^ 1) for i in range(NG) if i % 2 == 0])
-    sw_b = lax.ppermute(got_b, "grp", [(i, i ^ 1) for i in range(NG) if i % 2 == 1])
-    got_a = jnp.where(core == 0, got_a, sw_a)
-    got_b = jnp.where(core == 0, sw_b, got_b)
-    out = lax.dynamic_update_slice(out, got_a, (z4, 0))
-    out = lax.dynamic_update_slice(out, got_b, (z4, cut))
+    half = NST // 2
+    gots = [
+        lax.ppermute(c, ("grp", "shard"), first if i < half else second)
+        for i, c in enumerate(cur)
+    ]
+    for i, (got, (lo, _)) in enumerate(zip(gots, spans)):
+        side = 0 if i < half else 1
+        sw = lax.ppermute(got, "grp", [(j, j ^ 1) for j in range(NG) if j % 2 == side])
+        fin = jnp.where(core == side, got, sw)
+        out = lax.dynamic_update_slice(out, fin, (z4, lo))
     return out
 
 

time: 87.9 us -> 109 us (1.24)
  starting transfers between devices: 22.6 us -> 50.5 us
  waiting for transfers between devices: 39.1 us -> 18.9 us
  local copies, waits for them, and re-layouts: 12.9 us -> 23.3 us
  other arithmetic: 4.43 us -> 8.46 us
  matrix products: 7.2 us -> 6.09 us
    ppermute x6 -> x12, waiting for transfers between devices: 19.7 us -> 2.18 us  [gather_copy(): cur = [lax.ppermute(c, ('grp', 'shard'), zpairs) for c in cur]]
    ppermute x6 -> x12, starting transfers between devices: 7.59 us -> 19.6 us  [gather_copy(): mate = [lax.ppermute(c, 'grp', swap) for c in cur]]
    dynamic_update_slice x19 -> x24, local copies, waits for them, and re-layouts: 6.98 us -> 16.4 us  [the longest x12 8.2 us: gather_copy(): out = lax.dynamic_update_slice(out, m, (mate_at, lo))]
    ppermute x4 -> x8, starting transfers between devices: 5.17 us -> 13.8 us  [the longest x4 6.93 us: gather_copy(): lax.ppermute(got, 'grp', [(j, j ^ 1) for j in range(NG) if j % 2 == side])]
    ppermute x4 -> x8, waiting for transfers between devices: 7.02 us -> 0.02 us  [the longest x4 0.01 us: gather_copy(): lax.ppermute(got, 'grp', [(j, j ^ 1) for j in range(NG) if j % 2 == side])]
    ppermute x6 -> x12, starting transfers between devices: 3.37 us -> 9.46 us  [gather_copy(): cur = [lax.ppermute(c, ('grp', 'shard'), zpairs) for c in cur]]
    dynamic_update_slice x2 -> x5, other arithmetic: 0.19 us -> 3.88 us  [the longest x4 2.86 us: gather_copy(): out = lax.dynamic_update_slice(out, fin, (z4, lo))]
    ppermute x3, waiting for transfers between devices: 3.41 us -> 6.65 us  [gather_copy(): lax.ppermute(b50, 'shard', [(sidx(zxy(s)[0], zxy(s)[1] + k, zxy(s)[2]), s...]
  transfers between devices with their start and end apart: 24 -> 40, of which waited for: 11 -> 6; matrix products, arithmetic and copies ran while one was open for 22% -> 31% of each run, Pallas kernels for 0% -> 0%
where the time goes in v7:
time: 109 us
  starting transfers between devices  50.5 us (46%)
  local copies, waits for them, and re-layouts  23.3 us (21%)
  waiting for transfers between devices  18.9 us (17%)
  other arithmetic  8.46 us (8%)
  matrix products  6.09 us (6%)
  between operations  1.21 us (1%)
    ppermute x12, starting transfers between devices, gather_copy(): mate = [lax.ppermute(c, 'grp', swap) for c in cur]  19.6 us
    ppermute x12, starting transfers between devices, gather_copy(): cur = [lax.ppermute(c, ('grp', 'shard'), zpairs) for c in cur]  9.46 us
    dynamic_update_slice x12, local copies, waits for them, and re-layouts, gather_copy(): out = lax.dynamic_update_slice(out, m, (mate_at, lo))  8.2 us
    dynamic_update_slice x12, local copies, waits for them, and re-layouts, gather_copy(): out = lax.dynamic_update_slice(out, c, (mine_at, lo))  8.18 us
    ppermute x4, starting transfers between devices, gather_copy(): lax.ppermute(got, 'grp', [(j, j ^ 1) for j in range(NG) if j % 2 == side])  6.93 us
    ppermute x4, starting transfers between devices, gather_copy(): lax.ppermute(c, ('grp', 'shard'), first if i < half else second)  6.86 us
    ppermute x3, waiting for transfers between devices, gather_copy(): lax.ppermute(b50, 'shard', [(sidx(zxy(s)[0], zxy(s)[1] + k, zxy(s)[2]), s...  6.65 us
    ppermute x1, waiting for transfers between devices, butterfly_sum(): far = lax.ppermute(v, 'grp', [(i, i ^ 2) for i in range(NG)])  6.25 us
  transfers between devices with their start and end apart: 40, of which 6 were waited for; matrix products, arithmetic and copies ran while one was open for 31% of the time, Pallas kernels for 0%

profile of v7, /device:TPU:1, one launch (start us, length us, event | category | flops | bytes accessed | tf_op | source)
XLA Modules:
  0.0 108.5 jit_solution(1182476802326809483)
XLA Ops:
  0.6 1.1 %bitcast_subtract_fusion = f32[25,1600]{1,0:T(8,128)S(1)} fusion(f32[25,1600]{1,0:T(8,128)} %param.10, f32[1,25,1600]{2,0,1:T(1,128)} %param.9), kind=kLoop, calls=%fused_computation.9 | loop fusion | flops 40000 | bytes 480000 | tf_op jit(solution)/shard_map/sub | solution.py:121
  1.7 3.3 %collective-permute-start = (f32[25,1600]{1,0:T(8,128)S(1)}, f32[25,1600]{1,0:T(8,128)}, u32[]{:S(2)}, u32[]{:S(2)}) collective-permute-start(f32[25,1600]{1,0:T(8,128)S(1)} %bitcast_subtract_fusion), channel_id=1, source_target_pairs={{0,64},{64,0},{128,192},{192,128},{1,65},{65,1},{129,193},{193,129... | collective-permute-start | bytes 480008 | tf_op jit(solution)/shard_map/ppermute | solution.py:38
  5.0 1.9 %dot_general.12 = f32[4,100,1600]{2,1,0:T(8,128)S(1)} reshape(f32[1,400,1600]{2,1,0:T(8,128)} %param.12) | data formatting | bytes 5120000 | tf_op jit(solution)/shard_map/dot_general | solution.py:107
  7.0 3.3 %fusion = f32[4,100,64]{1,2,0:T(8,128)S(1)} fusion(f32[4,100,1600]{2,1,0:T(8,128)S(1)} %dot_general.12, f32[1600,64]{0,1:T(8,128)S(1)} %copy-done), kind=kOutput, calls=%fused_computation.7 | convolution fusion | flops 491520000 | bytes 3072000 | tf_op jit(solution)/shard_map/dot_general | solution.py:107
  11.9 1.0 add.149
  13.1 6.2 %collective-permute-done.1 = f32[25,1600]{1,0:T(8,128)S(1)} collective-permute-done((f32[25,1600]{1,0:T(8,128)S(1)}, f32[25,1600]{1,0:T(8,128)S(1)}, u32[]{:S(2)}, u32[]{:S(2)}) %collective-permute-start.1) | collective-permute-done | bytes 160032 | tf_op jit(solution)/shard_map/ppermute | solution.py:39
  19.3 1.9 %fusion.12 = (bf16[25,1600]{1,0:T(8,128)(2,1)S(1)}, f32[25,1600]{1,0:T(8,128)}, f32[25,1600]{1,0:T(8,128)}) fusion(f32[25,1600]{1,0:T(8,128)} %param.10, f32[25,1600]{1,0:T(8,128)S(1)} %add.149, f32[25,1600]{1,0:T(8,128)S(1)} %collective-permute-done.1, f32[25,1600]{1,0:T(8,128)} %param.11), kind=kLoop, calls=%fused_computation.73 | loop fusion | flops 360000 | bytes 1040000 | tf_op jit(solution)/shard_map/convert_element_type | solution.py:124
  21.2 1.0 collective-permute-start.2
  22.2 3.7 %collective-permute-done.2 = bf16[25,1600]{1,0:T(8,128)(2,1)S(1)} collective-permute-done((bf16[25,1600]{1,0:T(8,128)(2,1)S(1)}, bf16[25,1600]{1,0:T(8,128)(2,1)S(1)}, u32[]{:S(2)}, u32[]{:S(2)}) %collective-permute-start.2) | collective-permute-done | bytes 80032 | tf_op jit(solution)/shard_map/ppermute | solution.py:54
  26.1 2.0 %collective-permute-start.4 = (bf16[50,1600]{1,0:T(8,128)(2,1)S(1)}, bf16[50,1600]{1,0:T(8,128)(2,1)S(1)}, u32[]{:S(2)}, u32[]{:S(2)}) collective-permute-start(bf16[50,1600]{1,0:T(8,128)(2,1)S(1)} %maximum_select_fusion.1), channel_id=1, source_target_pairs={{4,0},{5,1},{6,2},{7,3},{0,4},{1,5},{2,6},{3,7},{12,8},{13,9},{14,... | collective-permute-start | bytes 480008 | tf_op jit(solution)/shard_map/ppermute | solution.py:61
  28.1 1.2 %collective-permute-start.3 = (bf16[50,1600]{1,0:T(8,128)(2,1)S(1)}, bf16[50,1600]{1,0:T(8,128)(2,1)S(1)}, u32[]{:S(2)}, u32[]{:S(2)}) collective-permute-start(bf16[50,1600]{1,0:T(8,128)(2,1)S(1)} %maximum_select_fusion.1), channel_id=1, source_target_pairs={{2,0},{3,1},{4,2},{5,3},{6,4},{7,5},{0,6},{1,7},{10,8},{11,9},{12,... | collective-permute-start | bytes 480008 | tf_op jit(solution)/shard_map/ppermute | solution.py:61
  29.4 4.8 %collective-permute-done.5 = bf16[50,1600]{1,0:T(8,128)(2,1)S(1)} collective-permute-done((bf16[50,1600]{1,0:T(8,128)(2,1)S(1)}, bf16[50,1600]{1,0:T(8,128)(2,1)S(1)}, u32[]{:S(2)}, u32[]{:S(2)}) %collective-permute-start.5) | collective-permute-done | bytes 160032 | tf_op jit(solution)/shard_map/ppermute | solution.py:61
  34.2 1.8 %collective-permute-done.3 = bf16[50,1600]{1,0:T(8,128)(2,1)S(1)} collective-permute-done((bf16[50,1600]{1,0:T(8,128)(2,1)S(1)}, bf16[50,1600]{1,0:T(8,128)(2,1)S(1)}, u32[]{:S(2)}, u32[]{:S(2)}) %collective-permute-start.3) | collective-permute-done | bytes 160032 | tf_op jit(solution)/shard_map/ppermute | solution.py:61
  37.2 2.8 %broadcast_in_dim.26 = bf16[1600,1600]{1,0:T(8,128)(2,1)} broadcast(bf16[]{:T(256)} %constant.130.clone.1), dimensions={} | broadcast | bytes 5120002 | tf_op jit(solution)/shard_map/broadcast_in_dim | solution.py:79
  39.9 1.0 constant_dynamic-update-slice_fusion.24
  41.1 0.9 fusion.14
  42.1 1.5 %collective-permute-start.8 = (bf16[200,384]{1,0:T(8,128)(2,1)S(1)}, bf16[200,384]{1,0:T(8,128)(2,1)S(1)}, u32[]{:S(2)}, u32[]{:S(2)}) collective-permute-start(bf16[200,384]{1,0:T(8,128)(2,1)S(1)} %get-tuple-element.18), channel_id=1, source_target_pairs={{0,56},{1,57},{2,58},{3,59},{4,60},{5,61},{6,62},{7,63},{8,0},{9,1... | collective-permute-start | bytes 460808 | tf_op jit(solution)/shard_map/ppermute | solution.py:82
  43.7 1.6 %collective-permute-start.10 = (bf16[200,384]{1,0:T(8,128)(2,1)S(1)}, bf16[200,384]{1,0:T(8,128)(2,1)S(1)}, u32[]{:S(2)}, u32[]{:S(2)}) collective-permute-start(bf16[200,384]{1,0:T(8,128)(2,1)S(1)} %get-tuple-element.17), channel_id=1, source_target_pairs={{0,56},{1,57},{2,58},{3,59},{4,60},{5,61},{6,62},{7,63},{8,0},{9,1... | collective-permute-start | bytes 460808 | tf_op jit(solution)/shard_map/ppermute | solution.py:82
  45.3 2.2 %collective-permute-done.6 = bf16[200,384]{1,0:T(8,128)(2,1)S(1)} collective-permute-done((bf16[200,384]{1,0:T(8,128)(2,1)S(1)}, bf16[200,384]{1,0:T(8,128)(2,1)S(1)}, u32[]{:S(2)}, u32[]{:S(2)}) %collective-permute-start.6) | collective-permute-done | bytes 153632 | tf_op jit(solution)/shard_map/ppermute | solution.py:82
  47.4 4.4 %collective-permute-start.7 = (bf16[200,384]{1,0:T(8,128)(2,1)S(1)}, bf16[200,384]{1,0:T(8,128)(2,1)S(1)}, u32[]{:S(2)}, u32[]{:S(2)}) collective-permute-start(bf16[200,384]{1,0:T(8,128)(2,1)S(1)} %collective-permute-done.6), channel_id=1, source_target_pairs={{0,64},{64,0},{128,192},{192,128},{1,65},{65,1},{129,193},{193,129... | collective-permute-start | bytes 460808 | tf_op jit(solution)/shard_map/ppermute | solution.py:83
  51.8 1.9 %multiply_subtract_fusion = (f32[100,1600]{1,0:T(8,128)}, f32[100,1600]{1,0:T(8,128)}) fusion(f32[100,1600]{1,0:T(8,128)S(1)} %copy-done.1, f32[100,1600]{1,0:T(8,128)S(1)} %copy-done.2, f32[1600,64]{0,1:T(8,128)S(1)} %copy-done, f32[100,64]{0,1:T(8,128)S(1)} %fusion.14, f32[100,64]{0,1:T(8,128)S(1)} %collective-permute-done.39, ...), kind=kOutput, calls=%fused_computation.4 | convolution fusion | flops 123859200 | bytes 3188736 | tf_op jit(solution)/shard_map/dot_general | solution.py:118
  53.8 0.8 collective-permute-start.12
  54.6 0.7 collective-permute-start.14
  55.3 1.9 %collective-permute-start.9 = (bf16[200,384]{1,0:T(8,128)(2,1)S(1)}, bf16[200,384]{1,0:T(8,128)(2,1)S(1)}, u32[]{:S(2)}, u32[]{:S(2)}) collective-permute-start(bf16[200,384]{1,0:T(8,128)(2,1)S(1)} %collective-permute-done.8), channel_id=1, source_target_pairs={{0,64},{64,0},{128,192},{192,128},{1,65},{65,1},{129,193},{193,129... | collective-permute-start | bytes 460808 | tf_op jit(solution)/shard_map/ppermute | solution.py:83
  57.2 0.7 constant_dynamic-update-slice_fusion.23
  57.9 1.7 %collective-permute-start.16 = (bf16[200,384]{1,0:T(8,128)(2,1)S(1)}, bf16[200,384]{1,0:T(8,128)(2,1)S(1)}, u32[]{:S(2)}, u32[]{:S(2)}) collective-permute-start(bf16[200,384]{1,0:T(8,128)(2,1)S(1)} %collective-permute-done.8), channel_id=1, source_target_pairs={{0,56},{1,57},{2,58},{3,59},{4,60},{5,61},{6,62},{7,63},{8,0},{9,1... | collective-permute-start | bytes 460808 | tf_op jit(solution)/shard_map/ppermute | solution.py:82
  59.6 0.7 constant_dynamic-update-slice_fusion.22
  60.3 0.7 constant_dynamic-update-slice_fusion.17
  61.1 3.1 %collective-permute-start.13 = (bf16[200,448]{1,0:T(8,128)(2,1)S(1)}, bf16[200,448]{1,0:T(8,128)(2,1)S(1)}, u32[]{:S(2)}, u32[]{:S(2)}) collective-permute-start(bf16[200,448]{1,0:T(8,128)(2,1)S(1)} %collective-permute-done.12), channel_id=1, source_target_pairs={{0,64},{64,0},{128,192},{192,128},{1,65},{65,1},{129,193},{193,129... | collective-permute-start | bytes 537608 | tf_op jit(solution)/shard_map/ppermute | solution.py:83
  64.1 0.7 constant_dynamic-update-slice_fusion.16
  64.8 0.7 constant_dynamic-update-slice_fusion.11
  65.8 0.7 constant_dynamic-update-slice_fusion.10
  66.5 0.7 constant_dynamic-update-slice_fusion.5
  67.2 1.5 %collective-permute-start.22 = (bf16[200,384]{1,0:T(8,128)(2,1)S(1)}, bf16[200,384]{1,0:T(8,128)(2,1)S(1)}, u32[]{:S(2)}, u32[]{:S(2)}) collective-permute-start(bf16[200,384]{1,0:T(8,128)(2,1)S(1)} %collective-permute-done.14), channel_id=1, source_target_pairs={{0,56},{1,57},{2,58},{3,59},{4,60},{5,61},{6,62},{7,63},{8,0},{9,1... | collective-permute-start | bytes 460808 | tf_op jit(solution)/shard_map/ppermute | solution.py:82
  68.6 1.7 %collective-permute-start.17 = (bf16[200,384]{1,0:T(8,128)(2,1)S(1)}, bf16[200,384]{1,0:T(8,128)(2,1)S(1)}, u32[]{:S(2)}, u32[]{:S(2)}) collective-permute-start(bf16[200,384]{1,0:T(8,128)(2,1)S(1)} %collective-permute-done.16), channel_id=1, source_target_pairs={{0,64},{64,0},{128,192},{192,128},{1,65},{65,1},{129,193},{193,129... | collective-permute-start | bytes 460808 | tf_op jit(solution)/shard_map/ppermute | solution.py:83
  70.3 0.7 constant_dynamic-update-slice_fusion.4
  71.0 0.7 constant_dynamic-update-slice_fusion.21
  72.0 0.7 constant_dynamic-update-slice_fusion.20
  72.7 0.7 constant_dynamic-update-slice_fusion.15
  73.4 1.5 %collective-permute-start.26 = (bf16[200,384]{1,0:T(8,128)(2,1)S(1)}, bf16[200,384]{1,0:T(8,128)(2,1)S(1)}, u32[]{:S(2)}, u32[]{:S(2)}) collective-permute-start(bf16[200,384]{1,0:T(8,128)(2,1)S(1)} %collective-permute-done.18), channel_id=1, source_target_pairs={{0,56},{1,57},{2,58},{3,59},{4,60},{5,61},{6,62},{7,63},{8,0},{9,1... | collective-permute-start | bytes 460808 | tf_op jit(solution)/shard_map/ppermute | solution.py:82
  74.8 1.7 %collective-permute-start.21 = (bf16[200,448]{1,0:T(8,128)(2,1)S(1)}, bf16[200,448]{1,0:T(8,128)(2,1)S(1)}, u32[]{:S(2)}, u32[]{:S(2)}) collective-permute-start(bf16[200,448]{1,0:T(8,128)(2,1)S(1)} %collective-permute-done.20), channel_id=1, source_target_pairs={{0,64},{64,0},{128,192},{192,128},{1,65},{65,1},{129,193},{193,129... | collective-permute-start | bytes 537608 | tf_op jit(solution)/shard_map/ppermute | solution.py:83
  76.6 0.7 constant_dynamic-update-slice_fusion.14
  78.2 0.7 constant_dynamic-update-slice_fusion.8
  78.9 0.7 constant_dynamic-update-slice_fusion.3
  80.3 4.5 %collective-permute-start.25 = (bf16[200,384]{1,0:T(8,128)(2,1)S(1)}, bf16[200,384]{1,0:T(8,128)(2,1)S(1)}, u32[]{:S(2)}, u32[]{:S(2)}) collective-permute-start(bf16[200,384]{1,0:T(8,128)(2,1)S(1)} %collective-permute-done.24), channel_id=1, source_target_pairs={{0,64},{64,0},{128,192},{192,128},{1,65},{65,1},{129,193},{193,129... | collective-permute-start | bytes 460808 | tf_op jit(solution)/shard_map/ppermute | solution.py:83
  84.8 0.7 constant_dynamic-update-slice_fusion.2
  86.8 1.4 %collective-permute-start.27 = (bf16[200,384]{1,0:T(8,128)(2,1)S(1)}, bf16[200,384]{1,0:T(8,128)(2,1)S(1)}, u32[]{:S(2)}, u32[]{:S(2)}) collective-permute-start(bf16[200,384]{1,0:T(8,128)(2,1)S(1)} %collective-permute-done.26), channel_id=1, source_target_pairs={{0,64},{64,0},{128,192},{192,128},{1,65},{65,1},{129,193},{193,129... | collective-permute-start | bytes 460808 | tf_op jit(solution)/shard_map/ppermute | solution.py:83
  88.2 0.7 constant_dynamic-update-slice_fusion.18
  88.8 0.7 constant_dynamic-update-slice_fusion.13
  89.5 3.6 %collective-permute-start.34 = (bf16[200,384]{1,0:T(8,128)(2,1)S(1)}, bf16[200,384]{1,0:T(8,128)(2,1)S(1)}, u32[]{:S(2)}, u32[]{:S(2)}) collective-permute-start(bf16[200,384]{1,0:T(8,128)(2,1)S(1)} %collective-permute-done.26), channel_id=1, source_target_pairs={{64,72},{65,73},{66,74},{67,75},{68,76},{69,77},{70,78},{71,79},{7... | collective-permute-start | bytes 460808 | tf_op jit(solution)/shard_map/ppermute | solution.py:94
  93.3 0.7 constant_dynamic-update-slice_fusion.12
  94.0 0.7 constant_dynamic-update-slice_fusion.7
  94.6 1.9 %collective-permute-start.36 = (bf16[200,448]{1,0:T(8,128)(2,1)S(1)}, bf16[200,448]{1,0:T(8,128)(2,1)S(1)}, u32[]{:S(2)}, u32[]{:S(2)}) collective-permute-start(bf16[200,448]{1,0:T(8,128)(2,1)S(1)} %collective-permute-done.28), channel_id=1, source_target_pairs={{64,72},{65,73},{66,74},{67,75},{68,76},{69,77},{70,78},{71,79},{7... | collective-permute-start | bytes 537608 | tf_op jit(solution)/shard_map/ppermute | solution.py:94
  96.6 1.3 %collective-permute-start.31 = (bf16[200,384]{1,0:T(8,128)(2,1)S(1)}, bf16[200,384]{1,0:T(8,128)(2,1)S(1)}, u32[]{:S(2)}, u32[]{:S(2)}) collective-permute-start(bf16[200,384]{1,0:T(8,128)(2,1)S(1)} %collective-permute-done.30), channel_id=1, source_target_pairs={{0,64},{128,192},{1,65},{129,193},{2,66},{130,194},{3,67},{131,195... | collective-permute-start | bytes 460808 | tf_op jit(solution)/shard_map/ppermute | solution.py:99
  97.9 0.7 constant_dynamic-update-slice_fusion.6
  98.6 0.7 constant_dynamic-update-slice_fusion.1
  99.3 1.3 %collective-permute-start.33 = (bf16[200,384]{1,0:T(8,128)(2,1)S(1)}, bf16[200,384]{1,0:T(8,128)(2,1)S(1)}, u32[]{:S(2)}, u32[]{:S(2)}) collective-permute-start(bf16[200,384]{1,0:T(8,128)(2,1)S(1)} %collective-permute-done.32), channel_id=1, source_target_pairs={{0,64},{128,192},{1,65},{129,193},{2,66},{130,194},{3,67},{131,195... | collective-permute-start | bytes 460808 | tf_op jit(solution)/shard_map/ppermute | solution.py:99
  100.6 3.1 %collective-permute-start.35 = (bf16[200,384]{1,0:T(8,128)(2,1)S(1)}, bf16[200,384]{1,0:T(8,128)(2,1)S(1)}, u32[]{:S(2)}, u32[]{:S(2)}) collective-permute-start(bf16[200,384]{1,0:T(8,128)(2,1)S(1)} %collective-permute-done.34), channel_id=1, source_target_pairs={{64,0},{192,128},{65,1},{193,129},{66,2},{194,130},{67,3},{195,131... | collective-permute-start | bytes 460808 | tf_op jit(solution)/shard_map/ppermute | solution.py:99
  103.6 1.3 %collective-permute-start.37 = (bf16[200,448]{1,0:T(8,128)(2,1)S(1)}, bf16[200,448]{1,0:T(8,128)(2,1)S(1)}, u32[]{:S(2)}, u32[]{:S(2)}) collective-permute-start(bf16[200,448]{1,0:T(8,128)(2,1)S(1)} %collective-permute-done.36), channel_id=1, source_target_pairs={{64,0},{192,128},{65,1},{193,129},{66,2},{194,130},{67,3},{195,131... | collective-permute-start | bytes 537608 | tf_op jit(solution)/shard_map/ppermute | solution.py:99
  104.9 0.7 constant_dynamic-update-slice_fusion
  105.7 0.7 select_dynamic-update-slice_fusion.3
  106.4 0.7 select_dynamic-update-slice_fusion.2
  107.1 0.7 select_dynamic-update-slice_fusion.1
  107.8 0.7 select_dynamic-update-slice_fusion
  (80 shorter events, 7.2 us)
Async XLA Ops:
  0.6 6.4 %copy-start = (f32[1600,64]{0,1:T(8,128)S(1)}, f32[1600,64]{0,1:T(8,128)}, u32[]{:S(2)}) copy-start(f32[1600,64]{0,1:T(8,128)} %param.15) | copy-start | bytes 1228804
  1.7 10.2 %collective-permute-start = (f32[25,1600]{1,0:T(8,128)S(1)}, f32[25,1600]{1,0:T(8,128)}, u32[]{:S(2)}, u32[]{:S(2)}) collective-permute-start(f32[25,1600]{1,0:T(8,128)S(1)} %bitcast_subtract_fusion), channel_id=1, source_target_pairs={{0,64},{64,0},{128,192},{192,128},{1,65},{65,1},{129,193},{193,129... | collective-permute-start | bytes 480008 | tf_op jit(solution)/shard_map/ppermute | solution.py:38
  10.9 2.0 %collective-permute-start.38 = (f32[2,100,64]{1,2,0:T(8,128)S(1)}, f32[2,100,64]{1,2,0:T(8,128)S(1)}, u32[]{:S(2)}, u32[]{:S(2)}) collective-permute-start(f32[2,100,64]{1,2,0:T(8,128)S(1)} %broadcast_select_fusion.1), channel_id=1, source_target_pairs={{0,64},{64,0},{128,192},{192,128},{1,65},{65,1},{129,193},{193,129... | collective-permute-start | bytes 153608 | tf_op jit(solution)/shard_map/ppermute | solution.py:113
  12.9 6.4 %collective-permute-start.1 = (f32[25,1600]{1,0:T(8,128)S(1)}, f32[25,1600]{1,0:T(8,128)S(1)}, u32[]{:S(2)}, u32[]{:S(2)}) collective-permute-start(f32[25,1600]{1,0:T(8,128)S(1)} %add.149), channel_id=1, source_target_pairs={{0,128},{64,192},{128,0},{192,64},{1,129},{65,193},{129,1},{193,65... | collective-permute-start | bytes 480008 | tf_op jit(solution)/shard_map/ppermute | solution.py:39
  21.2 4.8 %collective-permute-start.2 = (bf16[25,1600]{1,0:T(8,128)(2,1)S(1)}, bf16[25,1600]{1,0:T(8,128)(2,1)S(1)}, u32[]{:S(2)}, u32[]{:S(2)}) collective-permute-start(bf16[25,1600]{1,0:T(8,128)(2,1)S(1)} %get-tuple-element.14), channel_id=1, source_target_pairs={{0,129},{1,128},{2,131},{3,130},{4,133},{5,132},{6,135},{7,134},{8... | collective-permute-start | bytes 240008 | tf_op jit(solution)/shard_map/ppermute | solution.py:54
  22.2 29.6 %collective-permute-start.39 = (f32[100,64]{0,1:T(8,128)S(1)}, f32[100,64]{0,1:T(8,128)S(1)}, u32[]{:S(2)}, u32[]{:S(2)}) collective-permute-start(f32[100,64]{0,1:T(8,128)S(1)} %slice_bitcast_fusion), channel_id=1, source_target_pairs={{0,128},{64,192},{128,0},{192,64},{1,129},{65,193},{129,1},{193,65... | collective-permute-start | bytes 76808 | tf_op jit(solution)/shard_map/ppermute | solution.py:116
  26.0 8.1 %collective-permute-start.5 = (bf16[50,1600]{1,0:T(8,128)(2,1)S(1)}, bf16[50,1600]{1,0:T(8,128)(2,1)S(1)}, u32[]{:S(2)}, u32[]{:S(2)}) collective-permute-start(bf16[50,1600]{1,0:T(8,128)(2,1)S(1)} %maximum_select_fusion.1), channel_id=1, source_target_pairs={{6,0},{7,1},{0,2},{1,3},{2,4},{3,5},{4,6},{5,7},{14,8},{15,9},{8,1... | collective-permute-start | bytes 480008 | tf_op jit(solution)/shard_map/ppermute | solution.py:61
  26.1 8.1 %collective-permute-start.4 = (bf16[50,1600]{1,0:T(8,128)(2,1)S(1)}, bf16[50,1600]{1,0:T(8,128)(2,1)S(1)}, u32[]{:S(2)}, u32[]{:S(2)}) collective-permute-start(bf16[50,1600]{1,0:T(8,128)(2,1)S(1)} %maximum_select_fusion.1), channel_id=1, source_target_pairs={{4,0},{5,1},{6,2},{7,3},{0,4},{1,5},{2,6},{3,7},{12,8},{13,9},{14,... | collective-permute-start | bytes 480008 | tf_op jit(solution)/shard_map/ppermute | solution.py:61
  28.1 7.9 %collective-permute-start.3 = (bf16[50,1600]{1,0:T(8,128)(2,1)S(1)}, bf16[50,1600]{1,0:T(8,128)(2,1)S(1)}, u32[]{:S(2)}, u32[]{:S(2)}) collective-permute-start(bf16[50,1600]{1,0:T(8,128)(2,1)S(1)} %maximum_select_fusion.1), channel_id=1, source_target_pairs={{2,0},{3,1},{4,2},{5,3},{6,4},{7,5},{0,6},{1,7},{10,8},{11,9},{12,... | collective-permute-start | bytes 480008 | tf_op jit(solution)/shard_map/ppermute | solution.py:61
  36.2 4.9 %copy-start.1 = (f32[100,1600]{1,0:T(8,128)S(1)}, f32[100,1600]{1,0:T(8,128)}, u32[]{:S(2)}) copy-start(f32[100,1600]{1,0:T(8,128)} %param.13) | copy-start | bytes 1920004
  37.2 14.7 %copy-start.2 = (f32[100,1600]{1,0:T(8,128)S(1)}, f32[100,1600]{1,0:T(8,128)}, u32[]{:S(2)}) copy-start(f32[100,1600]{1,0:T(8,128)} %param.14) | copy-start | bytes 1920004
  41.0 6.4 %collective-permute-start.6 = (bf16[200,384]{1,0:T(8,128)(2,1)S(1)}, bf16[200,384]{1,0:T(8,128)(2,1)S(1)}, u32[]{:S(2)}, u32[]{:S(2)}) collective-permute-start(bf16[200,384]{1,0:T(8,128)(2,1)S(1)} %get-tuple-element.19), channel_id=1, source_target_pairs={{0,56},{1,57},{2,58},{3,59},{4,60},{5,61},{6,62},{7,63},{8,0},{9,1... | collective-permute-start | bytes 460808 | tf_op jit(solution)/shard_map/ppermute | solution.py:82
  42.1 13.2 %collective-permute-start.8 = (bf16[200,384]{1,0:T(8,128)(2,1)S(1)}, bf16[200,384]{1,0:T(8,128)(2,1)S(1)}, u32[]{:S(2)}, u32[]{:S(2)}) collective-permute-start(bf16[200,384]{1,0:T(8,128)(2,1)S(1)} %get-tuple-element.18), channel_id=1, source_target_pairs={{0,56},{1,57},{2,58},{3,59},{4,60},{5,61},{6,62},{7,63},{8,0},{9,1... | collective-permute-start | bytes 460808 | tf_op jit(solution)/shard_map/ppermute | solution.py:82
  43.7 14.3 %collective-permute-start.10 = (bf16[200,384]{1,0:T(8,128)(2,1)S(1)}, bf16[200,384]{1,0:T(8,128)(2,1)S(1)}, u32[]{:S(2)}, u32[]{:S(2)}) collective-permute-start(bf16[200,384]{1,0:T(8,128)(2,1)S(1)} %get-tuple-element.17), channel_id=1, source_target_pairs={{0,56},{1,57},{2,58},{3,59},{4,60},{5,61},{6,62},{7,63},{8,0},{9,1... | collective-permute-start | bytes 460808 | tf_op jit(solution)/shard_map/ppermute | solution.py:82
  47.4 12.1 %collective-permute-start.7 = (bf16[200,384]{1,0:T(8,128)(2,1)S(1)}, bf16[200,384]{1,0:T(8,128)(2,1)S(1)}, u32[]{:S(2)}, u32[]{:S(2)}) collective-permute-start(bf16[200,384]{1,0:T(8,128)(2,1)S(1)} %collective-permute-done.6), channel_id=1, source_target_pairs={{0,64},{64,0},{128,192},{192,128},{1,65},{65,1},{129,193},{193,129... | collective-permute-start | bytes 460808 | tf_op jit(solution)/shard_map/ppermute | solution.py:83
  53.8 7.2 %collective-permute-start.12 = (bf16[200,448]{1,0:T(8,128)(2,1)S(1)}, bf16[200,448]{1,0:T(8,128)(2,1)S(1)}, u32[]{:S(2)}, u32[]{:S(2)}) collective-permute-start(bf16[200,448]{1,0:T(8,128)(2,1)S(1)} %slice.33), channel_id=1, source_target_pairs={{0,56},{1,57},{2,58},{3,59},{4,60},{5,61},{6,62},{7,63},{8,0},{9,1... | collective-permute-start | bytes 537608 | tf_op jit(solution)/shard_map/ppermute | solution.py:82
  54.6 10.9 %collective-permute-start.14 = (bf16[200,384]{1,0:T(8,128)(2,1)S(1)}, bf16[200,384]{1,0:T(8,128)(2,1)S(1)}, u32[]{:S(2)}, u32[]{:S(2)}) collective-permute-start(bf16[200,384]{1,0:T(8,128)(2,1)S(1)} %collective-permute-done.6), channel_id=1, source_target_pairs={{0,56},{1,57},{2,58},{3,59},{4,60},{5,61},{6,62},{7,63},{8,0},{9,1... | collective-permute-start | bytes 460808 | tf_op jit(solution)/shard_map/ppermute | solution.py:82
  55.3 5.7 %collective-permute-start.9 = (bf16[200,384]{1,0:T(8,128)(2,1)S(1)}, bf16[200,384]{1,0:T(8,128)(2,1)S(1)}, u32[]{:S(2)}, u32[]{:S(2)}) collective-permute-start(bf16[200,384]{1,0:T(8,128)(2,1)S(1)} %collective-permute-done.8), channel_id=1, source_target_pairs={{0,64},{64,0},{128,192},{192,128},{1,65},{65,1},{129,193},{193,129... | collective-permute-start | bytes 460808 | tf_op jit(solution)/shard_map/ppermute | solution.py:83
  57.9 9.2 %collective-permute-start.16 = (bf16[200,384]{1,0:T(8,128)(2,1)S(1)}, bf16[200,384]{1,0:T(8,128)(2,1)S(1)}, u32[]{:S(2)}, u32[]{:S(2)}) collective-permute-start(bf16[200,384]{1,0:T(8,128)(2,1)S(1)} %collective-permute-done.8), channel_id=1, source_target_pairs={{0,56},{1,57},{2,58},{3,59},{4,60},{5,61},{6,62},{7,63},{8,0},{9,1... | collective-permute-start | bytes 460808 | tf_op jit(solution)/shard_map/ppermute | solution.py:82
  59.6 5.9 %collective-permute-start.11 = (bf16[200,384]{1,0:T(8,128)(2,1)S(1)}, bf16[200,384]{1,0:T(8,128)(2,1)S(1)}, u32[]{:S(2)}, u32[]{:S(2)}) collective-permute-start(bf16[200,384]{1,0:T(8,128)(2,1)S(1)} %collective-permute-done.10), channel_id=1, source_target_pairs={{0,64},{64,0},{128,192},{192,128},{1,65},{65,1},{129,193},{193,129... | collective-permute-start | bytes 460808 | tf_op jit(solution)/shard_map/ppermute | solution.py:83
  61.0 10.8 %collective-permute-start.18 = (bf16[200,384]{1,0:T(8,128)(2,1)S(1)}, bf16[200,384]{1,0:T(8,128)(2,1)S(1)}, u32[]{:S(2)}, u32[]{:S(2)}) collective-permute-start(bf16[200,384]{1,0:T(8,128)(2,1)S(1)} %collective-permute-done.10), channel_id=1, source_target_pairs={{0,56},{1,57},{2,58},{3,59},{4,60},{5,61},{6,62},{7,63},{8,0},{9,1... | collective-permute-start | bytes 460808 | tf_op jit(solution)/shard_map/ppermute | solution.py:82
  61.1 7.6 %collective-permute-start.13 = (bf16[200,448]{1,0:T(8,128)(2,1)S(1)}, bf16[200,448]{1,0:T(8,128)(2,1)S(1)}, u32[]{:S(2)}, u32[]{:S(2)}) collective-permute-start(bf16[200,448]{1,0:T(8,128)(2,1)S(1)} %collective-permute-done.12), channel_id=1, source_target_pairs={{0,64},{64,0},{128,192},{192,128},{1,65},{65,1},{129,193},{193,129... | collective-permute-start | bytes 537608 | tf_op jit(solution)/shard_map/ppermute | solution.py:83
  65.5 7.9 %collective-permute-start.20 = (bf16[200,448]{1,0:T(8,128)(2,1)S(1)}, bf16[200,448]{1,0:T(8,128)(2,1)S(1)}, u32[]{:S(2)}, u32[]{:S(2)}) collective-permute-start(bf16[200,448]{1,0:T(8,128)(2,1)S(1)} %collective-permute-done.12), channel_id=1, source_target_pairs={{0,56},{1,57},{2,58},{3,59},{4,60},{5,61},{6,62},{7,63},{8,0},{9,1... | collective-permute-start | bytes 537608 | tf_op jit(solution)/shard_map/ppermute | solution.py:82
  65.5 6.2 %collective-permute-start.15 = (bf16[200,384]{1,0:T(8,128)(2,1)S(1)}, bf16[200,384]{1,0:T(8,128)(2,1)S(1)}, u32[]{:S(2)}, u32[]{:S(2)}) collective-permute-start(bf16[200,384]{1,0:T(8,128)(2,1)S(1)} %collective-permute-done.14), channel_id=1, source_target_pairs={{0,64},{64,0},{128,192},{192,128},{1,65},{65,1},{129,193},{193,129... | collective-permute-start | bytes 460808 | tf_op jit(solution)/shard_map/ppermute | solution.py:83
  67.2 10.8 %collective-permute-start.22 = (bf16[200,384]{1,0:T(8,128)(2,1)S(1)}, bf16[200,384]{1,0:T(8,128)(2,1)S(1)}, u32[]{:S(2)}, u32[]{:S(2)}) collective-permute-start(bf16[200,384]{1,0:T(8,128)(2,1)S(1)} %collective-permute-done.14), channel_id=1, source_target_pairs={{0,56},{1,57},{2,58},{3,59},{4,60},{5,61},{6,62},{7,63},{8,0},{9,1... | collective-permute-start | bytes 460808 | tf_op jit(solution)/shard_map/ppermute | solution.py:82
  68.6 6.2 %collective-permute-start.17 = (bf16[200,384]{1,0:T(8,128)(2,1)S(1)}, bf16[200,384]{1,0:T(8,128)(2,1)S(1)}, u32[]{:S(2)}, u32[]{:S(2)}) collective-permute-start(bf16[200,384]{1,0:T(8,128)(2,1)S(1)} %collective-permute-done.16), channel_id=1, source_target_pairs={{0,64},{64,0},{128,192},{192,128},{1,65},{65,1},{129,193},{193,129... | collective-permute-start | bytes 460808 | tf_op jit(solution)/shard_map/ppermute | solution.py:83
  71.7 7.9 %collective-permute-start.24 = (bf16[200,384]{1,0:T(8,128)(2,1)S(1)}, bf16[200,384]{1,0:T(8,128)(2,1)S(1)}, u32[]{:S(2)}, u32[]{:S(2)}) collective-permute-start(bf16[200,384]{1,0:T(8,128)(2,1)S(1)} %collective-permute-done.16), channel_id=1, source_target_pairs={{0,56},{1,57},{2,58},{3,59},{4,60},{5,61},{6,62},{7,63},{8,0},{9,1... | collective-permute-start | bytes 460808 | tf_op jit(solution)/shard_map/ppermute | solution.py:82
  71.7 6.2 %collective-permute-start.19 = (bf16[200,384]{1,0:T(8,128)(2,1)S(1)}, bf16[200,384]{1,0:T(8,128)(2,1)S(1)}, u32[]{:S(2)}, u32[]{:S(2)}) collective-permute-start(bf16[200,384]{1,0:T(8,128)(2,1)S(1)} %collective-permute-done.18), channel_id=1, source_target_pairs={{0,64},{64,0},{128,192},{192,128},{1,65},{65,1},{129,193},{193,129... | collective-permute-start | bytes 460808 | tf_op jit(solution)/shard_map/ppermute | solution.py:83
  73.4 12.8 %collective-permute-start.26 = (bf16[200,384]{1,0:T(8,128)(2,1)S(1)}, bf16[200,384]{1,0:T(8,128)(2,1)S(1)}, u32[]{:S(2)}, u32[]{:S(2)}) collective-permute-start(bf16[200,384]{1,0:T(8,128)(2,1)S(1)} %collective-permute-done.18), channel_id=1, source_target_pairs={{0,56},{1,57},{2,58},{3,59},{4,60},{5,61},{6,62},{7,63},{8,0},{9,1... | collective-permute-start | bytes 460808 | tf_op jit(solution)/shard_map/ppermute | solution.py:82
  74.8 5.4 %collective-permute-start.21 = (bf16[200,448]{1,0:T(8,128)(2,1)S(1)}, bf16[200,448]{1,0:T(8,128)(2,1)S(1)}, u32[]{:S(2)}, u32[]{:S(2)}) collective-permute-start(bf16[200,448]{1,0:T(8,128)(2,1)S(1)} %collective-permute-done.20), channel_id=1, source_target_pairs={{0,64},{64,0},{128,192},{192,128},{1,65},{65,1},{129,193},{193,129... | collective-permute-start | bytes 537608 | tf_op jit(solution)/shard_map/ppermute | solution.py:83
  77.9 11.6 %collective-permute-start.28 = (bf16[200,448]{1,0:T(8,128)(2,1)S(1)}, bf16[200,448]{1,0:T(8,128)(2,1)S(1)}, u32[]{:S(2)}, u32[]{:S(2)}) collective-permute-start(bf16[200,448]{1,0:T(8,128)(2,1)S(1)} %collective-permute-done.20), channel_id=1, source_target_pairs={{0,56},{1,57},{2,58},{3,59},{4,60},{5,61},{6,62},{7,63},{8,0},{9,1... | collective-permute-start | bytes 537608 | tf_op jit(solution)/shard_map/ppermute | solution.py:82
  77.9 8.9 %collective-permute-start.23 = (bf16[200,384]{1,0:T(8,128)(2,1)S(1)}, bf16[200,384]{1,0:T(8,128)(2,1)S(1)}, u32[]{:S(2)}, u32[]{:S(2)}) collective-permute-start(bf16[200,384]{1,0:T(8,128)(2,1)S(1)} %collective-permute-done.22), channel_id=1, source_target_pairs={{0,64},{64,0},{128,192},{192,128},{1,65},{65,1},{129,193},{193,129... | collective-permute-start | bytes 460808 | tf_op jit(solution)/shard_map/ppermute | solution.py:83
  79.6 17.0 %collective-permute-start.30 = (bf16[200,384]{1,0:T(8,128)(2,1)S(1)}, bf16[200,384]{1,0:T(8,128)(2,1)S(1)}, u32[]{:S(2)}, u32[]{:S(2)}) collective-permute-start(bf16[200,384]{1,0:T(8,128)(2,1)S(1)} %collective-permute-done.22), channel_id=1, source_target_pairs={{0,56},{1,57},{2,58},{3,59},{4,60},{5,61},{6,62},{7,63},{8,0},{9,1... | collective-permute-start | bytes 460808 | tf_op jit(solution)/shard_map/ppermute | solution.py:94
  80.3 12.9 %collective-permute-start.25 = (bf16[200,384]{1,0:T(8,128)(2,1)S(1)}, bf16[200,384]{1,0:T(8,128)(2,1)S(1)}, u32[]{:S(2)}, u32[]{:S(2)}) collective-permute-start(bf16[200,384]{1,0:T(8,128)(2,1)S(1)} %collective-permute-done.24), channel_id=1, source_target_pairs={{0,64},{64,0},{128,192},{192,128},{1,65},{65,1},{129,193},{193,129... | collective-permute-start | bytes 460808 | tf_op jit(solution)/shard_map/ppermute | solution.py:83
  86.1 13.1 %collective-permute-start.32 = (bf16[200,384]{1,0:T(8,128)(2,1)S(1)}, bf16[200,384]{1,0:T(8,128)(2,1)S(1)}, u32[]{:S(2)}, u32[]{:S(2)}) collective-permute-start(bf16[200,384]{1,0:T(8,128)(2,1)S(1)} %collective-permute-done.24), channel_id=1, source_target_pairs={{0,56},{1,57},{2,58},{3,59},{4,60},{5,61},{6,62},{7,63},{8,0},{9,1... | collective-permute-start | bytes 460808 | tf_op jit(solution)/shard_map/ppermute | solution.py:94
  86.8 7.8 %collective-permute-start.27 = (bf16[200,384]{1,0:T(8,128)(2,1)S(1)}, bf16[200,384]{1,0:T(8,128)(2,1)S(1)}, u32[]{:S(2)}, u32[]{:S(2)}) collective-permute-start(bf16[200,384]{1,0:T(8,128)(2,1)S(1)} %collective-permute-done.26), channel_id=1, source_target_pairs={{0,64},{64,0},{128,192},{192,128},{1,65},{65,1},{129,193},{193,129... | collective-permute-start | bytes 460808 | tf_op jit(solution)/shard_map/ppermute | solution.py:83
  89.5 11.0 %collective-permute-start.34 = (bf16[200,384]{1,0:T(8,128)(2,1)S(1)}, bf16[200,384]{1,0:T(8,128)(2,1)S(1)}, u32[]{:S(2)}, u32[]{:S(2)}) collective-permute-start(bf16[200,384]{1,0:T(8,128)(2,1)S(1)} %collective-permute-done.26), channel_id=1, source_target_pairs={{64,72},{65,73},{66,74},{67,75},{68,76},{69,77},{70,78},{71,79},{7... | collective-permute-start | bytes 460808 | tf_op jit(solution)/shard_map/ppermute | solution.py:94
  93.2 11.8 %collective-permute-start.29 = (bf16[200,448]{1,0:T(8,128)(2,1)S(1)}, bf16[200,448]{1,0:T(8,128)(2,1)S(1)}, u32[]{:S(2)}, u32[]{:S(2)}) collective-permute-start(bf16[200,448]{1,0:T(8,128)(2,1)S(1)} %collective-permute-done.28), channel_id=1, source_target_pairs={{0,64},{64,0},{128,192},{192,128},{1,65},{65,1},{129,193},{193,129... | collective-permute-start | bytes 537608 | tf_op jit(solution)/shard_map/ppermute | solution.py:83
  94.6 9.0 %collective-permute-start.36 = (bf16[200,448]{1,0:T(8,128)(2,1)S(1)}, bf16[200,448]{1,0:T(8,128)(2,1)S(1)}, u32[]{:S(2)}, u32[]{:S(2)}) collective-permute-start(bf16[200,448]{1,0:T(8,128)(2,1)S(1)} %collective-permute-done.28), channel_id=1, source_target_pairs={{64,72},{65,73},{66,74},{67,75},{68,76},{69,77},{70,78},{71,79},{7... | collective-permute-start | bytes 537608 | tf_op jit(solution)/shard_map/ppermute | solution.py:94
  96.6 9.1 %collective-permute-start.31 = (bf16[200,384]{1,0:T(8,128)(2,1)S(1)}, bf16[200,384]{1,0:T(8,128)(2,1)S(1)}, u32[]{:S(2)}, u32[]{:S(2)}) collective-permute-start(bf16[200,384]{1,0:T(8,128)(2,1)S(1)} %collective-permute-done.30), channel_id=1, source_target_pairs={{0,64},{128,192},{1,65},{129,193},{2,66},{130,194},{3,67},{131,195... | collective-permute-start | bytes 460808 | tf_op jit(solution)/shard_map/ppermute | solution.py:99
  99.3 7.1 %collective-permute-start.33 = (bf16[200,384]{1,0:T(8,128)(2,1)S(1)}, bf16[200,384]{1,0:T(8,128)(2,1)S(1)}, u32[]{:S(2)}, u32[]{:S(2)}) collective-permute-start(bf16[200,384]{1,0:T(8,128)(2,1)S(1)} %collective-permute-done.32), channel_id=1, source_target_pairs={{0,64},{128,192},{1,65},{129,193},{2,66},{130,194},{3,67},{131,195... | collective-permute-start | bytes 460808 | tf_op jit(solution)/shard_map/ppermute | solution.py:99
  100.6 6.5 %collective-permute-start.35 = (bf16[200,384]{1,0:T(8,128)(2,1)S(1)}, bf16[200,384]{1,0:T(8,128)(2,1)S(1)}, u32[]{:S(2)}, u32[]{:S(2)}) collective-permute-start(bf16[200,384]{1,0:T(8,128)(2,1)S(1)} %collective-permute-done.34), channel_id=1, source_target_pairs={{64,0},{192,128},{65,1},{193,129},{66,2},{194,130},{67,3},{195,131... | collective-permute-start | bytes 460808 | tf_op jit(solution)/shard_map/ppermute | solution.py:99
  103.6 4.2 %collective-permute-start.37 = (bf16[200,448]{1,0:T(8,128)(2,1)S(1)}, bf16[200,448]{1,0:T(8,128)(2,1)S(1)}, u32[]{:S(2)}, u32[]{:S(2)}) collective-permute-start(bf16[200,448]{1,0:T(8,128)(2,1)S(1)} %collective-permute-done.36), channel_id=1, source_target_pairs={{64,0},{192,128},{65,1},{193,129},{66,2},{194,130},{67,3},{195,131... | collective-permute-start | bytes 537608 | tf_op jit(solution)/shard_map/ppermute | solution.py:99

commit v8 on v6

--- a/solution.py
+++ b/solution.py
@@ -51,19 +51,20 @@
     ns = NZ * NX * NYH
 
     other = lax.ppermute(blk, ("grp", "shard"), both(lambda g, s: (g ^ 2, s ^ 1)))
-    b50 = jnp.zeros((NYH * rows, d), blk.dtype)
-    b50 = lax.dynamic_update_slice(b50, blk, (yh * rows, 0))
-    b50 = lax.dynamic_update_slice(b50, other, ((1 - yh) * rows, 0))
+    b50 = jnp.where(yh == 0, jnp.concatenate([blk, other]), jnp.concatenate([other, blk]))
 
     zb = NX * NYH * rows
-    b200 = lax.dynamic_update_slice(jnp.zeros((zb, d), blk.dtype), b50, (x * NYH * rows, 0))
+    rel = [b50]
     for k in range(1, NX):
-        got = lax.ppermute(
-            b50,
-            "shard",
-            [(sidx(zxy(s)[0], zxy(s)[1] + k, zxy(s)[2]), s) for s in range(NZ * NX * NYH)],
+        rel.append(
+            lax.ppermute(
+                b50,
+                "shard",
+                [(sidx(zxy(s)[0], zxy(s)[1] + k, zxy(s)[2]), s) for s in range(NZ * NX * NYH)],
+            )
         )
-        b200 = lax.dynamic_update_slice(b200, got, (((x + k) % NX) * NYH * rows, 0))
+    xi = (jnp.arange(NX) - x) % NX
+    b200 = jnp.take(jnp.stack(rel), xi, axis=0).reshape(zb, d)
 
     def zring(g, s):
         zz, xx, yy = zxy(s)

time: 87.9 us -> 88.8 us (1.010)
  waiting for transfers between devices: 39.1 us -> 31.5 us
  starting transfers between devices: 22.6 us -> 26.7 us
  local copies, waits for them, and re-layouts: 12.9 us -> 16 us
  other arithmetic: 4.43 us -> 7.21 us
  matrix products: 7.2 us -> 6.08 us
    ppermute x6, waiting for transfers between devices: 19.7 us -> 12.5 us  [gather_copy(): cur = [lax.ppermute(c, ('grp', 'shard'), zpairs) for c in cur]]
    dynamic_update_slice x7 -> x0, local copies, waits for them, and re-layouts: 6.56 us -> none  [the longest x3 3.64 us: gather_copy(): b200 = lax.dynamic_update_slice(b200, got, ((x + k) % NX * NYH * rows, 0))]
    ppermute x6, starting transfers between devices: 7.59 us -> 12.2 us  [gather_copy(): mate = [lax.ppermute(c, 'grp', swap) for c in cur]]
    dynamic_update_slice x6, local copies, waits for them, and re-layouts: 0.21 us -> 4.53 us  [gather_copy(): out = lax.dynamic_update_slice(out, m, (mate_at, col))]
    dynamic_update_slice x6, local copies, waits for them, and re-layouts: 0.22 us -> 4.5 us  [gather_copy(): out = lax.dynamic_update_slice(out, c, (mine_at, col))]
    ppermute x3, waiting for transfers between devices: 3.41 us -> 6.65 us  [gather_copy(): lax.ppermute(b50, 'shard', [(sidx(zxy(s)[0], zxy(s)[1] + k, zxy(s)[2]), s...]
    ppermute x1, waiting for transfers between devices: 5.92 us -> 3.1 us  [gather_copy(): got_b = lax.ppermute(cur[1], ('grp', 'shard'), second)]
    broadcast_in_dim x1, local copies, waits for them, and re-layouts: 0.37 us -> 2.76 us  [gather_copy(): jnp.zeros((NZ * zb, d), blk.dtype)]
  transfers between devices with their start and end apart: 24 -> 24, of which waited for: 11 -> 11; matrix products, arithmetic and copies ran while one was open for 22% -> 25% of each run, Pallas kernels for 0% -> 0%
where the time goes in v8:
time: 88.8 us; the launch traced here: 88.5 us
  waiting for transfers between devices  31.5 us (35%)
  starting transfers between devices  26.7 us (30%)
  local copies, waits for them, and re-layouts  16 us (18%)
  other arithmetic  7.21 us (8%)
  matrix products  6.08 us (7%)
  between operations  1.12 us (1%)
    ppermute x6, waiting for transfers between devices, gather_copy(): cur = [lax.ppermute(c, ('grp', 'shard'), zpairs) for c in cur]  12.5 us
    ppermute x6, starting transfers between devices, gather_copy(): mate = [lax.ppermute(c, 'grp', swap) for c in cur]  12.2 us
    ppermute x3, waiting for transfers between devices, gather_copy(): lax.ppermute(b50, 'shard', [(sidx(zxy(s)[0], zxy(s)[1] + k, zxy(s)[2]), s...  6.65 us
    ppermute x1, waiting for transfers between devices, butterfly_sum(): far = lax.ppermute(v, 'grp', [(i, i ^ 2) for i in range(NG)])  5.55 us
    dynamic_update_slice x6, local copies, waits for them, and re-layouts, gather_copy(): out = lax.dynamic_update_slice(out, m, (mate_at, col))  4.53 us
    dynamic_update_slice x6, local copies, waits for them, and re-layouts, gather_copy(): out = lax.dynamic_update_slice(out, c, (mine_at, col))  4.5 us
    ppermute x1, waiting for transfers between devices, gather_copy(): lax.ppermute(blk, ('grp', 'shard'), both(lambda g, s: (g ^ 2, s ^ 1)))  3.66 us
    ppermute x1, starting transfers between devices, butterfly_sum(): v = v + lax.ppermute(v, 'grp', [(i, i ^ 1) for i in range(NG)])  3.29 us
  transfers between devices with their start and end apart: 24, of which 11 were waited for; matrix products, arithmetic and copies ran while one was open for 25% of the time, Pallas kernels for 0%

profile of v8, /device:TPU:1, one launch (start us, length us, event | category | flops | bytes accessed | tf_op | source)
XLA Modules:
  0.0 88.5 jit_solution(10433177066924357816)
XLA Ops:
  0.6 1.1 %bitcast_subtract_fusion = f32[25,1600]{1,0:T(8,128)S(1)} fusion(f32[25,1600]{1,0:T(8,128)} %param.10, f32[1,25,1600]{2,0,1:T(1,128)} %param.9), kind=kLoop, calls=%fused_computation.11 | loop fusion | flops 40000 | bytes 480000 | tf_op jit(solution)/shard_map/sub | solution.py:116
  1.7 3.3 %collective-permute-start = (f32[25,1600]{1,0:T(8,128)S(1)}, f32[25,1600]{1,0:T(8,128)}, u32[]{:S(2)}, u32[]{:S(2)}) collective-permute-start(f32[25,1600]{1,0:T(8,128)S(1)} %bitcast_subtract_fusion), channel_id=1, source_target_pairs={{0,64},{64,0},{128,192},{192,128},{1,65},{65,1},{129,193},{193,129... | collective-permute-start | bytes 480008 | tf_op jit(solution)/shard_map/ppermute | solution.py:37
  5.0 1.9 %dot_general.12 = f32[4,100,1600]{2,1,0:T(8,128)S(1)} reshape(f32[1,400,1600]{2,1,0:T(8,128)} %param.12) | data formatting | bytes 5120000 | tf_op jit(solution)/shard_map/dot_general | solution.py:102
  6.9 0.1 compare_and_fusion
  7.0 3.3 %fusion = f32[4,100,64]{1,2,0:T(8,128)S(1)} fusion(f32[4,100,1600]{2,1,0:T(8,128)S(1)} %dot_general.12, f32[1600,64]{0,1:T(8,128)S(1)} %copy-done), kind=kOutput, calls=%fused_computation.7 | convolution fusion | flops 491520000 | bytes 3072000 | tf_op jit(solution)/shard_map/dot_general | solution.py:102
  10.3 0.6 gather_fusion.2
  10.9 0.1 broadcast_select_fusion.1
  11.0 0.1 compare_and_fusion.1
  11.1 1.0 %add.135 = f32[25,1600]{1,0:T(8,128)S(1)} add(f32[25,1600]{1,0:T(8,128)S(1)} %bitcast_subtract_fusion, f32[25,1600]{1,0:T(8,128)} %collective-permute-done) | non-fusion elementwise | flops 40000 | bytes 480000 | tf_op jit(solution)/shard_map/add | solution.py:37
  12.1 0.1 collective-permute-start.1
  12.3 0.1 broadcast_in_dim.28
  12.4 0.6 gather_fusion.1
  13.0 5.5 %collective-permute-done.1 = f32[25,1600]{1,0:T(8,128)S(1)} collective-permute-done((f32[25,1600]{1,0:T(8,128)S(1)}, f32[25,1600]{1,0:T(8,128)S(1)}, u32[]{:S(2)}, u32[]{:S(2)}) %collective-permute-start.1) | collective-permute-done | bytes 160032 | tf_op jit(solution)/shard_map/ppermute | solution.py:38
  18.5 1.9 %fusion.12 = (bf16[25,1600]{1,0:T(8,128)(2,1)S(1)}, f32[25,1600]{1,0:T(8,128)}, f32[25,1600]{1,0:T(8,128)}) fusion(f32[25,1600]{1,0:T(8,128)} %param.10, f32[25,1600]{1,0:T(8,128)S(1)} %add.135, f32[25,1600]{1,0:T(8,128)S(1)} %collective-permute-done.1, f32[25,1600]{1,0:T(8,128)} %param.11), kind=kLoop, calls=%fused_computation.59 | loop fusion | flops 360000 | bytes 1040000 | tf_op jit(solution)/shard_map/convert_element_type | solution.py:119
  20.4 1.0 %collective-permute-start.2 = (bf16[25,1600]{1,0:T(8,128)(2,1)S(1)}, bf16[25,1600]{1,0:T(8,128)(2,1)S(1)}, u32[]{:S(2)}, u32[]{:S(2)}) collective-permute-start(bf16[25,1600]{1,0:T(8,128)(2,1)S(1)} %get-tuple-element.14), channel_id=1, source_target_pairs={{0,129},{1,128},{2,131},{3,130},{4,133},{5,132},{6,135},{7,134},{8... | collective-permute-start | bytes 240008 | tf_op jit(solution)/shard_map/ppermute | solution.py:53
  21.4 0.1 select_add_fusion
  21.5 3.7 %collective-permute-done.2 = bf16[25,1600]{1,0:T(8,128)(2,1)S(1)} collective-permute-done((bf16[25,1600]{1,0:T(8,128)(2,1)S(1)}, bf16[25,1600]{1,0:T(8,128)(2,1)S(1)}, u32[]{:S(2)}, u32[]{:S(2)}) %collective-permute-start.2) | collective-permute-done | bytes 80032 | tf_op jit(solution)/shard_map/ppermute | solution.py:53
  25.2 0.1 maximum_select_fusion.1
  25.2 0.1 collective-permute-start.5
  25.3 2.0 %collective-permute-start.4 = (bf16[50,1600]{1,0:T(8,128)(2,1)S(1)}, bf16[50,1600]{1,0:T(8,128)(2,1)S(1)}, u32[]{:S(2)}, u32[]{:S(2)}) collective-permute-start(bf16[50,1600]{1,0:T(8,128)(2,1)S(1)} %maximum_select_fusion.1), channel_id=1, source_target_pairs={{4,0},{5,1},{6,2},{7,3},{0,4},{1,5},{2,6},{3,7},{12,8},{13,9},{14,... | collective-permute-start | bytes 480008 | tf_op jit(solution)/shard_map/ppermute | solution.py:60
  27.3 1.2 %collective-permute-start.3 = (bf16[50,1600]{1,0:T(8,128)(2,1)S(1)}, bf16[50,1600]{1,0:T(8,128)(2,1)S(1)}, u32[]{:S(2)}, u32[]{:S(2)}) collective-permute-start(bf16[50,1600]{1,0:T(8,128)(2,1)S(1)} %maximum_select_fusion.1), channel_id=1, source_target_pairs={{2,0},{3,1},{4,2},{5,3},{6,4},{7,5},{0,6},{1,7},{10,8},{11,9},{12,... | collective-permute-start | bytes 480008 | tf_op jit(solution)/shard_map/ppermute | solution.py:60
  28.5 0.1 maximum_select_fusion
  28.6 4.8 %collective-permute-done.5 = bf16[50,1600]{1,0:T(8,128)(2,1)S(1)} collective-permute-done((bf16[50,1600]{1,0:T(8,128)(2,1)S(1)}, bf16[50,1600]{1,0:T(8,128)(2,1)S(1)}, u32[]{:S(2)}, u32[]{:S(2)}) %collective-permute-start.5) | collective-permute-done | bytes 160032 | tf_op jit(solution)/shard_map/ppermute | solution.py:60
  33.4 1.8 %collective-permute-done.3 = bf16[50,1600]{1,0:T(8,128)(2,1)S(1)} collective-permute-done((bf16[50,1600]{1,0:T(8,128)(2,1)S(1)}, bf16[50,1600]{1,0:T(8,128)(2,1)S(1)}, u32[]{:S(2)}, u32[]{:S(2)}) %collective-permute-start.3) | collective-permute-done | bytes 160032 | tf_op jit(solution)/shard_map/ppermute | solution.py:60
  35.2 0.1 pad_maximum_fusion
  35.4 0.7 gather_fusion
  36.0 0.3 gather.10
  36.4 2.8 %broadcast_in_dim.26 = bf16[1600,1600]{1,0:T(8,128)(2,1)} broadcast(bf16[]{:T(256)} %constant.128.clone.1), dimensions={} | broadcast | bytes 5120002 | tf_op jit(solution)/shard_map/broadcast_in_dim | solution.py:76
  39.1 1.0 %constant_dynamic-update-slice_fusion.12 = (bf16[1600,1600]{1,0:T(8,128)(2,1)}, bf16[200,1600]{1,0:T(8,128)(2,1)S(1)}) fusion(bf16[1600,1600]{1,0:T(8,128)(2,1)} %broadcast_in_dim.26, s32[]{:T(128)S(6)} %select_n.174, bf16[200,1600]{1,0:T(8,128)(2,1)S(1)} %gather.10, pred[200]{0:T(512)(128)(4,1)S(1)} %broadcast_in_dim.28), kind=kLoop, calls=%fused_computation.49 | loop fusion | flops 320000 | bytes 1945804 | tf_op jit(solution)/shard_map/dynamic_update_slice | solution.py:76
  40.2 0.1 collective-permute-start.6
  40.3 0.1 collective-permute-start.23
  40.4 1.4 %collective-permute-start.8 = (bf16[200,832]{1,0:T(8,128)(2,1)S(1)}, bf16[200,832]{1,0:T(8,128)(2,1)S(1)}, u32[]{:S(2)}, u32[]{:S(2)}) collective-permute-start(bf16[200,832]{1,0:T(8,128)(2,1)S(1)} %slice.23), channel_id=1, source_target_pairs={{0,56},{1,57},{2,58},{3,59},{4,60},{5,61},{6,62},{7,63},{8,0},{9,1... | collective-permute-start | bytes 998408 | tf_op jit(solution)/shard_map/ppermute | solution.py:79
  41.8 0.9 fusion.13
  42.9 5.4 %collective-permute-done.6 = bf16[200,768]{1,0:T(8,128)(2,1)S(1)} collective-permute-done((bf16[200,768]{1,0:T(8,128)(2,1)S(1)}, bf16[200,768]{1,0:T(8,128)(2,1)S(1)}, u32[]{:S(2)}, u32[]{:S(2)}) %collective-permute-start.6) | collective-permute-done | bytes 307232 | tf_op jit(solution)/shard_map/ppermute | solution.py:79
  48.3 4.0 %collective-permute-start.7 = (bf16[200,768]{1,0:T(8,128)(2,1)S(1)}, bf16[200,768]{1,0:T(8,128)(2,1)S(1)}, u32[]{:S(2)}, u32[]{:S(2)}) collective-permute-start(bf16[200,768]{1,0:T(8,128)(2,1)S(1)} %collective-permute-done.6), channel_id=1, source_target_pairs={{0,64},{64,0},{128,192},{192,128},{1,65},{65,1},{129,193},{193,129... | collective-permute-start | bytes 921608 | tf_op jit(solution)/shard_map/ppermute | solution.py:80
  52.2 1.9 %multiply_subtract_fusion = (f32[100,1600]{1,0:T(8,128)}, f32[100,1600]{1,0:T(8,128)}) fusion(f32[100,1600]{1,0:T(8,128)S(1)} %copy-done.1, f32[100,1600]{1,0:T(8,128)S(1)} %copy-done.2, f32[1600,64]{0,1:T(8,128)S(1)} %copy-done, f32[100,64]{0,1:T(8,128)S(1)} %fusion.13, f32[100,64]{0,1:T(8,128)S(1)} %collective-permute-done.23, ...), kind=kOutput, calls=%fused_computation.4 | convolution fusion | flops 123859200 | bytes 3188736 | tf_op jit(solution)/shard_map/dot_general | solution.py:113
  54.2 3.7 %collective-permute-start.9 = (bf16[200,832]{1,0:T(8,128)(2,1)S(1)}, bf16[200,832]{1,0:T(8,128)(2,1)S(1)}, u32[]{:S(2)}, u32[]{:S(2)}) collective-permute-start(bf16[200,832]{1,0:T(8,128)(2,1)S(1)} %collective-permute-done.8), channel_id=1, source_target_pairs={{0,64},{64,0},{128,192},{192,128},{1,65},{65,1},{129,193},{193,129... | collective-permute-start | bytes 998408 | tf_op jit(solution)/shard_map/ppermute | solution.py:80
  57.9 0.7 constant_dynamic-update-slice_fusion.11
  58.6 1.3 %collective-permute-done.10 = bf16[200,768]{1,0:T(8,128)(2,1)S(1)} collective-permute-done((bf16[200,768]{1,0:T(8,128)(2,1)S(1)}, bf16[200,768]{1,0:T(8,128)(2,1)S(1)}, u32[]{:S(2)}, u32[]{:S(2)}) %collective-permute-start.10) | collective-permute-done | bytes 307232 | tf_op jit(solution)/shard_map/ppermute | solution.py:79
  59.9 0.6 collective-permute-start.11
  60.5 0.7 constant_dynamic-update-slice_fusion.10
  61.2 0.8 constant_dynamic-update-slice_fusion.5
  62.0 3.3 %collective-permute-done.12 = bf16[200,832]{1,0:T(8,128)(2,1)S(1)} collective-permute-done((bf16[200,832]{1,0:T(8,128)(2,1)S(1)}, bf16[200,832]{1,0:T(8,128)(2,1)S(1)}, u32[]{:S(2)}, u32[]{:S(2)}) %collective-permute-start.12) | collective-permute-done | bytes 332832 | tf_op jit(solution)/shard_map/ppermute | solution.py:79
  65.3 0.2 collective-permute-start.13
  65.5 0.8 constant_dynamic-update-slice_fusion.4
  66.3 0.7 constant_dynamic-update-slice_fusion.9
  67.0 1.6 %collective-permute-done.14 = bf16[200,768]{1,0:T(8,128)(2,1)S(1)} collective-permute-done((bf16[200,768]{1,0:T(8,128)(2,1)S(1)}, bf16[200,768]{1,0:T(8,128)(2,1)S(1)}, u32[]{:S(2)}, u32[]{:S(2)}) %collective-permute-start.14) | collective-permute-done | bytes 307232 | tf_op jit(solution)/shard_map/ppermute | solution.py:79
  68.6 1.3 %collective-permute-start.15 = (bf16[200,768]{1,0:T(8,128)(2,1)S(1)}, bf16[200,768]{1,0:T(8,128)(2,1)S(1)}, u32[]{:S(2)}, u32[]{:S(2)}) collective-permute-start(bf16[200,768]{1,0:T(8,128)(2,1)S(1)} %collective-permute-done.14), channel_id=1, source_target_pairs={{0,64},{64,0},{128,192},{192,128},{1,65},{65,1},{129,193},{193,129... | collective-permute-start | bytes 921608 | tf_op jit(solution)/shard_map/ppermute | solution.py:80
  69.9 0.7 collective-permute-start.18
  70.6 0.7 constant_dynamic-update-slice_fusion.8
  71.3 0.8 constant_dynamic-update-slice_fusion.3
  72.1 0.9 collective-permute-done.16
  73.0 2.5 %collective-permute-start.17 = (bf16[200,832]{1,0:T(8,128)(2,1)S(1)}, bf16[200,832]{1,0:T(8,128)(2,1)S(1)}, u32[]{:S(2)}, u32[]{:S(2)}) collective-permute-start(bf16[200,832]{1,0:T(8,128)(2,1)S(1)} %collective-permute-done.16), channel_id=1, source_target_pairs={{0,64},{64,0},{128,192},{192,128},{1,65},{65,1},{129,193},{193,129... | collective-permute-start | bytes 998408 | tf_op jit(solution)/shard_map/ppermute | solution.py:80
  75.5 1.9 %collective-permute-start.20 = (bf16[200,832]{1,0:T(8,128)(2,1)S(1)}, bf16[200,832]{1,0:T(8,128)(2,1)S(1)}, u32[]{:S(2)}, u32[]{:S(2)}) collective-permute-start(bf16[200,832]{1,0:T(8,128)(2,1)S(1)} %collective-permute-done.16), channel_id=1, source_target_pairs={{64,72},{65,73},{66,74},{67,75},{68,76},{69,77},{70,78},{71,79},{7... | collective-permute-start | bytes 998408 | tf_op jit(solution)/shard_map/ppermute | solution.py:90
  77.4 0.8 constant_dynamic-update-slice_fusion.2
  78.2 0.7 constant_dynamic-update-slice_fusion.7
  78.9 1.3 %collective-permute-start.19 = (bf16[200,768]{1,0:T(8,128)(2,1)S(1)}, bf16[200,768]{1,0:T(8,128)(2,1)S(1)}, u32[]{:S(2)}, u32[]{:S(2)}) collective-permute-start(bf16[200,768]{1,0:T(8,128)(2,1)S(1)} %collective-permute-done.18), channel_id=1, source_target_pairs={{0,64},{128,192},{1,65},{129,193},{2,66},{130,194},{3,67},{131,195... | collective-permute-start | bytes 921608 | tf_op jit(solution)/shard_map/ppermute | solution.py:91
  80.2 0.7 constant_dynamic-update-slice_fusion.6
  81.0 0.8 constant_dynamic-update-slice_fusion.1
  81.7 3.1 %collective-permute-done.20 = bf16[200,832]{1,0:T(8,128)(2,1)S(1)} collective-permute-done((bf16[200,832]{1,0:T(8,128)(2,1)S(1)}, bf16[200,832]{1,0:T(8,128)(2,1)S(1)}, u32[]{:S(2)}, u32[]{:S(2)}) %collective-permute-start.20) | collective-permute-done | bytes 332832 | tf_op jit(solution)/shard_map/ppermute | solution.py:90
  84.8 1.3 %collective-permute-start.21 = (bf16[200,832]{1,0:T(8,128)(2,1)S(1)}, bf16[200,832]{1,0:T(8,128)(2,1)S(1)}, u32[]{:S(2)}, u32[]{:S(2)}) collective-permute-start(bf16[200,832]{1,0:T(8,128)(2,1)S(1)} %collective-permute-done.20), channel_id=1, source_target_pairs={{64,0},{192,128},{65,1},{193,129},{66,2},{194,130},{67,3},{195,131... | collective-permute-start | bytes 998408 | tf_op jit(solution)/shard_map/ppermute | solution.py:92
  86.2 0.8 constant_dynamic-update-slice_fusion
  86.9 0.8 select_dynamic-update-slice_fusion.1
  87.7 0.8 select_dynamic-update-slice_fusion
  (34 shorter events, 0.3 us)
Async XLA Ops:
  0.6 6.4 %copy-start = (f32[1600,64]{0,1:T(8,128)S(1)}, f32[1600,64]{0,1:T(8,128)}, u32[]{:S(2)}) copy-start(f32[1600,64]{0,1:T(8,128)} %param.15) | copy-start | bytes 1228804
  1.7 9.4 %collective-permute-start = (f32[25,1600]{1,0:T(8,128)S(1)}, f32[25,1600]{1,0:T(8,128)}, u32[]{:S(2)}, u32[]{:S(2)}) collective-permute-start(f32[25,1600]{1,0:T(8,128)S(1)} %bitcast_subtract_fusion), channel_id=1, source_target_pairs={{0,64},{64,0},{128,192},{192,128},{1,65},{65,1},{129,193},{193,129... | collective-permute-start | bytes 480008 | tf_op jit(solution)/shard_map/ppermute | solution.py:37
  10.9 10.5 %collective-permute-start.22 = (f32[2,100,64]{1,2,0:T(8,128)S(1)}, f32[2,100,64]{1,2,0:T(8,128)S(1)}, u32[]{:S(2)}, u32[]{:S(2)}) collective-permute-start(f32[2,100,64]{1,2,0:T(8,128)S(1)} %broadcast_select_fusion.1), channel_id=1, source_target_pairs={{0,64},{64,0},{128,192},{192,128},{1,65},{65,1},{129,193},{193,129... | collective-permute-start | bytes 153608 | tf_op jit(solution)/shard_map/ppermute | solution.py:108
  12.1 6.4 %collective-permute-start.1 = (f32[25,1600]{1,0:T(8,128)S(1)}, f32[25,1600]{1,0:T(8,128)S(1)}, u32[]{:S(2)}, u32[]{:S(2)}) collective-permute-start(f32[25,1600]{1,0:T(8,128)S(1)} %add.135), channel_id=1, source_target_pairs={{0,128},{64,192},{128,0},{192,64},{1,129},{65,193},{129,1},{193,65... | collective-permute-start | bytes 480008 | tf_op jit(solution)/shard_map/ppermute | solution.py:38
  20.4 4.8 %collective-permute-start.2 = (bf16[25,1600]{1,0:T(8,128)(2,1)S(1)}, bf16[25,1600]{1,0:T(8,128)(2,1)S(1)}, u32[]{:S(2)}, u32[]{:S(2)}) collective-permute-start(bf16[25,1600]{1,0:T(8,128)(2,1)S(1)} %get-tuple-element.14), channel_id=1, source_target_pairs={{0,129},{1,128},{2,131},{3,130},{4,133},{5,132},{6,135},{7,134},{8... | collective-permute-start | bytes 240008 | tf_op jit(solution)/shard_map/ppermute | solution.py:53
  25.2 8.1 %collective-permute-start.5 = (bf16[50,1600]{1,0:T(8,128)(2,1)S(1)}, bf16[50,1600]{1,0:T(8,128)(2,1)S(1)}, u32[]{:S(2)}, u32[]{:S(2)}) collective-permute-start(bf16[50,1600]{1,0:T(8,128)(2,1)S(1)} %maximum_select_fusion.1), channel_id=1, source_target_pairs={{6,0},{7,1},{0,2},{1,3},{2,4},{3,5},{4,6},{5,7},{14,8},{15,9},{8,1... | collective-permute-start | bytes 480008 | tf_op jit(solution)/shard_map/ppermute | solution.py:60
  25.3 8.1 %collective-permute-start.4 = (bf16[50,1600]{1,0:T(8,128)(2,1)S(1)}, bf16[50,1600]{1,0:T(8,128)(2,1)S(1)}, u32[]{:S(2)}, u32[]{:S(2)}) collective-permute-start(bf16[50,1600]{1,0:T(8,128)(2,1)S(1)} %maximum_select_fusion.1), channel_id=1, source_target_pairs={{4,0},{5,1},{6,2},{7,3},{0,4},{1,5},{2,6},{3,7},{12,8},{13,9},{14,... | collective-permute-start | bytes 480008 | tf_op jit(solution)/shard_map/ppermute | solution.py:60
  27.3 7.9 %collective-permute-start.3 = (bf16[50,1600]{1,0:T(8,128)(2,1)S(1)}, bf16[50,1600]{1,0:T(8,128)(2,1)S(1)}, u32[]{:S(2)}, u32[]{:S(2)}) collective-permute-start(bf16[50,1600]{1,0:T(8,128)(2,1)S(1)} %maximum_select_fusion.1), channel_id=1, source_target_pairs={{2,0},{3,1},{4,2},{5,3},{6,4},{7,5},{0,6},{1,7},{10,8},{11,9},{12,... | collective-permute-start | bytes 480008 | tf_op jit(solution)/shard_map/ppermute | solution.py:60
  36.0 5.8 %copy-start.1 = (f32[100,1600]{1,0:T(8,128)S(1)}, f32[100,1600]{1,0:T(8,128)}, u32[]{:S(2)}) copy-start(f32[100,1600]{1,0:T(8,128)} %param.13) | copy-start | bytes 1920004
  36.4 15.9 %copy-start.2 = (f32[100,1600]{1,0:T(8,128)S(1)}, f32[100,1600]{1,0:T(8,128)}, u32[]{:S(2)}) copy-start(f32[100,1600]{1,0:T(8,128)} %param.14) | copy-start | bytes 1920004
  40.2 8.1 %collective-permute-start.6 = (bf16[200,768]{1,0:T(8,128)(2,1)S(1)}, bf16[200,768]{1,0:T(8,128)(2,1)S(1)}, u32[]{:S(2)}, u32[]{:S(2)}) collective-permute-start(bf16[200,768]{1,0:T(8,128)(2,1)S(1)} %slice.22), channel_id=1, source_target_pairs={{0,56},{1,57},{2,58},{3,59},{4,60},{5,61},{6,62},{7,63},{8,0},{9,1... | collective-permute-start | bytes 921608 | tf_op jit(solution)/shard_map/ppermute | solution.py:79
  40.3 11.9 %collective-permute-start.23 = (f32[100,64]{0,1:T(8,128)S(1)}, f32[100,64]{0,1:T(8,128)S(1)}, u32[]{:S(2)}, u32[]{:S(2)}) collective-permute-start(f32[100,64]{0,1:T(8,128)S(1)} %slice_bitcast_fusion), channel_id=1, source_target_pairs={{0,128},{64,192},{128,0},{192,64},{1,129},{65,193},{129,1},{193,65... | collective-permute-start | bytes 76808 | tf_op jit(solution)/shard_map/ppermute | solution.py:111
  40.4 13.8 %collective-permute-start.8 = (bf16[200,832]{1,0:T(8,128)(2,1)S(1)}, bf16[200,832]{1,0:T(8,128)(2,1)S(1)}, u32[]{:S(2)}, u32[]{:S(2)}) collective-permute-start(bf16[200,832]{1,0:T(8,128)(2,1)S(1)} %slice.23), channel_id=1, source_target_pairs={{0,56},{1,57},{2,58},{3,59},{4,60},{5,61},{6,62},{7,63},{8,0},{9,1... | collective-permute-start | bytes 998408 | tf_op jit(solution)/shard_map/ppermute | solution.py:79
  48.3 12.2 %collective-permute-start.7 = (bf16[200,768]{1,0:T(8,128)(2,1)S(1)}, bf16[200,768]{1,0:T(8,128)(2,1)S(1)}, u32[]{:S(2)}, u32[]{:S(2)}) collective-permute-start(bf16[200,768]{1,0:T(8,128)(2,1)S(1)} %collective-permute-done.6), channel_id=1, source_target_pairs={{0,64},{64,0},{128,192},{192,128},{1,65},{65,1},{129,193},{193,129... | collective-permute-start | bytes 921608 | tf_op jit(solution)/shard_map/ppermute | solution.py:80
  52.2 7.7 %collective-permute-start.10 = (bf16[200,768]{1,0:T(8,128)(2,1)S(1)}, bf16[200,768]{1,0:T(8,128)(2,1)S(1)}, u32[]{:S(2)}, u32[]{:S(2)}) collective-permute-start(bf16[200,768]{1,0:T(8,128)(2,1)S(1)} %collective-permute-done.6), channel_id=1, source_target_pairs={{0,56},{1,57},{2,58},{3,59},{4,60},{5,61},{6,62},{7,63},{8,0},{9,1... | collective-permute-start | bytes 921608 | tf_op jit(solution)/shard_map/ppermute | solution.py:79
  54.2 11.3 %collective-permute-start.9 = (bf16[200,832]{1,0:T(8,128)(2,1)S(1)}, bf16[200,832]{1,0:T(8,128)(2,1)S(1)}, u32[]{:S(2)}, u32[]{:S(2)}) collective-permute-start(bf16[200,832]{1,0:T(8,128)(2,1)S(1)} %collective-permute-done.8), channel_id=1, source_target_pairs={{0,64},{64,0},{128,192},{192,128},{1,65},{65,1},{129,193},{193,129... | collective-permute-start | bytes 998408 | tf_op jit(solution)/shard_map/ppermute | solution.py:80
  57.9 7.5 %collective-permute-start.12 = (bf16[200,832]{1,0:T(8,128)(2,1)S(1)}, bf16[200,832]{1,0:T(8,128)(2,1)S(1)}, u32[]{:S(2)}, u32[]{:S(2)}) collective-permute-start(bf16[200,832]{1,0:T(8,128)(2,1)S(1)} %collective-permute-done.8), channel_id=1, source_target_pairs={{0,56},{1,57},{2,58},{3,59},{4,60},{5,61},{6,62},{7,63},{8,0},{9,1... | collective-permute-start | bytes 998408 | tf_op jit(solution)/shard_map/ppermute | solution.py:79
  59.9 10.7 %collective-permute-start.11 = (bf16[200,768]{1,0:T(8,128)(2,1)S(1)}, bf16[200,768]{1,0:T(8,128)(2,1)S(1)}, u32[]{:S(2)}, u32[]{:S(2)}) collective-permute-start(bf16[200,768]{1,0:T(8,128)(2,1)S(1)} %collective-permute-done.10), channel_id=1, source_target_pairs={{0,64},{64,0},{128,192},{192,128},{1,65},{65,1},{129,193},{193,129... | collective-permute-start | bytes 921608 | tf_op jit(solution)/shard_map/ppermute | solution.py:80
  60.5 8.1 %collective-permute-start.14 = (bf16[200,768]{1,0:T(8,128)(2,1)S(1)}, bf16[200,768]{1,0:T(8,128)(2,1)S(1)}, u32[]{:S(2)}, u32[]{:S(2)}) collective-permute-start(bf16[200,768]{1,0:T(8,128)(2,1)S(1)} %collective-permute-done.10), channel_id=1, source_target_pairs={{0,56},{1,57},{2,58},{3,59},{4,60},{5,61},{6,62},{7,63},{8,0},{9,1... | collective-permute-start | bytes 921608 | tf_op jit(solution)/shard_map/ppermute | solution.py:79
  65.3 12.1 %collective-permute-start.13 = (bf16[200,832]{1,0:T(8,128)(2,1)S(1)}, bf16[200,832]{1,0:T(8,128)(2,1)S(1)}, u32[]{:S(2)}, u32[]{:S(2)}) collective-permute-start(bf16[200,832]{1,0:T(8,128)(2,1)S(1)} %collective-permute-done.12), channel_id=1, source_target_pairs={{0,64},{64,0},{128,192},{192,128},{1,65},{65,1},{129,193},{193,129... | collective-permute-start | bytes 998408 | tf_op jit(solution)/shard_map/ppermute | solution.py:80
  65.5 7.5 %collective-permute-start.16 = (bf16[200,832]{1,0:T(8,128)(2,1)S(1)}, bf16[200,832]{1,0:T(8,128)(2,1)S(1)}, u32[]{:S(2)}, u32[]{:S(2)}) collective-permute-start(bf16[200,832]{1,0:T(8,128)(2,1)S(1)} %collective-permute-done.12), channel_id=1, source_target_pairs={{0,56},{1,57},{2,58},{3,59},{4,60},{5,61},{6,62},{7,63},{8,0},{9,1... | collective-permute-start | bytes 998408 | tf_op jit(solution)/shard_map/ppermute | solution.py:79
  68.6 11.6 %collective-permute-start.15 = (bf16[200,768]{1,0:T(8,128)(2,1)S(1)}, bf16[200,768]{1,0:T(8,128)(2,1)S(1)}, u32[]{:S(2)}, u32[]{:S(2)}) collective-permute-start(bf16[200,768]{1,0:T(8,128)(2,1)S(1)} %collective-permute-done.14), channel_id=1, source_target_pairs={{0,64},{64,0},{128,192},{192,128},{1,65},{65,1},{129,193},{193,129... | collective-permute-start | bytes 921608 | tf_op jit(solution)/shard_map/ppermute | solution.py:80
  69.9 9.0 %collective-permute-start.18 = (bf16[200,768]{1,0:T(8,128)(2,1)S(1)}, bf16[200,768]{1,0:T(8,128)(2,1)S(1)}, u32[]{:S(2)}, u32[]{:S(2)}) collective-permute-start(bf16[200,768]{1,0:T(8,128)(2,1)S(1)} %collective-permute-done.14), channel_id=1, source_target_pairs={{0,56},{1,57},{2,58},{3,59},{4,60},{5,61},{6,62},{7,63},{8,0},{9,1... | collective-permute-start | bytes 921608 | tf_op jit(solution)/shard_map/ppermute | solution.py:89
  73.0 13.2 %collective-permute-start.17 = (bf16[200,832]{1,0:T(8,128)(2,1)S(1)}, bf16[200,832]{1,0:T(8,128)(2,1)S(1)}, u32[]{:S(2)}, u32[]{:S(2)}) collective-permute-start(bf16[200,832]{1,0:T(8,128)(2,1)S(1)} %collective-permute-done.16), channel_id=1, source_target_pairs={{0,64},{64,0},{128,192},{192,128},{1,65},{65,1},{129,193},{193,129... | collective-permute-start | bytes 998408 | tf_op jit(solution)/shard_map/ppermute | solution.py:80
  75.5 9.3 %collective-permute-start.20 = (bf16[200,832]{1,0:T(8,128)(2,1)S(1)}, bf16[200,832]{1,0:T(8,128)(2,1)S(1)}, u32[]{:S(2)}, u32[]{:S(2)}) collective-permute-start(bf16[200,832]{1,0:T(8,128)(2,1)S(1)} %collective-permute-done.16), channel_id=1, source_target_pairs={{64,72},{65,73},{66,74},{67,75},{68,76},{69,77},{70,78},{71,79},{7... | collective-permute-start | bytes 998408 | tf_op jit(solution)/shard_map/ppermute | solution.py:90
  78.9 8.0 %collective-permute-start.19 = (bf16[200,768]{1,0:T(8,128)(2,1)S(1)}, bf16[200,768]{1,0:T(8,128)(2,1)S(1)}, u32[]{:S(2)}, u32[]{:S(2)}) collective-permute-start(bf16[200,768]{1,0:T(8,128)(2,1)S(1)} %collective-permute-done.18), channel_id=1, source_target_pairs={{0,64},{128,192},{1,65},{129,193},{2,66},{130,194},{3,67},{131,195... | collective-permute-start | bytes 921608 | tf_op jit(solution)/shard_map/ppermute | solution.py:91
  84.8 2.9 %collective-permute-start.21 = (bf16[200,832]{1,0:T(8,128)(2,1)S(1)}, bf16[200,832]{1,0:T(8,128)(2,1)S(1)}, u32[]{:S(2)}, u32[]{:S(2)}) collective-permute-start(bf16[200,832]{1,0:T(8,128)(2,1)S(1)} %collective-permute-done.20), channel_id=1, source_target_pairs={{64,0},{192,128},{65,1},{193,129},{66,2},{194,130},{67,3},{195,131... | collective-permute-start | bytes 998408 | tf_op jit(solution)/shard_map/ppermute | solution.py:92

commit v9 on v8

--- a/solution.py
+++ b/solution.py
@@ -54,15 +54,29 @@
     b50 = jnp.where(yh == 0, jnp.concatenate([blk, other]), jnp.concatenate([other, blk]))
 
     zb = NX * NYH * rows
-    rel = [b50]
-    for k in range(1, NX):
-        rel.append(
-            lax.ppermute(
-                b50,
-                "shard",
-                [(sidx(zxy(s)[0], zxy(s)[1] + k, zxy(s)[2]), s) for s in range(NZ * NX * NYH)],
-            )
-        )
+
+    def xnear(g, s):
+        zz, xx, yy = zxy(s)
+        return g, sidx(zz, xx - 1, yy) if g % 2 == 0 else sidx(zz, xx + 1, yy)
+
+    def xfar(g, s):
+        zz, xx, yy = zxy(s)
+        return g, sidx(zz, xx + 2, yy)
+
+    cutx = (d // 2) // 128 * 128
+    near = lax.ppermute(b50, ("grp", "shard"), both(xnear))
+    far = lax.ppermute(
+        lax.dynamic_slice_in_dim(b50, core * cutx, d - cutx, 1), ("grp", "shard"), both(xfar)
+    )
+    near_m = lax.ppermute(near, "grp", swap)
+    far_m = lax.ppermute(far, "grp", swap)
+    c0 = core == 0
+    xp2 = jnp.where(
+        c0,
+        jnp.concatenate([far[:, :cutx], far_m], 1),
+        jnp.concatenate([far_m[:, :cutx], far], 1),
+    )
+    rel = [b50, jnp.where(c0, near, near_m), xp2, jnp.where(c0, near_m, near)]
     xi = (jnp.arange(NX) - x) % NX
     b200 = jnp.take(jnp.stack(rel), xi, axis=0).reshape(zb, d)
 
@@ -121,7 +135,7 @@
 
 
 def solution(mesh):
-    assert mesh.shape["shard"] == NZ * NX * NYH and mesh.shape["grp"] == NG
+    assert mesh.shape["shard"] == NZ * NX * NYH and mesh.shape["grp"] == NG and NX == 4
     in_specs = (
         P("grp", "shard", None),
         P("shard", None),

time: 88.8 us -> 88.7 us (level)
    ppermute x6, starting transfers between devices: 12.2 us -> 7.45 us  [gather_copy(): mate = [lax.ppermute(c, 'grp', swap) for c in cur]]
    ppermute x3 -> x4, starting transfers between devices: 3.24 us -> 5.97 us  [the longest x1 3.71 us: gather_copy(): far_m = lax.ppermute(far, 'grp', swap)]
    ppermute x6, starting transfers between devices: 1.5 us -> 3.62 us  [gather_copy(): cur = [lax.ppermute(c, ('grp', 'shard'), zpairs) for c in cur]]
    ppermute x3 -> x4, waiting for transfers between devices: 6.65 us -> 5.2 us  [the longest x1 3.85 us: gather_copy(): lax.ppermute(lax.dynamic_slice_in_dim(b50, core * cutx, d - cutx, 1), ('g...]
    ppermute x6, waiting for transfers between devices: 12.5 us -> 13.6 us  [gather_copy(): cur = [lax.ppermute(c, ('grp', 'shard'), zpairs) for c in cur]]
  transfers between devices with their start and end apart: 24 -> 25, of which waited for: 11 -> 12; matrix products, arithmetic and copies ran while one was open for 25% -> 25% of each run, Pallas kernels for 0% -> 0%
where the time goes in v9:
time: 88.7 us; the launch traced here: 88.5 us
  waiting for transfers between devices  31.1 us (35%)
  starting transfers between devices  26.8 us (30%)
  local copies, waits for them, and re-layouts  16.1 us (18%)
  other arithmetic  7.32 us (8%)
  matrix products  6.11 us (7%)
  between operations  1.13 us (1%)
    ppermute x6, waiting for transfers between devices, gather_copy(): cur = [lax.ppermute(c, ('grp', 'shard'), zpairs) for c in cur]  13.6 us
    ppermute x6, starting transfers between devices, gather_copy(): mate = [lax.ppermute(c, 'grp', swap) for c in cur]  7.45 us
    ppermute x1, waiting for transfers between devices, butterfly_sum(): far = lax.ppermute(v, 'grp', [(i, i ^ 2) for i in range(NG)])  5.52 us
    dynamic_update_slice x6, local copies, waits for them, and re-layouts, gather_copy(): out = lax.dynamic_update_slice(out, m, (mate_at, col))  4.53 us
    dynamic_update_slice x6, local copies, waits for them, and re-layouts, gather_copy(): out = lax.dynamic_update_slice(out, c, (mine_at, col))  4.5 us
    ppermute x1, waiting for transfers between devices, gather_copy(): lax.ppermute(lax.dynamic_slice_in_dim(b50, core * cutx, d - cutx, 1), ('g...  3.85 us
    ppermute x1, starting transfers between devices, gather_copy(): far_m = lax.ppermute(far, 'grp', swap)  3.71 us
    ppermute x1, waiting for transfers between devices, gather_copy(): lax.ppermute(blk, ('grp', 'shard'), both(lambda g, s: (g ^ 2, s ^ 1)))  3.66 us
  transfers between devices with their start and end apart: 25, of which 12 were waited for; matrix products, arithmetic and copies ran while one was open for 25% of the time, Pallas kernels for 0%

profile of v9, /device:TPU:1, one launch (start us, length us, event | category | flops | bytes accessed | tf_op | source)
XLA Modules:
  0.0 88.5 jit_solution(3301367984648533837)
XLA Ops:
  0.6 1.1 %bitcast_subtract_fusion = f32[25,1600]{1,0:T(8,128)S(1)} fusion(f32[25,1600]{1,0:T(8,128)} %param.10, f32[1,25,1600]{2,0,1:T(1,128)} %param.9), kind=kLoop, calls=%fused_computation.11 | loop fusion | flops 40000 | bytes 480000 | tf_op jit(solution)/shard_map/sub | solution.py:130
  1.7 3.3 %collective-permute-start = (f32[25,1600]{1,0:T(8,128)S(1)}, f32[25,1600]{1,0:T(8,128)}, u32[]{:S(2)}, u32[]{:S(2)}) collective-permute-start(f32[25,1600]{1,0:T(8,128)S(1)} %bitcast_subtract_fusion), channel_id=1, source_target_pairs={{0,64},{64,0},{128,192},{192,128},{1,65},{65,1},{129,193},{193,129... | collective-permute-start | bytes 480008 | tf_op jit(solution)/shard_map/ppermute | solution.py:37
  5.0 1.9 %dot_general.12 = f32[4,100,1600]{2,1,0:T(8,128)S(1)} reshape(f32[1,400,1600]{2,1,0:T(8,128)} %param.12) | data formatting | bytes 5120000 | tf_op jit(solution)/shard_map/dot_general | solution.py:116
  6.9 0.1 compare_and_fusion
  7.0 3.3 %fusion = f32[4,100,64]{1,2,0:T(8,128)S(1)} fusion(f32[4,100,1600]{2,1,0:T(8,128)S(1)} %dot_general.12, f32[1600,64]{0,1:T(8,128)S(1)} %copy-done), kind=kOutput, calls=%fused_computation.7 | convolution fusion | flops 491520000 | bytes 3072000 | tf_op jit(solution)/shard_map/dot_general | solution.py:116
  10.3 0.6 gather_fusion.2
  11.0 0.1 compare_and_fusion.1
  11.1 1.0 %add.138 = f32[25,1600]{1,0:T(8,128)S(1)} add(f32[25,1600]{1,0:T(8,128)S(1)} %bitcast_subtract_fusion, f32[25,1600]{1,0:T(8,128)} %collective-permute-done) | non-fusion elementwise | flops 40000 | bytes 480000 | tf_op jit(solution)/shard_map/add | solution.py:37
  12.1 0.1 collective-permute-start.1
  12.3 0.1 broadcast_in_dim.28
  12.4 0.6 gather_fusion.1
  13.0 5.5 %collective-permute-done.1 = f32[25,1600]{1,0:T(8,128)S(1)} collective-permute-done((f32[25,1600]{1,0:T(8,128)S(1)}, f32[25,1600]{1,0:T(8,128)S(1)}, u32[]{:S(2)}, u32[]{:S(2)}) %collective-permute-start.1) | collective-permute-done | bytes 160032 | tf_op jit(solution)/shard_map/ppermute | solution.py:38
  18.5 1.9 %fusion.12 = (bf16[25,1600]{1,0:T(8,128)(2,1)S(1)}, f32[25,1600]{1,0:T(8,128)}, f32[25,1600]{1,0:T(8,128)}) fusion(f32[25,1600]{1,0:T(8,128)} %param.10, f32[25,1600]{1,0:T(8,128)S(1)} %add.138, f32[25,1600]{1,0:T(8,128)S(1)} %collective-permute-done.1, f32[25,1600]{1,0:T(8,128)} %param.11), kind=kLoop, calls=%fused_computation.65 | loop fusion | flops 360000 | bytes 1040000 | tf_op jit(solution)/shard_map/convert_element_type | solution.py:133
  20.4 1.0 %collective-permute-start.2 = (bf16[25,1600]{1,0:T(8,128)(2,1)S(1)}, bf16[25,1600]{1,0:T(8,128)(2,1)S(1)}, u32[]{:S(2)}, u32[]{:S(2)}) collective-permute-start(bf16[25,1600]{1,0:T(8,128)(2,1)S(1)} %get-tuple-element.14), channel_id=1, source_target_pairs={{0,129},{1,128},{2,131},{3,130},{4,133},{5,132},{6,135},{7,134},{8... | collective-permute-start | bytes 240008 | tf_op jit(solution)/shard_map/ppermute | solution.py:53
  21.5 3.7 %collective-permute-done.2 = bf16[25,1600]{1,0:T(8,128)(2,1)S(1)} collective-permute-done((bf16[25,1600]{1,0:T(8,128)(2,1)S(1)}, bf16[25,1600]{1,0:T(8,128)(2,1)S(1)}, u32[]{:S(2)}, u32[]{:S(2)}) %collective-permute-start.2) | collective-permute-done | bytes 80032 | tf_op jit(solution)/shard_map/ppermute | solution.py:53
  25.2 0.1 collective-permute-start.3
  25.3 0.1 constant_dynamic-slice_fusion
  25.4 2.1 %collective-permute-start.5 = (bf16[50,832]{1,0:T(8,128)(2,1)S(1)}, bf16[50,832]{1,0:T(8,128)(2,1)S(1)}, u32[]{:S(2)}, u32[]{:S(2)}) collective-permute-start(bf16[50,832]{1,0:T(8,128)(2,1)S(1)} %constant_dynamic-slice_fusion), channel_id=1, source_target_pairs={{0,4},{1,5},{2,6},{3,7},{4,0},{5,1},{6,2},{7,3},{8,12},{9,13},{10,... | collective-permute-start | bytes 249608 | tf_op jit(solution)/shard_map/ppermute | solution.py:68
  27.6 3.8 %collective-permute-done.5 = bf16[50,832]{1,0:T(8,128)(2,1)S(1)} collective-permute-done((bf16[50,832]{1,0:T(8,128)(2,1)S(1)}, bf16[50,832]{1,0:T(8,128)(2,1)S(1)}, u32[]{:S(2)}, u32[]{:S(2)}) %collective-permute-start.5) | collective-permute-done | bytes 83232 | tf_op jit(solution)/shard_map/ppermute | solution.py:68
  31.5 3.7 %collective-permute-start.6 = (bf16[50,832]{1,0:T(8,128)(2,1)S(1)}, bf16[50,832]{1,0:T(8,128)(2,1)S(1)}, u32[]{:S(2)}, u32[]{:S(2)}) collective-permute-start(bf16[50,832]{1,0:T(8,128)(2,1)S(1)} %collective-permute-done.5), channel_id=1, source_target_pairs={{0,64},{64,0},{128,192},{192,128},{1,65},{65,1},{129,193},{193,129... | collective-permute-start | bytes 249608 | tf_op jit(solution)/shard_map/ppermute | solution.py:72
  35.2 0.1 collective-permute-start.4
  35.3 0.8 collective-permute-done.6
  36.2 0.5 collective-permute-done.4
  36.7 0.1 pad_maximum_fusion
  36.9 0.7 gather_fusion
  37.6 0.3 gather.10
  37.9 2.8 %broadcast_in_dim.26 = bf16[1600,1600]{1,0:T(8,128)(2,1)} broadcast(bf16[]{:T(256)} %constant.128.clone.1), dimensions={} | broadcast | bytes 5120002 | tf_op jit(solution)/shard_map/broadcast_in_dim | solution.py:90
  40.6 1.0 %constant_dynamic-update-slice_fusion.6 = (bf16[1600,1600]{1,0:T(8,128)(2,1)}, bf16[200,1600]{1,0:T(8,128)(2,1)S(1)}) fusion(bf16[1600,1600]{1,0:T(8,128)(2,1)} %broadcast_in_dim.26, s32[]{:T(128)S(6)} %select_n.207, bf16[200,1600]{1,0:T(8,128)(2,1)S(1)} %gather.10, pred[200]{0:T(512)(128)(4,1)S(1)} %broadcast_in_dim.28), kind=kLoop, calls=%fused_computation.44 | loop fusion | flops 320000 | bytes 1945804 | tf_op jit(solution)/shard_map/dynamic_update_slice | solution.py:90
  41.7 1.7 %collective-permute-start.7 = (bf16[200,768]{1,0:T(8,128)(2,1)S(1)}, bf16[200,768]{1,0:T(8,128)(2,1)S(1)}, u32[]{:S(2)}, u32[]{:S(2)}) collective-permute-start(bf16[200,768]{1,0:T(8,128)(2,1)S(1)} %slice.32), channel_id=1, source_target_pairs={{0,56},{1,57},{2,58},{3,59},{4,60},{5,61},{6,62},{7,63},{8,0},{9,1... | collective-permute-start | bytes 921608 | tf_op jit(solution)/shard_map/ppermute | solution.py:93
  43.4 0.1 collective-permute-start.24
  43.5 1.9 %collective-permute-start.9 = (bf16[200,832]{1,0:T(8,128)(2,1)S(1)}, bf16[200,832]{1,0:T(8,128)(2,1)S(1)}, u32[]{:S(2)}, u32[]{:S(2)}) collective-permute-start(bf16[200,832]{1,0:T(8,128)(2,1)S(1)} %slice.33), channel_id=1, source_target_pairs={{0,56},{1,57},{2,58},{3,59},{4,60},{5,61},{6,62},{7,63},{8,0},{9,1... | collective-permute-start | bytes 998408 | tf_op jit(solution)/shard_map/ppermute | solution.py:93
  45.4 0.9 fusion.13
  46.5 5.1 %collective-permute-done.7 = bf16[200,768]{1,0:T(8,128)(2,1)S(1)} collective-permute-done((bf16[200,768]{1,0:T(8,128)(2,1)S(1)}, bf16[200,768]{1,0:T(8,128)(2,1)S(1)}, u32[]{:S(2)}, u32[]{:S(2)}) %collective-permute-start.7) | collective-permute-done | bytes 307232 | tf_op jit(solution)/shard_map/ppermute | solution.py:93
  51.6 0.5 collective-permute-start.8
  52.1 2.0 %multiply_subtract_fusion = (f32[100,1600]{1,0:T(8,128)}, f32[100,1600]{1,0:T(8,128)}) fusion(f32[100,1600]{1,0:T(8,128)S(1)} %copy-done.1, f32[100,1600]{1,0:T(8,128)S(1)} %copy-done.2, f32[1600,64]{0,1:T(8,128)S(1)} %copy-done, f32[100,64]{0,1:T(8,128)S(1)} %fusion.13, f32[100,64]{0,1:T(8,128)S(1)} %collective-permute-done.24, ...), kind=kOutput, calls=%fused_computation.4 | convolution fusion | flops 123859200 | bytes 3188736 | tf_op jit(solution)/shard_map/dot_general | solution.py:127
  54.1 1.3 %collective-permute-done.9 = bf16[200,832]{1,0:T(8,128)(2,1)S(1)} collective-permute-done((bf16[200,832]{1,0:T(8,128)(2,1)S(1)}, bf16[200,832]{1,0:T(8,128)(2,1)S(1)}, u32[]{:S(2)}, u32[]{:S(2)}) %collective-permute-start.9) | collective-permute-done | bytes 332832 | tf_op jit(solution)/shard_map/ppermute | solution.py:93
  55.4 2.4 %collective-permute-start.10 = (bf16[200,832]{1,0:T(8,128)(2,1)S(1)}, bf16[200,832]{1,0:T(8,128)(2,1)S(1)}, u32[]{:S(2)}, u32[]{:S(2)}) collective-permute-start(bf16[200,832]{1,0:T(8,128)(2,1)S(1)} %collective-permute-done.9), channel_id=1, source_target_pairs={{0,64},{64,0},{128,192},{192,128},{1,65},{65,1},{129,193},{193,129... | collective-permute-start | bytes 998408 | tf_op jit(solution)/shard_map/ppermute | solution.py:94
  57.8 0.7 constant_dynamic-update-slice_fusion.5
  58.5 1.3 %collective-permute-done.11 = bf16[200,768]{1,0:T(8,128)(2,1)S(1)} collective-permute-done((bf16[200,768]{1,0:T(8,128)(2,1)S(1)}, bf16[200,768]{1,0:T(8,128)(2,1)S(1)}, u32[]{:S(2)}, u32[]{:S(2)}) %collective-permute-start.11) | collective-permute-done | bytes 307232 | tf_op jit(solution)/shard_map/ppermute | solution.py:93
  59.8 0.6 collective-permute-start.12
  60.4 0.7 constant_dynamic-update-slice_fusion.4
  61.2 0.8 constant_dynamic-update-slice_fusion.12
  61.9 3.3 %collective-permute-done.13 = bf16[200,832]{1,0:T(8,128)(2,1)S(1)} collective-permute-done((bf16[200,832]{1,0:T(8,128)(2,1)S(1)}, bf16[200,832]{1,0:T(8,128)(2,1)S(1)}, u32[]{:S(2)}, u32[]{:S(2)}) %collective-permute-start.13) | collective-permute-done | bytes 332832 | tf_op jit(solution)/shard_map/ppermute | solution.py:93
  65.3 0.1 collective-permute-start.14
  65.4 0.8 constant_dynamic-update-slice_fusion.11
  66.2 0.7 constant_dynamic-update-slice_fusion.3
  66.9 1.6 %collective-permute-done.15 = bf16[200,768]{1,0:T(8,128)(2,1)S(1)} collective-permute-done((bf16[200,768]{1,0:T(8,128)(2,1)S(1)}, bf16[200,768]{1,0:T(8,128)(2,1)S(1)}, u32[]{:S(2)}, u32[]{:S(2)}) %collective-permute-start.15) | collective-permute-done | bytes 307232 | tf_op jit(solution)/shard_map/ppermute | solution.py:93
  68.6 1.2 %collective-permute-start.16 = (bf16[200,768]{1,0:T(8,128)(2,1)S(1)}, bf16[200,768]{1,0:T(8,128)(2,1)S(1)}, u32[]{:S(2)}, u32[]{:S(2)}) collective-permute-start(bf16[200,768]{1,0:T(8,128)(2,1)S(1)} %collective-permute-done.15), channel_id=1, source_target_pairs={{0,64},{64,0},{128,192},{192,128},{1,65},{65,1},{129,193},{193,129... | collective-permute-start | bytes 921608 | tf_op jit(solution)/shard_map/ppermute | solution.py:94
  69.8 0.7 collective-permute-start.19
  70.5 0.7 constant_dynamic-update-slice_fusion.2
  71.2 0.8 constant_dynamic-update-slice_fusion.10
  72.0 0.9 collective-permute-done.17
  72.9 2.5 %collective-permute-start.18 = (bf16[200,832]{1,0:T(8,128)(2,1)S(1)}, bf16[200,832]{1,0:T(8,128)(2,1)S(1)}, u32[]{:S(2)}, u32[]{:S(2)}) collective-permute-start(bf16[200,832]{1,0:T(8,128)(2,1)S(1)} %collective-permute-done.17), channel_id=1, source_target_pairs={{0,64},{64,0},{128,192},{192,128},{1,65},{65,1},{129,193},{193,129... | collective-permute-start | bytes 998408 | tf_op jit(solution)/shard_map/ppermute | solution.py:94
  75.4 1.9 %collective-permute-start.21 = (bf16[200,832]{1,0:T(8,128)(2,1)S(1)}, bf16[200,832]{1,0:T(8,128)(2,1)S(1)}, u32[]{:S(2)}, u32[]{:S(2)}) collective-permute-start(bf16[200,832]{1,0:T(8,128)(2,1)S(1)} %collective-permute-done.17), channel_id=1, source_target_pairs={{64,72},{65,73},{66,74},{67,75},{68,76},{69,77},{70,78},{71,79},{7... | collective-permute-start | bytes 998408 | tf_op jit(solution)/shard_map/ppermute | solution.py:104
  77.3 0.8 constant_dynamic-update-slice_fusion.9
  78.1 0.7 constant_dynamic-update-slice_fusion.1
  78.8 1.3 %collective-permute-start.20 = (bf16[200,768]{1,0:T(8,128)(2,1)S(1)}, bf16[200,768]{1,0:T(8,128)(2,1)S(1)}, u32[]{:S(2)}, u32[]{:S(2)}) collective-permute-start(bf16[200,768]{1,0:T(8,128)(2,1)S(1)} %collective-permute-done.19), channel_id=1, source_target_pairs={{0,64},{128,192},{1,65},{129,193},{2,66},{130,194},{3,67},{131,195... | collective-permute-start | bytes 921608 | tf_op jit(solution)/shard_map/ppermute | solution.py:105
  80.1 0.7 constant_dynamic-update-slice_fusion
  80.9 0.8 constant_dynamic-update-slice_fusion.8
  81.6 3.1 %collective-permute-done.21 = bf16[200,832]{1,0:T(8,128)(2,1)S(1)} collective-permute-done((bf16[200,832]{1,0:T(8,128)(2,1)S(1)}, bf16[200,832]{1,0:T(8,128)(2,1)S(1)}, u32[]{:S(2)}, u32[]{:S(2)}) %collective-permute-start.21) | collective-permute-done | bytes 332832 | tf_op jit(solution)/shard_map/ppermute | solution.py:104
  84.7 1.3 %collective-permute-start.22 = (bf16[200,832]{1,0:T(8,128)(2,1)S(1)}, bf16[200,832]{1,0:T(8,128)(2,1)S(1)}, u32[]{:S(2)}, u32[]{:S(2)}) collective-permute-start(bf16[200,832]{1,0:T(8,128)(2,1)S(1)} %collective-permute-done.21), channel_id=1, source_target_pairs={{64,0},{192,128},{65,1},{193,129},{66,2},{194,130},{67,3},{195,131... | collective-permute-start | bytes 998408 | tf_op jit(solution)/shard_map/ppermute | solution.py:106
  86.1 0.8 constant_dynamic-update-slice_fusion.7
  86.8 0.8 select_dynamic-update-slice_fusion.1
  87.6 0.8 select_dynamic-update-slice_fusion
  (41 shorter events, 0.7 us)
Async XLA Ops:
  0.6 6.4 %copy-start = (f32[1600,64]{0,1:T(8,128)S(1)}, f32[1600,64]{0,1:T(8,128)}, u32[]{:S(2)}) copy-start(f32[1600,64]{0,1:T(8,128)} %param.15) | copy-start | bytes 1228804
  1.7 9.4 %collective-permute-start = (f32[25,1600]{1,0:T(8,128)S(1)}, f32[25,1600]{1,0:T(8,128)}, u32[]{:S(2)}, u32[]{:S(2)}) collective-permute-start(f32[25,1600]{1,0:T(8,128)S(1)} %bitcast_subtract_fusion), channel_id=1, source_target_pairs={{0,64},{64,0},{128,192},{192,128},{1,65},{65,1},{129,193},{193,129... | collective-permute-start | bytes 480008 | tf_op jit(solution)/shard_map/ppermute | solution.py:37
  10.9 10.5 %collective-permute-start.23 = (f32[2,100,64]{1,2,0:T(8,128)S(1)}, f32[2,100,64]{1,2,0:T(8,128)S(1)}, u32[]{:S(2)}, u32[]{:S(2)}) collective-permute-start(f32[2,100,64]{1,2,0:T(8,128)S(1)} %broadcast_select_fusion.1), channel_id=1, source_target_pairs={{0,64},{64,0},{128,192},{192,128},{1,65},{65,1},{129,193},{193,129... | collective-permute-start | bytes 153608 | tf_op jit(solution)/shard_map/ppermute | solution.py:122
  12.1 6.4 %collective-permute-start.1 = (f32[25,1600]{1,0:T(8,128)S(1)}, f32[25,1600]{1,0:T(8,128)S(1)}, u32[]{:S(2)}, u32[]{:S(2)}) collective-permute-start(f32[25,1600]{1,0:T(8,128)S(1)} %add.138), channel_id=1, source_target_pairs={{0,128},{64,192},{128,0},{192,64},{1,129},{65,193},{129,1},{193,65... | collective-permute-start | bytes 480008 | tf_op jit(solution)/shard_map/ppermute | solution.py:38
  20.4 4.8 %collective-permute-start.2 = (bf16[25,1600]{1,0:T(8,128)(2,1)S(1)}, bf16[25,1600]{1,0:T(8,128)(2,1)S(1)}, u32[]{:S(2)}, u32[]{:S(2)}) collective-permute-start(bf16[25,1600]{1,0:T(8,128)(2,1)S(1)} %get-tuple-element.14), channel_id=1, source_target_pairs={{0,129},{1,128},{2,131},{3,130},{4,133},{5,132},{6,135},{7,134},{8... | collective-permute-start | bytes 240008 | tf_op jit(solution)/shard_map/ppermute | solution.py:53
  25.2 9.9 %collective-permute-start.3 = (bf16[50,1600]{1,0:T(8,128)(2,1)S(1)}, bf16[50,1600]{1,0:T(8,128)(2,1)S(1)}, u32[]{:S(2)}, u32[]{:S(2)}) collective-permute-start(bf16[50,1600]{1,0:T(8,128)(2,1)S(1)} %maximum_select_fusion.1), channel_id=1, source_target_pairs={{0,6},{1,7},{2,0},{3,1},{4,2},{5,3},{6,4},{7,5},{8,14},{9,15},{10,... | collective-permute-start | bytes 480008 | tf_op jit(solution)/shard_map/ppermute | solution.py:67
  25.4 6.0 %collective-permute-start.5 = (bf16[50,832]{1,0:T(8,128)(2,1)S(1)}, bf16[50,832]{1,0:T(8,128)(2,1)S(1)}, u32[]{:S(2)}, u32[]{:S(2)}) collective-permute-start(bf16[50,832]{1,0:T(8,128)(2,1)S(1)} %constant_dynamic-slice_fusion), channel_id=1, source_target_pairs={{0,4},{1,5},{2,6},{3,7},{4,0},{5,1},{6,2},{7,3},{8,12},{9,13},{10,... | collective-permute-start | bytes 249608 | tf_op jit(solution)/shard_map/ppermute | solution.py:68
  31.5 4.7 %collective-permute-start.6 = (bf16[50,832]{1,0:T(8,128)(2,1)S(1)}, bf16[50,832]{1,0:T(8,128)(2,1)S(1)}, u32[]{:S(2)}, u32[]{:S(2)}) collective-permute-start(bf16[50,832]{1,0:T(8,128)(2,1)S(1)} %collective-permute-done.5), channel_id=1, source_target_pairs={{0,64},{64,0},{128,192},{192,128},{1,65},{65,1},{129,193},{193,129... | collective-permute-start | bytes 249608 | tf_op jit(solution)/shard_map/ppermute | solution.py:72
  35.2 1.5 %collective-permute-start.4 = (bf16[50,1600]{1,0:T(8,128)(2,1)S(1)}, bf16[50,1600]{1,0:T(8,128)(2,1)S(1)}, u32[]{:S(2)}, u32[]{:S(2)}) collective-permute-start(bf16[50,1600]{1,0:T(8,128)(2,1)S(1)} %collective-permute-done.3), channel_id=1, source_target_pairs={{0,64},{64,0},{128,192},{192,128},{1,65},{65,1},{129,193},{193,129... | collective-permute-start | bytes 480008 | tf_op jit(solution)/shard_map/ppermute | solution.py:71
  37.6 7.9 %copy-start.1 = (f32[100,1600]{1,0:T(8,128)S(1)}, f32[100,1600]{1,0:T(8,128)}, u32[]{:S(2)}) copy-start(f32[100,1600]{1,0:T(8,128)} %param.13) | copy-start | bytes 1920004
  37.9 14.3 %copy-start.2 = (f32[100,1600]{1,0:T(8,128)S(1)}, f32[100,1600]{1,0:T(8,128)}, u32[]{:S(2)}) copy-start(f32[100,1600]{1,0:T(8,128)} %param.14) | copy-start | bytes 1920004
  41.7 9.9 %collective-permute-start.7 = (bf16[200,768]{1,0:T(8,128)(2,1)S(1)}, bf16[200,768]{1,0:T(8,128)(2,1)S(1)}, u32[]{:S(2)}, u32[]{:S(2)}) collective-permute-start(bf16[200,768]{1,0:T(8,128)(2,1)S(1)} %slice.32), channel_id=1, source_target_pairs={{0,56},{1,57},{2,58},{3,59},{4,60},{5,61},{6,62},{7,63},{8,0},{9,1... | collective-permute-start | bytes 921608 | tf_op jit(solution)/shard_map/ppermute | solution.py:93
  43.4 8.7 %collective-permute-start.24 = (f32[100,64]{0,1:T(8,128)S(1)}, f32[100,64]{0,1:T(8,128)S(1)}, u32[]{:S(2)}, u32[]{:S(2)}) collective-permute-start(f32[100,64]{0,1:T(8,128)S(1)} %slice_bitcast_fusion.2), channel_id=1, source_target_pairs={{0,128},{64,192},{128,0},{192,64},{1,129},{65,193},{129,1},{193,65... | collective-permute-start | bytes 76808 | tf_op jit(solution)/shard_map/ppermute | solution.py:125
  43.5 11.9 %collective-permute-start.9 = (bf16[200,832]{1,0:T(8,128)(2,1)S(1)}, bf16[200,832]{1,0:T(8,128)(2,1)S(1)}, u32[]{:S(2)}, u32[]{:S(2)}) collective-permute-start(bf16[200,832]{1,0:T(8,128)(2,1)S(1)} %slice.33), channel_id=1, source_target_pairs={{0,56},{1,57},{2,58},{3,59},{4,60},{5,61},{6,62},{7,63},{8,0},{9,1... | collective-permute-start | bytes 998408 | tf_op jit(solution)/shard_map/ppermute | solution.py:93
  51.6 8.8 %collective-permute-start.8 = (bf16[200,768]{1,0:T(8,128)(2,1)S(1)}, bf16[200,768]{1,0:T(8,128)(2,1)S(1)}, u32[]{:S(2)}, u32[]{:S(2)}) collective-permute-start(bf16[200,768]{1,0:T(8,128)(2,1)S(1)} %collective-permute-done.7), channel_id=1, source_target_pairs={{0,64},{64,0},{128,192},{192,128},{1,65},{65,1},{129,193},{193,129... | collective-permute-start | bytes 921608 | tf_op jit(solution)/shard_map/ppermute | solution.py:94
  52.1 7.7 %collective-permute-start.11 = (bf16[200,768]{1,0:T(8,128)(2,1)S(1)}, bf16[200,768]{1,0:T(8,128)(2,1)S(1)}, u32[]{:S(2)}, u32[]{:S(2)}) collective-permute-start(bf16[200,768]{1,0:T(8,128)(2,1)S(1)} %collective-permute-done.7), channel_id=1, source_target_pairs={{0,56},{1,57},{2,58},{3,59},{4,60},{5,61},{6,62},{7,63},{8,0},{9,1... | collective-permute-start | bytes 921608 | tf_op jit(solution)/shard_map/ppermute | solution.py:93
  55.4 10.0 %collective-permute-start.10 = (bf16[200,832]{1,0:T(8,128)(2,1)S(1)}, bf16[200,832]{1,0:T(8,128)(2,1)S(1)}, u32[]{:S(2)}, u32[]{:S(2)}) collective-permute-start(bf16[200,832]{1,0:T(8,128)(2,1)S(1)} %collective-permute-done.9), channel_id=1, source_target_pairs={{0,64},{64,0},{128,192},{192,128},{1,65},{65,1},{129,193},{193,129... | collective-permute-start | bytes 998408 | tf_op jit(solution)/shard_map/ppermute | solution.py:94
  57.8 7.5 %collective-permute-start.13 = (bf16[200,832]{1,0:T(8,128)(2,1)S(1)}, bf16[200,832]{1,0:T(8,128)(2,1)S(1)}, u32[]{:S(2)}, u32[]{:S(2)}) collective-permute-start(bf16[200,832]{1,0:T(8,128)(2,1)S(1)} %collective-permute-done.9), channel_id=1, source_target_pairs={{0,56},{1,57},{2,58},{3,59},{4,60},{5,61},{6,62},{7,63},{8,0},{9,1... | collective-permute-start | bytes 998408 | tf_op jit(solution)/shard_map/ppermute | solution.py:93
  59.8 10.7 %collective-permute-start.12 = (bf16[200,768]{1,0:T(8,128)(2,1)S(1)}, bf16[200,768]{1,0:T(8,128)(2,1)S(1)}, u32[]{:S(2)}, u32[]{:S(2)}) collective-permute-start(bf16[200,768]{1,0:T(8,128)(2,1)S(1)} %collective-permute-done.11), channel_id=1, source_target_pairs={{0,64},{64,0},{128,192},{192,128},{1,65},{65,1},{129,193},{193,129... | collective-permute-start | bytes 921608 | tf_op jit(solution)/shard_map/ppermute | solution.py:94
  60.4 8.1 %collective-permute-start.15 = (bf16[200,768]{1,0:T(8,128)(2,1)S(1)}, bf16[200,768]{1,0:T(8,128)(2,1)S(1)}, u32[]{:S(2)}, u32[]{:S(2)}) collective-permute-start(bf16[200,768]{1,0:T(8,128)(2,1)S(1)} %collective-permute-done.11), channel_id=1, source_target_pairs={{0,56},{1,57},{2,58},{3,59},{4,60},{5,61},{6,62},{7,63},{8,0},{9,1... | collective-permute-start | bytes 921608 | tf_op jit(solution)/shard_map/ppermute | solution.py:93
  65.3 12.1 %collective-permute-start.14 = (bf16[200,832]{1,0:T(8,128)(2,1)S(1)}, bf16[200,832]{1,0:T(8,128)(2,1)S(1)}, u32[]{:S(2)}, u32[]{:S(2)}) collective-permute-start(bf16[200,832]{1,0:T(8,128)(2,1)S(1)} %collective-permute-done.13), channel_id=1, source_target_pairs={{0,64},{64,0},{128,192},{192,128},{1,65},{65,1},{129,193},{193,129... | collective-permute-start | bytes 998408 | tf_op jit(solution)/shard_map/ppermute | solution.py:94
  65.4 7.5 %collective-permute-start.17 = (bf16[200,832]{1,0:T(8,128)(2,1)S(1)}, bf16[200,832]{1,0:T(8,128)(2,1)S(1)}, u32[]{:S(2)}, u32[]{:S(2)}) collective-permute-start(bf16[200,832]{1,0:T(8,128)(2,1)S(1)} %collective-permute-done.13), channel_id=1, source_target_pairs={{0,56},{1,57},{2,58},{3,59},{4,60},{5,61},{6,62},{7,63},{8,0},{9,1... | collective-permute-start | bytes 998408 | tf_op jit(solution)/shard_map/ppermute | solution.py:93
  68.6 11.6 %collective-permute-start.16 = (bf16[200,768]{1,0:T(8,128)(2,1)S(1)}, bf16[200,768]{1,0:T(8,128)(2,1)S(1)}, u32[]{:S(2)}, u32[]{:S(2)}) collective-permute-start(bf16[200,768]{1,0:T(8,128)(2,1)S(1)} %collective-permute-done.15), channel_id=1, source_target_pairs={{0,64},{64,0},{128,192},{192,128},{1,65},{65,1},{129,193},{193,129... | collective-permute-start | bytes 921608 | tf_op jit(solution)/shard_map/ppermute | solution.py:94
  69.8 9.0 %collective-permute-start.19 = (bf16[200,768]{1,0:T(8,128)(2,1)S(1)}, bf16[200,768]{1,0:T(8,128)(2,1)S(1)}, u32[]{:S(2)}, u32[]{:S(2)}) collective-permute-start(bf16[200,768]{1,0:T(8,128)(2,1)S(1)} %collective-permute-done.15), channel_id=1, source_target_pairs={{0,56},{1,57},{2,58},{3,59},{4,60},{5,61},{6,62},{7,63},{8,0},{9,1... | collective-permute-start | bytes 921608 | tf_op jit(solution)/shard_map/ppermute | solution.py:103
  72.9 13.2 %collective-permute-start.18 = (bf16[200,832]{1,0:T(8,128)(2,1)S(1)}, bf16[200,832]{1,0:T(8,128)(2,1)S(1)}, u32[]{:S(2)}, u32[]{:S(2)}) collective-permute-start(bf16[200,832]{1,0:T(8,128)(2,1)S(1)} %collective-permute-done.17), channel_id=1, source_target_pairs={{0,64},{64,0},{128,192},{192,128},{1,65},{65,1},{129,193},{193,129... | collective-permute-start | bytes 998408 | tf_op jit(solution)/shard_map/ppermute | solution.py:94
  75.4 9.3 %collective-permute-start.21 = (bf16[200,832]{1,0:T(8,128)(2,1)S(1)}, bf16[200,832]{1,0:T(8,128)(2,1)S(1)}, u32[]{:S(2)}, u32[]{:S(2)}) collective-permute-start(bf16[200,832]{1,0:T(8,128)(2,1)S(1)} %collective-permute-done.17), channel_id=1, source_target_pairs={{64,72},{65,73},{66,74},{67,75},{68,76},{69,77},{70,78},{71,79},{7... | collective-permute-start | bytes 998408 | tf_op jit(solution)/shard_map/ppermute | solution.py:104
  78.8 8.0 %collective-permute-start.20 = (bf16[200,768]{1,0:T(8,128)(2,1)S(1)}, bf16[200,768]{1,0:T(8,128)(2,1)S(1)}, u32[]{:S(2)}, u32[]{:S(2)}) collective-permute-start(bf16[200,768]{1,0:T(8,128)(2,1)S(1)} %collective-permute-done.19), channel_id=1, source_target_pairs={{0,64},{128,192},{1,65},{129,193},{2,66},{130,194},{3,67},{131,195... | collective-permute-start | bytes 921608 | tf_op jit(solution)/shard_map/ppermute | solution.py:105
  84.7 2.9 %collective-permute-start.22 = (bf16[200,832]{1,0:T(8,128)(2,1)S(1)}, bf16[200,832]{1,0:T(8,128)(2,1)S(1)}, u32[]{:S(2)}, u32[]{:S(2)}) collective-permute-start(bf16[200,832]{1,0:T(8,128)(2,1)S(1)} %collective-permute-done.21), channel_id=1, source_target_pairs={{64,0},{192,128},{65,1},{193,129},{66,2},{194,130},{67,3},{195,131... | collective-permute-start | bytes 998408 | tf_op jit(solution)/shard_map/ppermute | solution.py:106

commit v10 on v9

--- a/solution.py
+++ b/solution.py
@@ -35,8 +35,18 @@
 
 def butterfly_sum(v):
     v = v + lax.ppermute(v, "grp", [(i, i ^ 1) for i in range(NG)])
-    far = lax.ppermute(v, "grp", [(i, i ^ 2) for i in range(NG)])
-    return v + far
+    d = v.shape[1]
+    cut = (d // 2) // 128 * 128
+    core = lax.axis_index("grp") % 2
+    mine = lax.dynamic_slice_in_dim(v, core * cut, d - cut, 1)
+    far = lax.ppermute(mine, "grp", [(i, i ^ 2) for i in range(NG)])
+    part = mine + far
+    other = lax.ppermute(part, "grp", [(i, i ^ 1) for i in range(NG)])
+    return jnp.where(
+        core == 0,
+        jnp.concatenate([part[:, :cut], other], 1),
+        jnp.concatenate([other[:, :cut], part], 1),
+    )
 
 
 def gather_copy(blk):

time: 88.7 us -> 89.9 us (1.014)
    ppermute x1 -> x2, starting transfers between devices: 0.09 us -> 1.51 us  [the longest x1 1.42 us: butterfly_sum(): other = lax.ppermute(part, 'grp', [(i, i ^ 1) for i in range(NG)])]
    ppermute x1, starting transfers between devices: 3.71 us -> 2.47 us  [gather_copy(): far_m = lax.ppermute(far, 'grp', swap)]
    ppermute x1 -> x2, waiting for transfers between devices: 5.52 us -> 5.15 us  [the longest x1 4.2 us: butterfly_sum(): far = lax.ppermute(mine, 'grp', [(i, i ^ 2) for i in range(NG)])]
  transfers between devices with their start and end apart: 25 -> 26, of which waited for: 12 -> 13; matrix products, arithmetic and copies ran while one was open for 25% -> 25% of each run, Pallas kernels for 0% -> 0%
where the time goes in v10:
time: 89.9 us; the launch traced here: 89.6 us
  waiting for transfers between devices  31.4 us (35%)
  starting transfers between devices  26.9 us (30%)
  local copies, waits for them, and re-layouts  16.1 us (18%)
  other arithmetic  8.06 us (9%)
  matrix products  6.1 us (7%)
  between operations  1.11 us (1%)
    ppermute x6, waiting for transfers between devices, gather_copy(): cur = [lax.ppermute(c, ('grp', 'shard'), zpairs) for c in cur]  13.6 us
    ppermute x6, starting transfers between devices, gather_copy(): mate = [lax.ppermute(c, 'grp', swap) for c in cur]  7.46 us
    dynamic_update_slice x6, local copies, waits for them, and re-layouts, gather_copy(): out = lax.dynamic_update_slice(out, m, (mate_at, col))  4.53 us
    dynamic_update_slice x6, local copies, waits for them, and re-layouts, gather_copy(): out = lax.dynamic_update_slice(out, c, (mine_at, col))  4.5 us
    ppermute x1, waiting for transfers between devices, gather_copy(): lax.ppermute(blk, ('grp', 'shard'), both(lambda g, s: (g ^ 2, s ^ 1)))  4.27 us
    ppermute x1, waiting for transfers between devices, butterfly_sum(): far = lax.ppermute(mine, 'grp', [(i, i ^ 2) for i in range(NG)])  4.2 us
    ppermute x1, waiting for transfers between devices, gather_copy(): lax.ppermute(lax.dynamic_slice_in_dim(b50, core * cutx, d - cutx, 1), ('g...  3.85 us
    ppermute x6, starting transfers between devices, gather_copy(): cur = [lax.ppermute(c, ('grp', 'shard'), zpairs) for c in cur]  3.62 us
  transfers between devices with their start and end apart: 26, of which 13 were waited for; matrix products, arithmetic and copies ran while one was open for 25% of the time, Pallas kernels for 0%

profile of v10, /device:TPU:1, one launch (start us, length us, event | category | flops | bytes accessed | tf_op | source)
XLA Modules:
  0.0 89.6 jit_solution(13279586497704596999)
XLA Ops:
  0.6 1.8 %bitcast_subtract_fusion = f32[25,1600]{1,0:T(8,128)} fusion(f32[25,1600]{1,0:T(8,128)} %param.10, f32[1,25,1600]{2,0,1:T(1,128)} %param.9), kind=kLoop, calls=%fused_computation.13 | loop fusion | flops 40000 | bytes 480000 | tf_op jit(solution)/shard_map/sub | solution.py:140
  2.4 3.2 %collective-permute-start = (f32[25,1600]{1,0:T(8,128)}, f32[25,1600]{1,0:T(8,128)}, u32[]{:S(2)}, u32[]{:S(2)}) collective-permute-start(f32[25,1600]{1,0:T(8,128)} %bitcast_subtract_fusion), channel_id=1, source_target_pairs={{0,64},{64,0},{128,192},{192,128},{1,65},{65,1},{129,193},{193,129... | collective-permute-start | bytes 480008 | tf_op jit(solution)/shard_map/ppermute | solution.py:37
  5.6 1.9 %dot_general.12 = f32[4,100,1600]{2,1,0:T(8,128)S(1)} reshape(f32[1,400,1600]{2,1,0:T(8,128)} %param.12) | data formatting | bytes 5120000 | tf_op jit(solution)/shard_map/dot_general | solution.py:126
  7.5 0.1 compare_and_fusion
  7.6 3.3 %fusion = f32[4,100,64]{1,2,0:T(8,128)S(1)} fusion(f32[4,100,1600]{2,1,0:T(8,128)S(1)} %dot_general.12, f32[1600,64]{0,1:T(8,128)S(1)} %copy-done), kind=kOutput, calls=%fused_computation.7 | convolution fusion | flops 491520000 | bytes 3072000 | tf_op jit(solution)/shard_map/dot_general | solution.py:126
  10.9 0.6 gather_fusion.2
  11.8 0.1 broadcast_in_dim.28
  11.9 0.6 gather_fusion.1
  12.5 1.1 %dynamic-slice_add_fusion = f32[25,832]{1,0:T(8,128)S(1)} fusion(f32[25,1600]{1,0:T(8,128)} %collective-permute-done, s32[]{:T(128)S(6)} %select_n.200, f32[25,1600]{1,0:T(8,128)} %bitcast_subtract_fusion), kind=kLoop, calls=%fused_computation.21 | loop fusion | flops 20800 | bytes 249604 | tf_op jit(solution)/shard_map/add | solution.py:37
  13.6 0.1 collective-permute-start.1
  13.7 4.2 %collective-permute-done.1 = f32[25,832]{1,0:T(8,128)S(1)} collective-permute-done((f32[25,832]{1,0:T(8,128)S(1)}, f32[25,832]{1,0:T(8,128)S(1)}, u32[]{:S(2)}, u32[]{:S(2)}) %collective-permute-start.1) | collective-permute-done | bytes 83232 | tf_op jit(solution)/shard_map/ppermute | solution.py:42
  17.9 1.4 %collective-permute-start.2 = (f32[25,832]{1,0:T(8,128)S(1)}, f32[25,832]{1,0:T(8,128)S(1)}, u32[]{:S(2)}, u32[]{:S(2)}) collective-permute-start(f32[25,832]{1,0:T(8,128)S(1)} %add.143), channel_id=1, source_target_pairs={{0,64},{64,0},{128,192},{192,128},{1,65},{65,1},{129,193},{193,129... | collective-permute-start | bytes 249608 | tf_op jit(solution)/shard_map/ppermute | solution.py:44
  19.4 0.9 %collective-permute-done.2 = f32[25,832]{1,0:T(8,128)S(1)} collective-permute-done((f32[25,832]{1,0:T(8,128)S(1)}, f32[25,832]{1,0:T(8,128)S(1)}, u32[]{:S(2)}, u32[]{:S(2)}) %collective-permute-start.2) | collective-permute-done | bytes 83232 | tf_op jit(solution)/shard_map/ppermute | solution.py:44
  20.3 1.8 %fusion.13 = (bf16[25,1600]{1,0:T(8,128)(2,1)S(1)}, f32[25,1600]{1,0:T(8,128)}, f32[25,1600]{1,0:T(8,128)}) fusion(f32[25,1600]{1,0:T(8,128)S(1)} %copy-done.2, f32[25,832]{1,0:T(8,128)S(1)} %add.143, f32[25,768]{1,0:T(8,128)S(1)} %slice.39, f32[25,832]{1,0:T(8,128)S(1)} %collective-permute-done.2, f32[25,768]{1,0:T(8,128)S(1)} %slice.38, pred[]{:T(512)S(6)} %eq.23, ...), kind=kLoop, calls=%fused_computation.67 | loop fusion | flops 440000 | bytes 1040001 | tf_op jit(solution)/shard_map/convert_element_type | solution.py:143
  22.1 1.0 %collective-permute-start.3 = (bf16[25,1600]{1,0:T(8,128)(2,1)S(1)}, bf16[25,1600]{1,0:T(8,128)(2,1)S(1)}, u32[]{:S(2)}, u32[]{:S(2)}) collective-permute-start(bf16[25,1600]{1,0:T(8,128)(2,1)S(1)} %get-tuple-element.14), channel_id=1, source_target_pairs={{0,129},{1,128},{2,131},{3,130},{4,133},{5,132},{6,135},{7,134},{8... | collective-permute-start | bytes 240008 | tf_op jit(solution)/shard_map/ppermute | solution.py:63
  23.2 4.3 %collective-permute-done.3 = bf16[25,1600]{1,0:T(8,128)(2,1)S(1)} collective-permute-done((bf16[25,1600]{1,0:T(8,128)(2,1)S(1)}, bf16[25,1600]{1,0:T(8,128)(2,1)S(1)}, u32[]{:S(2)}, u32[]{:S(2)}) %collective-permute-start.3) | collective-permute-done | bytes 80032 | tf_op jit(solution)/shard_map/ppermute | solution.py:63
  27.6 0.1 collective-permute-start.4
  27.6 0.1 constant_dynamic-slice_fusion
  27.8 2.1 %collective-permute-start.6 = (bf16[50,832]{1,0:T(8,128)(2,1)S(1)}, bf16[50,832]{1,0:T(8,128)(2,1)S(1)}, u32[]{:S(2)}, u32[]{:S(2)}) collective-permute-start(bf16[50,832]{1,0:T(8,128)(2,1)S(1)} %constant_dynamic-slice_fusion), channel_id=1, source_target_pairs={{0,4},{1,5},{2,6},{3,7},{4,0},{5,1},{6,2},{7,3},{8,12},{9,13},{10,... | collective-permute-start | bytes 249608 | tf_op jit(solution)/shard_map/ppermute | solution.py:78
  30.0 3.9 %collective-permute-done.6 = bf16[50,832]{1,0:T(8,128)(2,1)S(1)} collective-permute-done((bf16[50,832]{1,0:T(8,128)(2,1)S(1)}, bf16[50,832]{1,0:T(8,128)(2,1)S(1)}, u32[]{:S(2)}, u32[]{:S(2)}) %collective-permute-start.6) | collective-permute-done | bytes 83232 | tf_op jit(solution)/shard_map/ppermute | solution.py:78
  33.8 2.5 %collective-permute-start.7 = (bf16[50,832]{1,0:T(8,128)(2,1)S(1)}, bf16[50,832]{1,0:T(8,128)(2,1)S(1)}, u32[]{:S(2)}, u32[]{:S(2)}) collective-permute-start(bf16[50,832]{1,0:T(8,128)(2,1)S(1)} %collective-permute-done.6), channel_id=1, source_target_pairs={{0,64},{64,0},{128,192},{192,128},{1,65},{65,1},{129,193},{193,129... | collective-permute-start | bytes 249608 | tf_op jit(solution)/shard_map/ppermute | solution.py:82
  36.3 0.1 collective-permute-start.5
  36.4 0.8 collective-permute-done.7
  37.3 0.5 collective-permute-done.5
  37.9 0.1 pad_maximum_fusion
  38.0 0.7 gather_fusion
  38.7 0.3 gather.10
  39.0 2.8 %broadcast_in_dim.26 = bf16[1600,1600]{1,0:T(8,128)(2,1)} broadcast(bf16[]{:T(256)} %constant.137.clone.1), dimensions={} | broadcast | bytes 5120002 | tf_op jit(solution)/shard_map/broadcast_in_dim | solution.py:100
  41.8 1.0 %constant_dynamic-update-slice_fusion.6 = (bf16[1600,1600]{1,0:T(8,128)(2,1)}, bf16[200,1600]{1,0:T(8,128)(2,1)S(1)}) fusion(bf16[1600,1600]{1,0:T(8,128)(2,1)} %broadcast_in_dim.26, s32[]{:T(128)S(6)} %select_n.220, bf16[200,1600]{1,0:T(8,128)(2,1)S(1)} %gather.10, pred[200]{0:T(512)(128)(4,1)S(1)} %broadcast_in_dim.28), kind=kLoop, calls=%fused_computation.46 | loop fusion | flops 320000 | bytes 1945804 | tf_op jit(solution)/shard_map/dynamic_update_slice | solution.py:100
  42.8 1.7 %collective-permute-start.8 = (bf16[200,768]{1,0:T(8,128)(2,1)S(1)}, bf16[200,768]{1,0:T(8,128)(2,1)S(1)}, u32[]{:S(2)}, u32[]{:S(2)}) collective-permute-start(bf16[200,768]{1,0:T(8,128)(2,1)S(1)} %slice.42), channel_id=1, source_target_pairs={{0,56},{1,57},{2,58},{3,59},{4,60},{5,61},{6,62},{7,63},{8,0},{9,1... | collective-permute-start | bytes 921608 | tf_op jit(solution)/shard_map/ppermute | solution.py:103
  44.6 1.9 %collective-permute-start.10 = (bf16[200,832]{1,0:T(8,128)(2,1)S(1)}, bf16[200,832]{1,0:T(8,128)(2,1)S(1)}, u32[]{:S(2)}, u32[]{:S(2)}) collective-permute-start(bf16[200,832]{1,0:T(8,128)(2,1)S(1)} %slice.43), channel_id=1, source_target_pairs={{0,56},{1,57},{2,58},{3,59},{4,60},{5,61},{6,62},{7,63},{8,0},{9,1... | collective-permute-start | bytes 998408 | tf_op jit(solution)/shard_map/ppermute | solution.py:103
  46.5 0.9 fusion.14
  47.5 5.2 %collective-permute-done.8 = bf16[200,768]{1,0:T(8,128)(2,1)S(1)} collective-permute-done((bf16[200,768]{1,0:T(8,128)(2,1)S(1)}, bf16[200,768]{1,0:T(8,128)(2,1)S(1)}, u32[]{:S(2)}, u32[]{:S(2)}) %collective-permute-start.8) | collective-permute-done | bytes 307232 | tf_op jit(solution)/shard_map/ppermute | solution.py:103
  52.7 0.5 collective-permute-start.9
  53.3 2.0 %multiply_subtract_fusion = (f32[100,1600]{1,0:T(8,128)}, f32[100,1600]{1,0:T(8,128)}) fusion(f32[100,1600]{1,0:T(8,128)S(1)} %copy-done.1, f32[100,1600]{1,0:T(8,128)S(1)} %copy-done.3, f32[1600,64]{0,1:T(8,128)S(1)} %copy-done, f32[100,64]{0,1:T(8,128)S(1)} %fusion.14, f32[100,64]{0,1:T(8,128)S(1)} %collective-permute-done.25, ...), kind=kOutput, calls=%fused_computation.4 | convolution fusion | flops 123859200 | bytes 3188736 | tf_op jit(solution)/shard_map/dot_general | solution.py:137
  55.2 1.3 %collective-permute-done.10 = bf16[200,832]{1,0:T(8,128)(2,1)S(1)} collective-permute-done((bf16[200,832]{1,0:T(8,128)(2,1)S(1)}, bf16[200,832]{1,0:T(8,128)(2,1)S(1)}, u32[]{:S(2)}, u32[]{:S(2)}) %collective-permute-start.10) | collective-permute-done | bytes 332832 | tf_op jit(solution)/shard_map/ppermute | solution.py:103
  56.6 2.4 %collective-permute-start.11 = (bf16[200,832]{1,0:T(8,128)(2,1)S(1)}, bf16[200,832]{1,0:T(8,128)(2,1)S(1)}, u32[]{:S(2)}, u32[]{:S(2)}) collective-permute-start(bf16[200,832]{1,0:T(8,128)(2,1)S(1)} %collective-permute-done.10), channel_id=1, source_target_pairs={{0,64},{64,0},{128,192},{192,128},{1,65},{65,1},{129,193},{193,129... | collective-permute-start | bytes 998408 | tf_op jit(solution)/shard_map/ppermute | solution.py:104
  58.9 0.7 constant_dynamic-update-slice_fusion.5
  59.7 1.3 %collective-permute-done.12 = bf16[200,768]{1,0:T(8,128)(2,1)S(1)} collective-permute-done((bf16[200,768]{1,0:T(8,128)(2,1)S(1)}, bf16[200,768]{1,0:T(8,128)(2,1)S(1)}, u32[]{:S(2)}, u32[]{:S(2)}) %collective-permute-start.12) | collective-permute-done | bytes 307232 | tf_op jit(solution)/shard_map/ppermute | solution.py:103
  60.9 0.6 collective-permute-start.13
  61.6 0.7 constant_dynamic-update-slice_fusion.4
  62.3 0.8 constant_dynamic-update-slice_fusion.12
  63.1 3.3 %collective-permute-done.14 = bf16[200,832]{1,0:T(8,128)(2,1)S(1)} collective-permute-done((bf16[200,832]{1,0:T(8,128)(2,1)S(1)}, bf16[200,832]{1,0:T(8,128)(2,1)S(1)}, u32[]{:S(2)}, u32[]{:S(2)}) %collective-permute-start.14) | collective-permute-done | bytes 332832 | tf_op jit(solution)/shard_map/ppermute | solution.py:103
  66.4 0.1 collective-permute-start.15
  66.6 0.8 constant_dynamic-update-slice_fusion.11
  67.3 0.7 constant_dynamic-update-slice_fusion.3
  68.1 1.6 %collective-permute-done.16 = bf16[200,768]{1,0:T(8,128)(2,1)S(1)} collective-permute-done((bf16[200,768]{1,0:T(8,128)(2,1)S(1)}, bf16[200,768]{1,0:T(8,128)(2,1)S(1)}, u32[]{:S(2)}, u32[]{:S(2)}) %collective-permute-start.16) | collective-permute-done | bytes 307232 | tf_op jit(solution)/shard_map/ppermute | solution.py:103
  69.7 1.2 %collective-permute-start.17 = (bf16[200,768]{1,0:T(8,128)(2,1)S(1)}, bf16[200,768]{1,0:T(8,128)(2,1)S(1)}, u32[]{:S(2)}, u32[]{:S(2)}) collective-permute-start(bf16[200,768]{1,0:T(8,128)(2,1)S(1)} %collective-permute-done.16), channel_id=1, source_target_pairs={{0,64},{64,0},{128,192},{192,128},{1,65},{65,1},{129,193},{193,129... | collective-permute-start | bytes 921608 | tf_op jit(solution)/shard_map/ppermute | solution.py:104
  70.9 0.7 collective-permute-start.20
  71.6 0.7 constant_dynamic-update-slice_fusion.2
  72.4 0.8 constant_dynamic-update-slice_fusion.10
  73.1 0.9 collective-permute-done.18
  74.0 2.5 %collective-permute-start.19 = (bf16[200,832]{1,0:T(8,128)(2,1)S(1)}, bf16[200,832]{1,0:T(8,128)(2,1)S(1)}, u32[]{:S(2)}, u32[]{:S(2)}) collective-permute-start(bf16[200,832]{1,0:T(8,128)(2,1)S(1)} %collective-permute-done.18), channel_id=1, source_target_pairs={{0,64},{64,0},{128,192},{192,128},{1,65},{65,1},{129,193},{193,129... | collective-permute-start | bytes 998408 | tf_op jit(solution)/shard_map/ppermute | solution.py:104
  76.5 1.9 %collective-permute-start.22 = (bf16[200,832]{1,0:T(8,128)(2,1)S(1)}, bf16[200,832]{1,0:T(8,128)(2,1)S(1)}, u32[]{:S(2)}, u32[]{:S(2)}) collective-permute-start(bf16[200,832]{1,0:T(8,128)(2,1)S(1)} %collective-permute-done.18), channel_id=1, source_target_pairs={{64,72},{65,73},{66,74},{67,75},{68,76},{69,77},{70,78},{71,79},{7... | collective-permute-start | bytes 998408 | tf_op jit(solution)/shard_map/ppermute | solution.py:114
  78.5 0.8 constant_dynamic-update-slice_fusion.9
  79.2 0.7 constant_dynamic-update-slice_fusion.1
  80.0 1.3 %collective-permute-start.21 = (bf16[200,768]{1,0:T(8,128)(2,1)S(1)}, bf16[200,768]{1,0:T(8,128)(2,1)S(1)}, u32[]{:S(2)}, u32[]{:S(2)}) collective-permute-start(bf16[200,768]{1,0:T(8,128)(2,1)S(1)} %collective-permute-done.20), channel_id=1, source_target_pairs={{0,64},{128,192},{1,65},{129,193},{2,66},{130,194},{3,67},{131,195... | collective-permute-start | bytes 921608 | tf_op jit(solution)/shard_map/ppermute | solution.py:115
  81.3 0.7 constant_dynamic-update-slice_fusion
  82.0 0.8 constant_dynamic-update-slice_fusion.8
  82.8 3.1 %collective-permute-done.22 = bf16[200,832]{1,0:T(8,128)(2,1)S(1)} collective-permute-done((bf16[200,832]{1,0:T(8,128)(2,1)S(1)}, bf16[200,832]{1,0:T(8,128)(2,1)S(1)}, u32[]{:S(2)}, u32[]{:S(2)}) %collective-permute-start.22) | collective-permute-done | bytes 332832 | tf_op jit(solution)/shard_map/ppermute | solution.py:114
  85.9 1.3 %collective-permute-start.23 = (bf16[200,832]{1,0:T(8,128)(2,1)S(1)}, bf16[200,832]{1,0:T(8,128)(2,1)S(1)}, u32[]{:S(2)}, u32[]{:S(2)}) collective-permute-start(bf16[200,832]{1,0:T(8,128)(2,1)S(1)} %collective-permute-done.22), channel_id=1, source_target_pairs={{64,0},{192,128},{65,1},{193,129},{66,2},{194,130},{67,3},{195,131... | collective-permute-start | bytes 998408 | tf_op jit(solution)/shard_map/ppermute | solution.py:116
  87.2 0.8 constant_dynamic-update-slice_fusion.7
  88.0 0.8 select_dynamic-update-slice_fusion.1
  88.8 0.8 select_dynamic-update-slice_fusion
  (48 shorter events, 0.9 us)
Async XLA Ops:
  0.6 7.0 %copy-start = (f32[1600,64]{0,1:T(8,128)S(1)}, f32[1600,64]{0,1:T(8,128)}, u32[]{:S(2)}) copy-start(f32[1600,64]{0,1:T(8,128)} %param.15) | copy-start | bytes 1228804
  2.4 17.9 %copy-start.2 = (f32[25,1600]{1,0:T(8,128)S(1)}, f32[25,1600]{1,0:T(8,128)}, u32[]{:S(2)}) copy-start(f32[25,1600]{1,0:T(8,128)} %param.10) | copy-start | bytes 480004
  2.4 10.1 %collective-permute-start = (f32[25,1600]{1,0:T(8,128)}, f32[25,1600]{1,0:T(8,128)}, u32[]{:S(2)}, u32[]{:S(2)}) collective-permute-start(f32[25,1600]{1,0:T(8,128)} %bitcast_subtract_fusion), channel_id=1, source_target_pairs={{0,64},{64,0},{128,192},{192,128},{1,65},{65,1},{129,193},{193,129... | collective-permute-start | bytes 480008 | tf_op jit(solution)/shard_map/ppermute | solution.py:37
  11.5 11.6 %collective-permute-start.24 = (f32[2,100,64]{1,2,0:T(8,128)S(1)}, f32[2,100,64]{1,2,0:T(8,128)S(1)}, u32[]{:S(2)}, u32[]{:S(2)}) collective-permute-start(f32[2,100,64]{1,2,0:T(8,128)S(1)} %broadcast_select_fusion.1), channel_id=1, source_target_pairs={{0,64},{64,0},{128,192},{192,128},{1,65},{65,1},{129,193},{193,129... | collective-permute-start | bytes 153608 | tf_op jit(solution)/shard_map/ppermute | solution.py:132
  13.6 4.3 %collective-permute-start.1 = (f32[25,832]{1,0:T(8,128)S(1)}, f32[25,832]{1,0:T(8,128)S(1)}, u32[]{:S(2)}, u32[]{:S(2)}) collective-permute-start(f32[25,832]{1,0:T(8,128)S(1)} %dynamic-slice_add_fusion), channel_id=1, source_target_pairs={{0,128},{64,192},{128,0},{192,64},{1,129},{65,193},{129,1},{193,65... | collective-permute-start | bytes 249608 | tf_op jit(solution)/shard_map/ppermute | solution.py:42
  17.9 2.4 %collective-permute-start.2 = (f32[25,832]{1,0:T(8,128)S(1)}, f32[25,832]{1,0:T(8,128)S(1)}, u32[]{:S(2)}, u32[]{:S(2)}) collective-permute-start(f32[25,832]{1,0:T(8,128)S(1)} %add.143), channel_id=1, source_target_pairs={{0,64},{64,0},{128,192},{192,128},{1,65},{65,1},{129,193},{193,129... | collective-permute-start | bytes 249608 | tf_op jit(solution)/shard_map/ppermute | solution.py:44
  22.1 5.4 %collective-permute-start.3 = (bf16[25,1600]{1,0:T(8,128)(2,1)S(1)}, bf16[25,1600]{1,0:T(8,128)(2,1)S(1)}, u32[]{:S(2)}, u32[]{:S(2)}) collective-permute-start(bf16[25,1600]{1,0:T(8,128)(2,1)S(1)} %get-tuple-element.14), channel_id=1, source_target_pairs={{0,129},{1,128},{2,131},{3,130},{4,133},{5,132},{6,135},{7,134},{8... | collective-permute-start | bytes 240008 | tf_op jit(solution)/shard_map/ppermute | solution.py:63
  27.6 8.8 %collective-permute-start.4 = (bf16[50,1600]{1,0:T(8,128)(2,1)S(1)}, bf16[50,1600]{1,0:T(8,128)(2,1)S(1)}, u32[]{:S(2)}, u32[]{:S(2)}) collective-permute-start(bf16[50,1600]{1,0:T(8,128)(2,1)S(1)} %maximum_select_fusion.2), channel_id=1, source_target_pairs={{0,6},{1,7},{2,0},{3,1},{4,2},{5,3},{6,4},{7,5},{8,14},{9,15},{10,... | collective-permute-start | bytes 480008 | tf_op jit(solution)/shard_map/ppermute | solution.py:77
  27.8 6.1 %collective-permute-start.6 = (bf16[50,832]{1,0:T(8,128)(2,1)S(1)}, bf16[50,832]{1,0:T(8,128)(2,1)S(1)}, u32[]{:S(2)}, u32[]{:S(2)}) collective-permute-start(bf16[50,832]{1,0:T(8,128)(2,1)S(1)} %constant_dynamic-slice_fusion), channel_id=1, source_target_pairs={{0,4},{1,5},{2,6},{3,7},{4,0},{5,1},{6,2},{7,3},{8,12},{9,13},{10,... | collective-permute-start | bytes 249608 | tf_op jit(solution)/shard_map/ppermute | solution.py:78
  33.8 3.4 %collective-permute-start.7 = (bf16[50,832]{1,0:T(8,128)(2,1)S(1)}, bf16[50,832]{1,0:T(8,128)(2,1)S(1)}, u32[]{:S(2)}, u32[]{:S(2)}) collective-permute-start(bf16[50,832]{1,0:T(8,128)(2,1)S(1)} %collective-permute-done.6), channel_id=1, source_target_pairs={{0,64},{64,0},{128,192},{192,128},{1,65},{65,1},{129,193},{193,129... | collective-permute-start | bytes 249608 | tf_op jit(solution)/shard_map/ppermute | solution.py:82
  36.3 1.5 %collective-permute-start.5 = (bf16[50,1600]{1,0:T(8,128)(2,1)S(1)}, bf16[50,1600]{1,0:T(8,128)(2,1)S(1)}, u32[]{:S(2)}, u32[]{:S(2)}) collective-permute-start(bf16[50,1600]{1,0:T(8,128)(2,1)S(1)} %collective-permute-done.4), channel_id=1, source_target_pairs={{0,64},{64,0},{128,192},{192,128},{1,65},{65,1},{129,193},{193,129... | collective-permute-start | bytes 480008 | tf_op jit(solution)/shard_map/ppermute | solution.py:81
  38.7 7.8 %copy-start.1 = (f32[100,1600]{1,0:T(8,128)S(1)}, f32[100,1600]{1,0:T(8,128)}, u32[]{:S(2)}) copy-start(f32[100,1600]{1,0:T(8,128)} %param.13) | copy-start | bytes 1920004
  39.0 14.3 %copy-start.3 = (f32[100,1600]{1,0:T(8,128)S(1)}, f32[100,1600]{1,0:T(8,128)}, u32[]{:S(2)}) copy-start(f32[100,1600]{1,0:T(8,128)} %param.14) | copy-start | bytes 1920004
  42.8 9.9 %collective-permute-start.8 = (bf16[200,768]{1,0:T(8,128)(2,1)S(1)}, bf16[200,768]{1,0:T(8,128)(2,1)S(1)}, u32[]{:S(2)}, u32[]{:S(2)}) collective-permute-start(bf16[200,768]{1,0:T(8,128)(2,1)S(1)} %slice.42), channel_id=1, source_target_pairs={{0,56},{1,57},{2,58},{3,59},{4,60},{5,61},{6,62},{7,63},{8,0},{9,1... | collective-permute-start | bytes 921608 | tf_op jit(solution)/shard_map/ppermute | solution.py:103
  44.5 8.7 %collective-permute-start.25 = (f32[100,64]{0,1:T(8,128)S(1)}, f32[100,64]{0,1:T(8,128)S(1)}, u32[]{:S(2)}, u32[]{:S(2)}) collective-permute-start(f32[100,64]{0,1:T(8,128)S(1)} %slice_bitcast_fusion.2), channel_id=1, source_target_pairs={{0,128},{64,192},{128,0},{192,64},{1,129},{65,193},{129,1},{193,65... | collective-permute-start | bytes 76808 | tf_op jit(solution)/shard_map/ppermute | solution.py:135
  44.6 12.0 %collective-permute-start.10 = (bf16[200,832]{1,0:T(8,128)(2,1)S(1)}, bf16[200,832]{1,0:T(8,128)(2,1)S(1)}, u32[]{:S(2)}, u32[]{:S(2)}) collective-permute-start(bf16[200,832]{1,0:T(8,128)(2,1)S(1)} %slice.43), channel_id=1, source_target_pairs={{0,56},{1,57},{2,58},{3,59},{4,60},{5,61},{6,62},{7,63},{8,0},{9,1... | collective-permute-start | bytes 998408 | tf_op jit(solution)/shard_map/ppermute | solution.py:103
  52.7 8.8 %collective-permute-start.9 = (bf16[200,768]{1,0:T(8,128)(2,1)S(1)}, bf16[200,768]{1,0:T(8,128)(2,1)S(1)}, u32[]{:S(2)}, u32[]{:S(2)}) collective-permute-start(bf16[200,768]{1,0:T(8,128)(2,1)S(1)} %collective-permute-done.8), channel_id=1, source_target_pairs={{0,64},{64,0},{128,192},{192,128},{1,65},{65,1},{129,193},{193,129... | collective-permute-start | bytes 921608 | tf_op jit(solution)/shard_map/ppermute | solution.py:104
  53.3 7.7 %collective-permute-start.12 = (bf16[200,768]{1,0:T(8,128)(2,1)S(1)}, bf16[200,768]{1,0:T(8,128)(2,1)S(1)}, u32[]{:S(2)}, u32[]{:S(2)}) collective-permute-start(bf16[200,768]{1,0:T(8,128)(2,1)S(1)} %collective-permute-done.8), channel_id=1, source_target_pairs={{0,56},{1,57},{2,58},{3,59},{4,60},{5,61},{6,62},{7,63},{8,0},{9,1... | collective-permute-start | bytes 921608 | tf_op jit(solution)/shard_map/ppermute | solution.py:103
  56.6 10.0 %collective-permute-start.11 = (bf16[200,832]{1,0:T(8,128)(2,1)S(1)}, bf16[200,832]{1,0:T(8,128)(2,1)S(1)}, u32[]{:S(2)}, u32[]{:S(2)}) collective-permute-start(bf16[200,832]{1,0:T(8,128)(2,1)S(1)} %collective-permute-done.10), channel_id=1, source_target_pairs={{0,64},{64,0},{128,192},{192,128},{1,65},{65,1},{129,193},{193,129... | collective-permute-start | bytes 998408 | tf_op jit(solution)/shard_map/ppermute | solution.py:104
  58.9 7.5 %collective-permute-start.14 = (bf16[200,832]{1,0:T(8,128)(2,1)S(1)}, bf16[200,832]{1,0:T(8,128)(2,1)S(1)}, u32[]{:S(2)}, u32[]{:S(2)}) collective-permute-start(bf16[200,832]{1,0:T(8,128)(2,1)S(1)} %collective-permute-done.10), channel_id=1, source_target_pairs={{0,56},{1,57},{2,58},{3,59},{4,60},{5,61},{6,62},{7,63},{8,0},{9,1... | collective-permute-start | bytes 998408 | tf_op jit(solution)/shard_map/ppermute | solution.py:103
  60.9 10.7 %collective-permute-start.13 = (bf16[200,768]{1,0:T(8,128)(2,1)S(1)}, bf16[200,768]{1,0:T(8,128)(2,1)S(1)}, u32[]{:S(2)}, u32[]{:S(2)}) collective-permute-start(bf16[200,768]{1,0:T(8,128)(2,1)S(1)} %collective-permute-done.12), channel_id=1, source_target_pairs={{0,64},{64,0},{128,192},{192,128},{1,65},{65,1},{129,193},{193,129... | collective-permute-start | bytes 921608 | tf_op jit(solution)/shard_map/ppermute | solution.py:104
  61.5 8.1 %collective-permute-start.16 = (bf16[200,768]{1,0:T(8,128)(2,1)S(1)}, bf16[200,768]{1,0:T(8,128)(2,1)S(1)}, u32[]{:S(2)}, u32[]{:S(2)}) collective-permute-start(bf16[200,768]{1,0:T(8,128)(2,1)S(1)} %collective-permute-done.12), channel_id=1, source_target_pairs={{0,56},{1,57},{2,58},{3,59},{4,60},{5,61},{6,62},{7,63},{8,0},{9,1... | collective-permute-start | bytes 921608 | tf_op jit(solution)/shard_map/ppermute | solution.py:103
  66.4 12.1 %collective-permute-start.15 = (bf16[200,832]{1,0:T(8,128)(2,1)S(1)}, bf16[200,832]{1,0:T(8,128)(2,1)S(1)}, u32[]{:S(2)}, u32[]{:S(2)}) collective-permute-start(bf16[200,832]{1,0:T(8,128)(2,1)S(1)} %collective-permute-done.14), channel_id=1, source_target_pairs={{0,64},{64,0},{128,192},{192,128},{1,65},{65,1},{129,193},{193,129... | collective-permute-start | bytes 998408 | tf_op jit(solution)/shard_map/ppermute | solution.py:104
  66.5 7.5 %collective-permute-start.18 = (bf16[200,832]{1,0:T(8,128)(2,1)S(1)}, bf16[200,832]{1,0:T(8,128)(2,1)S(1)}, u32[]{:S(2)}, u32[]{:S(2)}) collective-permute-start(bf16[200,832]{1,0:T(8,128)(2,1)S(1)} %collective-permute-done.14), channel_id=1, source_target_pairs={{0,56},{1,57},{2,58},{3,59},{4,60},{5,61},{6,62},{7,63},{8,0},{9,1... | collective-permute-start | bytes 998408 | tf_op jit(solution)/shard_map/ppermute | solution.py:103
  69.7 11.6 %collective-permute-start.17 = (bf16[200,768]{1,0:T(8,128)(2,1)S(1)}, bf16[200,768]{1,0:T(8,128)(2,1)S(1)}, u32[]{:S(2)}, u32[]{:S(2)}) collective-permute-start(bf16[200,768]{1,0:T(8,128)(2,1)S(1)} %collective-permute-done.16), channel_id=1, source_target_pairs={{0,64},{64,0},{128,192},{192,128},{1,65},{65,1},{129,193},{193,129... | collective-permute-start | bytes 921608 | tf_op jit(solution)/shard_map/ppermute | solution.py:104
  70.9 9.0 %collective-permute-start.20 = (bf16[200,768]{1,0:T(8,128)(2,1)S(1)}, bf16[200,768]{1,0:T(8,128)(2,1)S(1)}, u32[]{:S(2)}, u32[]{:S(2)}) collective-permute-start(bf16[200,768]{1,0:T(8,128)(2,1)S(1)} %collective-permute-done.16), channel_id=1, source_target_pairs={{0,56},{1,57},{2,58},{3,59},{4,60},{5,61},{6,62},{7,63},{8,0},{9,1... | collective-permute-start | bytes 921608 | tf_op jit(solution)/shard_map/ppermute | solution.py:113
  74.0 13.2 %collective-permute-start.19 = (bf16[200,832]{1,0:T(8,128)(2,1)S(1)}, bf16[200,832]{1,0:T(8,128)(2,1)S(1)}, u32[]{:S(2)}, u32[]{:S(2)}) collective-permute-start(bf16[200,832]{1,0:T(8,128)(2,1)S(1)} %collective-permute-done.18), channel_id=1, source_target_pairs={{0,64},{64,0},{128,192},{192,128},{1,65},{65,1},{129,193},{193,129... | collective-permute-start | bytes 998408 | tf_op jit(solution)/shard_map/ppermute | solution.py:104
  76.5 9.3 %collective-permute-start.22 = (bf16[200,832]{1,0:T(8,128)(2,1)S(1)}, bf16[200,832]{1,0:T(8,128)(2,1)S(1)}, u32[]{:S(2)}, u32[]{:S(2)}) collective-permute-start(bf16[200,832]{1,0:T(8,128)(2,1)S(1)} %collective-permute-done.18), channel_id=1, source_target_pairs={{64,72},{65,73},{66,74},{67,75},{68,76},{69,77},{70,78},{71,79},{7... | collective-permute-start | bytes 998408 | tf_op jit(solution)/shard_map/ppermute | solution.py:114
  80.0 8.0 %collective-permute-start.21 = (bf16[200,768]{1,0:T(8,128)(2,1)S(1)}, bf16[200,768]{1,0:T(8,128)(2,1)S(1)}, u32[]{:S(2)}, u32[]{:S(2)}) collective-permute-start(bf16[200,768]{1,0:T(8,128)(2,1)S(1)} %collective-permute-done.20), channel_id=1, source_target_pairs={{0,64},{128,192},{1,65},{129,193},{2,66},{130,194},{3,67},{131,195... | collective-permute-start | bytes 921608 | tf_op jit(solution)/shard_map/ppermute | solution.py:115
  85.9 2.9 %collective-permute-start.23 = (bf16[200,832]{1,0:T(8,128)(2,1)S(1)}, bf16[200,832]{1,0:T(8,128)(2,1)S(1)}, u32[]{:S(2)}, u32[]{:S(2)}) collective-permute-start(bf16[200,832]{1,0:T(8,128)(2,1)S(1)} %collective-permute-done.22), channel_id=1, source_target_pairs={{64,0},{192,128},{65,1},{193,129},{66,2},{194,130},{67,3},{195,131... | collective-permute-start | bytes 998408 | tf_op jit(solution)/shard_map/ppermute | solution.py:116
